TPU v7x, 256 devices: a whole 4x4x8 slice. The times are simulated.
256 devices in a mesh: lat: 32 (over x, z_lo, core), lev: 8 (over y, z_hi).
Axes of the slice: x: 4, y: 4, z: 8 (z_hi: 2, z_lo: 4; z = z_hi * 4 + z_lo), core: 2. Of those that a mesh axis runs over, the one named last changes fastest.
Arguments:
- zonal_wind: float32 [32, 512, 2880], P('lev', 'lat'), may hold values from -6 to 6
- merid_wind: float32 [32, 512, 2880], P('lev', 'lat'), may hold values from -6 to 6
- tracer: float32 [32, 512, 2880], P('lev', 'lat'), may hold values from -6 to 6
- vertical_wind: float32 [32, 512, 2880], P('lev', 'lat'), may hold values from -6 to 6
- cutoff: int32 [512], replicated, may hold values from 1 to 1440, as said below
Outputs:
- zonal_next: float32 [32, 512, 2880], P('lev', 'lat')
- merid_next: float32 [32, 512, 2880], P('lev', 'lat')
- tracer_next: float32 [32, 512, 2880], P('lev', 'lat')
Inputs may be any that keep to these rules, and one draw needn't show every extreme that they name: With d the distance of latitude j in rows from the nearer pole (d = 1 for the first and last latitude): cutoff is 1 at d = 1, 719 at d = 80, between 1 and 719 for d < 80, and 1440 for d > 80.
All inputs are finite; a program needn't handle non-finite values.
Results may differ from a plain program's by a relative error of at most 0.0001.
Values sent between devices are 32-bit elements; how exact they have to be, the bound alone decides.
No kernel may reach another device: no remote copies, remote signals or barrier semaphores. Data moves between devices by JAX's collectives and lax.ppermute only.
A program may use at most 128 MiB of HBM per device.

v0:
```python
import math

import jax
import numpy as np
import jax.numpy as jnp
from jax import lax
from jax.sharding import PartitionSpec as P

NLON = 2880
KMAX = 720
HALF = NLON // 2

zonal_scale = 0.1
merid_scale = 0.1
vertical_scale = 0.1
mxu_precision = lax.Precision.HIGH


def shift(x, axis, up):
    size = lax.axis_size(axis)
    pairs = [(i, i + 1) for i in range(size - 1)]
    if not up:
        pairs = [(j, i) for i, j in pairs]
    return lax.ppermute(x, axis, pairs)


def split_angles(modes):
    low = 48
    m_lo = np.arange(low)[:, None]
    m_hi = (low * np.arange(HALF // low))[:, None]
    k = np.asarray(modes)[None, :]
    step = 2.0 * np.pi / NLON
    lo = (m_lo * k) % NLON * step
    hi = (m_hi * k) % NLON * step
    as_f32 = lambda v: jnp.asarray(v.astype(np.float32))
    return as_f32(np.cos(lo)), as_f32(np.sin(lo)), as_f32(np.cos(hi)), as_f32(np.sin(hi))


def parity_table(parity):
    modes = np.arange(parity, KMAX, 2)
    cos_lo, sin_lo, cos_hi, sin_hi = split_angles(modes)
    cos_lo, sin_lo = cos_lo[None], sin_lo[None]
    cos_hi, sin_hi = cos_hi[:, None], sin_hi[:, None]
    cosines = cos_lo * cos_hi - sin_lo * sin_hi
    sines = sin_lo * cos_hi + cos_lo * sin_hi
    return jnp.concatenate([cosines, sines], axis=-1).reshape(HALF, KMAX)


def parity_weight(parity, cut):
    modes = np.arange(parity, KMAX, 2)
    mode_ids = jnp.asarray(np.concatenate([modes, modes]).astype(np.int32))
    factor = jnp.where(mode_ids == 0, jnp.float32(1.0), jnp.float32(2.0)) / NLON
    return jnp.where(mode_ids[None, :] <= cut[:, None], factor[None, :], jnp.float32(0.0))


def lowpass_rows(x, cut, tables):
    even_table, odd_table = tables
    first, second = x[:, :HALF], x[:, HALF:]
    spec_even = jnp.dot(first + second, even_table, precision=mxu_precision,
                        preferred_element_type=jnp.float32)
    spec_odd = jnp.dot(first - second, odd_table, precision=mxu_precision,
                       preferred_element_type=jnp.float32)
    dims = (((1,), (1,)), ((), ()))
    even_out = lax.dot_general(spec_even * parity_weight(0, cut), even_table, dims,
                               precision=mxu_precision, preferred_element_type=jnp.float32)
    odd_out = lax.dot_general(spec_odd * parity_weight(1, cut), odd_table, dims,
                              precision=mxu_precision, preferred_element_type=jnp.float32)
    summed = jnp.concatenate([even_out + odd_out, even_out - odd_out], axis=1)
    return jnp.where((cut < HALF)[:, None], summed, x)


def filtered(x, cut, tables):
    shape = x.shape
    rows = x.reshape(-1, NLON)
    cuts = jnp.broadcast_to(cut, shape[:-1]).reshape(-1)
    out = lax.cond(jnp.any(cut < HALF), lambda: lowpass_rows(rows, cuts, tables), lambda: rows)
    return out.reshape(shape)


def on_device(zonal_wind, merid_wind, tracer, vertical_wind, cutoff):
    lat_rows = zonal_wind.shape[1]
    lat_count = lax.axis_size("lat")
    lat_index = lax.axis_index("lat")
    total_rows = lat_rows * lat_count
    row_start = lat_index * lat_rows
    own_cut = lax.dynamic_slice_in_dim(cutoff, row_start, lat_rows)
    halo_ids = jnp.stack([row_start - 1, row_start + lat_rows])
    halo_cut = cutoff[jnp.clip(halo_ids, 0, total_rows - 1)]

    stacked = jnp.stack([zonal_wind, merid_wind, tracer])
    levels = stacked.shape[1]
    top = jnp.concatenate([stacked[:, levels - 1], vertical_wind[levels - 1 :]], axis=0)
    bottom = jnp.concatenate([stacked[:, 0], vertical_wind[:1]], axis=0)
    below = shift(top, "lev", True)
    above = shift(bottom, "lev", False)
    south = shift(stacked[:, :, lat_rows - 1 :], "lat", True)
    north = shift(stacked[:, :, :1], "lat", False)

    tables = (parity_table(0), parity_table(1))
    field = filtered(stacked, own_cut, tables)
    lat_rows_raw = jnp.concatenate([south, north], axis=2).reshape(-1, NLON)
    lev_rows_raw = jnp.stack([below[:3], above[:3]], axis=1).reshape(-1, NLON)
    lat_cuts = jnp.broadcast_to(halo_cut, south.shape[:2] + (2,)).reshape(-1)
    lev_cuts = jnp.broadcast_to(own_cut, (3, 2, lat_rows)).reshape(-1)
    halo_rows = filtered(jnp.concatenate([lat_rows_raw, lev_rows_raw]),
                         jnp.concatenate([lat_cuts, lev_cuts]), tables)
    lat_count_rows = lat_rows_raw.shape[0]
    lat_halo = halo_rows[:lat_count_rows].reshape(3, levels, 2, NLON)
    lev_halo = halo_rows[lat_count_rows:].reshape(3, 2, lat_rows, NLON)

    vertical_pad = jnp.concatenate([below[3:], vertical_wind, above[3:]], axis=0)
    field_lat = jnp.concatenate([lat_halo[:, :, :1], field, lat_halo[:, :, 1:]], axis=2)
    field_lev = jnp.concatenate([lev_halo[:, :1], field, lev_halo[:, 1:]], axis=1)

    face_ids = (row_start + jnp.arange(lat_rows + 1, dtype=jnp.int32)).astype(jnp.float32)
    face_cos = jnp.sin(face_ids * (math.pi / total_rows))
    center_ids = (row_start + jnp.arange(lat_rows, dtype=jnp.int32)).astype(jnp.float32)
    center_cos = jnp.sin((center_ids + 0.5) * (math.pi / total_rows))
    zonal_now = field[0]
    east_wind = 0.5 * (zonal_now + jnp.roll(zonal_now, -1, axis=2))
    flux_x = zonal_scale * east_wind[None] * (0.5 * (field + jnp.roll(field, -1, axis=3)))
    div_x = flux_x - jnp.roll(flux_x, 1, axis=3)
    merid_lat = field_lat[1]
    north_wind = 0.5 * (merid_lat[:, :-1] + merid_lat[:, 1:])
    flux_y = (
        merid_scale
        * face_cos[None, None, :, None]
        * north_wind[None]
        * (0.5 * (field_lat[:, :, :-1] + field_lat[:, :, 1:]))
    )
    div_y = flux_y[:, :, 1:] - flux_y[:, :, :-1]
    upward = 0.5 * (vertical_pad[:-1] + vertical_pad[1:])
    flux_z = vertical_scale * upward[None] * (0.5 * (field_lev[:, :-1] + field_lev[:, 1:]))
    div_z = flux_z[:, 1:] - flux_z[:, :-1]
    updated = field - (div_x + div_y) / center_cos[None, None, :, None] - div_z
    return (updated[0], updated[1], updated[2])


def solution(mesh):
    in_specs = (
        P("lev", "lat", None),
        P("lev", "lat", None),
        P("lev", "lat", None),
        P("lev", "lat", None),
        P(),
    )
    out_specs = (P("lev", "lat", None), P("lev", "lat", None), P("lev", "lat", None))
    return jax.shard_map(
        on_device, mesh=mesh, in_specs=in_specs, out_specs=out_specs, check_vma=False
    )
```

profile of v0, /device:TPU:25, one launch (start us, length us, event | category | flops | bytes accessed | tf_op | source)
XLA Modules:
  0.0 117.7 jit_solution(13020851196188940173)
XLA Ops:
  0.6 1.8 %pad_maximum_fusion.2 = f32[3,4,16,2880]{3,2,0,1:T(8,128)S(1)} fusion(f32[1,4,16,2880]{3,2,0,1:T(8,128)} %bitcast.68, f32[1,4,16,2880]{3,2,0,1:T(8,128)} %bitcast.69, f32[1,4,16,2880]{3,2,0,1:T(8,128)} %bitcast.70), kind=kLoop, calls=%fused_computation.37 | loop fusion | flops 1105920 | bytes 4423680 | tf_op jit(solution)/shard_map/stack | solution.py:90
  2.6 0.9 pad_maximum_fusion.8
  3.5 9.0 %collective-permute-start.3 = (f32[4,16,2880]{2,1,0:T(8,128)}, f32[4,16,2880]{2,1,0:T(8,128)}, u32[]{:S(2)}, u32[]{:S(2)}) collective-permute-start(f32[4,16,2880]{2,1,0:T(8,128)} %pad_maximum_fusion.8), channel_id=1, source_target_pairs={{1,0},{2,1},{3,2},{4,3},{5,4},{6,5},{7,6},{9,8},{10,9},{11,10},{12... | collective-permute-start | bytes 2211848 | tf_op jit(solution)/shard_map/ppermute | solution.py:24
  12.5 0.9 pad_maximum_fusion.7
  13.4 2.0 %collective-permute-start.2 = (f32[4,16,2880]{2,1,0:T(8,128)}, f32[4,16,2880]{2,1,0:T(8,128)}, u32[]{:S(2)}, u32[]{:S(2)}) collective-permute-start(f32[4,16,2880]{2,1,0:T(8,128)} %pad_maximum_fusion.7), channel_id=1, source_target_pairs={{0,1},{1,2},{2,3},{3,4},{4,5},{5,6},{6,7},{8,9},{9,10},{10,11},{11... | collective-permute-start | bytes 2211848 | tf_op jit(solution)/shard_map/ppermute | solution.py:24
  15.4 0.9 fusion.27
  16.3 3.7 %collective-permute-start = (f32[3,4,1,2880]{3,2,0,1:T(1,128)}, f32[3,4,1,2880]{3,2,0,1:T(1,128)S(1)}, u32[]{:S(2)}, u32[]{:S(2)}) collective-permute-start(f32[3,4,1,2880]{3,2,0,1:T(1,128)} %get-tuple-element.79), channel_id=1, source_target_pairs={{0,8},{8,16},{16,24},{24,32},{32,40},{40,48},{48,56},{56,64},{64,7... | collective-permute-start | bytes 414728 | tf_op jit(solution)/shard_map/ppermute | solution.py:24
  20.1 1.9 %collective-permute-start.1 = (f32[3,4,1,2880]{3,2,0,1:T(1,128)}, f32[3,4,1,2880]{3,2,0,1:T(1,128)}, u32[]{:S(2)}, u32[]{:S(2)}) collective-permute-start(f32[3,4,1,2880]{3,2,0,1:T(1,128)} %get-tuple-element.80), channel_id=1, source_target_pairs={{8,0},{16,8},{24,16},{32,24},{40,32},{48,40},{56,48},{64,56},{72,6... | collective-permute-start | bytes 414728 | tf_op jit(solution)/shard_map/ppermute | solution.py:24
  22.2 0.4 copy-done
  22.7 0.7 compare_reduce_fusion.1
  24.1 0.5 multiply_subtract_fusion.1
  25.0 0.5 multiply_subtract_fusion
  25.5 5.2 %pad_maximum_fusion = (f32[1440,720]{1,0:T(8,128)}, f32[1440,720]{1,0:T(8,128)}) fusion(f32[1440,360]{1,0:T(8,128)S(1)} %bitcast.60, f32[1440,360]{1,0:T(8,128)S(1)} %bitcast.59, f32[1440,360]{1,0:T(8,128)S(1)} %bitcast.62, f32[1440,360]{1,0:T(8,128)S(1)} %bitcast.61), kind=kLoop, calls=%fused_computation.25 | loop fusion | flops 2073600 | bytes 16588800 | tf_op jit(solution)/shard_map/concatenate | solution.py:46
  30.7 14.1 %conditional.2 = (f32[192,2880]{1,0:T(8,128)S(1)}) conditional(s32[]{:T(128)} %convert_element_type.20, f32[192,2880]{1,0:T(8,128)S(1)} %bitcast.45, (s32[16]{0:T(128)S(1)}, f32[192,2880]{1,0:T(8,128)S(1)}, f32[1440,720]{1,0:T(8,128)}, s32[720]{0:T(1024)S(1)}, f32[1440,720]{1,0:T(8,128)}, /*index=5*/s32[720]{0:T(1024)S(1)}) %tuple.53), branch_computations={%region_1.2_spmd, %region_2.3_spmd} | conditional | flops 4780619776 | bytes 48159480 | solution.py:76
  30.8 4.3 %convolution_multiply_fusion = f32[192,720]{1,0:T(8,128)S(1)} fusion(f32[1440,720]{1,0:T(8,128)} %get-tuple-element.51, f32[192,2880]{1,0:T(8,128)S(1)} %get-tuple-element.48, f32[720]{0:T(1024)S(1)} %get-tuple-element.69, s32[720]{0:T(1024)S(1)} %get-tuple-element.52, s32[192]{0:T(256)S(1)} %reshape.169), kind=kOutput, calls=%fused_computation.2 | convolution fusion | flops 1195084800 | bytes 7068672 | tf_op jit(solution)/shard_map/cond/branch_1_fun/dot_general | solution.py:61
  35.1 4.4 %fusion.31 = f32[192,1440]{1,0:T(8,128)S(1)} fusion(f32[192,720]{1,0:T(8,128)S(1)} %convolution_multiply_fusion, f32[1440,720]{1,0:T(8,128)} %get-tuple-element.51), kind=kOutput, calls=%fused_computation.82 | convolution fusion | flops 1194393600 | bytes 5806080 | tf_op jit(solution)/shard_map/cond/branch_1_fun/dot_general | solution.py:66
  39.5 2.2 %convolution_multiply_fusion.1 = f32[192,720]{1,0:T(8,128)S(1)} fusion(f32[1440,720]{1,0:T(8,128)S(1)} %bitcast.55, f32[192,2880]{1,0:T(8,128)S(1)} %get-tuple-element.48, f32[720]{0:T(1024)S(1)} %get-tuple-element.70, s32[720]{0:T(1024)S(1)} %get-tuple-element.50, s32[192]{0:T(256)S(1)} %reshape.169), kind=kOutput, calls=%fused_computation.3 | convolution fusion | flops 1195084800 | bytes 7345152 | tf_op jit(solution)/shard_map/cond/branch_1_fun/dot_general | solution.py:59
  41.7 2.3 %fusion.25 = (f32[192,1440]{1,0:T(8,128)S(1)}, f32[192,1440]{1,0:T(8,128)S(1)}) fusion(f32[192,1440]{1,0:T(8,128)S(1)} %fusion.31, f32[192,720]{1,0:T(8,128)S(1)} %convolution_multiply_fusion.1, f32[1440,720]{1,0:T(8,128)S(1)} %bitcast.55), kind=kOutput, calls=%fused_computation.76 | convolution fusion | flops 1194946560 | bytes 8017920 | tf_op jit(solution)/shard_map/cond/branch_1_fun/dot_general | solution.py:64
  44.0 0.7 maximum_select_fusion
  44.8 1.1 slice.170
  45.9 2.0 %slice.167 = f32[3,4,16,2879]{3,2,1,0:T(8,128)} slice(f32[3,4,16,2880]{3,2,1,0:T(8,128)S(1)} %bitcast.47), slice={[0:3], [0:4], [0:16], [1:2880]} | slice | bytes 4422144 | tf_op jit(solution)/shard_map/jit(_roll_static)/slice | solution.py:121
  48.1 1.4 %fusion.23 = f32[4,16,2880]{2,1,0:T(8,128)S(1)} fusion(f32[4,16,2880]{2,1,0:T(8,128)S(1)} %bitcast.65, f32[4,16,1]{2,1,0:T(8,128)S(1)} %slice.171, f32[4,16,2879]{2,1,0:T(8,128)} %slice.170), kind=kLoop, calls=%fused_computation.59 | loop fusion | flops 552960 | bytes 2211840 | tf_op jit(solution)/shard_map/mul | solution.py:121
  49.9 1.6 %fusion.18 = f32[3,4,16,2880]{3,2,1,0:T(8,128)} fusion(f32[3,4,16,2880]{3,2,1,0:T(8,128)S(1)} %bitcast.49, f32[3,4,16,1]{3,2,1,0:T(8,128)S(1)} %slice.168, f32[3,4,16,2879]{3,2,1,0:T(8,128)S(1)} %copy-done.2, f32[4,16,2880]{2,1,0:T(8,128)S(1)} %fusion.23), kind=kLoop, calls=%fused_computation.39 | loop fusion | flops 1658880 | bytes 7372800 | tf_op jit(solution)/shard_map/mul | solution.py:121
  51.6 0.6 gather_fusion
  52.4 0.7 compare_reduce_fusion
  53.1 1.0 slice.172
  54.7 8.6 %collective-permute-done = f32[3,4,1,2880]{3,2,0,1:T(1,128)S(1)} collective-permute-done((f32[3,4,1,2880]{3,2,0,1:T(1,128)}, f32[3,4,1,2880]{3,2,0,1:T(1,128)S(1)}, u32[]{:S(2)}, u32[]{:S(2)}) %collective-permute-start) | collective-permute-done | bytes 138272 | tf_op jit(solution)/shard_map/ppermute | solution.py:24
  63.4 18.8 %collective-permute-done.1 = f32[3,4,1,2880]{3,2,0,1:T(1,128)} collective-permute-done((f32[3,4,1,2880]{3,2,0,1:T(1,128)}, f32[3,4,1,2880]{3,2,0,1:T(1,128)}, u32[]{:S(2)}, u32[]{:S(2)}) %collective-permute-start.1) | collective-permute-done | bytes 138272 | tf_op jit(solution)/shard_map/ppermute | solution.py:24
  82.2 1.2 pad_maximum_fusion.9
  83.6 1.1 slice_bitcast_fusion.3
  84.7 1.1 slice_bitcast_fusion.5
  86.0 1.2 %pad_maximum_fusion.3 = f32[120,2880]{1,0:T(8,128)} fusion(f32[96,2880]{1,0:T(8,128)S(1)} %bitcast.67, f32[24,2880]{1,0:T(8,128)S(1)} %reshape.182), kind=kLoop, calls=%fused_computation.45 | loop fusion | flops 345600 | bytes 2764800 | tf_op jit(solution)/shard_map/concatenate | solution.py:105
  87.2 16.9 %conditional.3 = (f32[120,2880]{1,0:T(8,128)}) conditional(s32[]{:T(128)} %convert_element_type.21, f32[120,2880]{1,0:T(8,128)} %pad_maximum_fusion.3, (s32[120]{0:T(128)S(1)}, f32[120,2880]{1,0:T(8,128)}, f32[1440,720]{1,0:T(8,128)}, s32[720]{0:T(1024)S(1)}, f32[1440,720]{1,0:T(8,128)}, /*index=5*/s32[720]{0:T(1024)S(1)}) %tuple.54), branch_computations={%region_4.5_spmd, %region_5.6_spmd} | conditional | flops 2987889152 | bytes 41404616 | solution.py:76
  87.3 4.3 %convolution_multiply_fusion.2 = f32[120,720]{1,0:T(8,128)S(1)} fusion(f32[1440,720]{1,0:T(8,128)} %get-tuple-element.57, f32[120,2880]{1,0:T(8,128)} %get-tuple-element.54, f32[720]{0:T(1024)S(1)} %get-tuple-element.74, s32[720]{0:T(1024)S(1)} %get-tuple-element.58, s32[120]{0:T(128)S(1)} %get-tuple-element.53), kind=kOutput, calls=%fused_computation.14 | convolution fusion | flops 746928000 | bytes 6250080 | tf_op jit(solution)/shard_map/cond/branch_1_fun/dot_general | solution.py:61
  91.5 4.4 %fusion.32 = f32[120,1440]{1,0:T(8,128)S(1)} fusion(f32[120,720]{1,0:T(8,128)S(1)} %convolution_multiply_fusion.2, f32[1440,720]{1,0:T(8,128)} %get-tuple-element.57), kind=kOutput, calls=%fused_computation.83 | convolution fusion | flops 746496000 | bytes 5184000 | tf_op jit(solution)/shard_map/cond/branch_1_fun/dot_general | solution.py:66
  96.0 3.0 %convolution_multiply_fusion.3 = f32[120,720]{1,0:T(8,128)S(1)} fusion(f32[1440,720]{1,0:T(8,128)S(1)} %bitcast.57, f32[120,2880]{1,0:T(8,128)} %get-tuple-element.54, f32[720]{0:T(1024)S(1)} %get-tuple-element.75, s32[720]{0:T(1024)S(1)} %get-tuple-element.56, s32[120]{0:T(128)S(1)} %get-tuple-element.53), kind=kOutput, calls=%fused_computation.15 | convolution fusion | flops 746928000 | bytes 5973600 | tf_op jit(solution)/shard_map/cond/branch_1_fun/dot_general | solution.py:59
  99.0 2.2 %fusion.26 = (f32[120,1440]{1,0:T(8,128)S(1)}, f32[120,1440]{1,0:T(8,128)S(1)}) fusion(f32[120,1440]{1,0:T(8,128)S(1)} %fusion.32, f32[120,720]{1,0:T(8,128)S(1)} %convolution_multiply_fusion.3, f32[1440,720]{1,0:T(8,128)S(1)} %bitcast.57), kind=kOutput, calls=%fused_computation.77 | convolution fusion | flops 746841600 | bytes 6566400 | tf_op jit(solution)/shard_map/cond/branch_1_fun/dot_general | solution.py:64
  101.3 2.9 %maximum_select_fusion.1 = f32[120,2880]{1,0:T(8,128)} fusion(f32[120,2880]{1,0:T(8,128)} %get-tuple-element.54, f32[120,1440]{1,0:T(8,128)S(1)} %get-tuple-element.72, f32[120,1440]{1,0:T(8,128)S(1)} %get-tuple-element.71, pred[120]{0:T(512)(128)(4,1)S(1)} %broadcast_compare_fusion.1), kind=kLoop, calls=%fused_computation.13 | loop fusion | flops 691200 | bytes 4147320 | tf_op jit(solution)/shard_map/cond/branch_1_fun/jit(_where)/select_n | solution.py:69
  104.2 1.7 %slice.180 = f32[24,2880]{1,0:T(8,128)} slice(f32[120,2880]{1,0:T(8,128)} %get-tuple-element.96), slice={[0:24], [0:2880]} | slice | bytes 552960 | tf_op jit(solution)/shard_map/slice | solution.py:108
  105.8 1.3 %slice.187 = f32[96,2880]{1,0:T(8,128)S(1)} slice(f32[120,2880]{1,0:T(8,128)} %get-tuple-element.96), slice={[24:120], [0:2880]} | slice | bytes 2211840 | tf_op jit(solution)/shard_map/slice | solution.py:109
  107.2 1.8 %reshape.184 = f32[3,4,2,2880]{3,2,1,0:T(2,128)} reshape(f32[24,2880]{1,0:T(8,128)} %slice.180) | data formatting | bytes 552960 | tf_op jit(solution)/shard_map/reshape | solution.py:108
  109.0 1.4 %fusion.30 = (f32[3,4,1,2880]{3,2,1,0:T(1,128)S(1)}, f32[3,4,1,2880]{3,2,1,0:T(1,128)S(1)}) fusion(f32[3,4,2,2880]{3,2,1,0:T(2,128)} %reshape.184), kind=kLoop, calls=%fused_computation.81 | loop fusion | bytes 552960 | tf_op jit(solution)/shard_map/slice | solution.py:112
  110.8 0.6 fusion.12
  111.5 1.0 slice.190
  112.4 0.9 slice.191
  113.8 1.3 %copy-done.1 = f32[3,4,16,2880]{3,2,1,0:T(8,128)S(1)} copy-done((f32[3,4,16,2880]{3,2,1,0:T(8,128)S(1)}, f32[3,4,16,2880]{3,2,1,0:T(8,128)}, u32[]{:S(2)}) %copy-start.1) | copy-done | bytes 2211864
  115.1 1.2 fusion.14
  116.3 1.4 %slice_bitcast_fusion = (f32[4,16,2880]{2,1,0:T(8,128)}, f32[4,16,2880]{2,1,0:T(8,128)}, f32[4,16,2880]{2,1,0:T(8,128)}) fusion(f32[3,4,16,2880]{3,2,1,0:T(8,128)S(1)} %fusion.14), kind=kLoop, calls=%fused_computation.55 | loop fusion | bytes 4423680 | tf_op jit(solution)/shard_map/squeeze | solution.py:136
  (69 shorter events, 3.0 us)
Async XLA Ops:
  0.6 1.9 %copy-start.3 = (f32[4,16,2880]{2,1,0:T(8,128)S(1)}, f32[4,16,2880]{2,1,0:T(8,128)}, u32[]{:S(2)}) copy-start(f32[4,16,2880]{2,1,0:T(8,128)} %param.24) | copy-start | bytes 2211844
  3.5 80.1 %collective-permute-start.3 = (f32[4,16,2880]{2,1,0:T(8,128)}, f32[4,16,2880]{2,1,0:T(8,128)}, u32[]{:S(2)}, u32[]{:S(2)}) collective-permute-start(f32[4,16,2880]{2,1,0:T(8,128)} %pad_maximum_fusion.8), channel_id=1, source_target_pairs={{1,0},{2,1},{3,2},{4,3},{5,4},{6,5},{7,6},{9,8},{10,9},{11,10},{12... | collective-permute-start | bytes 2211848 | tf_op jit(solution)/shard_map/ppermute | solution.py:24
  13.4 71.3 %collective-permute-start.2 = (f32[4,16,2880]{2,1,0:T(8,128)}, f32[4,16,2880]{2,1,0:T(8,128)}, u32[]{:S(2)}, u32[]{:S(2)}) collective-permute-start(f32[4,16,2880]{2,1,0:T(8,128)} %pad_maximum_fusion.7), channel_id=1, source_target_pairs={{0,1},{1,2},{2,3},{3,4},{4,5},{5,6},{6,7},{8,9},{9,10},{10,11},{11... | collective-permute-start | bytes 2211848 | tf_op jit(solution)/shard_map/ppermute | solution.py:24
  16.3 47.0 %collective-permute-start = (f32[3,4,1,2880]{3,2,0,1:T(1,128)}, f32[3,4,1,2880]{3,2,0,1:T(1,128)S(1)}, u32[]{:S(2)}, u32[]{:S(2)}) collective-permute-start(f32[3,4,1,2880]{3,2,0,1:T(1,128)} %get-tuple-element.79), channel_id=1, source_target_pairs={{0,8},{8,16},{16,24},{24,32},{32,40},{40,48},{48,56},{56,64},{64,7... | collective-permute-start | bytes 414728 | tf_op jit(solution)/shard_map/ppermute | solution.py:24
  20.1 62.1 %collective-permute-start.1 = (f32[3,4,1,2880]{3,2,0,1:T(1,128)}, f32[3,4,1,2880]{3,2,0,1:T(1,128)}, u32[]{:S(2)}, u32[]{:S(2)}) collective-permute-start(f32[3,4,1,2880]{3,2,0,1:T(1,128)} %get-tuple-element.80), channel_id=1, source_target_pairs={{8,0},{16,8},{24,16},{32,24},{40,32},{48,40},{56,48},{64,56},{72,6... | collective-permute-start | bytes 414728 | tf_op jit(solution)/shard_map/ppermute | solution.py:24
  22.0 0.7 copy-start
  22.0 2.0 %copy-start.7 = (f32[48,360]{1,0:T(8,128)S(1)}, f32[48,360]{1,0:T(8,128)}, u32[]{:S(2)}) copy-start(f32[48,360]{1,0:T(8,128)} %constant.100.clone) | copy-start | bytes 207364
  22.0 2.0 %copy-start.8 = (f32[48,360]{1,0:T(8,128)S(1)}, f32[48,360]{1,0:T(8,128)}, u32[]{:S(2)}) copy-start(f32[48,360]{1,0:T(8,128)} %constant.99.clone) | copy-start | bytes 207364
  22.0 2.0 %copy-start.13 = (f32[30,360]{1,0:T(8,128)S(1)}, f32[30,360]{1,0:T(8,128)}, u32[]{:S(2)}) copy-start(f32[30,360]{1,0:T(8,128)} %constant.101.clone) | copy-start | bytes 129604
  22.0 2.0 %copy-start.14 = (f32[30,360]{1,0:T(8,128)S(1)}, f32[30,360]{1,0:T(8,128)}, u32[]{:S(2)}) copy-start(f32[30,360]{1,0:T(8,128)} %constant.102.clone) | copy-start | bytes 129604
  24.1 0.9 copy-start.5
  24.1 0.9 copy-start.6
  24.1 0.9 copy-start.11
  24.1 0.9 copy-start.12
  25.5 5.2 %copy-start.9 = (s32[720]{0:T(1024)S(1)}, s32[720]{0:T(1024)}, u32[]{:S(2)}) copy-start(s32[720]{0:T(1024)} %constant.107.clone) | copy-start | bytes 8644
  25.5 5.2 %copy-start.10 = (s32[720]{0:T(1024)S(1)}, s32[720]{0:T(1024)}, u32[]{:S(2)}) copy-start(s32[720]{0:T(1024)} %constant.108.clone) | copy-start | bytes 8644
  30.8 8.7 %slice-start = ((s8[4423680]{0:T(1024)(128)(4,1)}), s8[4194304]{0:T(1024)(128)(4,1)S(1)}, s32[]{:S(2)}) async-start(s8[4423680]{0:T(1024)(128)(4,1)} %bitcast.54), calls=%async_computation | async-start | bytes 8388608 | tf_op jit(solution)/shard_map/cond
  30.8 8.7 %slice-start.1 = ((s8[4423680]{0:T(1024)(128)(4,1)}), s8[229376]{0:T(1024)(128)(4,1)S(1)}, s32[]{:S(2)}) async-start(s8[4423680]{0:T(1024)(128)(4,1)} %bitcast.54), calls=%async_computation.1 | async-start | bytes 458752 | tf_op jit(solution)/shard_map/cond
  48.0 1.9 %copy-start.2 = (f32[3,4,16,2879]{3,2,1,0:T(8,128)S(1)}, f32[3,4,16,2879]{3,2,1,0:T(8,128)}, u32[]{:S(2)}) copy-start(f32[3,4,16,2879]{3,2,1,0:T(8,128)} %slice.167) | copy-start | bytes 6633220
  87.2 8.7 %slice-start.2 = ((s8[4423680]{0:T(1024)(128)(4,1)}), s8[4194304]{0:T(1024)(128)(4,1)S(1)}, s32[]{:S(2)}) async-start(s8[4423680]{0:T(1024)(128)(4,1)} %bitcast.56), calls=%async_computation.2 | async-start | bytes 8388608 | tf_op jit(solution)/shard_map/cond
  87.3 8.7 %slice-start.3 = ((s8[4423680]{0:T(1024)(128)(4,1)}), s8[229376]{0:T(1024)(128)(4,1)S(1)}, s32[]{:S(2)}) async-start(s8[4423680]{0:T(1024)(128)(4,1)} %bitcast.56), calls=%async_computation.3 | async-start | bytes 458752 | tf_op jit(solution)/shard_map/cond
  111.4 2.0 %copy-start.4 = (f32[4,16,2880]{2,1,0:T(8,128)S(1)}, f32[4,16,2880]{2,1,0:T(8,128)}, u32[]{:S(2)}) copy-start(f32[4,16,2880]{2,1,0:T(8,128)} %param.24) | copy-start | bytes 2211844
  113.5 1.6 %copy-start.1 = (f32[3,4,16,2880]{3,2,1,0:T(8,128)S(1)}, f32[3,4,16,2880]{3,2,1,0:T(8,128)}, u32[]{:S(2)}) copy-start(f32[3,4,16,2880]{3,2,1,0:T(8,128)} %fusion.18) | copy-start | bytes 6635524
where the time goes:
time: 119 us; the launch traced here: 118 us
  waiting for transfers between devices  27.4 us (23%)
  matrix products  27.1 us (23%)
  other arithmetic  23 us (19%)
  local copies, waits for them, and re-layouts  21 us (18%)
  starting transfers between devices  16.6 us (14%)
  between operations  2.33 us (2%)
    ppermute x4, waiting for transfers between devices, shift(): return lax.ppermute(x, axis, pairs)  27.4 us
    ppermute x4, starting transfers between devices, shift(): return lax.ppermute(x, axis, pairs)  16.6 us
    dot_general x2, matrix products, lowpass_rows(): lax.dot_general(spec_odd * parity_weight(1, cut), odd_table, dims, precis...  8.77 us
    dot_general x2, matrix products, lowpass_rows(): jnp.dot(first - second, odd_table, precision=mxu_precision, preferred_ele...  8.57 us
    dot_general x2, matrix products, lowpass_rows(): jnp.dot(first + second, even_table, precision=mxu_precision, preferred_el...  5.22 us
    concatenate x1, other arithmetic, parity_table(): return jnp.concatenate([cosines, sines], axis=-1).reshape(HALF, KMAX)  5.17 us
    dot_general x2, matrix products, lowpass_rows(): lax.dot_general(spec_even * parity_weight(0, cut), even_table, dims, prec...  4.55 us
    select_n x2, other arithmetic, lowpass_rows(): return jnp.where((cut < HALF)[:, None], summed, x)  3.58 us
  transfers between devices with their start and end apart: 4, of which 2 were waited for; matrix products, arithmetic and copies ran while one was open for 29% of the time, Pallas kernels for 0%

commit v1 on v0

--- a/solution.py
+++ b/solution.py
@@ -56,14 +56,15 @@
 def lowpass_rows(x, cut, tables):
     even_table, odd_table = tables
     first, second = x[:, :HALF], x[:, HALF:]
-    spec_even = jnp.dot(first + second, even_table, precision=mxu_precision,
-                        preferred_element_type=jnp.float32)
-    spec_odd = jnp.dot(first - second, odd_table, precision=mxu_precision,
-                       preferred_element_type=jnp.float32)
-    dims = (((1,), (1,)), ((), ()))
-    even_out = lax.dot_general(spec_even * parity_weight(0, cut), even_table, dims,
+    forward = (((0,), (1,)), ((), ()))
+    spec_even = lax.dot_general(even_table, first + second, forward, precision=mxu_precision,
+                                preferred_element_type=jnp.float32)
+    spec_odd = lax.dot_general(odd_table, first - second, forward, precision=mxu_precision,
+                               preferred_element_type=jnp.float32)
+    inverse = (((0,), (1,)), ((), ()))
+    even_out = lax.dot_general(spec_even * parity_weight(0, cut).T, even_table, inverse,
                                precision=mxu_precision, preferred_element_type=jnp.float32)
-    odd_out = lax.dot_general(spec_odd * parity_weight(1, cut), odd_table, dims,
+    odd_out = lax.dot_general(spec_odd * parity_weight(1, cut).T, odd_table, inverse,
                               precision=mxu_precision, preferred_element_type=jnp.float32)
     summed = jnp.concatenate([even_out + odd_out, even_out - odd_out], axis=1)
     return jnp.where((cut < HALF)[:, None], summed, x)

time: 119 us -> 119 us (level)
  no operation moved by 1% of the time
where the time goes in v1:
time: 119 us; the launch traced here: 118 us
  waiting for transfers between devices  27.4 us (23%)
  matrix products  27.1 us (23%)
  other arithmetic  23 us (19%)
  local copies, waits for them, and re-layouts  21 us (18%)
  starting transfers between devices  16.6 us (14%)
  between operations  2.33 us (2%)
    ppermute x4, waiting for transfers between devices, shift(): return lax.ppermute(x, axis, pairs)  27.4 us
    ppermute x4, starting transfers between devices, shift(): return lax.ppermute(x, axis, pairs)  16.6 us
    dot_general x2, matrix products, lowpass_rows(): lax.dot_general(spec_odd * parity_weight(1, cut).T, odd_table, inverse, p...  8.77 us
    dot_general x2, matrix products, lowpass_rows(): lax.dot_general(odd_table, first - second, forward, precision=mxu_precisi...  8.57 us
    dot_general x2, matrix products, lowpass_rows(): lax.dot_general(even_table, first + second, forward, precision=mxu_precis...  5.22 us
    concatenate x1, other arithmetic, parity_table(): return jnp.concatenate([cosines, sines], axis=-1).reshape(HALF, KMAX)  5.17 us
    dot_general x2, matrix products, lowpass_rows(): lax.dot_general(spec_even * parity_weight(0, cut).T, even_table, inverse,...  4.55 us
    select_n x2, other arithmetic, lowpass_rows(): return jnp.where((cut < HALF)[:, None], summed, x)  3.58 us
  transfers between devices with their start and end apart: 4, of which 2 were waited for; matrix products, arithmetic and copies ran while one was open for 29% of the time, Pallas kernels for 0%

profile of v1, /device:TPU:25, one launch (start us, length us, event | category | flops | bytes accessed | tf_op | source)
XLA Modules:
  0.0 117.7 jit_solution(865837145491322004)
XLA Ops:
  0.6 1.8 %pad_maximum_fusion.2 = f32[3,4,16,2880]{3,2,0,1:T(8,128)S(1)} fusion(f32[1,4,16,2880]{3,2,0,1:T(8,128)} %bitcast.84, f32[1,4,16,2880]{3,2,0,1:T(8,128)} %bitcast.85, f32[1,4,16,2880]{3,2,0,1:T(8,128)} %bitcast.86), kind=kLoop, calls=%fused_computation.41 | loop fusion | flops 1105920 | bytes 4423680 | tf_op jit(solution)/shard_map/stack | solution.py:91
  2.6 0.9 pad_maximum_fusion.8
  3.5 9.0 %collective-permute-start.3 = (f32[4,16,2880]{2,1,0:T(8,128)}, f32[4,16,2880]{2,1,0:T(8,128)}, u32[]{:S(2)}, u32[]{:S(2)}) collective-permute-start(f32[4,16,2880]{2,1,0:T(8,128)} %pad_maximum_fusion.8), channel_id=1, source_target_pairs={{1,0},{2,1},{3,2},{4,3},{5,4},{6,5},{7,6},{9,8},{10,9},{11,10},{12... | collective-permute-start | bytes 2211848 | tf_op jit(solution)/shard_map/ppermute | solution.py:24
  12.5 0.9 pad_maximum_fusion.7
  13.4 2.0 %collective-permute-start.2 = (f32[4,16,2880]{2,1,0:T(8,128)}, f32[4,16,2880]{2,1,0:T(8,128)}, u32[]{:S(2)}, u32[]{:S(2)}) collective-permute-start(f32[4,16,2880]{2,1,0:T(8,128)} %pad_maximum_fusion.7), channel_id=1, source_target_pairs={{0,1},{1,2},{2,3},{3,4},{4,5},{5,6},{6,7},{8,9},{9,10},{10,11},{11... | collective-permute-start | bytes 2211848 | tf_op jit(solution)/shard_map/ppermute | solution.py:24
  15.4 0.9 fusion.31
  16.3 3.7 %collective-permute-start = (f32[3,4,1,2880]{3,2,0,1:T(1,128)}, f32[3,4,1,2880]{3,2,0,1:T(1,128)S(1)}, u32[]{:S(2)}, u32[]{:S(2)}) collective-permute-start(f32[3,4,1,2880]{3,2,0,1:T(1,128)} %get-tuple-element.79), channel_id=1, source_target_pairs={{0,8},{8,16},{16,24},{24,32},{32,40},{40,48},{48,56},{56,64},{64,7... | collective-permute-start | bytes 414728 | tf_op jit(solution)/shard_map/ppermute | solution.py:24
  20.1 1.9 %collective-permute-start.1 = (f32[3,4,1,2880]{3,2,0,1:T(1,128)}, f32[3,4,1,2880]{3,2,0,1:T(1,128)}, u32[]{:S(2)}, u32[]{:S(2)}) collective-permute-start(f32[3,4,1,2880]{3,2,0,1:T(1,128)} %get-tuple-element.80), channel_id=1, source_target_pairs={{8,0},{16,8},{24,16},{32,24},{40,32},{48,40},{56,48},{64,56},{72,6... | collective-permute-start | bytes 414728 | tf_op jit(solution)/shard_map/ppermute | solution.py:24
  22.2 0.4 copy-done
  22.7 0.7 compare_reduce_fusion.1
  24.1 0.5 multiply_subtract_fusion
  25.0 0.5 multiply_subtract_fusion.1
  25.5 5.2 %pad_maximum_fusion = (f32[1440,720]{1,0:T(8,128)}, f32[1440,720]{1,0:T(8,128)}) fusion(f32[1440,360]{1,0:T(8,128)S(1)} %bitcast.78, f32[1440,360]{1,0:T(8,128)S(1)} %bitcast.77, f32[1440,360]{1,0:T(8,128)S(1)} %bitcast.76, f32[1440,360]{1,0:T(8,128)S(1)} %bitcast.75), kind=kLoop, calls=%fused_computation.29 | loop fusion | flops 2073600 | bytes 16588800 | tf_op jit(solution)/shard_map/concatenate | solution.py:46
  30.7 14.1 %conditional.2 = (f32[192,2880]{1,0:T(8,128)S(1)}) conditional(s32[]{:T(128)} %convert_element_type.20, f32[192,2880]{1,0:T(8,128)S(1)} %bitcast.61, (s32[16]{0:T(128)S(1)}, f32[192,2880]{1,0:T(8,128)S(1)}, f32[1440,720]{1,0:T(8,128)}, s32[720]{0:T(1024)S(1)}, f32[1440,720]{1,0:T(8,128)}, /*index=5*/s32[720]{0:T(1024)S(1)}) %tuple.53), branch_computations={%region_1.2_spmd, %region_2.3_spmd} | conditional | flops 4780619776 | bytes 48159480 | solution.py:77
  30.8 4.3 %fusion = f32[720,192]{0,1:T(8,128)S(1)} fusion(f32[1440,720]{1,0:T(8,128)} %get-tuple-element.51, f32[192,2880]{1,0:T(8,128)S(1)} %get-tuple-element.48, f32[720]{0:T(1024)S(1)} %get-tuple-element.69, s32[720]{0:T(1024)S(1)} %get-tuple-element.52, s32[192]{0:T(256)S(1)} %reshape.169), kind=kOutput, calls=%fused_computation.3 | convolution fusion | flops 1195084800 | bytes 7068672 | tf_op jit(solution)/shard_map/cond/branch_1_fun/dot_general | solution.py:62
  35.1 4.4 %fusion.35 = f32[192,1440]{1,0:T(8,128)S(1)} fusion(f32[720,192]{0,1:T(8,128)S(1)} %fusion, f32[1440,720]{1,0:T(8,128)} %get-tuple-element.51), kind=kOutput, calls=%fused_computation.86 | convolution fusion | flops 1194393600 | bytes 5806080 | tf_op jit(solution)/shard_map/cond/branch_1_fun/dot_general | solution.py:67
  39.5 2.2 %fusion.1 = f32[720,192]{0,1:T(8,128)S(1)} fusion(f32[1440,720]{1,0:T(8,128)S(1)} %bitcast.71, f32[192,2880]{1,0:T(8,128)S(1)} %get-tuple-element.48, f32[720]{0:T(1024)S(1)} %get-tuple-element.70, s32[720]{0:T(1024)S(1)} %get-tuple-element.50, s32[192]{0:T(256)S(1)} %reshape.169), kind=kOutput, calls=%fused_computation.5 | convolution fusion | flops 1195084800 | bytes 7345152 | tf_op jit(solution)/shard_map/cond/branch_1_fun/dot_general | solution.py:60
  41.7 2.3 %fusion.29 = (f32[192,1440]{1,0:T(8,128)S(1)}, f32[192,1440]{1,0:T(8,128)S(1)}) fusion(f32[192,1440]{1,0:T(8,128)S(1)} %fusion.35, f32[720,192]{0,1:T(8,128)S(1)} %fusion.1, f32[1440,720]{1,0:T(8,128)S(1)} %bitcast.71), kind=kOutput, calls=%fused_computation.80 | convolution fusion | flops 1194946560 | bytes 8017920 | tf_op jit(solution)/shard_map/cond/branch_1_fun/dot_general | solution.py:65
  44.0 0.7 maximum_select_fusion
  44.8 1.1 slice.170
  45.9 2.0 %slice.167 = f32[3,4,16,2879]{3,2,1,0:T(8,128)} slice(f32[3,4,16,2880]{3,2,1,0:T(8,128)S(1)} %bitcast.63), slice={[0:3], [0:4], [0:16], [1:2880]} | slice | bytes 4422144 | tf_op jit(solution)/shard_map/jit(_roll_static)/slice | solution.py:122
  48.1 1.4 %fusion.27 = f32[4,16,2880]{2,1,0:T(8,128)S(1)} fusion(f32[4,16,2880]{2,1,0:T(8,128)S(1)} %bitcast.81, f32[4,16,1]{2,1,0:T(8,128)S(1)} %slice.171, f32[4,16,2879]{2,1,0:T(8,128)} %slice.170), kind=kLoop, calls=%fused_computation.63 | loop fusion | flops 552960 | bytes 2211840 | tf_op jit(solution)/shard_map/mul | solution.py:122
  49.9 1.6 %fusion.22 = f32[3,4,16,2880]{3,2,1,0:T(8,128)} fusion(f32[3,4,16,2880]{3,2,1,0:T(8,128)S(1)} %bitcast.65, f32[3,4,16,1]{3,2,1,0:T(8,128)S(1)} %slice.168, f32[3,4,16,2879]{3,2,1,0:T(8,128)S(1)} %copy-done.2, f32[4,16,2880]{2,1,0:T(8,128)S(1)} %fusion.27), kind=kLoop, calls=%fused_computation.43 | loop fusion | flops 1658880 | bytes 7372800 | tf_op jit(solution)/shard_map/mul | solution.py:122
  51.6 0.6 gather_fusion
  52.4 0.7 compare_reduce_fusion
  53.1 1.0 slice.172
  54.7 8.6 %collective-permute-done = f32[3,4,1,2880]{3,2,0,1:T(1,128)S(1)} collective-permute-done((f32[3,4,1,2880]{3,2,0,1:T(1,128)}, f32[3,4,1,2880]{3,2,0,1:T(1,128)S(1)}, u32[]{:S(2)}, u32[]{:S(2)}) %collective-permute-start) | collective-permute-done | bytes 138272 | tf_op jit(solution)/shard_map/ppermute | solution.py:24
  63.4 18.8 %collective-permute-done.1 = f32[3,4,1,2880]{3,2,0,1:T(1,128)} collective-permute-done((f32[3,4,1,2880]{3,2,0,1:T(1,128)}, f32[3,4,1,2880]{3,2,0,1:T(1,128)}, u32[]{:S(2)}, u32[]{:S(2)}) %collective-permute-start.1) | collective-permute-done | bytes 138272 | tf_op jit(solution)/shard_map/ppermute | solution.py:24
  82.2 1.2 pad_maximum_fusion.9
  83.6 1.1 slice_bitcast_fusion.3
  84.7 1.1 slice_bitcast_fusion.5
  86.0 1.2 %pad_maximum_fusion.3 = f32[120,2880]{1,0:T(8,128)} fusion(f32[96,2880]{1,0:T(8,128)S(1)} %bitcast.83, f32[24,2880]{1,0:T(8,128)S(1)} %reshape.182), kind=kLoop, calls=%fused_computation.49 | loop fusion | flops 345600 | bytes 2764800 | tf_op jit(solution)/shard_map/concatenate | solution.py:106
  87.2 16.9 %conditional.3 = (f32[120,2880]{1,0:T(8,128)}) conditional(s32[]{:T(128)} %convert_element_type.21, f32[120,2880]{1,0:T(8,128)} %pad_maximum_fusion.3, (s32[120]{0:T(128)S(1)}, f32[120,2880]{1,0:T(8,128)}, f32[1440,720]{1,0:T(8,128)}, s32[720]{0:T(1024)S(1)}, f32[1440,720]{1,0:T(8,128)}, /*index=5*/s32[720]{0:T(1024)S(1)}) %tuple.54), branch_computations={%region_4.5_spmd, %region_5.6_spmd} | conditional | flops 2987889152 | bytes 41404616 | solution.py:77
  87.3 4.3 %fusion.9 = f32[720,120]{0,1:T(8,128)S(1)} fusion(f32[1440,720]{1,0:T(8,128)} %get-tuple-element.57, f32[120,2880]{1,0:T(8,128)} %get-tuple-element.54, f32[720]{0:T(1024)S(1)} %get-tuple-element.74, s32[720]{0:T(1024)S(1)} %get-tuple-element.58, s32[120]{0:T(128)S(1)} %get-tuple-element.53), kind=kOutput, calls=%fused_computation.19 | convolution fusion | flops 746928000 | bytes 6250080 | tf_op jit(solution)/shard_map/cond/branch_1_fun/dot_general | solution.py:62
  91.5 4.4 %fusion.36 = f32[120,1440]{1,0:T(8,128)S(1)} fusion(f32[720,120]{0,1:T(8,128)S(1)} %fusion.9, f32[1440,720]{1,0:T(8,128)} %get-tuple-element.57), kind=kOutput, calls=%fused_computation.87 | convolution fusion | flops 746496000 | bytes 5184000 | tf_op jit(solution)/shard_map/cond/branch_1_fun/dot_general | solution.py:67
  96.0 3.0 %fusion.8 = f32[720,120]{0,1:T(8,128)S(1)} fusion(f32[1440,720]{1,0:T(8,128)S(1)} %bitcast.73, f32[120,2880]{1,0:T(8,128)} %get-tuple-element.54, f32[720]{0:T(1024)S(1)} %get-tuple-element.75, s32[720]{0:T(1024)S(1)} %get-tuple-element.56, s32[120]{0:T(128)S(1)} %get-tuple-element.53), kind=kOutput, calls=%fused_computation.18 | convolution fusion | flops 746928000 | bytes 5973600 | tf_op jit(solution)/shard_map/cond/branch_1_fun/dot_general | solution.py:60
  99.0 2.2 %fusion.30 = (f32[120,1440]{1,0:T(8,128)S(1)}, f32[120,1440]{1,0:T(8,128)S(1)}) fusion(f32[120,1440]{1,0:T(8,128)S(1)} %fusion.36, f32[720,120]{0,1:T(8,128)S(1)} %fusion.8, f32[1440,720]{1,0:T(8,128)S(1)} %bitcast.73), kind=kOutput, calls=%fused_computation.81 | convolution fusion | flops 746841600 | bytes 6566400 | tf_op jit(solution)/shard_map/cond/branch_1_fun/dot_general | solution.py:65
  101.3 2.9 %maximum_select_fusion.1 = f32[120,2880]{1,0:T(8,128)} fusion(f32[120,2880]{1,0:T(8,128)} %get-tuple-element.54, f32[120,1440]{1,0:T(8,128)S(1)} %get-tuple-element.72, f32[120,1440]{1,0:T(8,128)S(1)} %get-tuple-element.71, pred[120]{0:T(512)(128)(4,1)S(1)} %broadcast_compare_fusion.1), kind=kLoop, calls=%fused_computation.15 | loop fusion | flops 691200 | bytes 4147320 | tf_op jit(solution)/shard_map/cond/branch_1_fun/jit(_where)/select_n | solution.py:70
  104.2 1.7 %slice.180 = f32[24,2880]{1,0:T(8,128)} slice(f32[120,2880]{1,0:T(8,128)} %get-tuple-element.96), slice={[0:24], [0:2880]} | slice | bytes 552960 | tf_op jit(solution)/shard_map/slice | solution.py:109
  105.8 1.3 %slice.187 = f32[96,2880]{1,0:T(8,128)S(1)} slice(f32[120,2880]{1,0:T(8,128)} %get-tuple-element.96), slice={[24:120], [0:2880]} | slice | bytes 2211840 | tf_op jit(solution)/shard_map/slice | solution.py:110
  107.2 1.8 %reshape.184 = f32[3,4,2,2880]{3,2,1,0:T(2,128)} reshape(f32[24,2880]{1,0:T(8,128)} %slice.180) | data formatting | bytes 552960 | tf_op jit(solution)/shard_map/reshape | solution.py:109
  109.0 1.4 %fusion.34 = (f32[3,4,1,2880]{3,2,1,0:T(1,128)S(1)}, f32[3,4,1,2880]{3,2,1,0:T(1,128)S(1)}) fusion(f32[3,4,2,2880]{3,2,1,0:T(2,128)} %reshape.184), kind=kLoop, calls=%fused_computation.85 | loop fusion | bytes 552960 | tf_op jit(solution)/shard_map/slice | solution.py:113
  110.8 0.6 fusion.16
  111.5 1.0 slice.190
  112.4 0.9 slice.191
  113.8 1.3 %copy-done.1 = f32[3,4,16,2880]{3,2,1,0:T(8,128)S(1)} copy-done((f32[3,4,16,2880]{3,2,1,0:T(8,128)S(1)}, f32[3,4,16,2880]{3,2,1,0:T(8,128)}, u32[]{:S(2)}) %copy-start.1) | copy-done | bytes 2211864
  115.1 1.2 fusion.18
  116.3 1.4 %slice_bitcast_fusion = (f32[4,16,2880]{2,1,0:T(8,128)}, f32[4,16,2880]{2,1,0:T(8,128)}, f32[4,16,2880]{2,1,0:T(8,128)}) fusion(f32[3,4,16,2880]{3,2,1,0:T(8,128)S(1)} %fusion.18), kind=kLoop, calls=%fused_computation.59 | loop fusion | bytes 4423680 | tf_op jit(solution)/shard_map/squeeze | solution.py:137
  (69 shorter events, 3.0 us)
Async XLA Ops:
  0.6 1.9 %copy-start.3 = (f32[4,16,2880]{2,1,0:T(8,128)S(1)}, f32[4,16,2880]{2,1,0:T(8,128)}, u32[]{:S(2)}) copy-start(f32[4,16,2880]{2,1,0:T(8,128)} %param.24) | copy-start | bytes 2211844
  3.5 80.1 %collective-permute-start.3 = (f32[4,16,2880]{2,1,0:T(8,128)}, f32[4,16,2880]{2,1,0:T(8,128)}, u32[]{:S(2)}, u32[]{:S(2)}) collective-permute-start(f32[4,16,2880]{2,1,0:T(8,128)} %pad_maximum_fusion.8), channel_id=1, source_target_pairs={{1,0},{2,1},{3,2},{4,3},{5,4},{6,5},{7,6},{9,8},{10,9},{11,10},{12... | collective-permute-start | bytes 2211848 | tf_op jit(solution)/shard_map/ppermute | solution.py:24
  13.4 71.3 %collective-permute-start.2 = (f32[4,16,2880]{2,1,0:T(8,128)}, f32[4,16,2880]{2,1,0:T(8,128)}, u32[]{:S(2)}, u32[]{:S(2)}) collective-permute-start(f32[4,16,2880]{2,1,0:T(8,128)} %pad_maximum_fusion.7), channel_id=1, source_target_pairs={{0,1},{1,2},{2,3},{3,4},{4,5},{5,6},{6,7},{8,9},{9,10},{10,11},{11... | collective-permute-start | bytes 2211848 | tf_op jit(solution)/shard_map/ppermute | solution.py:24
  16.3 47.0 %collective-permute-start = (f32[3,4,1,2880]{3,2,0,1:T(1,128)}, f32[3,4,1,2880]{3,2,0,1:T(1,128)S(1)}, u32[]{:S(2)}, u32[]{:S(2)}) collective-permute-start(f32[3,4,1,2880]{3,2,0,1:T(1,128)} %get-tuple-element.79), channel_id=1, source_target_pairs={{0,8},{8,16},{16,24},{24,32},{32,40},{40,48},{48,56},{56,64},{64,7... | collective-permute-start | bytes 414728 | tf_op jit(solution)/shard_map/ppermute | solution.py:24
  20.1 62.1 %collective-permute-start.1 = (f32[3,4,1,2880]{3,2,0,1:T(1,128)}, f32[3,4,1,2880]{3,2,0,1:T(1,128)}, u32[]{:S(2)}, u32[]{:S(2)}) collective-permute-start(f32[3,4,1,2880]{3,2,0,1:T(1,128)} %get-tuple-element.80), channel_id=1, source_target_pairs={{8,0},{16,8},{24,16},{32,24},{40,32},{48,40},{56,48},{64,56},{72,6... | collective-permute-start | bytes 414728 | tf_op jit(solution)/shard_map/ppermute | solution.py:24
  22.0 0.7 copy-start
  22.0 2.0 %copy-start.7 = (f32[48,360]{1,0:T(8,128)S(1)}, f32[48,360]{1,0:T(8,128)}, u32[]{:S(2)}) copy-start(f32[48,360]{1,0:T(8,128)} %constant.103.clone) | copy-start | bytes 207364
  22.0 2.0 %copy-start.8 = (f32[48,360]{1,0:T(8,128)S(1)}, f32[48,360]{1,0:T(8,128)}, u32[]{:S(2)}) copy-start(f32[48,360]{1,0:T(8,128)} %constant.104.clone) | copy-start | bytes 207364
  22.0 2.0 %copy-start.13 = (f32[30,360]{1,0:T(8,128)S(1)}, f32[30,360]{1,0:T(8,128)}, u32[]{:S(2)}) copy-start(f32[30,360]{1,0:T(8,128)} %constant.105.clone) | copy-start | bytes 129604
  22.0 2.0 %copy-start.14 = (f32[30,360]{1,0:T(8,128)S(1)}, f32[30,360]{1,0:T(8,128)}, u32[]{:S(2)}) copy-start(f32[30,360]{1,0:T(8,128)} %constant.106.clone) | copy-start | bytes 129604
  24.1 0.9 copy-start.5
  24.1 0.9 copy-start.6
  24.1 0.9 copy-start.11
  24.1 0.9 copy-start.12
  25.5 5.2 %copy-start.9 = (s32[720]{0:T(1024)S(1)}, s32[720]{0:T(1024)}, u32[]{:S(2)}) copy-start(s32[720]{0:T(1024)} %constant.107.clone) | copy-start | bytes 8644
  25.5 5.2 %copy-start.10 = (s32[720]{0:T(1024)S(1)}, s32[720]{0:T(1024)}, u32[]{:S(2)}) copy-start(s32[720]{0:T(1024)} %constant.108.clone) | copy-start | bytes 8644
  30.8 8.7 %slice-start = ((s8[4423680]{0:T(1024)(128)(4,1)}), s8[4194304]{0:T(1024)(128)(4,1)S(1)}, s32[]{:S(2)}) async-start(s8[4423680]{0:T(1024)(128)(4,1)} %bitcast.70), calls=%async_computation | async-start | bytes 8388608 | tf_op jit(solution)/shard_map/cond
  30.8 8.7 %slice-start.1 = ((s8[4423680]{0:T(1024)(128)(4,1)}), s8[229376]{0:T(1024)(128)(4,1)S(1)}, s32[]{:S(2)}) async-start(s8[4423680]{0:T(1024)(128)(4,1)} %bitcast.70), calls=%async_computation.1 | async-start | bytes 458752 | tf_op jit(solution)/shard_map/cond
  48.0 1.9 %copy-start.2 = (f32[3,4,16,2879]{3,2,1,0:T(8,128)S(1)}, f32[3,4,16,2879]{3,2,1,0:T(8,128)}, u32[]{:S(2)}) copy-start(f32[3,4,16,2879]{3,2,1,0:T(8,128)} %slice.167) | copy-start | bytes 6633220
  87.2 8.7 %slice-start.2 = ((s8[4423680]{0:T(1024)(128)(4,1)}), s8[4194304]{0:T(1024)(128)(4,1)S(1)}, s32[]{:S(2)}) async-start(s8[4423680]{0:T(1024)(128)(4,1)} %bitcast.72), calls=%async_computation.2 | async-start | bytes 8388608 | tf_op jit(solution)/shard_map/cond
  87.3 8.7 %slice-start.3 = ((s8[4423680]{0:T(1024)(128)(4,1)}), s8[229376]{0:T(1024)(128)(4,1)S(1)}, s32[]{:S(2)}) async-start(s8[4423680]{0:T(1024)(128)(4,1)} %bitcast.72), calls=%async_computation.3 | async-start | bytes 458752 | tf_op jit(solution)/shard_map/cond
  111.4 2.0 %copy-start.4 = (f32[4,16,2880]{2,1,0:T(8,128)S(1)}, f32[4,16,2880]{2,1,0:T(8,128)}, u32[]{:S(2)}) copy-start(f32[4,16,2880]{2,1,0:T(8,128)} %param.24) | copy-start | bytes 2211844
  113.5 1.6 %copy-start.1 = (f32[3,4,16,2880]{3,2,1,0:T(8,128)S(1)}, f32[3,4,16,2880]{3,2,1,0:T(8,128)}, u32[]{:S(2)}) copy-start(f32[3,4,16,2880]{3,2,1,0:T(8,128)} %fusion.22) | copy-start | bytes 6635524

commit v2 on v0

--- a/solution.py
+++ b/solution.py
@@ -89,17 +89,19 @@
 
     stacked = jnp.stack([zonal_wind, merid_wind, tracer])
     levels = stacked.shape[1]
-    top = jnp.concatenate([stacked[:, levels - 1], vertical_wind[levels - 1 :]], axis=0)
-    bottom = jnp.concatenate([stacked[:, 0], vertical_wind[:1]], axis=0)
-    below = shift(top, "lev", True)
-    above = shift(bottom, "lev", False)
+    below_fields = shift(stacked[:, levels - 1], "lev", True)
+    above_fields = shift(stacked[:, 0], "lev", False)
+    top_wind, bottom_wind, _ = lax.optimization_barrier(
+        (vertical_wind[levels - 1 :], vertical_wind[:1], (below_fields, above_fields)))
+    below_wind = shift(top_wind, "lev", True)
+    above_wind = shift(bottom_wind, "lev", False)
     south = shift(stacked[:, :, lat_rows - 1 :], "lat", True)
     north = shift(stacked[:, :, :1], "lat", False)
 
     tables = (parity_table(0), parity_table(1))
     field = filtered(stacked, own_cut, tables)
     lat_rows_raw = jnp.concatenate([south, north], axis=2).reshape(-1, NLON)
-    lev_rows_raw = jnp.stack([below[:3], above[:3]], axis=1).reshape(-1, NLON)
+    lev_rows_raw = jnp.stack([below_fields, above_fields], axis=1).reshape(-1, NLON)
     lat_cuts = jnp.broadcast_to(halo_cut, south.shape[:2] + (2,)).reshape(-1)
     lev_cuts = jnp.broadcast_to(own_cut, (3, 2, lat_rows)).reshape(-1)
     halo_rows = filtered(jnp.concatenate([lat_rows_raw, lev_rows_raw]),
@@ -108,7 +110,7 @@
     lat_halo = halo_rows[:lat_count_rows].reshape(3, levels, 2, NLON)
     lev_halo = halo_rows[lat_count_rows:].reshape(3, 2, lat_rows, NLON)
 
-    vertical_pad = jnp.concatenate([below[3:], vertical_wind, above[3:]], axis=0)
+    vertical_pad = jnp.concatenate([below_wind, vertical_wind, above_wind], axis=0)
     field_lat = jnp.concatenate([lat_halo[:, :, :1], field, lat_halo[:, :, 1:]], axis=2)
     field_lev = jnp.concatenate([lev_halo[:, :1], field, lev_halo[:, 1:]], axis=1)
 

time: 119 us -> 123 us (1.034)
  the two profiles are of different devices: /device:TPU:25 before, /device:TPU:9 now
where the time goes in v2:
time: 123 us; the launch traced here: 122 us
  matrix products  27.1 us (22%)
  starting transfers between devices  26.7 us (22%)
  waiting for transfers between devices  26.2 us (21%)
  other arithmetic  21 us (17%)
  local copies, waits for them, and re-layouts  18.7 us (15%)
  between operations  2.34 us (2%)
    ppermute x6, starting transfers between devices, shift(): return lax.ppermute(x, axis, pairs)  26.7 us
    ppermute x6, waiting for transfers between devices, shift(): return lax.ppermute(x, axis, pairs)  26.2 us
    dot_general x2, matrix products, lowpass_rows(): lax.dot_general(spec_odd * parity_weight(1, cut), odd_table, dims, precis...  8.77 us
    dot_general x2, matrix products, lowpass_rows(): jnp.dot(first - second, odd_table, precision=mxu_precision, preferred_ele...  8.57 us
    dot_general x2, matrix products, lowpass_rows(): jnp.dot(first + second, even_table, precision=mxu_precision, preferred_el...  5.22 us
    concatenate x1, other arithmetic, parity_table(): return jnp.concatenate([cosines, sines], axis=-1).reshape(HALF, KMAX)  5.18 us
    dot_general x2, matrix products, lowpass_rows(): lax.dot_general(spec_even * parity_weight(0, cut), even_table, dims, prec...  4.55 us
    select_n x2, other arithmetic, lowpass_rows(): return jnp.where((cut < HALF)[:, None], summed, x)  3.6 us
  transfers between devices with their start and end apart: 6, of which 4 were waited for; matrix products, arithmetic and copies ran while one was open for 26% of the time, Pallas kernels for 0%

profile of v2, /device:TPU:9, one launch (start us, length us, event | category | flops | bytes accessed | tf_op | source)
XLA Modules:
  0.0 122.2 jit_solution(17474862548625598840)
XLA Ops:
  0.6 1.7 %pad_maximum_fusion.2 = f32[3,4,16,2880]{3,2,1,0:T(8,128)S(1)} fusion(f32[1,4,16,2880]{3,2,1,0:T(8,128)} %bitcast.68, f32[1,4,16,2880]{3,2,1,0:T(8,128)} %bitcast.69, f32[1,4,16,2880]{3,2,1,0:T(8,128)} %bitcast.70), kind=kLoop, calls=%fused_computation.37 | loop fusion | flops 1105920 | bytes 4423680 | tf_op jit(solution)/shard_map/stack | solution.py:90
  2.4 1.1 slice_bitcast_fusion.4
  3.5 8.8 %collective-permute-start.2 = (f32[3,16,2880]{2,1,0:T(8,128)}, f32[3,16,2880]{2,1,0:T(8,128)}, u32[]{:S(2)}, u32[]{:S(2)}) collective-permute-start(f32[3,16,2880]{2,1,0:T(8,128)} %get-tuple-element.85), channel_id=1, source_target_pairs={{0,1},{1,2},{2,3},{3,4},{4,5},{5,6},{6,7},{8,9},{9,10},{10,11},{11... | collective-permute-start | bytes 1658888 | tf_op jit(solution)/shard_map/ppermute | solution.py:24
  12.3 1.9 %collective-permute-start.3 = (f32[3,16,2880]{2,1,0:T(8,128)}, f32[3,16,2880]{2,1,0:T(8,128)}, u32[]{:S(2)}, u32[]{:S(2)}) collective-permute-start(f32[3,16,2880]{2,1,0:T(8,128)} %get-tuple-element.86), channel_id=1, source_target_pairs={{1,0},{2,1},{3,2},{4,3},{5,4},{6,5},{7,6},{9,8},{10,9},{11,10},{12... | collective-permute-start | bytes 1658888 | tf_op jit(solution)/shard_map/ppermute | solution.py:24
  14.2 0.9 fusion.27
  15.2 4.0 %collective-permute-start = (f32[3,4,1,2880]{3,2,1,0:T(1,128)}, f32[3,4,1,2880]{3,2,1,0:T(1,128)S(1)}, u32[]{:S(2)}, u32[]{:S(2)}) collective-permute-start(f32[3,4,1,2880]{3,2,1,0:T(1,128)} %get-tuple-element.83), channel_id=1, source_target_pairs={{0,8},{8,16},{16,24},{24,32},{32,40},{40,48},{48,56},{56,64},{64,7... | collective-permute-start | bytes 414728 | tf_op jit(solution)/shard_map/ppermute | solution.py:24
  19.2 1.9 %collective-permute-start.1 = (f32[3,4,1,2880]{3,2,1,0:T(1,128)}, f32[3,4,1,2880]{3,2,1,0:T(1,128)}, u32[]{:S(2)}, u32[]{:S(2)}) collective-permute-start(f32[3,4,1,2880]{3,2,1,0:T(1,128)} %get-tuple-element.84), channel_id=1, source_target_pairs={{8,0},{16,8},{24,16},{32,24},{40,32},{48,40},{56,48},{64,56},{72,6... | collective-permute-start | bytes 414728 | tf_op jit(solution)/shard_map/ppermute | solution.py:24
  21.1 0.7 compare_reduce_fusion.1
  22.6 0.5 multiply_subtract_fusion.1
  23.0 0.4 copy-done.7
  23.4 0.5 multiply_subtract_fusion
  23.9 5.2 %pad_maximum_fusion = (f32[1440,720]{1,0:T(8,128)}, f32[1440,720]{1,0:T(8,128)}) fusion(f32[1440,360]{1,0:T(8,128)S(1)} %bitcast.60, f32[1440,360]{1,0:T(8,128)S(1)} %bitcast.59, f32[1440,360]{1,0:T(8,128)S(1)} %bitcast.62, f32[1440,360]{1,0:T(8,128)S(1)} %bitcast.61), kind=kLoop, calls=%fused_computation.25 | loop fusion | flops 2073600 | bytes 16588800 | tf_op jit(solution)/shard_map/concatenate | solution.py:46
  29.1 14.1 %conditional.2 = (f32[192,2880]{1,0:T(8,128)S(1)}) conditional(s32[]{:T(128)} %convert_element_type.20, f32[192,2880]{1,0:T(8,128)S(1)} %bitcast.45, (s32[16]{0:T(128)S(1)}, f32[192,2880]{1,0:T(8,128)S(1)}, f32[1440,720]{1,0:T(8,128)}, s32[720]{0:T(1024)S(1)}, f32[1440,720]{1,0:T(8,128)}, /*index=5*/s32[720]{0:T(1024)S(1)}) %tuple.55), branch_computations={%region_1.2_spmd, %region_2.3_spmd} | conditional | flops 4780619776 | bytes 48159480 | solution.py:76
  29.2 4.3 %convolution_multiply_fusion = f32[192,720]{1,0:T(8,128)S(1)} fusion(f32[1440,720]{1,0:T(8,128)} %get-tuple-element.51, f32[192,2880]{1,0:T(8,128)S(1)} %get-tuple-element.48, f32[720]{0:T(1024)S(1)} %get-tuple-element.73, s32[720]{0:T(1024)S(1)} %get-tuple-element.52, s32[192]{0:T(256)S(1)} %reshape.169), kind=kOutput, calls=%fused_computation.2 | convolution fusion | flops 1195084800 | bytes 7068672 | tf_op jit(solution)/shard_map/cond/branch_1_fun/dot_general | solution.py:61
  33.5 4.4 %fusion.31 = f32[192,1440]{1,0:T(8,128)S(1)} fusion(f32[192,720]{1,0:T(8,128)S(1)} %convolution_multiply_fusion, f32[1440,720]{1,0:T(8,128)} %get-tuple-element.51), kind=kOutput, calls=%fused_computation.78 | convolution fusion | flops 1194393600 | bytes 5806080 | tf_op jit(solution)/shard_map/cond/branch_1_fun/dot_general | solution.py:66
  37.9 2.2 %convolution_multiply_fusion.1 = f32[192,720]{1,0:T(8,128)S(1)} fusion(f32[1440,720]{1,0:T(8,128)S(1)} %bitcast.55, f32[192,2880]{1,0:T(8,128)S(1)} %get-tuple-element.48, f32[720]{0:T(1024)S(1)} %get-tuple-element.74, s32[720]{0:T(1024)S(1)} %get-tuple-element.50, s32[192]{0:T(256)S(1)} %reshape.169), kind=kOutput, calls=%fused_computation.3 | convolution fusion | flops 1195084800 | bytes 7345152 | tf_op jit(solution)/shard_map/cond/branch_1_fun/dot_general | solution.py:59
  40.1 2.3 %fusion.25 = (f32[192,1440]{1,0:T(8,128)S(1)}, f32[192,1440]{1,0:T(8,128)S(1)}) fusion(f32[192,1440]{1,0:T(8,128)S(1)} %fusion.31, f32[192,720]{1,0:T(8,128)S(1)} %convolution_multiply_fusion.1, f32[1440,720]{1,0:T(8,128)S(1)} %bitcast.55), kind=kOutput, calls=%fused_computation.72 | convolution fusion | flops 1194946560 | bytes 8017920 | tf_op jit(solution)/shard_map/cond/branch_1_fun/dot_general | solution.py:64
  42.5 0.7 maximum_select_fusion
  43.2 1.1 slice.154
  44.4 2.0 %slice.151 = f32[3,4,16,2879]{3,2,1,0:T(8,128)} slice(f32[3,4,16,2880]{3,2,1,0:T(8,128)S(1)} %bitcast.47), slice={[0:3], [0:4], [0:16], [1:2880]} | slice | bytes 4422144 | tf_op jit(solution)/shard_map/jit(_roll_static)/slice | solution.py:123
  46.6 0.6 gather_fusion
  47.4 2.0 %fusion.29 = (f32[1,16,2880]{2,1,0:T(8,128)}, f32[1,16,2880]{2,1,0:T(8,128)}) fusion(f32[4,16,2880]{2,1,0:T(8,128)} %param.24), kind=kLoop, calls=%fused_computation.76 | loop fusion | bytes 737280 | tf_op jit(solution)/shard_map/slice | solution.py:95
  49.3 1.2 %fusion.23 = f32[4,16,2880]{2,1,0:T(8,128)S(1)} fusion(f32[4,16,2880]{2,1,0:T(8,128)S(1)} %bitcast.65, f32[4,16,1]{2,1,0:T(8,128)S(1)} %slice.155, f32[4,16,2879]{2,1,0:T(8,128)} %slice.154), kind=kLoop, calls=%fused_computation.59 | loop fusion | flops 552960 | bytes 2211840 | tf_op jit(solution)/shard_map/mul | solution.py:123
  50.9 0.9 compare_reduce_fusion
  51.7 0.5 copy-done.1
  53.0 10.2 %collective-permute-done = f32[3,4,1,2880]{3,2,1,0:T(1,128)S(1)} collective-permute-done((f32[3,4,1,2880]{3,2,1,0:T(1,128)}, f32[3,4,1,2880]{3,2,1,0:T(1,128)S(1)}, u32[]{:S(2)}, u32[]{:S(2)}) %collective-permute-start) | collective-permute-done | bytes 138272 | tf_op jit(solution)/shard_map/ppermute | solution.py:24
  63.2 2.3 %collective-permute-done.1 = f32[3,4,1,2880]{3,2,1,0:T(1,128)} collective-permute-done((f32[3,4,1,2880]{3,2,1,0:T(1,128)}, f32[3,4,1,2880]{3,2,1,0:T(1,128)}, u32[]{:S(2)}, u32[]{:S(2)}) %collective-permute-start.1) | collective-permute-done | bytes 138272 | tf_op jit(solution)/shard_map/ppermute | solution.py:24
  65.5 1.2 pad_maximum_fusion.7
  66.9 1.3 %pad_maximum_fusion.6 = f32[3,2,16,2880]{3,2,0,1:T(8,128)S(1)} fusion(f32[3,1,16,2880]{3,2,0,1:T(8,128)} %bitcast.16, f32[3,1,16,2880]{3,2,0,1:T(8,128)} %bitcast.14), kind=kLoop, calls=%fused_computation.52 | loop fusion | flops 276480 | bytes 2211840 | tf_op jit(solution)/shard_map/stack | solution.py:104
  68.3 1.3 %pad_maximum_fusion.3 = f32[120,2880]{1,0:T(8,128)} fusion(f32[96,2880]{1,0:T(8,128)S(1)} %bitcast.67, f32[24,2880]{1,0:T(8,128)S(1)} %reshape.182), kind=kLoop, calls=%fused_computation.45 | loop fusion | flops 345600 | bytes 2764800 | tf_op jit(solution)/shard_map/concatenate | solution.py:107
  69.6 16.9 %conditional.3 = (f32[120,2880]{1,0:T(8,128)}) conditional(s32[]{:T(128)} %convert_element_type.21, f32[120,2880]{1,0:T(8,128)} %pad_maximum_fusion.3, (s32[120]{0:T(128)S(1)}, f32[120,2880]{1,0:T(8,128)}, f32[1440,720]{1,0:T(8,128)}, s32[720]{0:T(1024)S(1)}, f32[1440,720]{1,0:T(8,128)}, /*index=5*/s32[720]{0:T(1024)S(1)}) %tuple.56), branch_computations={%region_4.5_spmd, %region_5.6_spmd} | conditional | flops 2987889152 | bytes 41404616 | solution.py:76
  69.6 4.3 %convolution_multiply_fusion.2 = f32[120,720]{1,0:T(8,128)S(1)} fusion(f32[1440,720]{1,0:T(8,128)} %get-tuple-element.57, f32[120,2880]{1,0:T(8,128)} %get-tuple-element.54, f32[720]{0:T(1024)S(1)} %get-tuple-element.78, s32[720]{0:T(1024)S(1)} %get-tuple-element.58, s32[120]{0:T(128)S(1)} %get-tuple-element.53), kind=kOutput, calls=%fused_computation.14 | convolution fusion | flops 746928000 | bytes 6250080 | tf_op jit(solution)/shard_map/cond/branch_1_fun/dot_general | solution.py:61
  73.9 4.4 %fusion.32 = f32[120,1440]{1,0:T(8,128)S(1)} fusion(f32[120,720]{1,0:T(8,128)S(1)} %convolution_multiply_fusion.2, f32[1440,720]{1,0:T(8,128)} %get-tuple-element.57), kind=kOutput, calls=%fused_computation.79 | convolution fusion | flops 746496000 | bytes 5184000 | tf_op jit(solution)/shard_map/cond/branch_1_fun/dot_general | solution.py:66
  78.3 3.0 %convolution_multiply_fusion.3 = f32[120,720]{1,0:T(8,128)S(1)} fusion(f32[1440,720]{1,0:T(8,128)S(1)} %bitcast.57, f32[120,2880]{1,0:T(8,128)} %get-tuple-element.54, f32[720]{0:T(1024)S(1)} %get-tuple-element.79, s32[720]{0:T(1024)S(1)} %get-tuple-element.56, s32[120]{0:T(128)S(1)} %get-tuple-element.53), kind=kOutput, calls=%fused_computation.15 | convolution fusion | flops 746928000 | bytes 5973600 | tf_op jit(solution)/shard_map/cond/branch_1_fun/dot_general | solution.py:59
  81.4 2.3 %fusion.26 = (f32[120,1440]{1,0:T(8,128)S(1)}, f32[120,1440]{1,0:T(8,128)S(1)}) fusion(f32[120,1440]{1,0:T(8,128)S(1)} %fusion.32, f32[120,720]{1,0:T(8,128)S(1)} %convolution_multiply_fusion.3, f32[1440,720]{1,0:T(8,128)S(1)} %bitcast.57), kind=kOutput, calls=%fused_computation.73 | convolution fusion | flops 746841600 | bytes 6566400 | tf_op jit(solution)/shard_map/cond/branch_1_fun/dot_general | solution.py:64
  83.6 2.9 %maximum_select_fusion.1 = f32[120,2880]{1,0:T(8,128)} fusion(f32[120,2880]{1,0:T(8,128)} %get-tuple-element.54, f32[120,1440]{1,0:T(8,128)S(1)} %get-tuple-element.76, f32[120,1440]{1,0:T(8,128)S(1)} %get-tuple-element.75, pred[120]{0:T(512)(128)(4,1)S(1)} %broadcast_compare_fusion.1), kind=kLoop, calls=%fused_computation.13 | loop fusion | flops 691200 | bytes 4147320 | tf_op jit(solution)/shard_map/cond/branch_1_fun/jit(_where)/select_n | solution.py:69
  86.5 1.7 %slice.162 = f32[24,2880]{1,0:T(8,128)} slice(f32[120,2880]{1,0:T(8,128)} %get-tuple-element.100), slice={[0:24], [0:2880]} | slice | bytes 552960 | tf_op jit(solution)/shard_map/slice | solution.py:110
  88.2 1.3 %slice.169 = f32[96,2880]{1,0:T(8,128)S(1)} slice(f32[120,2880]{1,0:T(8,128)} %get-tuple-element.100), slice={[24:120], [0:2880]} | slice | bytes 2211840 | tf_op jit(solution)/shard_map/slice | solution.py:111
  89.5 1.8 %reshape.184 = f32[3,4,2,2880]{3,2,1,0:T(2,128)} reshape(f32[24,2880]{1,0:T(8,128)} %slice.162) | data formatting | bytes 552960 | tf_op jit(solution)/shard_map/reshape | solution.py:110
  91.3 1.3 %fusion.30 = (f32[3,4,1,2880]{3,2,1,0:T(1,128)S(1)}, f32[3,4,1,2880]{3,2,1,0:T(1,128)S(1)}) fusion(f32[3,4,2,2880]{3,2,1,0:T(2,128)} %reshape.184), kind=kLoop, calls=%fused_computation.77 | loop fusion | bytes 552960 | tf_op jit(solution)/shard_map/slice | solution.py:114
  93.0 0.6 fusion.12
  93.9 1.9 %collective-permute-start.4 = (f32[1,16,2880]{2,1,0:T(8,128)S(1)}, f32[1,16,2880]{2,1,0:T(8,128)S(1)}, u32[]{:S(2)}, u32[]{:S(2)}) collective-permute-start(f32[1,16,2880]{2,1,0:T(8,128)S(1)} %copy-done.6), channel_id=1, source_target_pairs={{0,1},{1,2},{2,3},{3,4},{4,5},{5,6},{6,7},{8,9},{9,10},{10,11},{11... | collective-permute-start | bytes 552968 | tf_op jit(solution)/shard_map/ppermute | solution.py:24
  95.9 8.2 %collective-permute-start.5 = (f32[1,16,2880]{2,1,0:T(8,128)S(1)}, f32[1,16,2880]{2,1,0:T(8,128)S(1)}, u32[]{:S(2)}, u32[]{:S(2)}) collective-permute-start(f32[1,16,2880]{2,1,0:T(8,128)S(1)} %copy-done.5), channel_id=1, source_target_pairs={{1,0},{2,1},{3,2},{4,3},{5,4},{6,5},{7,6},{9,8},{10,9},{11,10},{12... | collective-permute-start | bytes 552968 | tf_op jit(solution)/shard_map/ppermute | solution.py:24
  104.1 2.9 %collective-permute-done.4 = f32[1,16,2880]{2,1,0:T(8,128)S(1)} collective-permute-done((f32[1,16,2880]{2,1,0:T(8,128)S(1)}, f32[1,16,2880]{2,1,0:T(8,128)S(1)}, u32[]{:S(2)}, u32[]{:S(2)}) %collective-permute-start.4) | collective-permute-done | bytes 184352 | tf_op jit(solution)/shard_map/ppermute | solution.py:24
  107.1 10.8 %collective-permute-done.5 = f32[1,16,2880]{2,1,0:T(8,128)S(1)} collective-permute-done((f32[1,16,2880]{2,1,0:T(8,128)S(1)}, f32[1,16,2880]{2,1,0:T(8,128)S(1)}, u32[]{:S(2)}, u32[]{:S(2)}) %collective-permute-start.5) | collective-permute-done | bytes 184352 | tf_op jit(solution)/shard_map/ppermute | solution.py:24
  118.3 1.3 %copy-done.2 = f32[3,4,16,2880]{3,2,1,0:T(8,128)S(1)} copy-done((f32[3,4,16,2880]{3,2,1,0:T(8,128)S(1)}, f32[3,4,16,2880]{3,2,1,0:T(8,128)}, u32[]{:S(2)}) %copy-start.2) | copy-done | bytes 2211864
  119.6 1.2 fusion.14
  120.8 1.4 %slice_bitcast_fusion = (f32[4,16,2880]{2,1,0:T(8,128)}, f32[4,16,2880]{2,1,0:T(8,128)}, f32[4,16,2880]{2,1,0:T(8,128)}) fusion(f32[3,4,16,2880]{3,2,1,0:T(8,128)S(1)} %fusion.14), kind=kLoop, calls=%fused_computation.55 | loop fusion | bytes 4423680 | tf_op jit(solution)/shard_map/squeeze | solution.py:138
  (69 shorter events, 2.5 us)
Async XLA Ops:
  2.4 18.7 %copy-start = (s32[512]{0:T(512)S(1)}, s32[512]{0:T(512)}, u32[]{:S(2)}) copy-start(s32[512]{0:T(512)} %param.25) | copy-start | bytes 6148
  2.4 20.1 %copy-start.9 = (f32[48,360]{1,0:T(8,128)S(1)}, f32[48,360]{1,0:T(8,128)}, u32[]{:S(2)}) copy-start(f32[48,360]{1,0:T(8,128)} %constant.100.clone) | copy-start | bytes 207364
  2.4 20.1 %copy-start.10 = (f32[48,360]{1,0:T(8,128)S(1)}, f32[48,360]{1,0:T(8,128)}, u32[]{:S(2)}) copy-start(f32[48,360]{1,0:T(8,128)} %constant.99.clone) | copy-start | bytes 207364
  2.4 20.1 %copy-start.15 = (f32[30,360]{1,0:T(8,128)S(1)}, f32[30,360]{1,0:T(8,128)}, u32[]{:S(2)}) copy-start(f32[30,360]{1,0:T(8,128)} %constant.101.clone) | copy-start | bytes 129604
  2.4 20.1 %copy-start.16 = (f32[30,360]{1,0:T(8,128)S(1)}, f32[30,360]{1,0:T(8,128)}, u32[]{:S(2)}) copy-start(f32[30,360]{1,0:T(8,128)} %constant.102.clone) | copy-start | bytes 129604
  3.5 63.4 %collective-permute-start.2 = (f32[3,16,2880]{2,1,0:T(8,128)}, f32[3,16,2880]{2,1,0:T(8,128)}, u32[]{:S(2)}, u32[]{:S(2)}) collective-permute-start(f32[3,16,2880]{2,1,0:T(8,128)} %get-tuple-element.85), channel_id=1, source_target_pairs={{0,1},{1,2},{2,3},{3,4},{4,5},{5,6},{6,7},{8,9},{9,10},{10,11},{11... | collective-permute-start | bytes 1658888 | tf_op jit(solution)/shard_map/ppermute | solution.py:24
  12.3 54.6 %collective-permute-start.3 = (f32[3,16,2880]{2,1,0:T(8,128)}, f32[3,16,2880]{2,1,0:T(8,128)}, u32[]{:S(2)}, u32[]{:S(2)}) collective-permute-start(f32[3,16,2880]{2,1,0:T(8,128)} %get-tuple-element.86), channel_id=1, source_target_pairs={{1,0},{2,1},{3,2},{4,3},{5,4},{6,5},{7,6},{9,8},{10,9},{11,10},{12... | collective-permute-start | bytes 1658888 | tf_op jit(solution)/shard_map/ppermute | solution.py:24
  15.2 48.0 %collective-permute-start = (f32[3,4,1,2880]{3,2,1,0:T(1,128)}, f32[3,4,1,2880]{3,2,1,0:T(1,128)S(1)}, u32[]{:S(2)}, u32[]{:S(2)}) collective-permute-start(f32[3,4,1,2880]{3,2,1,0:T(1,128)} %get-tuple-element.83), channel_id=1, source_target_pairs={{0,8},{8,16},{16,24},{24,32},{32,40},{40,48},{48,56},{56,64},{64,7... | collective-permute-start | bytes 414728 | tf_op jit(solution)/shard_map/ppermute | solution.py:24
  19.2 46.4 %collective-permute-start.1 = (f32[3,4,1,2880]{3,2,1,0:T(1,128)}, f32[3,4,1,2880]{3,2,1,0:T(1,128)}, u32[]{:S(2)}, u32[]{:S(2)}) collective-permute-start(f32[3,4,1,2880]{3,2,1,0:T(1,128)} %get-tuple-element.84), channel_id=1, source_target_pairs={{8,0},{16,8},{24,16},{32,24},{40,32},{48,40},{56,48},{64,56},{72,6... | collective-permute-start | bytes 414728 | tf_op jit(solution)/shard_map/ppermute | solution.py:24
  22.5 0.9 copy-start.7
  22.5 0.9 copy-start.8
  22.5 0.9 copy-start.13
  22.5 0.9 copy-start.14
  23.9 5.2 %copy-start.11 = (s32[720]{0:T(1024)S(1)}, s32[720]{0:T(1024)}, u32[]{:S(2)}) copy-start(s32[720]{0:T(1024)} %constant.107.clone) | copy-start | bytes 8644
  23.9 5.2 %copy-start.12 = (s32[720]{0:T(1024)S(1)}, s32[720]{0:T(1024)}, u32[]{:S(2)}) copy-start(s32[720]{0:T(1024)} %constant.108.clone) | copy-start | bytes 8644
  29.2 8.7 %slice-start = ((s8[4423680]{0:T(1024)(128)(4,1)}), s8[4194304]{0:T(1024)(128)(4,1)S(1)}, s32[]{:S(2)}) async-start(s8[4423680]{0:T(1024)(128)(4,1)} %bitcast.54), calls=%async_computation | async-start | bytes 8388608 | tf_op jit(solution)/shard_map/cond
  29.2 8.7 %slice-start.1 = ((s8[4423680]{0:T(1024)(128)(4,1)}), s8[229376]{0:T(1024)(128)(4,1)S(1)}, s32[]{:S(2)}) async-start(s8[4423680]{0:T(1024)(128)(4,1)} %bitcast.54), calls=%async_computation.1 | async-start | bytes 458752 | tf_op jit(solution)/shard_map/cond
  47.4 3.2 %copy-start.3 = (f32[3,4,16,2879]{3,2,1,0:T(8,128)S(1)}, f32[3,4,16,2879]{3,2,1,0:T(8,128)}, u32[]{:S(2)}) copy-start(f32[3,4,16,2879]{3,2,1,0:T(8,128)} %slice.151) | copy-start | bytes 6633220
  50.9 1.4 %copy-start.1 = (f32[3,4,16,2880]{3,2,1,0:T(8,128)}, f32[3,4,16,2880]{3,2,1,0:T(8,128)S(1)}, u32[]{:S(2)}) copy-start(f32[3,4,16,2880]{3,2,1,0:T(8,128)S(1)} %fusion.18) | copy-start | bytes 6635524
  69.6 8.7 %slice-start.2 = ((s8[4423680]{0:T(1024)(128)(4,1)}), s8[4194304]{0:T(1024)(128)(4,1)S(1)}, s32[]{:S(2)}) async-start(s8[4423680]{0:T(1024)(128)(4,1)} %bitcast.56), calls=%async_computation.2 | async-start | bytes 8388608 | tf_op jit(solution)/shard_map/cond
  69.6 8.7 %slice-start.3 = ((s8[4423680]{0:T(1024)(128)(4,1)}), s8[229376]{0:T(1024)(128)(4,1)S(1)}, s32[]{:S(2)}) async-start(s8[4423680]{0:T(1024)(128)(4,1)} %bitcast.56), calls=%async_computation.3 | async-start | bytes 458752 | tf_op jit(solution)/shard_map/cond
  93.0 0.9 copy-start.6
  93.0 2.8 %copy-start.5 = (f32[1,16,2880]{2,1,0:T(8,128)S(1)}, f32[1,16,2880]{2,1,0:T(8,128)}, u32[]{:S(2)}) copy-start(f32[1,16,2880]{2,1,0:T(8,128)} %get-tuple-element.65) | copy-start | bytes 552964
  93.6 24.2 %copy-start.4 = (f32[4,16,2880]{2,1,0:T(8,128)S(1)}, f32[4,16,2880]{2,1,0:T(8,128)}, u32[]{:S(2)}) copy-start(f32[4,16,2880]{2,1,0:T(8,128)} %param.24) | copy-start | bytes 2211844
  93.9 13.1 %collective-permute-start.4 = (f32[1,16,2880]{2,1,0:T(8,128)S(1)}, f32[1,16,2880]{2,1,0:T(8,128)S(1)}, u32[]{:S(2)}, u32[]{:S(2)}) collective-permute-start(f32[1,16,2880]{2,1,0:T(8,128)S(1)} %copy-done.6), channel_id=1, source_target_pairs={{0,1},{1,2},{2,3},{3,4},{4,5},{5,6},{6,7},{8,9},{9,10},{10,11},{11... | collective-permute-start | bytes 552968 | tf_op jit(solution)/shard_map/ppermute | solution.py:24
  95.9 22.0 %collective-permute-start.5 = (f32[1,16,2880]{2,1,0:T(8,128)S(1)}, f32[1,16,2880]{2,1,0:T(8,128)S(1)}, u32[]{:S(2)}, u32[]{:S(2)}) collective-permute-start(f32[1,16,2880]{2,1,0:T(8,128)S(1)} %copy-done.5), channel_id=1, source_target_pairs={{1,0},{2,1},{3,2},{4,3},{5,4},{6,5},{7,6},{9,8},{10,9},{11,10},{12... | collective-permute-start | bytes 552968 | tf_op jit(solution)/shard_map/ppermute | solution.py:24
  118.0 1.6 %copy-start.2 = (f32[3,4,16,2880]{3,2,1,0:T(8,128)S(1)}, f32[3,4,16,2880]{3,2,1,0:T(8,128)}, u32[]{:S(2)}) copy-start(f32[3,4,16,2880]{3,2,1,0:T(8,128)} %copy-done.1) | copy-start | bytes 6635524

commit v3 on v2

--- a/solution.py
+++ b/solution.py
@@ -84,35 +84,23 @@
     total_rows = lat_rows * lat_count
     row_start = lat_index * lat_rows
     own_cut = lax.dynamic_slice_in_dim(cutoff, row_start, lat_rows)
-    halo_ids = jnp.stack([row_start - 1, row_start + lat_rows])
-    halo_cut = cutoff[jnp.clip(halo_ids, 0, total_rows - 1)]
 
     stacked = jnp.stack([zonal_wind, merid_wind, tracer])
     levels = stacked.shape[1]
-    below_fields = shift(stacked[:, levels - 1], "lev", True)
-    above_fields = shift(stacked[:, 0], "lev", False)
-    top_wind, bottom_wind, _ = lax.optimization_barrier(
-        (vertical_wind[levels - 1 :], vertical_wind[:1], (below_fields, above_fields)))
-    below_wind = shift(top_wind, "lev", True)
-    above_wind = shift(bottom_wind, "lev", False)
-    south = shift(stacked[:, :, lat_rows - 1 :], "lat", True)
-    north = shift(stacked[:, :, :1], "lat", False)
+    below_wind = shift(vertical_wind[levels - 1 :], "lev", True)
+    above_wind = shift(vertical_wind[:1], "lev", False)
 
     tables = (parity_table(0), parity_table(1))
+    stacked, below_wind, above_wind = lax.optimization_barrier((stacked, below_wind, above_wind))
     field = filtered(stacked, own_cut, tables)
-    lat_rows_raw = jnp.concatenate([south, north], axis=2).reshape(-1, NLON)
-    lev_rows_raw = jnp.stack([below_fields, above_fields], axis=1).reshape(-1, NLON)
-    lat_cuts = jnp.broadcast_to(halo_cut, south.shape[:2] + (2,)).reshape(-1)
-    lev_cuts = jnp.broadcast_to(own_cut, (3, 2, lat_rows)).reshape(-1)
-    halo_rows = filtered(jnp.concatenate([lat_rows_raw, lev_rows_raw]),
-                         jnp.concatenate([lat_cuts, lev_cuts]), tables)
-    lat_count_rows = lat_rows_raw.shape[0]
-    lat_halo = halo_rows[:lat_count_rows].reshape(3, levels, 2, NLON)
-    lev_halo = halo_rows[lat_count_rows:].reshape(3, 2, lat_rows, NLON)
+    below = shift(field[:, levels - 1 :], "lev", True)
+    above = shift(field[:, :1], "lev", False)
+    south = shift(field[:, :, lat_rows - 1 :], "lat", True)
+    north = shift(field[:, :, :1], "lat", False)
 
     vertical_pad = jnp.concatenate([below_wind, vertical_wind, above_wind], axis=0)
-    field_lat = jnp.concatenate([lat_halo[:, :, :1], field, lat_halo[:, :, 1:]], axis=2)
-    field_lev = jnp.concatenate([lev_halo[:, :1], field, lev_halo[:, 1:]], axis=1)
+    field_lat = jnp.concatenate([south, field, north], axis=2)
+    field_lev = jnp.concatenate([below, field, above], axis=1)
 
     face_ids = (row_start + jnp.arange(lat_rows + 1, dtype=jnp.int32)).astype(jnp.float32)
     face_cos = jnp.sin(face_ids * (math.pi / total_rows))

time: 123 us -> 109 us (0.89)
  the two profiles are of different devices: /device:TPU:9 before, /device:TPU:47 now
where the time goes in v3:
time: 109 us
  waiting for transfers between devices  47.6 us (44%)
  starting transfers between devices  28.5 us (26%)
  matrix products  13.2 us (12%)
  other arithmetic  13.1 us (12%)
  local copies, waits for them, and re-layouts  4.34 us (4%)
  between operations  1.57 us (1%)
    ppermute x6, waiting for transfers between devices, shift(): return lax.ppermute(x, axis, pairs)  47.6 us
    ppermute x6, starting transfers between devices, shift(): return lax.ppermute(x, axis, pairs)  28.5 us
    concatenate x1, other arithmetic, parity_table(): return jnp.concatenate([cosines, sines], axis=-1).reshape(HALF, KMAX)  5.17 us
    dot_general x1, matrix products, lowpass_rows(): lax.dot_general(spec_odd * parity_weight(1, cut), odd_table, dims, precis...  4.38 us
    dot_general x1, matrix products, lowpass_rows(): jnp.dot(first - second, odd_table, precision=mxu_precision, preferred_ele...  4.3 us
    dot_general x1, matrix products, lowpass_rows(): lax.dot_general(spec_even * parity_weight(0, cut), even_table, dims, prec...  2.3 us
    dot_general x1, matrix products, lowpass_rows(): jnp.dot(first + second, even_table, precision=mxu_precision, preferred_el...  2.18 us
  transfers between devices with their start and end apart: 6, of which 4 were waited for; matrix products, arithmetic and copies ran while one was open for 10% of the time, Pallas kernels for 0%

profile of v3, /device:TPU:47, one launch (start us, length us, event | category | flops | bytes accessed | tf_op | source)
XLA Modules:
  0.0 108.6 jit_solution(6909298136201766340)
XLA Ops:
  0.6 1.0 fusion.21
  1.7 7.9 %collective-permute-start = (f32[1,16,2880]{2,1,0:T(8,128)S(1)}, f32[1,16,2880]{2,1,0:T(8,128)S(1)}, u32[]{:S(2)}, u32[]{:S(2)}) collective-permute-start(f32[1,16,2880]{2,1,0:T(8,128)S(1)} %get-tuple-element.71), channel_id=1, source_target_pairs={{0,1},{1,2},{2,3},{3,4},{4,5},{5,6},{6,7},{8,9},{9,10},{10,11},{11... | collective-permute-start | bytes 552968 | tf_op jit(solution)/shard_map/ppermute | solution.py:24
  9.6 2.2 %collective-permute-start.1 = (f32[1,16,2880]{2,1,0:T(8,128)S(1)}, f32[1,16,2880]{2,1,0:T(8,128)S(1)}, u32[]{:S(2)}, u32[]{:S(2)}) collective-permute-start(f32[1,16,2880]{2,1,0:T(8,128)S(1)} %get-tuple-element.70), channel_id=1, source_target_pairs={{1,0},{2,1},{3,2},{4,3},{5,4},{6,5},{7,6},{9,8},{10,9},{11,10},{12... | collective-permute-start | bytes 552968 | tf_op jit(solution)/shard_map/ppermute | solution.py:24
  11.8 1.4 %compare_reduce_fusion = (pred[]{:T(512)}, s32[16]{0:T(128)S(1)}) fusion(s32[512]{0:T(512)} %param.21, s32[]{:T(128)S(6)} %select_n.26), kind=kLoop, calls=%fused_computation.43 | loop fusion | flops 31 | bytes 133 | tf_op jit(solution)/shard_map/reduce_or | solution.py:76
  13.8 0.0 copy-start.3
  13.8 0.0 copy-start.4
  13.9 0.0 copy-start.7
  13.9 0.0 copy-start.8
  13.9 1.8 %pad_maximum_fusion.2 = f32[3,4,16,2880]{3,2,1,0:T(8,128)S(1)} fusion(f32[1,4,16,2880]{3,2,1,0:T(8,128)} %bitcast.46, f32[1,4,16,2880]{3,2,1,0:T(8,128)} %bitcast.47, f32[1,4,16,2880]{3,2,1,0:T(8,128)} %bitcast.48), kind=kLoop, calls=%fused_computation.22 | loop fusion | flops 1105920 | bytes 4423680 | tf_op jit(solution)/shard_map/stack | solution.py:88
  15.7 0.0 copy-start.1
  15.7 0.0 copy-start.5
  15.8 0.0 copy-start.6
  15.8 0.5 multiply_subtract_fusion.1
  16.2 0.4 copy-done.1
  16.6 0.0 copy-done.2
  16.6 0.5 multiply_subtract_fusion
  17.1 5.2 %pad_maximum_fusion = (f32[1440,720]{1,0:T(8,128)}, f32[1440,720]{1,0:T(8,128)}) fusion(f32[1440,360]{1,0:T(8,128)S(1)} %bitcast.40, f32[1440,360]{1,0:T(8,128)S(1)} %bitcast.39, f32[1440,360]{1,0:T(8,128)S(1)} %bitcast.42, f32[1440,360]{1,0:T(8,128)S(1)} %bitcast.41), kind=kLoop, calls=%fused_computation.10 | loop fusion | flops 2073600 | bytes 16588800 | tf_op jit(solution)/shard_map/concatenate | solution.py:46
  22.4 1.8 %collective-permute-done.1 = f32[1,16,2880]{2,1,0:T(8,128)S(1)} collective-permute-done((f32[1,16,2880]{2,1,0:T(8,128)S(1)}, f32[1,16,2880]{2,1,0:T(8,128)S(1)}, u32[]{:S(2)}, u32[]{:S(2)}) %collective-permute-start.1) | collective-permute-done | bytes 184352 | tf_op jit(solution)/shard_map/ppermute | solution.py:24
  24.2 14.3 %conditional.1 = (f32[192,2880]{1,0:T(8,128)S(1)}) conditional(s32[]{:T(128)} %convert_element_type.17, f32[192,2880]{1,0:T(8,128)S(1)} %bitcast.25, (s32[16]{0:T(128)S(1)}, f32[192,2880]{1,0:T(8,128)S(1)}, f32[1440,720]{1,0:T(8,128)}, f32[1440,720]{1,0:T(8,128)}) %tuple.39), branch_computations={%region_1.0_spmd, %region_2.3_spmd.clone} | conditional | flops 4780615680 | bytes 48165744 | solution.py:76
  24.2 0.1 reshape.116
  24.3 4.3 %convolution_multiply_fusion = f32[192,720]{1,0:T(8,128)S(1)} fusion(f32[1440,720]{1,0:T(8,128)} %get-tuple-element.53, f32[192,2880]{1,0:T(8,128)S(1)} %get-tuple-element.51, s32[720]{0:T(1024)} %constant.86.clone.2, s32[192]{0:T(256)S(1)} %reshape.116), kind=kOutput, calls=%fused_computation.1 | convolution fusion | flops 1195084800 | bytes 7063360 | tf_op jit(solution)/shard_map/cond/branch_1_fun/dot_general | solution.py:61
  28.6 0.0 copy-start.10
  28.6 4.4 %fusion.22 = f32[192,1440]{1,0:T(8,128)S(1)} fusion(f32[192,720]{1,0:T(8,128)S(1)} %convolution_multiply_fusion, f32[1440,720]{1,0:T(8,128)} %get-tuple-element.53), kind=kOutput, calls=%fused_computation.50 | convolution fusion | flops 1194393600 | bytes 5806080 | tf_op jit(solution)/shard_map/cond/branch_1_fun/dot_general | solution.py:66
  33.0 2.2 %convolution_multiply_fusion.1 = f32[192,720]{1,0:T(8,128)S(1)} fusion(f32[1440,720]{1,0:T(8,128)S(1)} %bitcast.37, f32[192,2880]{1,0:T(8,128)S(1)} %get-tuple-element.51, f32[720]{0:T(1024)S(1)} %copy-done.10, s32[720]{0:T(1024)S(1)} %copy-done.9, s32[192]{0:T(256)S(1)} %reshape.116), kind=kOutput, calls=%fused_computation.2 | convolution fusion | flops 1195084800 | bytes 7345152 | tf_op jit(solution)/shard_map/cond/branch_1_fun/dot_general | solution.py:59
  35.2 2.3 %fusion.18 = (f32[192,1440]{1,0:T(8,128)S(1)}, f32[192,1440]{1,0:T(8,128)S(1)}) fusion(f32[192,1440]{1,0:T(8,128)S(1)} %fusion.22, f32[192,720]{1,0:T(8,128)S(1)} %convolution_multiply_fusion.1, f32[1440,720]{1,0:T(8,128)S(1)} %bitcast.37), kind=kOutput, calls=%fused_computation.46 | convolution fusion | flops 1194946560 | bytes 8017920 | tf_op jit(solution)/shard_map/cond/branch_1_fun/dot_general | solution.py:64
  37.6 0.7 maximum_select_fusion
  38.5 0.1 slice.123
  38.5 0.3 slice.124
  38.8 0.6 slice.121
  39.5 0.2 fusion.19
  39.7 0.1 fusion.20
  39.7 0.1 fusion.17
  39.9 0.3 fusion.12
  40.2 0.1 slice.126
  40.3 6.4 %collective-permute-start.2 = (f32[3,4,1,2880]{3,2,1,0:T(1,128)S(1)}, f32[3,4,1,2880]{3,2,1,0:T(1,128)S(1)}, u32[]{:S(2)}, u32[]{:S(2)}) collective-permute-start(f32[3,4,1,2880]{3,2,1,0:T(1,128)S(1)} %get-tuple-element.67), channel_id=1, source_target_pairs={{0,8},{8,16},{16,24},{24,32},{32,40},{40,48},{48,56},{56,64},{64,7... | collective-permute-start | bytes 414728 | tf_op jit(solution)/shard_map/ppermute | solution.py:24
  46.7 1.9 %collective-permute-start.3 = (f32[3,4,1,2880]{3,2,1,0:T(1,128)S(1)}, f32[3,4,1,2880]{3,2,1,0:T(1,128)S(1)}, u32[]{:S(2)}, u32[]{:S(2)}) collective-permute-start(f32[3,4,1,2880]{3,2,1,0:T(1,128)S(1)} %get-tuple-element.66), channel_id=1, source_target_pairs={{8,0},{16,8},{24,16},{32,24},{40,32},{48,40},{56,48},{64,56},{72,6... | collective-permute-start | bytes 414728 | tf_op jit(solution)/shard_map/ppermute | solution.py:24
  48.7 7.4 %collective-permute-start.4 = (f32[3,1,16,2880]{3,2,1,0:T(8,128)S(1)}, f32[3,1,16,2880]{3,2,1,0:T(8,128)S(1)}, u32[]{:S(2)}, u32[]{:S(2)}) collective-permute-start(f32[3,1,16,2880]{3,2,1,0:T(8,128)S(1)} %get-tuple-element.69), channel_id=1, source_target_pairs={{0,1},{1,2},{2,3},{3,4},{4,5},{5,6},{6,7},{8,9},{9,10},{10,11},{11... | collective-permute-start | bytes 1658888 | tf_op jit(solution)/shard_map/ppermute | solution.py:24
  56.1 2.7 %collective-permute-start.5 = (f32[3,1,16,2880]{3,2,1,0:T(8,128)S(1)}, f32[3,1,16,2880]{3,2,1,0:T(8,128)S(1)}, u32[]{:S(2)}, u32[]{:S(2)}) collective-permute-start(f32[3,1,16,2880]{3,2,1,0:T(8,128)S(1)} %get-tuple-element.68), channel_id=1, source_target_pairs={{1,0},{2,1},{3,2},{4,3},{5,4},{6,5},{7,6},{9,8},{10,9},{11,10},{12... | collective-permute-start | bytes 1658888 | tf_op jit(solution)/shard_map/ppermute | solution.py:24
  58.8 0.1 fusion.16
  58.9 9.7 %collective-permute-done.2 = f32[3,4,1,2880]{3,2,1,0:T(1,128)S(1)} collective-permute-done((f32[3,4,1,2880]{3,2,1,0:T(1,128)S(1)}, f32[3,4,1,2880]{3,2,1,0:T(1,128)S(1)}, u32[]{:S(2)}, u32[]{:S(2)}) %collective-permute-start.2) | collective-permute-done | bytes 138272 | tf_op jit(solution)/shard_map/ppermute | solution.py:24
  68.6 0.2 fusion.15
  68.8 0.2 fusion.14
  69.0 0.6 fusion.6
  69.6 21.6 %collective-permute-done.4 = f32[3,1,16,2880]{3,2,1,0:T(8,128)S(1)} collective-permute-done((f32[3,1,16,2880]{3,2,1,0:T(8,128)S(1)}, f32[3,1,16,2880]{3,2,1,0:T(8,128)S(1)}, u32[]{:S(2)}, u32[]{:S(2)}) %collective-permute-start.4) | collective-permute-done | bytes 552992 | tf_op jit(solution)/shard_map/ppermute | solution.py:24
  91.2 14.5 %collective-permute-done.5 = f32[3,1,16,2880]{3,2,1,0:T(8,128)S(1)} collective-permute-done((f32[3,1,16,2880]{3,2,1,0:T(8,128)S(1)}, f32[3,1,16,2880]{3,2,1,0:T(8,128)S(1)}, u32[]{:S(2)}, u32[]{:S(2)}) %collective-permute-start.5) | collective-permute-done | bytes 552992 | tf_op jit(solution)/shard_map/ppermute | solution.py:24
  105.7 0.3 fusion.7
  106.0 1.2 %fusion.8 = f32[3,4,16,2880]{3,2,1,0:T(8,128)S(1)} fusion(f32[3,5,16,2880]{3,2,1,0:T(8,128)S(1)} %fusion.7, f32[3,4,16,2880]{3,2,1,0:T(8,128)S(1)} %bitcast.35, f32[3,4,17,2880]{3,2,1,0:T(8,128)S(1)} %fusion.6, f32[3,4,16,2880]{3,2,1,0:T(8,128)S(1)} %fusion.12, f32[3,4,16,2879]{3,2,1,0:T(8,128)S(1)} %bitcast.38, f32[3,4,16,1]{3,2,1,0:T(8,128)S(1)} %slice.126, ...), kind=kLoop, calls=%fused_computation.17 | loop fusion | flops 4423680 | bytes 17694784 | tf_op jit(solution)/shard_map/sub | solution.py:125
  107.2 1.4 %slice_bitcast_fusion = (f32[4,16,2880]{2,1,0:T(8,128)}, f32[4,16,2880]{2,1,0:T(8,128)}, f32[4,16,2880]{2,1,0:T(8,128)}) fusion(f32[3,4,16,2880]{3,2,1,0:T(8,128)S(1)} %fusion.8), kind=kLoop, calls=%fused_computation.38 | loop fusion | bytes 4423680 | tf_op jit(solution)/shard_map/squeeze | solution.py:126
  (25 shorter events, 0.2 us)
Async XLA Ops:
  1.7 20.7 %collective-permute-start = (f32[1,16,2880]{2,1,0:T(8,128)S(1)}, f32[1,16,2880]{2,1,0:T(8,128)S(1)}, u32[]{:S(2)}, u32[]{:S(2)}) collective-permute-start(f32[1,16,2880]{2,1,0:T(8,128)S(1)} %get-tuple-element.71), channel_id=1, source_target_pairs={{0,1},{1,2},{2,3},{3,4},{4,5},{5,6},{6,7},{8,9},{9,10},{10,11},{11... | collective-permute-start | bytes 552968 | tf_op jit(solution)/shard_map/ppermute | solution.py:24
  9.6 14.6 %collective-permute-start.1 = (f32[1,16,2880]{2,1,0:T(8,128)S(1)}, f32[1,16,2880]{2,1,0:T(8,128)S(1)}, u32[]{:S(2)}, u32[]{:S(2)}) collective-permute-start(f32[1,16,2880]{2,1,0:T(8,128)S(1)} %get-tuple-element.70), channel_id=1, source_target_pairs={{1,0},{2,1},{3,2},{4,3},{5,4},{6,5},{7,6},{9,8},{10,9},{11,10},{12... | collective-permute-start | bytes 552968 | tf_op jit(solution)/shard_map/ppermute | solution.py:24
  13.8 1.8 %copy-start.3 = (f32[48,360]{1,0:T(8,128)S(1)}, f32[48,360]{1,0:T(8,128)}, u32[]{:S(2)}) copy-start(f32[48,360]{1,0:T(8,128)} %constant.77.clone) | copy-start | bytes 207364
  13.8 1.8 %copy-start.4 = (f32[48,360]{1,0:T(8,128)S(1)}, f32[48,360]{1,0:T(8,128)}, u32[]{:S(2)}) copy-start(f32[48,360]{1,0:T(8,128)} %constant.78.clone) | copy-start | bytes 207364
  13.9 1.8 %copy-start.7 = (f32[30,360]{1,0:T(8,128)S(1)}, f32[30,360]{1,0:T(8,128)}, u32[]{:S(2)}) copy-start(f32[30,360]{1,0:T(8,128)} %constant.79.clone) | copy-start | bytes 129604
  13.9 1.8 %copy-start.8 = (f32[30,360]{1,0:T(8,128)S(1)}, f32[30,360]{1,0:T(8,128)}, u32[]{:S(2)}) copy-start(f32[30,360]{1,0:T(8,128)} %constant.80.clone) | copy-start | bytes 129604
  15.7 0.9 copy-start.1
  15.7 0.9 copy-start.2
  15.7 0.9 copy-start.5
  15.8 0.9 copy-start.6
  24.3 8.7 %slice-start = ((s8[4423680]{0:T(1024)(128)(4,1)}), s8[4194304]{0:T(1024)(128)(4,1)S(1)}, s32[]{:S(2)}) async-start(s8[4423680]{0:T(1024)(128)(4,1)} %bitcast.36), calls=%async_computation | async-start | bytes 8388608 | tf_op jit(solution)/shard_map/cond
  24.3 8.7 %slice-start.1 = ((s8[4423680]{0:T(1024)(128)(4,1)}), s8[229376]{0:T(1024)(128)(4,1)S(1)}, s32[]{:S(2)}) async-start(s8[4423680]{0:T(1024)(128)(4,1)} %bitcast.36), calls=%async_computation.1 | async-start | bytes 458752 | tf_op jit(solution)/shard_map/cond
  28.6 4.4 %copy-start.9 = (s32[720]{0:T(1024)S(1)}, s32[720]{0:T(1024)}, u32[]{:S(2)}) copy-start(s32[720]{0:T(1024)} %constant.85.clone.2) | copy-start | bytes 8644 | tf_op jit(solution)/shard_map/cond
  28.6 4.4 %copy-start.10 = (f32[720]{0:T(1024)S(1)}, f32[720]{0:T(1024)}, u32[]{:S(2)}) copy-start(f32[720]{0:T(1024)} %constant.93) | copy-start | bytes 8644 | tf_op jit(solution)/shard_map/cond
  39.8 18.9 %copy-start = (f32[4,16,2880]{2,1,0:T(8,128)S(1)}, f32[4,16,2880]{2,1,0:T(8,128)}, u32[]{:S(2)}) copy-start(f32[4,16,2880]{2,1,0:T(8,128)} %param.20) | copy-start | bytes 2211844
  40.3 28.3 %collective-permute-start.2 = (f32[3,4,1,2880]{3,2,1,0:T(1,128)S(1)}, f32[3,4,1,2880]{3,2,1,0:T(1,128)S(1)}, u32[]{:S(2)}, u32[]{:S(2)}) collective-permute-start(f32[3,4,1,2880]{3,2,1,0:T(1,128)S(1)} %get-tuple-element.67), channel_id=1, source_target_pairs={{0,8},{8,16},{16,24},{24,32},{32,40},{40,48},{48,56},{56,64},{64,7... | collective-permute-start | bytes 414728 | tf_op jit(solution)/shard_map/ppermute | solution.py:24
  46.7 21.9 %collective-permute-start.3 = (f32[3,4,1,2880]{3,2,1,0:T(1,128)S(1)}, f32[3,4,1,2880]{3,2,1,0:T(1,128)S(1)}, u32[]{:S(2)}, u32[]{:S(2)}) collective-permute-start(f32[3,4,1,2880]{3,2,1,0:T(1,128)S(1)} %get-tuple-element.66), channel_id=1, source_target_pairs={{8,0},{16,8},{24,16},{32,24},{40,32},{48,40},{56,48},{64,56},{72,6... | collective-permute-start | bytes 414728 | tf_op jit(solution)/shard_map/ppermute | solution.py:24
  48.7 42.5 %collective-permute-start.4 = (f32[3,1,16,2880]{3,2,1,0:T(8,128)S(1)}, f32[3,1,16,2880]{3,2,1,0:T(8,128)S(1)}, u32[]{:S(2)}, u32[]{:S(2)}) collective-permute-start(f32[3,1,16,2880]{3,2,1,0:T(8,128)S(1)} %get-tuple-element.69), channel_id=1, source_target_pairs={{0,1},{1,2},{2,3},{3,4},{4,5},{5,6},{6,7},{8,9},{9,10},{10,11},{11... | collective-permute-start | bytes 1658888 | tf_op jit(solution)/shard_map/ppermute | solution.py:24
  56.1 49.6 %collective-permute-start.5 = (f32[3,1,16,2880]{3,2,1,0:T(8,128)S(1)}, f32[3,1,16,2880]{3,2,1,0:T(8,128)S(1)}, u32[]{:S(2)}, u32[]{:S(2)}) collective-permute-start(f32[3,1,16,2880]{3,2,1,0:T(8,128)S(1)} %get-tuple-element.68), channel_id=1, source_target_pairs={{1,0},{2,1},{3,2},{4,3},{5,4},{6,5},{7,6},{9,8},{10,9},{11,10},{12... | collective-permute-start | bytes 1658888 | tf_op jit(solution)/shard_map/ppermute | solution.py:24

commit v4 on v3

--- a/solution.py
+++ b/solution.py
@@ -9,6 +9,7 @@
 NLON = 2880
 KMAX = 720
 HALF = NLON // 2
+CAP = 80
 
 zonal_scale = 0.1
 merid_scale = 0.1
@@ -22,6 +23,16 @@
     if not up:
         pairs = [(j, i) for i, j in pairs]
     return lax.ppermute(x, axis, pairs)
+
+
+def group_shift(x, lat_group, up):
+    lev_size = lax.axis_size("lev")
+    pairs = []
+    for lat in lat_group:
+        for lev in range(lev_size - 1):
+            source, target = lat * lev_size + lev, lat * lev_size + lev + 1
+            pairs.append((source, target) if up else (target, source))
+    return lax.ppermute(x, ("lat", "lev"), pairs)
 
 
 def split_angles(modes):
@@ -87,14 +98,23 @@
 
     stacked = jnp.stack([zonal_wind, merid_wind, tracer])
     levels = stacked.shape[1]
+    pole_rows = [min(j, total_rows - 1 - j) + 1 <= CAP for j in range(total_rows)]
+    filter_lat = [i for i in range(lat_count) if any(pole_rows[i * lat_rows:(i + 1) * lat_rows])]
+    plain_lat = [i for i in range(lat_count) if i not in filter_lat]
     below_wind = shift(vertical_wind[levels - 1 :], "lev", True)
     above_wind = shift(vertical_wind[:1], "lev", False)
+    below_plain = group_shift(stacked[:, levels - 1 :], plain_lat, True)
+    above_plain = group_shift(stacked[:, :1], plain_lat, False)
 
     tables = (parity_table(0), parity_table(1))
-    stacked, below_wind, above_wind = lax.optimization_barrier((stacked, below_wind, above_wind))
+    stacked, below_wind, above_wind, below_plain, above_plain = lax.optimization_barrier(
+        (stacked, below_wind, above_wind, below_plain, above_plain))
     field = filtered(stacked, own_cut, tables)
-    below = shift(field[:, levels - 1 :], "lev", True)
-    above = shift(field[:, :1], "lev", False)
+    below_filtered = group_shift(field[:, levels - 1 :], filter_lat, True)
+    above_filtered = group_shift(field[:, :1], filter_lat, False)
+    is_filter = jnp.any(lat_index == jnp.asarray(filter_lat, jnp.int32))
+    below = jnp.where(is_filter, below_filtered, below_plain)
+    above = jnp.where(is_filter, above_filtered, above_plain)
     south = shift(field[:, :, lat_rows - 1 :], "lat", True)
     north = shift(field[:, :, :1], "lat", False)
 

time: 109 us -> 101 us (0.927)
  the two profiles are of different devices: /device:TPU:47 before, /device:TPU:70 now
where the time goes in v4:
time: 101 us
  waiting for transfers between devices  43.9 us (43%)
  starting transfers between devices  19.2 us (19%)
  other arithmetic  17.4 us (17%)
  matrix products  12.8 us (13%)
  local copies, waits for them, and re-layouts  5.84 us (6%)
  between operations  1.62 us (2%)
    ppermute x4, waiting for transfers between devices, shift(): return lax.ppermute(x, axis, pairs)  43.9 us
    ppermute x4, starting transfers between devices, shift(): return lax.ppermute(x, axis, pairs)  14.4 us
    concatenate x1, other arithmetic, parity_table(): return jnp.concatenate([cosines, sines], axis=-1).reshape(HALF, KMAX)  5.17 us
    ppermute x4, starting transfers between devices, group_shift(): return lax.ppermute(x, ('lat', 'lev'), pairs)  4.78 us
    dot_general x1, matrix products, lowpass_rows(): lax.dot_general(spec_odd * parity_weight(1, cut), odd_table, dims, precis...  4.37 us
    dot_general x1, matrix products, lowpass_rows(): jnp.dot(first - second, odd_table, precision=mxu_precision, preferred_ele...  4.3 us
    dot_general x1, matrix products, lowpass_rows(): lax.dot_general(spec_even * parity_weight(0, cut), even_table, dims, prec...  2.16 us
  transfers between devices with their start and end apart: 8, of which 2 were waited for; matrix products, arithmetic and copies ran while one was open for 16% of the time, Pallas kernels for 0%

profile of v4, /device:TPU:70, one launch (start us, length us, event | category | flops | bytes accessed | tf_op | source)
XLA Modules:
  0.0 100.8 jit_solution(5704233810720501212)
XLA Ops:
  0.6 1.0 %fusion.22 = (f32[1,16,2880]{2,1,0:T(8,128)S(1)}, f32[1,16,2880]{2,1,0:T(8,128)S(1)}) fusion(f32[4,16,2880]{2,1,0:T(8,128)} %param.21), kind=kLoop, calls=%fused_computation.53 | loop fusion | bytes 737280 | tf_op jit(solution)/shard_map/slice | solution.py:105
  1.7 7.3 %collective-permute-start = (f32[1,16,2880]{2,1,0:T(8,128)S(1)}, f32[1,16,2880]{2,1,0:T(8,128)S(1)}, u32[]{:S(2)}, u32[]{:S(2)}) collective-permute-start(f32[1,16,2880]{2,1,0:T(8,128)S(1)} %get-tuple-element.77), channel_id=1, source_target_pairs={{0,1},{1,2},{2,3},{3,4},{4,5},{5,6},{6,7},{8,9},{9,10},{10,11},{11... | collective-permute-start | bytes 552968 | tf_op jit(solution)/shard_map/ppermute | solution.py:25
  9.0 1.3 %collective-permute-start.1 = (f32[1,16,2880]{2,1,0:T(8,128)S(1)}, f32[1,16,2880]{2,1,0:T(8,128)}, u32[]{:S(2)}, u32[]{:S(2)}) collective-permute-start(f32[1,16,2880]{2,1,0:T(8,128)S(1)} %get-tuple-element.76), channel_id=1, source_target_pairs={{1,0},{2,1},{3,2},{4,3},{5,4},{6,5},{7,6},{9,8},{10,9},{11,10},{12... | collective-permute-start | bytes 552968 | tf_op jit(solution)/shard_map/ppermute | solution.py:25
  10.3 1.7 %pad_maximum_fusion.2 = f32[3,4,16,2880]{3,2,1,0:T(8,128)S(1)} fusion(f32[1,4,16,2880]{3,2,1,0:T(8,128)} %bitcast.46, f32[1,4,16,2880]{3,2,1,0:T(8,128)} %bitcast.47, f32[1,4,16,2880]{3,2,1,0:T(8,128)} %bitcast.48), kind=kLoop, calls=%fused_computation.22 | loop fusion | flops 1105920 | bytes 4423680 | tf_op jit(solution)/shard_map/stack | solution.py:99
  12.0 0.0 copy-start.3
  12.0 0.0 copy-start.6
  12.0 1.1 %fusion.21 = (f32[3,1,16,2880]{3,2,1,0:T(8,128)}, f32[3,1,16,2880]{3,2,1,0:T(8,128)}) fusion(f32[3,4,16,2880]{3,2,1,0:T(8,128)S(1)} %pad_maximum_fusion.2), kind=kLoop, calls=%fused_computation.52 | loop fusion | bytes 2211840 | tf_op jit(solution)/shard_map/slice | solution.py:107
  13.1 1.5 %collective-permute-start.2 = (f32[3,1,16,2880]{3,2,1,0:T(8,128)}, f32[3,1,16,2880]{3,2,1,0:T(8,128)}, u32[]{:S(2)}, u32[]{:S(2)}) collective-permute-start(f32[3,1,16,2880]{3,2,1,0:T(8,128)} %get-tuple-element.75), channel_id=1, source_target_pairs={{40,41},{41,42},{42,43},{43,44},{44,45},{45,46},{46,47},{48,49},{4... | collective-permute-start | bytes 1658888 | tf_op jit(solution)/shard_map/ppermute | solution.py:35
  14.6 0.7 collective-permute-start.3
  15.3 0.6 sine_multiply_fusion
  15.8 1.4 %compare_reduce_fusion.1 = (pred[]{:T(512)}, s32[16]{0:T(128)S(1)}) fusion(s32[512]{0:T(512)} %param.22, s32[]{:T(128)S(6)} %select_n.38), kind=kLoop, calls=%fused_computation.46 | loop fusion | flops 31 | bytes 133 | tf_op jit(solution)/shard_map/reduce_or | solution.py:87
  17.9 0.0 copy-start.1
  17.9 0.0 copy-start.2
  17.9 0.0 copy-start.5
  18.0 1.4 %multiply_subtract_fusion.1 = (f32[30,48,360]{2,1,0:T(8,128)S(1)}, f32[30,48,360]{2,1,0:T(8,128)S(1)}) fusion(f32[30,360]{1,0:T(8,128)S(1)} %copy-done.6, f32[48,360]{1,0:T(8,128)S(1)} %copy-done.3, f32[30,360]{1,0:T(8,128)} %constant.81.clone, f32[48,360]{1,0:T(8,128)} %constant.79.clone), kind=kLoop, calls=%fused_computation.29 | loop fusion | flops 3110400 | bytes 4371840 | tf_op jit(solution)/shard_map/sub | solution.py:55
  19.4 0.5 multiply_subtract_fusion
  19.9 5.2 %pad_maximum_fusion = (f32[1440,720]{1,0:T(8,128)}, f32[1440,720]{1,0:T(8,128)}) fusion(f32[1440,360]{1,0:T(8,128)S(1)} %bitcast.40, f32[1440,360]{1,0:T(8,128)S(1)} %bitcast.39, f32[1440,360]{1,0:T(8,128)S(1)} %bitcast.42, f32[1440,360]{1,0:T(8,128)S(1)} %bitcast.41), kind=kLoop, calls=%fused_computation.10 | loop fusion | flops 2073600 | bytes 16588800 | tf_op jit(solution)/shard_map/concatenate | solution.py:57
  25.2 0.6 compare_reduce_fusion
  25.8 25.3 %collective-permute-done.1 = f32[1,16,2880]{2,1,0:T(8,128)} collective-permute-done((f32[1,16,2880]{2,1,0:T(8,128)S(1)}, f32[1,16,2880]{2,1,0:T(8,128)}, u32[]{:S(2)}, u32[]{:S(2)}) %collective-permute-start.1) | collective-permute-done | bytes 184352 | tf_op jit(solution)/shard_map/ppermute | solution.py:25
  51.1 13.7 %conditional.1 = (f32[192,2880]{1,0:T(8,128)S(1)}) conditional(s32[]{:T(128)} %convert_element_type.17, f32[192,2880]{1,0:T(8,128)S(1)} %bitcast.25, (s32[16]{0:T(128)S(1)}, f32[192,2880]{1,0:T(8,128)S(1)}, f32[1440,720]{1,0:T(8,128)}, f32[1440,720]{1,0:T(8,128)}) %tuple.40), branch_computations={%region_1.0_spmd, %region_2.3_spmd.clone} | conditional | flops 4780615680 | bytes 48165744 | solution.py:87
  51.1 0.1 reshape.116
  51.2 4.3 %convolution_multiply_fusion = f32[192,720]{1,0:T(8,128)S(1)} fusion(f32[1440,720]{1,0:T(8,128)} %get-tuple-element.57, f32[192,2880]{1,0:T(8,128)S(1)} %get-tuple-element.55, s32[720]{0:T(1024)} %constant.88.clone.2, s32[192]{0:T(256)S(1)} %reshape.116), kind=kOutput, calls=%fused_computation.1 | convolution fusion | flops 1195084800 | bytes 7063360 | tf_op jit(solution)/shard_map/cond/branch_1_fun/dot_general | solution.py:72
  55.5 4.4 %fusion.23 = f32[192,1440]{1,0:T(8,128)S(1)} fusion(f32[192,720]{1,0:T(8,128)S(1)} %convolution_multiply_fusion, f32[1440,720]{1,0:T(8,128)} %get-tuple-element.57), kind=kOutput, calls=%fused_computation.54 | convolution fusion | flops 1194393600 | bytes 5806080 | tf_op jit(solution)/shard_map/cond/branch_1_fun/dot_general | solution.py:77
  59.9 1.9 %convolution_multiply_fusion.1 = f32[192,720]{1,0:T(8,128)S(1)} fusion(f32[1440,720]{1,0:T(8,128)S(1)} %bitcast.37, f32[192,2880]{1,0:T(8,128)S(1)} %get-tuple-element.55, f32[720]{0:T(1024)S(1)} %copy-done.7, s32[720]{0:T(1024)S(1)} %copy-done.8, s32[192]{0:T(256)S(1)} %reshape.116), kind=kOutput, calls=%fused_computation.2 | convolution fusion | flops 1195084800 | bytes 7345152 | tf_op jit(solution)/shard_map/cond/branch_1_fun/dot_general | solution.py:70
  61.9 2.2 %fusion.18 = (f32[192,1440]{1,0:T(8,128)S(1)}, f32[192,1440]{1,0:T(8,128)S(1)}) fusion(f32[192,1440]{1,0:T(8,128)S(1)} %fusion.23, f32[192,720]{1,0:T(8,128)S(1)} %convolution_multiply_fusion.1, f32[1440,720]{1,0:T(8,128)S(1)} %bitcast.37), kind=kOutput, calls=%fused_computation.49 | convolution fusion | flops 1194946560 | bytes 8017920 | tf_op jit(solution)/shard_map/cond/branch_1_fun/dot_general | solution.py:75
  64.1 0.7 maximum_select_fusion
  64.8 0.1 fusion.20
  64.9 0.2 fusion.19
  65.1 0.6 slice.131
  65.8 0.3 slice.134
  66.1 1.3 %collective-permute-start.6 = (f32[3,1,16,2880]{3,2,1,0:T(8,128)S(1)}, f32[3,1,16,2880]{3,2,1,0:T(8,128)S(1)}, u32[]{:S(2)}, u32[]{:S(2)}) collective-permute-start(f32[3,1,16,2880]{3,2,1,0:T(8,128)S(1)} %get-tuple-element.73), channel_id=1, source_target_pairs={{0,1},{1,2},{2,3},{3,4},{4,5},{5,6},{6,7},{8,9},{9,10},{10,11},{11... | collective-permute-start | bytes 1658888 | tf_op jit(solution)/shard_map/ppermute | solution.py:35
  67.4 1.3 %collective-permute-start.7 = (f32[3,1,16,2880]{3,2,1,0:T(8,128)S(1)}, f32[3,1,16,2880]{3,2,1,0:T(8,128)S(1)}, u32[]{:S(2)}, u32[]{:S(2)}) collective-permute-start(f32[3,1,16,2880]{3,2,1,0:T(8,128)S(1)} %get-tuple-element.72), channel_id=1, source_target_pairs={{1,0},{2,1},{3,2},{4,3},{5,4},{6,5},{7,6},{9,8},{10,9},{11,10},{12... | collective-permute-start | bytes 1658888 | tf_op jit(solution)/shard_map/ppermute | solution.py:35
  68.7 1.9 %collective-permute-start.4 = (f32[3,4,1,2880]{3,2,1,0:T(1,128)S(1)}, f32[3,4,1,2880]{3,2,1,0:T(1,128)S(1)}, u32[]{:S(2)}, u32[]{:S(2)}) collective-permute-start(f32[3,4,1,2880]{3,2,1,0:T(1,128)S(1)} %get-tuple-element.71), channel_id=1, source_target_pairs={{0,8},{8,16},{16,24},{24,32},{32,40},{40,48},{48,56},{56,64},{64,7... | collective-permute-start | bytes 414728 | tf_op jit(solution)/shard_map/ppermute | solution.py:25
  70.6 3.9 %collective-permute-start.5 = (f32[3,4,1,2880]{3,2,1,0:T(1,128)S(1)}, f32[3,4,1,2880]{3,2,1,0:T(1,128)S(1)}, u32[]{:S(2)}, u32[]{:S(2)}) collective-permute-start(f32[3,4,1,2880]{3,2,1,0:T(1,128)S(1)} %get-tuple-element.70), channel_id=1, source_target_pairs={{8,0},{16,8},{24,16},{32,24},{40,32},{48,40},{56,48},{64,56},{72,6... | collective-permute-start | bytes 414728 | tf_op jit(solution)/shard_map/ppermute | solution.py:25
  74.5 0.1 fusion.17
  74.6 0.3 fusion.12
  74.9 0.8 copy-done
  75.7 1.0 %fusion.16 = f32[5,16,2880]{2,1,0:T(8,128)S(1)} fusion(f32[4,16,2880]{2,1,0:T(8,128)S(1)} %copy-done, f32[1,16,2880]{2,1,0:T(8,128)S(1)} %collective-permute-done, f32[1,16,2880]{2,1,0:T(8,128)} %collective-permute-done.1), kind=kLoop, calls=%fused_computation.37 | loop fusion | flops 921600 | bytes 2027520 | tf_op jit(solution)/shard_map/mul | solution.py:143
  76.8 0.1 slice.136
  76.9 18.6 %collective-permute-done.4 = f32[3,4,1,2880]{3,2,1,0:T(1,128)S(1)} collective-permute-done((f32[3,4,1,2880]{3,2,1,0:T(1,128)S(1)}, f32[3,4,1,2880]{3,2,1,0:T(1,128)S(1)}, u32[]{:S(2)}, u32[]{:S(2)}) %collective-permute-start.4) | collective-permute-done | bytes 138272 | tf_op jit(solution)/shard_map/ppermute | solution.py:25
  95.5 0.2 fusion.15
  95.7 0.2 fusion.14
  95.9 0.6 fusion.6
  96.5 0.7 broadcast_select_fusion.1
  97.2 0.7 broadcast_select_fusion
  98.0 0.3 fusion.7
  98.3 1.2 %fusion.8 = f32[3,4,16,2880]{3,2,1,0:T(8,128)S(1)} fusion(f32[3,5,16,2880]{3,2,1,0:T(8,128)S(1)} %fusion.7, f32[3,4,16,2880]{3,2,1,0:T(8,128)S(1)} %bitcast.35, f32[3,4,17,2880]{3,2,1,0:T(8,128)S(1)} %fusion.6, f32[3,4,16,2880]{3,2,1,0:T(8,128)S(1)} %fusion.12, f32[3,4,16,2879]{3,2,1,0:T(8,128)S(1)} %bitcast.38, f32[3,4,16,1]{3,2,1,0:T(8,128)S(1)} %slice.136, ...), kind=kLoop, calls=%fused_computation.17 | loop fusion | flops 4423680 | bytes 17694784 | tf_op jit(solution)/shard_map/sub | solution.py:145
  99.4 1.4 %slice_bitcast_fusion = (f32[4,16,2880]{2,1,0:T(8,128)}, f32[4,16,2880]{2,1,0:T(8,128)}, f32[4,16,2880]{2,1,0:T(8,128)}) fusion(f32[3,4,16,2880]{3,2,1,0:T(8,128)S(1)} %fusion.8), kind=kLoop, calls=%fused_computation.38 | loop fusion | bytes 4423680 | tf_op jit(solution)/shard_map/squeeze | solution.py:146
  (33 shorter events, 0.2 us)
Async XLA Ops:
  1.7 24.1 %collective-permute-start = (f32[1,16,2880]{2,1,0:T(8,128)S(1)}, f32[1,16,2880]{2,1,0:T(8,128)S(1)}, u32[]{:S(2)}, u32[]{:S(2)}) collective-permute-start(f32[1,16,2880]{2,1,0:T(8,128)S(1)} %get-tuple-element.77), channel_id=1, source_target_pairs={{0,1},{1,2},{2,3},{3,4},{4,5},{5,6},{6,7},{8,9},{9,10},{10,11},{11... | collective-permute-start | bytes 552968 | tf_op jit(solution)/shard_map/ppermute | solution.py:25
  9.0 42.1 %collective-permute-start.1 = (f32[1,16,2880]{2,1,0:T(8,128)S(1)}, f32[1,16,2880]{2,1,0:T(8,128)}, u32[]{:S(2)}, u32[]{:S(2)}) collective-permute-start(f32[1,16,2880]{2,1,0:T(8,128)S(1)} %get-tuple-element.76), channel_id=1, source_target_pairs={{1,0},{2,1},{3,2},{4,3},{5,4},{6,5},{7,6},{9,8},{10,9},{11,10},{12... | collective-permute-start | bytes 552968 | tf_op jit(solution)/shard_map/ppermute | solution.py:25
  12.0 5.9 %copy-start.3 = (f32[48,360]{1,0:T(8,128)S(1)}, f32[48,360]{1,0:T(8,128)}, u32[]{:S(2)}) copy-start(f32[48,360]{1,0:T(8,128)} %constant.80.clone) | copy-start | bytes 207364
  12.0 5.9 %copy-start.6 = (f32[30,360]{1,0:T(8,128)S(1)}, f32[30,360]{1,0:T(8,128)}, u32[]{:S(2)}) copy-start(f32[30,360]{1,0:T(8,128)} %constant.82.clone) | copy-start | bytes 129604
  13.1 38.0 %collective-permute-start.2 = (f32[3,1,16,2880]{3,2,1,0:T(8,128)}, f32[3,1,16,2880]{3,2,1,0:T(8,128)}, u32[]{:S(2)}, u32[]{:S(2)}) collective-permute-start(f32[3,1,16,2880]{3,2,1,0:T(8,128)} %get-tuple-element.75), channel_id=1, source_target_pairs={{40,41},{41,42},{42,43},{43,44},{44,45},{45,46},{46,47},{48,49},{4... | collective-permute-start | bytes 1658888 | tf_op jit(solution)/shard_map/ppermute | solution.py:35
  14.6 36.5 %collective-permute-start.3 = (f32[3,1,16,2880]{3,2,1,0:T(8,128)}, f32[3,1,16,2880]{3,2,1,0:T(8,128)S(1)}, u32[]{:S(2)}, u32[]{:S(2)}) collective-permute-start(f32[3,1,16,2880]{3,2,1,0:T(8,128)} %get-tuple-element.74), channel_id=1, source_target_pairs={{41,40},{42,41},{43,42},{44,43},{45,44},{46,45},{47,46},{49,48},{5... | collective-permute-start | bytes 1658888 | tf_op jit(solution)/shard_map/ppermute | solution.py:35
  17.9 1.5 %copy-start.1 = (f32[48,360]{1,0:T(8,128)S(1)}, f32[48,360]{1,0:T(8,128)}, u32[]{:S(2)}) copy-start(f32[48,360]{1,0:T(8,128)} %constant.84.clone) | copy-start | bytes 207364
  17.9 1.5 %copy-start.2 = (f32[48,360]{1,0:T(8,128)S(1)}, f32[48,360]{1,0:T(8,128)}, u32[]{:S(2)}) copy-start(f32[48,360]{1,0:T(8,128)} %constant.83.clone) | copy-start | bytes 207364
  17.9 1.5 %copy-start.4 = (f32[30,360]{1,0:T(8,128)S(1)}, f32[30,360]{1,0:T(8,128)}, u32[]{:S(2)}) copy-start(f32[30,360]{1,0:T(8,128)} %constant.86.clone) | copy-start | bytes 129604
  17.9 1.5 %copy-start.5 = (f32[30,360]{1,0:T(8,128)S(1)}, f32[30,360]{1,0:T(8,128)}, u32[]{:S(2)}) copy-start(f32[30,360]{1,0:T(8,128)} %constant.85.clone) | copy-start | bytes 129604
  19.9 5.2 %copy-start.10 = (s32[10]{0:T(128)S(1)}, s32[10]{0:T(128)}, u32[]{:S(2)}) copy-start(s32[10]{0:T(128)} %constant.89.clone) | copy-start | bytes 124
  51.1 8.8 %slice-start = ((s8[4423680]{0:T(1024)(128)(4,1)}), s8[229376]{0:T(1024)(128)(4,1)S(1)}, s32[]{:S(2)}) async-start(s8[4423680]{0:T(1024)(128)(4,1)} %bitcast.36), calls=%async_computation | async-start | bytes 458752 | tf_op jit(solution)/shard_map/cond
  51.2 8.7 %slice-start.1 = ((s8[4423680]{0:T(1024)(128)(4,1)}), s8[4194304]{0:T(1024)(128)(4,1)S(1)}, s32[]{:S(2)}) async-start(s8[4423680]{0:T(1024)(128)(4,1)} %bitcast.36), calls=%async_computation.1 | async-start | bytes 8388608 | tf_op jit(solution)/shard_map/cond
  55.5 4.4 %copy-start.7 = (f32[720]{0:T(1024)S(1)}, f32[720]{0:T(1024)}, u32[]{:S(2)}) copy-start(f32[720]{0:T(1024)} %constant.96) | copy-start | bytes 8644 | tf_op jit(solution)/shard_map/cond
  55.5 4.4 %copy-start.8 = (s32[720]{0:T(1024)S(1)}, s32[720]{0:T(1024)}, u32[]{:S(2)}) copy-start(s32[720]{0:T(1024)} %constant.87.clone.2) | copy-start | bytes 8644 | tf_op jit(solution)/shard_map/cond
  66.1 30.4 %collective-permute-start.6 = (f32[3,1,16,2880]{3,2,1,0:T(8,128)S(1)}, f32[3,1,16,2880]{3,2,1,0:T(8,128)S(1)}, u32[]{:S(2)}, u32[]{:S(2)}) collective-permute-start(f32[3,1,16,2880]{3,2,1,0:T(8,128)S(1)} %get-tuple-element.73), channel_id=1, source_target_pairs={{0,1},{1,2},{2,3},{3,4},{4,5},{5,6},{6,7},{8,9},{9,10},{10,11},{11... | collective-permute-start | bytes 1658888 | tf_op jit(solution)/shard_map/ppermute | solution.py:35
  67.4 29.8 %collective-permute-start.7 = (f32[3,1,16,2880]{3,2,1,0:T(8,128)S(1)}, f32[3,1,16,2880]{3,2,1,0:T(8,128)S(1)}, u32[]{:S(2)}, u32[]{:S(2)}) collective-permute-start(f32[3,1,16,2880]{3,2,1,0:T(8,128)S(1)} %get-tuple-element.72), channel_id=1, source_target_pairs={{1,0},{2,1},{3,2},{4,3},{5,4},{6,5},{7,6},{9,8},{10,9},{11,10},{12... | collective-permute-start | bytes 1658888 | tf_op jit(solution)/shard_map/ppermute | solution.py:35
  68.7 26.8 %collective-permute-start.4 = (f32[3,4,1,2880]{3,2,1,0:T(1,128)S(1)}, f32[3,4,1,2880]{3,2,1,0:T(1,128)S(1)}, u32[]{:S(2)}, u32[]{:S(2)}) collective-permute-start(f32[3,4,1,2880]{3,2,1,0:T(1,128)S(1)} %get-tuple-element.71), channel_id=1, source_target_pairs={{0,8},{8,16},{16,24},{24,32},{32,40},{40,48},{48,56},{56,64},{64,7... | collective-permute-start | bytes 414728 | tf_op jit(solution)/shard_map/ppermute | solution.py:25
  70.6 24.8 %collective-permute-start.5 = (f32[3,4,1,2880]{3,2,1,0:T(1,128)S(1)}, f32[3,4,1,2880]{3,2,1,0:T(1,128)S(1)}, u32[]{:S(2)}, u32[]{:S(2)}) collective-permute-start(f32[3,4,1,2880]{3,2,1,0:T(1,128)S(1)} %get-tuple-element.70), channel_id=1, source_target_pairs={{8,0},{16,8},{24,16},{32,24},{40,32},{48,40},{56,48},{64,56},{72,6... | collective-permute-start | bytes 414728 | tf_op jit(solution)/shard_map/ppermute | solution.py:25
  74.6 1.1 %copy-start = (f32[4,16,2880]{2,1,0:T(8,128)S(1)}, f32[4,16,2880]{2,1,0:T(8,128)}, u32[]{:S(2)}) copy-start(f32[4,16,2880]{2,1,0:T(8,128)} %param.21) | copy-start | bytes 2211844
  76.8 18.9 %copy-start.9 = (f32[17]{0:T(128)S(1)}, f32[17]{0:T(128)}, u32[]{:S(2)}) copy-start(f32[17]{0:T(128)} %sine_multiply_fusion) | copy-start | bytes 208

commit v5 on v4

--- a/solution.py
+++ b/solution.py
@@ -101,15 +101,16 @@
     pole_rows = [min(j, total_rows - 1 - j) + 1 <= CAP for j in range(total_rows)]
     filter_lat = [i for i in range(lat_count) if any(pole_rows[i * lat_rows:(i + 1) * lat_rows])]
     plain_lat = [i for i in range(lat_count) if i not in filter_lat]
-    below_wind = shift(vertical_wind[levels - 1 :], "lev", True)
-    above_wind = shift(vertical_wind[:1], "lev", False)
     below_plain = group_shift(stacked[:, levels - 1 :], plain_lat, True)
     above_plain = group_shift(stacked[:, :1], plain_lat, False)
 
     tables = (parity_table(0), parity_table(1))
-    stacked, below_wind, above_wind, below_plain, above_plain = lax.optimization_barrier(
-        (stacked, below_wind, above_wind, below_plain, above_plain))
+    stacked, below_plain, above_plain = lax.optimization_barrier((stacked, below_plain, above_plain))
     field = filtered(stacked, own_cut, tables)
+    top_wind, bottom_wind, field = lax.optimization_barrier(
+        (vertical_wind[levels - 1 :], vertical_wind[:1], field))
+    below_wind = shift(top_wind, "lev", True)
+    above_wind = shift(bottom_wind, "lev", False)
     below_filtered = group_shift(field[:, levels - 1 :], filter_lat, True)
     above_filtered = group_shift(field[:, :1], filter_lat, False)
     is_filter = jnp.any(lat_index == jnp.asarray(filter_lat, jnp.int32))

time: 101 us -> 114 us (1.13)
  the two profiles are of different devices: /device:TPU:70 before, /device:TPU:25 now
where the time goes in v5:
time: 114 us; the launch traced here: 113 us
  waiting for transfers between devices  42.2 us (37%)
  starting transfers between devices  28.5 us (25%)
  other arithmetic  23.6 us (21%)
  matrix products  13.2 us (12%)
  local copies, waits for them, and re-layouts  3.99 us (4%)
  between operations  1.55 us (1%)
    ppermute x4, waiting for transfers between devices, group_shift(): return lax.ppermute(x, ('lat', 'lev'), pairs)  41.3 us
    ppermute x4, starting transfers between devices, shift(): return lax.ppermute(x, axis, pairs)  16.1 us
    ppermute x4, starting transfers between devices, group_shift(): return lax.ppermute(x, ('lat', 'lev'), pairs)  12.4 us
    concatenate x1, other arithmetic, parity_table(): return jnp.concatenate([cosines, sines], axis=-1).reshape(HALF, KMAX)  8.76 us
    sub x2, other arithmetic, parity_table(): cosines = cos_lo * cos_hi - sin_lo * sin_hi  5.96 us
    dot_general x1, matrix products, lowpass_rows(): lax.dot_general(spec_odd * parity_weight(1, cut), odd_table, dims, precis...  4.37 us
    dot_general x1, matrix products, lowpass_rows(): jnp.dot(first - second, odd_table, precision=mxu_precision, preferred_ele...  4.3 us
    dot_general x1, matrix products, lowpass_rows(): lax.dot_general(spec_even * parity_weight(0, cut), even_table, dims, prec...  2.3 us
  transfers between devices with their start and end apart: 8, of which 3 were waited for; matrix products, arithmetic and copies ran while one was open for 17% of the time, Pallas kernels for 0%

profile of v5, /device:TPU:25, one launch (start us, length us, event | category | flops | bytes accessed | tf_op | source)
XLA Modules:
  0.0 113.3 jit_solution(18193440822891279107)
XLA Ops:
  0.6 1.7 %pad_maximum_fusion.2 = f32[3,4,16,2880]{3,2,1,0:T(8,128)S(1)} fusion(f32[1,4,16,2880]{3,2,1,0:T(8,128)} %bitcast.44, f32[1,4,16,2880]{3,2,1,0:T(8,128)} %bitcast.45, f32[1,4,16,2880]{3,2,1,0:T(8,128)} %bitcast.46), kind=kLoop, calls=%fused_computation.22 | loop fusion | flops 1105920 | bytes 4423680 | tf_op jit(solution)/shard_map/stack | solution.py:99
  2.4 0.0 copy-start.9
  2.4 0.0 copy-start.3
  2.4 0.0 copy-start.4
  2.4 1.1 fusion.22
  3.5 1.5 %collective-permute-start = (f32[3,1,16,2880]{3,2,1,0:T(8,128)}, f32[3,1,16,2880]{3,2,1,0:T(8,128)}, u32[]{:S(2)}, u32[]{:S(2)}) collective-permute-start(f32[3,1,16,2880]{3,2,1,0:T(8,128)} %get-tuple-element.84), channel_id=1, source_target_pairs={{40,41},{41,42},{42,43},{43,44},{44,45},{45,46},{46,47},{48,49},{4... | collective-permute-start | bytes 1658888 | tf_op jit(solution)/shard_map/ppermute | solution.py:35
  5.0 1.5 %collective-permute-start.1 = (f32[3,1,16,2880]{3,2,1,0:T(8,128)}, f32[3,1,16,2880]{3,2,1,0:T(8,128)}, u32[]{:S(2)}, u32[]{:S(2)}) collective-permute-start(f32[3,1,16,2880]{3,2,1,0:T(8,128)} %get-tuple-element.83), channel_id=1, source_target_pairs={{41,40},{42,41},{43,42},{44,43},{45,44},{46,45},{47,46},{49,48},{5... | collective-permute-start | bytes 1658888 | tf_op jit(solution)/shard_map/ppermute | solution.py:35
  6.6 0.7 compare_reduce_fusion
  7.2 0.0 copy-start.5
  7.2 0.0 copy-start.6
  7.3 3.5 %multiply_subtract_fusion.1 = (f32[30,48,360]{2,1,0:T(8,128)}, f32[30,48,360]{2,1,0:T(8,128)}) fusion(f32[30,360]{1,0:T(8,128)} %constant.82.clone, f32[48,360]{1,0:T(8,128)S(1)} %copy-done.4, f32[30,360]{1,0:T(8,128)} %constant.81.clone, f32[48,360]{1,0:T(8,128)S(1)} %copy-done.3), kind=kLoop, calls=%fused_computation.29 | loop fusion | flops 3110400 | bytes 4371840 | tf_op jit(solution)/shard_map/sub | solution.py:55
  10.7 2.5 %multiply_subtract_fusion = (f32[30,48,360]{2,1,0:T(8,128)}, f32[30,48,360]{2,1,0:T(8,128)}) fusion(f32[30,360]{1,0:T(8,128)S(1)} %copy-done.6, f32[48,360]{1,0:T(8,128)S(1)} %copy-done.2, f32[30,360]{1,0:T(8,128)S(1)} %copy-done.5, f32[48,360]{1,0:T(8,128)S(1)} %copy-done.1), kind=kLoop, calls=%fused_computation.27 | loop fusion | flops 3110400 | bytes 4371840 | tf_op jit(solution)/shard_map/sub | solution.py:55
  13.2 1.4 %compare_reduce_fusion.1 = (pred[]{:T(512)}, s32[16]{0:T(128)S(1)}) fusion(s32[512]{0:T(512)} %param.22, s32[]{:T(128)S(6)} %select_n.38), kind=kLoop, calls=%fused_computation.50 | loop fusion | flops 31 | bytes 133 | tf_op jit(solution)/shard_map/reduce_or | solution.py:87
  15.3 8.8 %pad_maximum_fusion = (f32[1440,720]{1,0:T(8,128)}, f32[1440,720]{1,0:T(8,128)}) fusion(f32[1440,360]{1,0:T(8,128)} %bitcast.41, f32[1440,360]{1,0:T(8,128)} %bitcast.40, f32[1440,360]{1,0:T(8,128)} %bitcast.43, f32[1440,360]{1,0:T(8,128)} %bitcast.42), kind=kLoop, calls=%fused_computation.10 | loop fusion | flops 2073600 | bytes 16588800 | tf_op jit(solution)/shard_map/concatenate | solution.py:57
  24.1 14.3 %conditional.1 = (f32[3,4,16,2880]{3,2,1,0:T(8,128)S(1)}) conditional(s32[]{:T(128)} %convert_element_type.17, f32[192,2880]{1,0:T(8,128)S(1)} %bitcast.33, (s32[16]{0:T(128)S(1)}, f32[192,2880]{1,0:T(8,128)S(1)}, f32[1440,720]{1,0:T(8,128)}, f32[1440,720]{1,0:T(8,128)}) %tuple.56), branch_computations={%region_1.0_spmd, %region_2.3_spmd.clone} | conditional | flops 4780615680 | bytes 48165744 | solution.py:87
  24.3 0.1 reshape.107
  24.4 4.3 %convolution_multiply_fusion = f32[192,720]{1,0:T(8,128)S(1)} fusion(f32[1440,720]{1,0:T(8,128)} %get-tuple-element.66, f32[192,2880]{1,0:T(8,128)S(1)} %get-tuple-element.64, s32[720]{0:T(1024)} %constant.88.clone.2, s32[192]{0:T(256)S(1)} %reshape.107), kind=kOutput, calls=%fused_computation.1 | convolution fusion | flops 1195084800 | bytes 7063360 | tf_op jit(solution)/shard_map/cond/branch_1_fun/dot_general | solution.py:72
  28.7 0.0 copy-start.7
  28.7 4.4 %fusion.24 = f32[192,1440]{1,0:T(8,128)S(1)} fusion(f32[192,720]{1,0:T(8,128)S(1)} %convolution_multiply_fusion, f32[1440,720]{1,0:T(8,128)} %get-tuple-element.66), kind=kOutput, calls=%fused_computation.58 | convolution fusion | flops 1194393600 | bytes 5806080 | tf_op jit(solution)/shard_map/cond/branch_1_fun/dot_general | solution.py:77
  33.1 2.2 %convolution_multiply_fusion.1 = f32[192,720]{1,0:T(8,128)S(1)} fusion(f32[1440,720]{1,0:T(8,128)S(1)} %bitcast.38, f32[192,2880]{1,0:T(8,128)S(1)} %get-tuple-element.64, f32[720]{0:T(1024)S(1)} %copy-done.8, s32[720]{0:T(1024)S(1)} %copy-done.7, s32[192]{0:T(256)S(1)} %reshape.107), kind=kOutput, calls=%fused_computation.2 | convolution fusion | flops 1195084800 | bytes 7345152 | tf_op jit(solution)/shard_map/cond/branch_1_fun/dot_general | solution.py:70
  35.3 2.3 %fusion.19 = (f32[192,1440]{1,0:T(8,128)S(1)}, f32[192,1440]{1,0:T(8,128)S(1)}) fusion(f32[192,1440]{1,0:T(8,128)S(1)} %fusion.24, f32[192,720]{1,0:T(8,128)S(1)} %convolution_multiply_fusion.1, f32[1440,720]{1,0:T(8,128)S(1)} %bitcast.38), kind=kOutput, calls=%fused_computation.53 | convolution fusion | flops 1194946560 | bytes 8017920 | tf_op jit(solution)/shard_map/cond/branch_1_fun/dot_general | solution.py:75
  37.6 0.7 maximum_select_fusion
  38.4 0.1 slice_bitcast_fusion.4
  38.4 0.3 slice_bitcast_fusion.3
  38.7 0.6 slice.105
  39.3 0.2 fusion.20
  39.5 4.1 %collective-permute-start.2 = (f32[3,4,1,2880]{3,2,1,0:T(1,128)S(1)}, f32[3,4,1,2880]{3,2,1,0:T(1,128)S(1)}, u32[]{:S(2)}, u32[]{:S(2)}) collective-permute-start(f32[3,4,1,2880]{3,2,1,0:T(1,128)S(1)} %get-tuple-element.80), channel_id=1, source_target_pairs={{0,8},{8,16},{16,24},{24,32},{32,40},{40,48},{48,56},{56,64},{64,7... | collective-permute-start | bytes 414728 | tf_op jit(solution)/shard_map/ppermute | solution.py:25
  43.7 1.9 %collective-permute-start.3 = (f32[3,4,1,2880]{3,2,1,0:T(1,128)S(1)}, f32[3,4,1,2880]{3,2,1,0:T(1,128)S(1)}, u32[]{:S(2)}, u32[]{:S(2)}) collective-permute-start(f32[3,4,1,2880]{3,2,1,0:T(1,128)S(1)} %get-tuple-element.79), channel_id=1, source_target_pairs={{8,0},{16,8},{24,16},{32,24},{40,32},{48,40},{56,48},{64,56},{72,6... | collective-permute-start | bytes 414728 | tf_op jit(solution)/shard_map/ppermute | solution.py:25
  45.6 0.1 fusion.18
  45.7 0.3 fusion.12
  46.0 0.1 fusion.21
  46.1 0.1 slice.132
  46.2 7.9 %collective-permute-start.6 = (f32[1,16,2880]{2,1,0:T(8,128)S(1)}, f32[1,16,2880]{2,1,0:T(8,128)S(1)}, u32[]{:S(2)}, u32[]{:S(2)}) collective-permute-start(f32[1,16,2880]{2,1,0:T(8,128)S(1)} %get-tuple-element.56), channel_id=1, source_target_pairs={{0,1},{1,2},{2,3},{3,4},{4,5},{5,6},{6,7},{8,9},{9,10},{10,11},{11... | collective-permute-start | bytes 552968 | tf_op jit(solution)/shard_map/ppermute | solution.py:25
  54.1 2.2 %collective-permute-start.7 = (f32[1,16,2880]{2,1,0:T(8,128)S(1)}, f32[1,16,2880]{2,1,0:T(8,128)S(1)}, u32[]{:S(2)}, u32[]{:S(2)}) collective-permute-start(f32[1,16,2880]{2,1,0:T(8,128)S(1)} %get-tuple-element.57), channel_id=1, source_target_pairs={{1,0},{2,1},{3,2},{4,3},{5,4},{6,5},{7,6},{9,8},{10,9},{11,10},{12... | collective-permute-start | bytes 552968 | tf_op jit(solution)/shard_map/ppermute | solution.py:25
  56.3 7.2 %collective-permute-start.5 = (f32[3,1,16,2880]{3,2,1,0:T(8,128)S(1)}, f32[3,1,16,2880]{3,2,1,0:T(8,128)S(1)}, u32[]{:S(2)}, u32[]{:S(2)}) collective-permute-start(f32[3,1,16,2880]{3,2,1,0:T(8,128)S(1)} %get-tuple-element.81), channel_id=1, source_target_pairs={{1,0},{2,1},{3,2},{4,3},{5,4},{6,5},{7,6},{9,8},{10,9},{11,10},{12... | collective-permute-start | bytes 1658888 | tf_op jit(solution)/shard_map/ppermute | solution.py:35
  63.5 2.2 %collective-permute-start.4 = (f32[3,1,16,2880]{3,2,1,0:T(8,128)S(1)}, f32[3,1,16,2880]{3,2,1,0:T(8,128)S(1)}, u32[]{:S(2)}, u32[]{:S(2)}) collective-permute-start(f32[3,1,16,2880]{3,2,1,0:T(8,128)S(1)} %get-tuple-element.82), channel_id=1, source_target_pairs={{0,1},{1,2},{2,3},{3,4},{4,5},{5,6},{6,7},{8,9},{9,10},{10,11},{11... | collective-permute-start | bytes 1658888 | tf_op jit(solution)/shard_map/ppermute | solution.py:35
  65.8 0.2 fusion.15
  65.9 0.2 fusion.14
  66.1 0.6 fusion.6
  66.7 0.9 collective-permute-done.7
  67.6 0.1 fusion.16
  67.7 19.1 %collective-permute-done.5 = f32[3,1,16,2880]{3,2,1,0:T(8,128)S(1)} collective-permute-done((f32[3,1,16,2880]{3,2,1,0:T(8,128)S(1)}, f32[3,1,16,2880]{3,2,1,0:T(8,128)S(1)}, u32[]{:S(2)}, u32[]{:S(2)}) %collective-permute-start.5) | collective-permute-done | bytes 552992 | tf_op jit(solution)/shard_map/ppermute | solution.py:35
  86.8 0.7 broadcast_select_fusion
  87.5 22.3 %collective-permute-done.4 = f32[3,1,16,2880]{3,2,1,0:T(8,128)S(1)} collective-permute-done((f32[3,1,16,2880]{3,2,1,0:T(8,128)S(1)}, f32[3,1,16,2880]{3,2,1,0:T(8,128)S(1)}, u32[]{:S(2)}, u32[]{:S(2)}) %collective-permute-start.4) | collective-permute-done | bytes 552992 | tf_op jit(solution)/shard_map/ppermute | solution.py:35
  109.8 0.7 broadcast_select_fusion.1
  110.5 0.3 fusion.7
  110.8 1.1 fusion.8
  111.9 1.4 %slice_bitcast_fusion = (f32[4,16,2880]{2,1,0:T(8,128)}, f32[4,16,2880]{2,1,0:T(8,128)}, f32[4,16,2880]{2,1,0:T(8,128)}) fusion(f32[3,4,16,2880]{3,2,1,0:T(8,128)S(1)} %fusion.8), kind=kLoop, calls=%fused_computation.38 | loop fusion | bytes 4423680 | tf_op jit(solution)/shard_map/squeeze | solution.py:147
  (31 shorter events, 0.2 us)
Async XLA Ops:
  2.4 4.1 %copy-start = (f32[4,16,2880]{2,1,0:T(8,128)S(1)}, f32[4,16,2880]{2,1,0:T(8,128)}, u32[]{:S(2)}) copy-start(f32[4,16,2880]{2,1,0:T(8,128)} %param.21) | copy-start | bytes 2211844
  2.4 4.2 %copy-start.9 = (s32[10]{0:T(128)S(1)}, s32[10]{0:T(128)}, u32[]{:S(2)}) copy-start(s32[10]{0:T(128)} %constant.89.clone) | copy-start | bytes 124
  2.4 4.8 %copy-start.3 = (f32[48,360]{1,0:T(8,128)S(1)}, f32[48,360]{1,0:T(8,128)}, u32[]{:S(2)}) copy-start(f32[48,360]{1,0:T(8,128)} %constant.79.clone) | copy-start | bytes 207364
  2.4 4.8 %copy-start.4 = (f32[48,360]{1,0:T(8,128)S(1)}, f32[48,360]{1,0:T(8,128)}, u32[]{:S(2)}) copy-start(f32[48,360]{1,0:T(8,128)} %constant.80.clone) | copy-start | bytes 207364
  3.5 20.6 %collective-permute-start = (f32[3,1,16,2880]{3,2,1,0:T(8,128)}, f32[3,1,16,2880]{3,2,1,0:T(8,128)}, u32[]{:S(2)}, u32[]{:S(2)}) collective-permute-start(f32[3,1,16,2880]{3,2,1,0:T(8,128)} %get-tuple-element.84), channel_id=1, source_target_pairs={{40,41},{41,42},{42,43},{43,44},{44,45},{45,46},{46,47},{48,49},{4... | collective-permute-start | bytes 1658888 | tf_op jit(solution)/shard_map/ppermute | solution.py:35
  5.0 19.1 %collective-permute-start.1 = (f32[3,1,16,2880]{3,2,1,0:T(8,128)}, f32[3,1,16,2880]{3,2,1,0:T(8,128)}, u32[]{:S(2)}, u32[]{:S(2)}) collective-permute-start(f32[3,1,16,2880]{3,2,1,0:T(8,128)} %get-tuple-element.83), channel_id=1, source_target_pairs={{41,40},{42,41},{43,42},{44,43},{45,44},{46,45},{47,46},{49,48},{5... | collective-permute-start | bytes 1658888 | tf_op jit(solution)/shard_map/ppermute | solution.py:35
  7.2 3.5 %copy-start.1 = (f32[48,360]{1,0:T(8,128)S(1)}, f32[48,360]{1,0:T(8,128)}, u32[]{:S(2)}) copy-start(f32[48,360]{1,0:T(8,128)} %constant.83.clone) | copy-start | bytes 207364
  7.2 3.5 %copy-start.2 = (f32[48,360]{1,0:T(8,128)S(1)}, f32[48,360]{1,0:T(8,128)}, u32[]{:S(2)}) copy-start(f32[48,360]{1,0:T(8,128)} %constant.84.clone) | copy-start | bytes 207364
  7.2 3.5 %copy-start.5 = (f32[30,360]{1,0:T(8,128)S(1)}, f32[30,360]{1,0:T(8,128)}, u32[]{:S(2)}) copy-start(f32[30,360]{1,0:T(8,128)} %constant.85.clone) | copy-start | bytes 129604
  7.2 3.5 %copy-start.6 = (f32[30,360]{1,0:T(8,128)S(1)}, f32[30,360]{1,0:T(8,128)}, u32[]{:S(2)}) copy-start(f32[30,360]{1,0:T(8,128)} %constant.86.clone) | copy-start | bytes 129604
  24.3 8.7 %slice-start = ((s8[4423680]{0:T(1024)(128)(4,1)}), s8[4194304]{0:T(1024)(128)(4,1)S(1)}, s32[]{:S(2)}) async-start(s8[4423680]{0:T(1024)(128)(4,1)} %bitcast.37), calls=%async_computation | async-start | bytes 8388608 | tf_op jit(solution)/shard_map/cond
  24.3 8.7 %slice-start.1 = ((s8[4423680]{0:T(1024)(128)(4,1)}), s8[229376]{0:T(1024)(128)(4,1)S(1)}, s32[]{:S(2)}) async-start(s8[4423680]{0:T(1024)(128)(4,1)} %bitcast.37), calls=%async_computation.1 | async-start | bytes 458752 | tf_op jit(solution)/shard_map/cond
  28.7 4.4 %copy-start.7 = (s32[720]{0:T(1024)S(1)}, s32[720]{0:T(1024)}, u32[]{:S(2)}) copy-start(s32[720]{0:T(1024)} %constant.87.clone.2) | copy-start | bytes 8644 | tf_op jit(solution)/shard_map/cond
  28.7 4.4 %copy-start.8 = (f32[720]{0:T(1024)S(1)}, f32[720]{0:T(1024)}, u32[]{:S(2)}) copy-start(f32[720]{0:T(1024)} %constant.96) | copy-start | bytes 8644 | tf_op jit(solution)/shard_map/cond
  39.5 23.9 %collective-permute-start.2 = (f32[3,4,1,2880]{3,2,1,0:T(1,128)S(1)}, f32[3,4,1,2880]{3,2,1,0:T(1,128)S(1)}, u32[]{:S(2)}, u32[]{:S(2)}) collective-permute-start(f32[3,4,1,2880]{3,2,1,0:T(1,128)S(1)} %get-tuple-element.80), channel_id=1, source_target_pairs={{0,8},{8,16},{16,24},{24,32},{32,40},{40,48},{48,56},{56,64},{64,7... | collective-permute-start | bytes 414728 | tf_op jit(solution)/shard_map/ppermute | solution.py:25
  43.7 22.1 %collective-permute-start.3 = (f32[3,4,1,2880]{3,2,1,0:T(1,128)S(1)}, f32[3,4,1,2880]{3,2,1,0:T(1,128)S(1)}, u32[]{:S(2)}, u32[]{:S(2)}) collective-permute-start(f32[3,4,1,2880]{3,2,1,0:T(1,128)S(1)} %get-tuple-element.79), channel_id=1, source_target_pairs={{8,0},{16,8},{24,16},{32,24},{40,32},{48,40},{56,48},{64,56},{72,6... | collective-permute-start | bytes 414728 | tf_op jit(solution)/shard_map/ppermute | solution.py:25
  46.2 20.6 %collective-permute-start.6 = (f32[1,16,2880]{2,1,0:T(8,128)S(1)}, f32[1,16,2880]{2,1,0:T(8,128)S(1)}, u32[]{:S(2)}, u32[]{:S(2)}) collective-permute-start(f32[1,16,2880]{2,1,0:T(8,128)S(1)} %get-tuple-element.56), channel_id=1, source_target_pairs={{0,1},{1,2},{2,3},{3,4},{4,5},{5,6},{6,7},{8,9},{9,10},{10,11},{11... | collective-permute-start | bytes 552968 | tf_op jit(solution)/shard_map/ppermute | solution.py:25
  54.1 13.5 %collective-permute-start.7 = (f32[1,16,2880]{2,1,0:T(8,128)S(1)}, f32[1,16,2880]{2,1,0:T(8,128)S(1)}, u32[]{:S(2)}, u32[]{:S(2)}) collective-permute-start(f32[1,16,2880]{2,1,0:T(8,128)S(1)} %get-tuple-element.57), channel_id=1, source_target_pairs={{1,0},{2,1},{3,2},{4,3},{5,4},{6,5},{7,6},{9,8},{10,9},{11,10},{12... | collective-permute-start | bytes 552968 | tf_op jit(solution)/shard_map/ppermute | solution.py:25
  56.3 30.5 %collective-permute-start.5 = (f32[3,1,16,2880]{3,2,1,0:T(8,128)S(1)}, f32[3,1,16,2880]{3,2,1,0:T(8,128)S(1)}, u32[]{:S(2)}, u32[]{:S(2)}) collective-permute-start(f32[3,1,16,2880]{3,2,1,0:T(8,128)S(1)} %get-tuple-element.81), channel_id=1, source_target_pairs={{1,0},{2,1},{3,2},{4,3},{5,4},{6,5},{7,6},{9,8},{10,9},{11,10},{12... | collective-permute-start | bytes 1658888 | tf_op jit(solution)/shard_map/ppermute | solution.py:35
  63.5 46.3 %collective-permute-start.4 = (f32[3,1,16,2880]{3,2,1,0:T(8,128)S(1)}, f32[3,1,16,2880]{3,2,1,0:T(8,128)S(1)}, u32[]{:S(2)}, u32[]{:S(2)}) collective-permute-start(f32[3,1,16,2880]{3,2,1,0:T(8,128)S(1)} %get-tuple-element.82), channel_id=1, source_target_pairs={{0,1},{1,2},{2,3},{3,4},{4,5},{5,6},{6,7},{8,9},{9,10},{10,11},{11... | collective-permute-start | bytes 1658888 | tf_op jit(solution)/shard_map/ppermute | solution.py:35

commit v6 on v5

--- a/solution.py
+++ b/solution.py
@@ -35,26 +35,20 @@
     return lax.ppermute(x, ("lat", "lev"), pairs)
 
 
-def split_angles(modes):
+def parity_table(parity):
     low = 48
-    m_lo = np.arange(low)[:, None]
-    m_hi = (low * np.arange(HALF // low))[:, None]
-    k = np.asarray(modes)[None, :]
+    modes = np.arange(parity, KMAX, 2)
+    k = np.concatenate([modes, modes])[None, :]
+    is_sin = np.arange(KMAX)[None, :] >= KMAX // 2
     step = 2.0 * np.pi / NLON
-    lo = (m_lo * k) % NLON * step
-    hi = (m_hi * k) % NLON * step
+    lo = (np.arange(low)[:, None] * k) % NLON * step
+    hi = (low * np.arange(HALF // low)[:, None] * k) % NLON * step
+    first = np.where(is_sin, np.sin(lo), np.cos(lo))
+    turn = np.where(is_sin, np.cos(lo), -np.sin(lo))
     as_f32 = lambda v: jnp.asarray(v.astype(np.float32))
-    return as_f32(np.cos(lo)), as_f32(np.sin(lo)), as_f32(np.cos(hi)), as_f32(np.sin(hi))
-
-
-def parity_table(parity):
-    modes = np.arange(parity, KMAX, 2)
-    cos_lo, sin_lo, cos_hi, sin_hi = split_angles(modes)
-    cos_lo, sin_lo = cos_lo[None], sin_lo[None]
-    cos_hi, sin_hi = cos_hi[:, None], sin_hi[:, None]
-    cosines = cos_lo * cos_hi - sin_lo * sin_hi
-    sines = sin_lo * cos_hi + cos_lo * sin_hi
-    return jnp.concatenate([cosines, sines], axis=-1).reshape(HALF, KMAX)
+    table = (as_f32(first)[None] * as_f32(np.cos(hi))[:, None]
+             + as_f32(turn)[None] * as_f32(np.sin(hi))[:, None])
+    return table.reshape(HALF, KMAX)
 
 
 def parity_weight(parity, cut):
@@ -101,21 +95,23 @@
     pole_rows = [min(j, total_rows - 1 - j) + 1 <= CAP for j in range(total_rows)]
     filter_lat = [i for i in range(lat_count) if any(pole_rows[i * lat_rows:(i + 1) * lat_rows])]
     plain_lat = [i for i in range(lat_count) if i not in filter_lat]
-    below_plain = group_shift(stacked[:, levels - 1 :], plain_lat, True)
-    above_plain = group_shift(stacked[:, :1], plain_lat, False)
+    top = jnp.concatenate([stacked[:, levels - 1], vertical_wind[levels - 1 :]], axis=0)
+    bottom = jnp.concatenate([stacked[:, 0], vertical_wind[:1]], axis=0)
+    below_plain = group_shift(top, plain_lat, True)
+    above_plain = group_shift(bottom, plain_lat, False)
 
     tables = (parity_table(0), parity_table(1))
     stacked, below_plain, above_plain = lax.optimization_barrier((stacked, below_plain, above_plain))
     field = filtered(stacked, own_cut, tables)
-    top_wind, bottom_wind, field = lax.optimization_barrier(
-        (vertical_wind[levels - 1 :], vertical_wind[:1], field))
-    below_wind = shift(top_wind, "lev", True)
-    above_wind = shift(bottom_wind, "lev", False)
-    below_filtered = group_shift(field[:, levels - 1 :], filter_lat, True)
-    above_filtered = group_shift(field[:, :1], filter_lat, False)
+    top = jnp.concatenate([field[:, levels - 1], vertical_wind[levels - 1 :]], axis=0)
+    bottom = jnp.concatenate([field[:, 0], vertical_wind[:1]], axis=0)
+    below_filtered = group_shift(top, filter_lat, True)
+    above_filtered = group_shift(bottom, filter_lat, False)
     is_filter = jnp.any(lat_index == jnp.asarray(filter_lat, jnp.int32))
-    below = jnp.where(is_filter, below_filtered, below_plain)
-    above = jnp.where(is_filter, above_filtered, above_plain)
+    below_all = jnp.where(is_filter, below_filtered, below_plain)
+    above_all = jnp.where(is_filter, above_filtered, above_plain)
+    below, below_wind = below_all[:3, None], below_all[3:]
+    above, above_wind = above_all[:3, None], above_all[3:]
     south = shift(field[:, :, lat_rows - 1 :], "lat", True)
     north = shift(field[:, :, :1], "lat", False)
 

time: 114 us -> 103 us (0.904)
  the two profiles are of different devices: /device:TPU:25 before, /device:TPU:233 now
where the time goes in v6:
time: 103 us
  starting transfers between devices  51.2 us (50%)
  waiting for transfers between devices  33.8 us (33%)
  other arithmetic  12.6 us (12%)
  local copies, waits for them, and re-layouts  3.98 us (4%)
  between operations  1.53 us (1%)
    ppermute x2, starting transfers between devices, shift(): return lax.ppermute(x, axis, pairs)  40.6 us
    ppermute x4, waiting for transfers between devices, group_shift(): return lax.ppermute(x, ('lat', 'lev'), pairs)  28.2 us
    ppermute x4, starting transfers between devices, group_shift(): return lax.ppermute(x, ('lat', 'lev'), pairs)  10.6 us
    ppermute x2, waiting for transfers between devices, shift(): return lax.ppermute(x, axis, pairs)  5.6 us
  transfers between devices with their start and end apart: 6, of which 3 were waited for; matrix products, arithmetic and copies ran while one was open for 6% of the time, Pallas kernels for 0%

profile of v6, /device:TPU:233, one launch (start us, length us, event | category | flops | bytes accessed | tf_op | source)
XLA Modules:
  0.0 103.1 jit_solution(8192812318801459690)
XLA Ops:
  0.6 1.7 %pad_maximum_fusion = f32[3,4,16,2880]{3,2,1,0:T(8,128)S(1)} fusion(f32[1,4,16,2880]{3,2,1,0:T(8,128)} %bitcast.64, f32[1,4,16,2880]{3,2,1,0:T(8,128)} %bitcast.65, f32[1,4,16,2880]{3,2,1,0:T(8,128)} %bitcast.66), kind=kLoop, calls=%fused_computation.22 | loop fusion | flops 1105920 | bytes 4423680 | tf_op jit(solution)/shard_map/stack | solution.py:93
  2.4 0.0 copy-start
  2.4 0.1 slice_bitcast_fusion.7
  2.5 1.0 copy-done
  3.5 0.0 copy-start.8
  3.5 0.9 pad_maximum_fusion.4
  4.5 4.1 %collective-permute-start = (f32[4,16,2880]{2,1,0:T(8,128)}, f32[4,16,2880]{2,1,0:T(8,128)}, u32[]{:S(2)}, u32[]{:S(2)}) collective-permute-start(f32[4,16,2880]{2,1,0:T(8,128)} %pad_maximum_fusion.4), channel_id=1, source_target_pairs={{40,41},{41,42},{42,43},{43,44},{44,45},{45,46},{46,47},{48,49},{4... | collective-permute-start | bytes 2211848 | tf_op jit(solution)/shard_map/ppermute | solution.py:35
  8.5 0.9 pad_maximum_fusion.6
  9.5 5.1 %collective-permute-start.1 = (f32[4,16,2880]{2,1,0:T(8,128)}, f32[4,16,2880]{2,1,0:T(8,128)}, u32[]{:S(2)}, u32[]{:S(2)}) collective-permute-start(f32[4,16,2880]{2,1,0:T(8,128)} %pad_maximum_fusion.6), channel_id=1, source_target_pairs={{41,40},{42,41},{43,42},{44,43},{45,44},{46,45},{47,46},{49,48},{5... | collective-permute-start | bytes 2211848 | tf_op jit(solution)/shard_map/ppermute | solution.py:35
  14.6 1.4 %compare_reduce_fusion.1 = (pred[]{:T(512)}, s32[16]{0:T(128)S(1)}) fusion(s32[512]{0:T(512)} %param.22, s32[]{:T(128)S(6)} %select_n.38), kind=kLoop, calls=%fused_computation.52 | loop fusion | flops 31 | bytes 133 | tf_op jit(solution)/shard_map/reduce_or | solution.py:81
  16.7 0.0 copy-done.8
  16.7 0.6 compare_reduce_fusion
  17.4 10.9 %collective-permute-done = f32[4,16,2880]{2,1,0:T(8,128)} collective-permute-done((f32[4,16,2880]{2,1,0:T(8,128)}, f32[4,16,2880]{2,1,0:T(8,128)}, u32[]{:S(2)}, u32[]{:S(2)}) %collective-permute-start) | collective-permute-done | bytes 737312 | tf_op jit(solution)/shard_map/ppermute | solution.py:35
  28.3 17.3 %collective-permute-done.1 = f32[4,16,2880]{2,1,0:T(8,128)} collective-permute-done((f32[4,16,2880]{2,1,0:T(8,128)}, f32[4,16,2880]{2,1,0:T(8,128)}, u32[]{:S(2)}, u32[]{:S(2)}) %collective-permute-start.1) | collective-permute-done | bytes 737312 | tf_op jit(solution)/shard_map/ppermute | solution.py:35
  45.6 0.3 slice.152
  45.9 0.6 slice.149
  46.6 0.2 fusion.19
  46.8 0.1 slice_bitcast_fusion.4
  46.8 0.1 fusion.17
  46.9 0.3 fusion.12
  47.3 0.1 slice.154
  47.4 38.7 %collective-permute-start.2 = (f32[3,4,1,2880]{3,2,1,0:T(1,128)S(1)}, f32[3,4,1,2880]{3,2,1,0:T(1,128)S(1)}, u32[]{:S(2)}, u32[]{:S(2)}) collective-permute-start(f32[3,4,1,2880]{3,2,1,0:T(1,128)S(1)} %get-tuple-element.131), channel_id=1, source_target_pairs={{0,8},{8,16},{16,24},{24,32},{32,40},{40,48},{48,56},{56,64},{64,7... | collective-permute-start | bytes 414728 | tf_op jit(solution)/shard_map/ppermute | solution.py:25
  86.1 1.9 %collective-permute-start.3 = (f32[3,4,1,2880]{3,2,1,0:T(1,128)S(1)}, f32[3,4,1,2880]{3,2,1,0:T(1,128)S(1)}, u32[]{:S(2)}, u32[]{:S(2)}) collective-permute-start(f32[3,4,1,2880]{3,2,1,0:T(1,128)S(1)} %get-tuple-element.130), channel_id=1, source_target_pairs={{8,0},{16,8},{24,16},{32,24},{40,32},{48,40},{56,48},{64,56},{72,6... | collective-permute-start | bytes 414728 | tf_op jit(solution)/shard_map/ppermute | solution.py:25
  88.0 0.1 pad_maximum_fusion.5
  88.1 0.7 collective-permute-start.5
  88.8 0.1 pad_maximum_fusion.3
  88.8 0.7 collective-permute-start.4
  89.6 0.0 collective-permute-done.2
  89.6 5.6 %collective-permute-done.3 = f32[3,4,1,2880]{3,2,1,0:T(1,128)S(1)} collective-permute-done((f32[3,4,1,2880]{3,2,1,0:T(1,128)S(1)}, f32[3,4,1,2880]{3,2,1,0:T(1,128)S(1)}, u32[]{:S(2)}, u32[]{:S(2)}) %collective-permute-start.3) | collective-permute-done | bytes 138272 | tf_op jit(solution)/shard_map/ppermute | solution.py:25
  95.2 0.2 fusion.15
  95.3 0.2 fusion.14
  95.5 0.6 fusion.6
  96.2 0.0 collective-permute-done.5
  96.2 1.9 %broadcast_select_fusion = f32[4,16,2880]{2,1,0:T(8,128)S(1)} fusion(f32[4,16,2880]{2,1,0:T(8,128)S(1)} %collective-permute-done.5, f32[4,16,2880]{2,1,0:T(8,128)} %collective-permute-done.1, pred[]{:T(512)} %compare_reduce_fusion), kind=kLoop, calls=%fused_computation.49 | loop fusion | flops 184320 | bytes 2211841 | tf_op jit(solution)/shard_map/jit(_where)/select_n | solution.py:112
  98.1 0.0 collective-permute-done.4
  98.1 1.9 %broadcast_select_fusion.1 = f32[4,16,2880]{2,1,0:T(8,128)S(1)} fusion(f32[4,16,2880]{2,1,0:T(8,128)S(1)} %collective-permute-done.4, f32[4,16,2880]{2,1,0:T(8,128)} %collective-permute-done, pred[]{:T(512)} %compare_reduce_fusion), kind=kLoop, calls=%fused_computation.50 | loop fusion | flops 184320 | bytes 2211841 | tf_op jit(solution)/shard_map/jit(_where)/select_n | solution.py:111
  100.1 0.1 fusion.16
  100.2 0.3 fusion.7
  100.5 1.2 %fusion.8 = f32[3,4,16,2880]{3,2,1,0:T(8,128)S(1)} fusion(f32[3,5,16,2880]{3,2,1,0:T(8,128)S(1)} %fusion.7, f32[3,4,16,2880]{3,2,1,0:T(8,128)S(1)} %bitcast.55, f32[3,4,17,2880]{3,2,1,0:T(8,128)S(1)} %fusion.6, f32[3,4,16,2880]{3,2,1,0:T(8,128)S(1)} %fusion.12, f32[3,4,16,2879]{3,2,1,0:T(8,128)S(1)} %bitcast.60, f32[3,4,16,1]{3,2,1,0:T(8,128)S(1)} %slice.154, ...), kind=kLoop, calls=%fused_computation.17 | loop fusion | flops 4423680 | bytes 17694784 | tf_op jit(solution)/shard_map/sub | solution.py:142
  101.7 1.4 %slice_bitcast_fusion = (f32[4,16,2880]{2,1,0:T(8,128)}, f32[4,16,2880]{2,1,0:T(8,128)}, f32[4,16,2880]{2,1,0:T(8,128)}) fusion(f32[3,4,16,2880]{3,2,1,0:T(8,128)S(1)} %fusion.8), kind=kLoop, calls=%fused_computation.38 | loop fusion | bytes 4423680 | tf_op jit(solution)/shard_map/squeeze | solution.py:143
  (11 shorter events, 0.3 us)
Async XLA Ops:
  2.4 1.1 %copy-start = (f32[4,16,2880]{2,1,0:T(8,128)S(1)}, f32[4,16,2880]{2,1,0:T(8,128)}, u32[]{:S(2)}) copy-start(f32[4,16,2880]{2,1,0:T(8,128)} %param.21) | copy-start | bytes 2211844
  3.5 13.2 %copy-start.8 = (s32[10]{0:T(128)S(1)}, s32[10]{0:T(128)}, u32[]{:S(2)}) copy-start(s32[10]{0:T(128)} %constant.89.clone) | copy-start | bytes 124
  4.5 23.8 %collective-permute-start = (f32[4,16,2880]{2,1,0:T(8,128)}, f32[4,16,2880]{2,1,0:T(8,128)}, u32[]{:S(2)}, u32[]{:S(2)}) collective-permute-start(f32[4,16,2880]{2,1,0:T(8,128)} %pad_maximum_fusion.4), channel_id=1, source_target_pairs={{40,41},{41,42},{42,43},{43,44},{44,45},{45,46},{46,47},{48,49},{4... | collective-permute-start | bytes 2211848 | tf_op jit(solution)/shard_map/ppermute | solution.py:35
  9.5 36.1 %collective-permute-start.1 = (f32[4,16,2880]{2,1,0:T(8,128)}, f32[4,16,2880]{2,1,0:T(8,128)}, u32[]{:S(2)}, u32[]{:S(2)}) collective-permute-start(f32[4,16,2880]{2,1,0:T(8,128)} %pad_maximum_fusion.6), channel_id=1, source_target_pairs={{41,40},{42,41},{43,42},{44,43},{45,44},{46,45},{47,46},{49,48},{5... | collective-permute-start | bytes 2211848 | tf_op jit(solution)/shard_map/ppermute | solution.py:35
  47.4 42.2 %collective-permute-start.2 = (f32[3,4,1,2880]{3,2,1,0:T(1,128)S(1)}, f32[3,4,1,2880]{3,2,1,0:T(1,128)S(1)}, u32[]{:S(2)}, u32[]{:S(2)}) collective-permute-start(f32[3,4,1,2880]{3,2,1,0:T(1,128)S(1)} %get-tuple-element.131), channel_id=1, source_target_pairs={{0,8},{8,16},{16,24},{24,32},{32,40},{40,48},{48,56},{56,64},{64,7... | collective-permute-start | bytes 414728 | tf_op jit(solution)/shard_map/ppermute | solution.py:25
  86.1 9.1 %collective-permute-start.3 = (f32[3,4,1,2880]{3,2,1,0:T(1,128)S(1)}, f32[3,4,1,2880]{3,2,1,0:T(1,128)S(1)}, u32[]{:S(2)}, u32[]{:S(2)}) collective-permute-start(f32[3,4,1,2880]{3,2,1,0:T(1,128)S(1)} %get-tuple-element.130), channel_id=1, source_target_pairs={{8,0},{16,8},{24,16},{32,24},{40,32},{48,40},{56,48},{64,56},{72,6... | collective-permute-start | bytes 414728 | tf_op jit(solution)/shard_map/ppermute | solution.py:25
  88.1 8.1 %collective-permute-start.5 = (f32[4,16,2880]{2,1,0:T(8,128)S(1)}, f32[4,16,2880]{2,1,0:T(8,128)S(1)}, u32[]{:S(2)}, u32[]{:S(2)}) collective-permute-start(f32[4,16,2880]{2,1,0:T(8,128)S(1)} %pad_maximum_fusion.5), channel_id=1, source_target_pairs={{1,0},{2,1},{3,2},{4,3},{5,4},{6,5},{7,6},{9,8},{10,9},{11,10},{12... | collective-permute-start | bytes 2211848 | tf_op jit(solution)/shard_map/ppermute | solution.py:35
  88.8 9.3 %collective-permute-start.4 = (f32[4,16,2880]{2,1,0:T(8,128)S(1)}, f32[4,16,2880]{2,1,0:T(8,128)S(1)}, u32[]{:S(2)}, u32[]{:S(2)}) collective-permute-start(f32[4,16,2880]{2,1,0:T(8,128)S(1)} %pad_maximum_fusion.3), channel_id=1, source_target_pairs={{0,1},{1,2},{2,3},{3,4},{4,5},{5,6},{6,7},{8,9},{9,10},{10,11},{11... | collective-permute-start | bytes 2211848 | tf_op jit(solution)/shard_map/ppermute | solution.py:35

commit v7 on v6

--- a/solution.py
+++ b/solution.py
@@ -32,6 +32,14 @@
         for lev in range(lev_size - 1):
             source, target = lat * lev_size + lev, lat * lev_size + lev + 1
             pairs.append((source, target) if up else (target, source))
+    return lax.ppermute(x, ("lat", "lev"), pairs)
+
+
+def lat_group_shift(x, sources, up):
+    lat_size, lev_size = lax.axis_size("lat"), lax.axis_size("lev")
+    step = 1 if up else -1
+    pairs = [(lat * lev_size + lev, (lat + step) * lev_size + lev)
+             for lat in sources if 0 <= lat + step < lat_size for lev in range(lev_size)]
     return lax.ppermute(x, ("lat", "lev"), pairs)
 
 
@@ -101,7 +109,10 @@
     above_plain = group_shift(bottom, plain_lat, False)
 
     tables = (parity_table(0), parity_table(1))
-    stacked, below_plain, above_plain = lax.optimization_barrier((stacked, below_plain, above_plain))
+    south_plain = lat_group_shift(stacked[:, :, lat_rows - 1 :], plain_lat, True)
+    north_plain = lat_group_shift(stacked[:, :, :1], plain_lat, False)
+    stacked, below_plain, above_plain, south_plain, north_plain = lax.optimization_barrier(
+        (stacked, below_plain, above_plain, south_plain, north_plain))
     field = filtered(stacked, own_cut, tables)
     top = jnp.concatenate([field[:, levels - 1], vertical_wind[levels - 1 :]], axis=0)
     bottom = jnp.concatenate([field[:, 0], vertical_wind[:1]], axis=0)
@@ -112,8 +123,12 @@
     above_all = jnp.where(is_filter, above_filtered, above_plain)
     below, below_wind = below_all[:3, None], below_all[3:]
     above, above_wind = above_all[:3, None], above_all[3:]
-    south = shift(field[:, :, lat_rows - 1 :], "lat", True)
-    north = shift(field[:, :, :1], "lat", False)
+    south_filtered = lat_group_shift(field[:, :, lat_rows - 1 :], filter_lat, True)
+    north_filtered = lat_group_shift(field[:, :, :1], filter_lat, False)
+    south_is_filter = jnp.any(lat_index - 1 == jnp.asarray(filter_lat, jnp.int32))
+    north_is_filter = jnp.any(lat_index + 1 == jnp.asarray(filter_lat, jnp.int32))
+    south = jnp.where(south_is_filter, south_filtered, south_plain)
+    north = jnp.where(north_is_filter, north_filtered, north_plain)
 
     vertical_pad = jnp.concatenate([below_wind, vertical_wind, above_wind], axis=0)
     field_lat = jnp.concatenate([south, field, north], axis=2)

time: 103 us -> 99.2 us (0.963)
  the two profiles are of different devices: /device:TPU:233 before, /device:TPU:80 now
where the time goes in v7:
time: 99.2 us; the launch traced here: 98.7 us
  waiting for transfers between devices  37.7 us (38%)
  starting transfers between devices  30.2 us (30%)
  other arithmetic  16.4 us (17%)
  matrix products  8.57 us (9%)
  local copies, waits for them, and re-layouts  4.04 us (4%)
  between operations  1.56 us (2%)
    ppermute x4, waiting for transfers between devices, lat_group_shift(): return lax.ppermute(x, ('lat', 'lev'), pairs)  37.7 us
    ppermute x4, starting transfers between devices, lat_group_shift(): return lax.ppermute(x, ('lat', 'lev'), pairs)  17.3 us
    ppermute x4, starting transfers between devices, group_shift(): return lax.ppermute(x, ('lat', 'lev'), pairs)  12.9 us
    add x2, other arithmetic, parity_table(): as_f32(first)[None] * as_f32(np.cos(hi))[:, None]  2.34 us
    dot_general x1, matrix products, lowpass_rows(): lax.dot_general(spec_odd * parity_weight(1, cut), odd_table, dims, precis...  2.28 us
    dot_general x1, matrix products, lowpass_rows(): jnp.dot(first - second, odd_table, precision=mxu_precision, preferred_ele...  2.19 us
    dot_general x1, matrix products, lowpass_rows(): lax.dot_general(spec_even * parity_weight(0, cut), even_table, dims, prec...  2.16 us
  transfers between devices with their start and end apart: 8, of which 2 were waited for; matrix products, arithmetic and copies ran while one was open for 9% of the time, Pallas kernels for 0%

profile of v7, /device:TPU:80, one launch (start us, length us, event | category | flops | bytes accessed | tf_op | source)
XLA Modules:
  0.0 98.7 jit_solution(5031566373972041890)
XLA Ops:
  0.6 1.8 %pad_maximum_fusion = f32[3,4,16,2880]{3,2,1,0:T(8,128)S(1)} fusion(f32[1,4,16,2880]{3,2,1,0:T(8,128)} %bitcast.64, f32[1,4,16,2880]{3,2,1,0:T(8,128)} %bitcast.65, f32[1,4,16,2880]{3,2,1,0:T(8,128)} %bitcast.66), kind=kLoop, calls=%fused_computation.22 | loop fusion | flops 1105920 | bytes 4423680 | tf_op jit(solution)/shard_map/stack | solution.py:101
  2.4 0.1 slice_bitcast_fusion.7
  2.6 0.9 pad_maximum_fusion.4
  3.5 1.6 %collective-permute-start = (f32[4,16,2880]{2,1,0:T(8,128)}, f32[4,16,2880]{2,1,0:T(8,128)}, u32[]{:S(2)}, u32[]{:S(2)}) collective-permute-start(f32[4,16,2880]{2,1,0:T(8,128)} %pad_maximum_fusion.4), channel_id=1, source_target_pairs={{40,41},{41,42},{42,43},{43,44},{44,45},{45,46},{46,47},{48,49},{4... | collective-permute-start | bytes 2211848 | tf_op jit(solution)/shard_map/ppermute | solution.py:35
  5.1 0.9 pad_maximum_fusion.6
  6.0 1.6 %collective-permute-start.1 = (f32[4,16,2880]{2,1,0:T(8,128)}, f32[4,16,2880]{2,1,0:T(8,128)}, u32[]{:S(2)}, u32[]{:S(2)}) collective-permute-start(f32[4,16,2880]{2,1,0:T(8,128)} %pad_maximum_fusion.6), channel_id=1, source_target_pairs={{41,40},{42,41},{43,42},{44,43},{45,44},{46,45},{47,46},{49,48},{5... | collective-permute-start | bytes 2211848 | tf_op jit(solution)/shard_map/ppermute | solution.py:35
  7.6 0.9 fusion.20
  8.5 0.7 collective-permute-start.2
  9.2 1.3 %collective-permute-start.3 = (f32[3,4,1,2880]{3,2,1,0:T(1,128)}, f32[3,4,1,2880]{3,2,1,0:T(1,128)}, u32[]{:S(2)}, u32[]{:S(2)}) collective-permute-start(f32[3,4,1,2880]{3,2,1,0:T(1,128)} %get-tuple-element.141), channel_id=1, source_target_pairs={{40,32},{41,33},{42,34},{43,35},{44,36},{45,37},{46,38},{47,39},{4... | collective-permute-start | bytes 414728 | tf_op jit(solution)/shard_map/ppermute | solution.py:43
  10.5 0.6 sine_multiply_fusion
  11.1 1.4 %compare_reduce_fusion.3 = (pred[]{:T(512)}, s32[16]{0:T(128)S(1)}) fusion(s32[512]{0:T(512)} %param.24, s32[]{:T(128)S(6)} %select_n.52), kind=kLoop, calls=%fused_computation.56 | loop fusion | flops 31 | bytes 133 | tf_op jit(solution)/shard_map/reduce_or | solution.py:89
  13.1 0.7 compare_reduce_fusion.1
  13.8 9.2 %collective-permute-done.3 = f32[3,4,1,2880]{3,2,1,0:T(1,128)} collective-permute-done((f32[3,4,1,2880]{3,2,1,0:T(1,128)}, f32[3,4,1,2880]{3,2,1,0:T(1,128)}, u32[]{:S(2)}, u32[]{:S(2)}) %collective-permute-start.3) | collective-permute-done | bytes 138272 | tf_op jit(solution)/shard_map/ppermute | solution.py:43
  23.1 12.1 %conditional.1 = (f32[192,2880]{1,0:T(8,128)S(1)}) conditional(s32[]{:T(128)} %convert_element_type.17, f32[192,2880]{1,0:T(8,128)S(1)} %bitcast.45, (s32[16]{0:T(128)S(1)}, f32[192,2880]{1,0:T(8,128)S(1)}) %tuple.92), branch_computations={%region_1.0_spmd, %region_2.3_spmd.clone} | conditional | flops 4786836480 | bytes 46174092 | solution.py:89
  23.1 0.1 reshape.114
  23.2 1.7 %multiply_add_fusion = f32[30,48,720]{2,1,0:T(8,128)S(1)} fusion(f32[30,720]{1,0:T(8,128)} %constant.90.clone.2, f32[48,720]{1,0:T(8,128)} %constant.89.clone.2, f32[30,720]{1,0:T(8,128)} %constant.88.clone.2, f32[48,720]{1,0:T(8,128)} %constant.87.clone.2), kind=kLoop, calls=%fused_computation | loop fusion | flops 3110400 | bytes 4596480 | tf_op jit(solution)/shard_map/add | solution.py:57
  24.9 2.2 %convolution_multiply_fusion = f32[192,720]{1,0:T(8,128)S(1)} fusion(f32[1440,720]{1,0:T(8,128)S(1)} %bitcast.58, f32[192,2880]{1,0:T(8,128)S(1)} %get-tuple-element.123, s32[720]{0:T(1024)S(1)} %copy-done.7, s32[192]{0:T(256)S(1)} %reshape.114), kind=kOutput, calls=%fused_computation.3 | convolution fusion | flops 1195084800 | bytes 7341056 | tf_op jit(solution)/shard_map/cond/branch_1_fun/dot_general | solution.py:74
  27.1 2.3 %fusion.22 = f32[192,1440]{1,0:T(8,128)S(1)} fusion(f32[192,720]{1,0:T(8,128)S(1)} %convolution_multiply_fusion, f32[1440,720]{1,0:T(8,128)S(1)} %bitcast.59), kind=kOutput, calls=%fused_computation.63 | convolution fusion | flops 1194393600 | bytes 5806080 | tf_op jit(solution)/shard_map/cond/branch_1_fun/dot_general | solution.py:79
  29.5 0.6 multiply_add_fusion.1
  30.2 1.9 %convolution_multiply_fusion.1 = f32[192,720]{1,0:T(8,128)S(1)} fusion(f32[1440,720]{1,0:T(8,128)S(1)} %bitcast.56, f32[192,2880]{1,0:T(8,128)S(1)} %get-tuple-element.123, f32[720]{0:T(1024)S(1)} %copy-done.5, s32[720]{0:T(1024)S(1)} %copy-done.6, s32[192]{0:T(256)S(1)} %reshape.114), kind=kOutput, calls=%fused_computation.4 | convolution fusion | flops 1195084800 | bytes 7345152 | tf_op jit(solution)/shard_map/cond/branch_1_fun/dot_general | solution.py:72
  32.1 2.2 %fusion.18 = (f32[192,1440]{1,0:T(8,128)S(1)}, f32[192,1440]{1,0:T(8,128)S(1)}) fusion(f32[192,1440]{1,0:T(8,128)S(1)} %fusion.22, f32[192,720]{1,0:T(8,128)S(1)} %convolution_multiply_fusion.1, f32[1440,720]{1,0:T(8,128)S(1)} %bitcast.57), kind=kOutput, calls=%fused_computation.59 | convolution fusion | flops 1194946560 | bytes 8017920 | tf_op jit(solution)/shard_map/cond/branch_1_fun/dot_general | solution.py:77
  34.3 0.7 maximum_select_fusion
  35.2 0.1 slice.161
  35.3 0.3 slice.162
  35.5 0.6 slice.159
  36.2 0.2 fusion.19
  36.4 0.1 slice_bitcast_fusion.4
  36.5 0.1 fusion.17
  36.6 0.4 fusion.12
  37.0 0.1 slice.164
  37.0 1.3 %collective-permute-start.5 = (f32[3,4,1,2880]{3,2,1,0:T(1,128)S(1)}, f32[3,4,1,2880]{3,2,1,0:T(1,128)S(1)}, u32[]{:S(2)}, u32[]{:S(2)}) collective-permute-start(f32[3,4,1,2880]{3,2,1,0:T(1,128)S(1)} %get-tuple-element.137), channel_id=1, source_target_pairs={{8,0},{9,1},{10,2},{11,3},{12,4},{13,5},{14,6},{15,7},{16,8},{17,9... | collective-permute-start | bytes 414728 | tf_op jit(solution)/shard_map/ppermute | solution.py:43
  38.4 14.0 %collective-permute-start.4 = (f32[3,4,1,2880]{3,2,1,0:T(1,128)S(1)}, f32[3,4,1,2880]{3,2,1,0:T(1,128)S(1)}, u32[]{:S(2)}, u32[]{:S(2)}) collective-permute-start(f32[3,4,1,2880]{3,2,1,0:T(1,128)S(1)} %get-tuple-element.138), channel_id=1, source_target_pairs={{0,8},{1,9},{2,10},{3,11},{4,12},{5,13},{6,14},{7,15},{8,16},{9,17... | collective-permute-start | bytes 414728 | tf_op jit(solution)/shard_map/ppermute | solution.py:43
  52.4 0.1 pad_maximum_fusion.5
  52.5 4.2 %collective-permute-start.7 = (f32[4,16,2880]{2,1,0:T(8,128)S(1)}, f32[4,16,2880]{2,1,0:T(8,128)S(1)}, u32[]{:S(2)}, u32[]{:S(2)}) collective-permute-start(f32[4,16,2880]{2,1,0:T(8,128)S(1)} %pad_maximum_fusion.5), channel_id=1, source_target_pairs={{1,0},{2,1},{3,2},{4,3},{5,4},{6,5},{7,6},{9,8},{10,9},{11,10},{12... | collective-permute-start | bytes 2211848 | tf_op jit(solution)/shard_map/ppermute | solution.py:35
  56.7 0.1 pad_maximum_fusion.3
  56.8 5.5 %collective-permute-start.6 = (f32[4,16,2880]{2,1,0:T(8,128)S(1)}, f32[4,16,2880]{2,1,0:T(8,128)S(1)}, u32[]{:S(2)}, u32[]{:S(2)}) collective-permute-start(f32[4,16,2880]{2,1,0:T(8,128)S(1)} %pad_maximum_fusion.3), channel_id=1, source_target_pairs={{0,1},{1,2},{2,3},{3,4},{4,5},{5,6},{6,7},{8,9},{9,10},{10,11},{11... | collective-permute-start | bytes 2211848 | tf_op jit(solution)/shard_map/ppermute | solution.py:35
  62.3 1.6 %broadcast_select_fusion.2 = f32[3,4,1,2880]{3,2,1,0:T(1,128)S(1)} fusion(f32[3,4,1,2880]{3,2,1,0:T(1,128)S(1)} %collective-permute-done.5, f32[3,4,1,2880]{3,2,1,0:T(1,128)} %collective-permute-done.3, pred[]{:T(512)} %get-tuple-element.126), kind=kLoop, calls=%fused_computation.51 | loop fusion | flops 34560 | bytes 414721 | tf_op jit(solution)/shard_map/jit(_where)/select_n | solution.py:131
  63.9 28.5 %collective-permute-done.4 = f32[3,4,1,2880]{3,2,1,0:T(1,128)S(1)} collective-permute-done((f32[3,4,1,2880]{3,2,1,0:T(1,128)S(1)}, f32[3,4,1,2880]{3,2,1,0:T(1,128)S(1)}, u32[]{:S(2)}, u32[]{:S(2)}) %collective-permute-start.4) | collective-permute-done | bytes 138272 | tf_op jit(solution)/shard_map/ppermute | solution.py:43
  92.4 0.8 broadcast_select_fusion.3
  93.2 0.2 fusion.15
  93.3 0.2 fusion.14
  93.6 0.6 fusion.6
  94.2 0.7 broadcast_select_fusion
  94.9 0.7 broadcast_select_fusion.1
  95.7 0.1 fusion.16
  95.8 0.3 fusion.7
  96.1 1.2 %fusion.8 = f32[3,4,16,2880]{3,2,1,0:T(8,128)S(1)} fusion(f32[3,5,16,2880]{3,2,1,0:T(8,128)S(1)} %fusion.7, f32[3,4,16,2880]{3,2,1,0:T(8,128)S(1)} %bitcast.55, f32[3,4,17,2880]{3,2,1,0:T(8,128)S(1)} %fusion.6, f32[3,4,16,2880]{3,2,1,0:T(8,128)S(1)} %fusion.12, f32[3,4,16,2879]{3,2,1,0:T(8,128)S(1)} %bitcast.60, f32[3,4,16,1]{3,2,1,0:T(8,128)S(1)} %slice.164, ...), kind=kLoop, calls=%fused_computation.17 | loop fusion | flops 4423680 | bytes 17694784 | tf_op jit(solution)/shard_map/sub | solution.py:157
  97.3 1.4 %slice_bitcast_fusion = (f32[4,16,2880]{2,1,0:T(8,128)}, f32[4,16,2880]{2,1,0:T(8,128)}, f32[4,16,2880]{2,1,0:T(8,128)}) fusion(f32[3,4,16,2880]{3,2,1,0:T(8,128)S(1)} %fusion.8), kind=kLoop, calls=%fused_computation.38 | loop fusion | bytes 4423680 | tf_op jit(solution)/shard_map/squeeze | solution.py:158
  (36 shorter events, 0.3 us)
Async XLA Ops:
  0.6 1.9 %copy-start = (f32[4,16,2880]{2,1,0:T(8,128)S(1)}, f32[4,16,2880]{2,1,0:T(8,128)}, u32[]{:S(2)}) copy-start(f32[4,16,2880]{2,1,0:T(8,128)} %param.23) | copy-start | bytes 2211844
  2.5 10.6 %copy-start.8 = (s32[10]{0:T(128)S(1)}, s32[10]{0:T(128)}, u32[]{:S(2)}) copy-start(s32[10]{0:T(128)} %constant.93.clone) | copy-start | bytes 124
  3.5 19.5 %collective-permute-start = (f32[4,16,2880]{2,1,0:T(8,128)}, f32[4,16,2880]{2,1,0:T(8,128)}, u32[]{:S(2)}, u32[]{:S(2)}) collective-permute-start(f32[4,16,2880]{2,1,0:T(8,128)} %pad_maximum_fusion.4), channel_id=1, source_target_pairs={{40,41},{41,42},{42,43},{43,44},{44,45},{45,46},{46,47},{48,49},{4... | collective-permute-start | bytes 2211848 | tf_op jit(solution)/shard_map/ppermute | solution.py:35
  6.0 17.1 %collective-permute-start.1 = (f32[4,16,2880]{2,1,0:T(8,128)}, f32[4,16,2880]{2,1,0:T(8,128)}, u32[]{:S(2)}, u32[]{:S(2)}) collective-permute-start(f32[4,16,2880]{2,1,0:T(8,128)} %pad_maximum_fusion.6), channel_id=1, source_target_pairs={{41,40},{42,41},{43,42},{44,43},{45,44},{46,45},{47,46},{49,48},{5... | collective-permute-start | bytes 2211848 | tf_op jit(solution)/shard_map/ppermute | solution.py:35
  8.5 5.3 %collective-permute-start.2 = (f32[3,4,1,2880]{3,2,1,0:T(1,128)}, f32[3,4,1,2880]{3,2,1,0:T(1,128)S(1)}, u32[]{:S(2)}, u32[]{:S(2)}) collective-permute-start(f32[3,4,1,2880]{3,2,1,0:T(1,128)} %get-tuple-element.142), channel_id=1, source_target_pairs={{40,48},{41,49},{42,50},{43,51},{44,52},{45,53},{46,54},{47,55},{4... | collective-permute-start | bytes 414728 | tf_op jit(solution)/shard_map/ppermute | solution.py:43
  9.2 13.9 %collective-permute-start.3 = (f32[3,4,1,2880]{3,2,1,0:T(1,128)}, f32[3,4,1,2880]{3,2,1,0:T(1,128)}, u32[]{:S(2)}, u32[]{:S(2)}) collective-permute-start(f32[3,4,1,2880]{3,2,1,0:T(1,128)} %get-tuple-element.141), channel_id=1, source_target_pairs={{40,32},{41,33},{42,34},{43,35},{44,36},{45,37},{46,38},{47,39},{4... | collective-permute-start | bytes 414728 | tf_op jit(solution)/shard_map/ppermute | solution.py:43
  23.2 1.7 %copy-start.7 = (s32[720]{0:T(1024)S(1)}, s32[720]{0:T(1024)}, u32[]{:S(2)}) copy-start(s32[720]{0:T(1024)} %constant.92.clone.2) | copy-start | bytes 8644 | tf_op jit(solution)/shard_map/cond
  27.1 2.3 %copy-start.1 = (f32[48,720]{1,0:T(8,128)S(1)}, f32[48,720]{1,0:T(8,128)}, u32[]{:S(2)}) copy-start(f32[48,720]{1,0:T(8,128)} %constant.83.clone.2) | copy-start | bytes 414724 | tf_op jit(solution)/shard_map/cond
  27.1 2.3 %copy-start.2 = (f32[48,720]{1,0:T(8,128)S(1)}, f32[48,720]{1,0:T(8,128)}, u32[]{:S(2)}) copy-start(f32[48,720]{1,0:T(8,128)} %constant.85.clone.2) | copy-start | bytes 414724 | tf_op jit(solution)/shard_map/cond
  27.1 2.3 %copy-start.3 = (f32[30,720]{1,0:T(8,128)S(1)}, f32[30,720]{1,0:T(8,128)}, u32[]{:S(2)}) copy-start(f32[30,720]{1,0:T(8,128)} %constant.84.clone.2) | copy-start | bytes 259204 | tf_op jit(solution)/shard_map/cond
  27.1 2.3 %copy-start.4 = (f32[30,720]{1,0:T(8,128)S(1)}, f32[30,720]{1,0:T(8,128)}, u32[]{:S(2)}) copy-start(f32[30,720]{1,0:T(8,128)} %constant.86.clone.2) | copy-start | bytes 259204 | tf_op jit(solution)/shard_map/cond
  29.5 0.7 copy-start.5
  29.5 0.7 copy-start.6
  37.0 25.2 %collective-permute-start.5 = (f32[3,4,1,2880]{3,2,1,0:T(1,128)S(1)}, f32[3,4,1,2880]{3,2,1,0:T(1,128)S(1)}, u32[]{:S(2)}, u32[]{:S(2)}) collective-permute-start(f32[3,4,1,2880]{3,2,1,0:T(1,128)S(1)} %get-tuple-element.137), channel_id=1, source_target_pairs={{8,0},{9,1},{10,2},{11,3},{12,4},{13,5},{14,6},{15,7},{16,8},{17,9... | collective-permute-start | bytes 414728 | tf_op jit(solution)/shard_map/ppermute | solution.py:43
  38.4 54.0 %collective-permute-start.4 = (f32[3,4,1,2880]{3,2,1,0:T(1,128)S(1)}, f32[3,4,1,2880]{3,2,1,0:T(1,128)S(1)}, u32[]{:S(2)}, u32[]{:S(2)}) collective-permute-start(f32[3,4,1,2880]{3,2,1,0:T(1,128)S(1)} %get-tuple-element.138), channel_id=1, source_target_pairs={{0,8},{1,9},{2,10},{3,11},{4,12},{5,13},{6,14},{7,15},{8,16},{9,17... | collective-permute-start | bytes 414728 | tf_op jit(solution)/shard_map/ppermute | solution.py:43
  52.5 41.7 %collective-permute-start.7 = (f32[4,16,2880]{2,1,0:T(8,128)S(1)}, f32[4,16,2880]{2,1,0:T(8,128)S(1)}, u32[]{:S(2)}, u32[]{:S(2)}) collective-permute-start(f32[4,16,2880]{2,1,0:T(8,128)S(1)} %pad_maximum_fusion.5), channel_id=1, source_target_pairs={{1,0},{2,1},{3,2},{4,3},{5,4},{6,5},{7,6},{9,8},{10,9},{11,10},{12... | collective-permute-start | bytes 2211848 | tf_op jit(solution)/shard_map/ppermute | solution.py:35
  56.8 38.2 %collective-permute-start.6 = (f32[4,16,2880]{2,1,0:T(8,128)S(1)}, f32[4,16,2880]{2,1,0:T(8,128)S(1)}, u32[]{:S(2)}, u32[]{:S(2)}) collective-permute-start(f32[4,16,2880]{2,1,0:T(8,128)S(1)} %pad_maximum_fusion.3), channel_id=1, source_target_pairs={{0,1},{1,2},{2,3},{3,4},{4,5},{5,6},{6,7},{8,9},{9,10},{10,11},{11... | collective-permute-start | bytes 2211848 | tf_op jit(solution)/shard_map/ppermute | solution.py:35
  62.3 31.0 %copy-start.9 = (f32[17]{0:T(128)S(1)}, f32[17]{0:T(128)}, u32[]{:S(2)}) copy-start(f32[17]{0:T(128)} %sine_multiply_fusion) | copy-start | bytes 208

commit v8 on v7

--- a/solution.py
+++ b/solution.py
@@ -35,11 +35,11 @@
     return lax.ppermute(x, ("lat", "lev"), pairs)
 
 
-def lat_group_shift(x, sources, up):
-    lat_size, lev_size = lax.axis_size("lat"), lax.axis_size("lev")
+def lat_group_shift(x, group, up):
+    lev_size = lax.axis_size("lev")
     step = 1 if up else -1
     pairs = [(lat * lev_size + lev, (lat + step) * lev_size + lev)
-             for lat in sources if 0 <= lat + step < lat_size for lev in range(lev_size)]
+             for lat in group if lat + step in group for lev in range(lev_size)]
     return lax.ppermute(x, ("lat", "lev"), pairs)
 
 
@@ -109,10 +109,9 @@
     above_plain = group_shift(bottom, plain_lat, False)
 
     tables = (parity_table(0), parity_table(1))
-    south_plain = lat_group_shift(stacked[:, :, lat_rows - 1 :], plain_lat, True)
-    north_plain = lat_group_shift(stacked[:, :, :1], plain_lat, False)
-    stacked, below_plain, above_plain, south_plain, north_plain = lax.optimization_barrier(
-        (stacked, below_plain, above_plain, south_plain, north_plain))
+    south_plain = shift(stacked[:, :, lat_rows - 1 :], "lat", True)
+    north_plain = shift(stacked[:, :, :1], "lat", False)
+    stacked, south_plain, north_plain = lax.optimization_barrier((stacked, south_plain, north_plain))
     field = filtered(stacked, own_cut, tables)
     top = jnp.concatenate([field[:, levels - 1], vertical_wind[levels - 1 :]], axis=0)
     bottom = jnp.concatenate([field[:, 0], vertical_wind[:1]], axis=0)
@@ -127,8 +126,16 @@
     north_filtered = lat_group_shift(field[:, :, :1], filter_lat, False)
     south_is_filter = jnp.any(lat_index - 1 == jnp.asarray(filter_lat, jnp.int32))
     north_is_filter = jnp.any(lat_index + 1 == jnp.asarray(filter_lat, jnp.int32))
-    south = jnp.where(south_is_filter, south_filtered, south_plain)
-    north = jnp.where(north_is_filter, north_filtered, north_plain)
+    halo_ids = jnp.stack([row_start - 1, row_start + lat_rows])
+    halo_cut = cutoff[jnp.clip(halo_ids, 0, total_rows - 1)]
+    halo_raw = jnp.concatenate([south_plain, north_plain], axis=2)
+    halo_rows = halo_raw.reshape(-1, NLON)
+    halo_cuts = jnp.broadcast_to(halo_cut, halo_raw.shape[:-1]).reshape(-1)
+    halo_own = lax.cond(jnp.logical_and(jnp.logical_not(is_filter), jnp.any(halo_cut < HALF)),
+                        lambda: lowpass_rows(halo_rows, halo_cuts, tables), lambda: halo_rows)
+    halo_own = halo_own.reshape(halo_raw.shape)
+    south = jnp.where(jnp.logical_and(is_filter, south_is_filter), south_filtered, halo_own[:, :, :1])
+    north = jnp.where(jnp.logical_and(is_filter, north_is_filter), north_filtered, halo_own[:, :, 1:])
 
     vertical_pad = jnp.concatenate([below_wind, vertical_wind, above_wind], axis=0)
     field_lat = jnp.concatenate([south, field, north], axis=2)

time: 99.2 us -> 124 us (1.25)
  the two profiles are of different devices: /device:TPU:80 before, /device:TPU:47 now
where the time goes in v8:
time: 124 us; the launch traced here: 122 us
  waiting for transfers between devices  44.1 us (36%)
  starting transfers between devices  25.6 us (21%)
  other arithmetic  23.2 us (19%)
  matrix products  12.8 us (10%)
  local copies, waits for them, and re-layouts  10.7 us (9%)
  between operations  5.39 us (4%)
    ppermute x2, waiting for transfers between devices, lat_group_shift(): return lax.ppermute(x, ('lat', 'lev'), pairs)  44.1 us
    ppermute x4, starting transfers between devices, group_shift(): return lax.ppermute(x, ('lat', 'lev'), pairs)  13.2 us
    add x2, other arithmetic, parity_table(): as_f32(first)[None] * as_f32(np.cos(hi))[:, None]  6.45 us
    ppermute x2, starting transfers between devices, lat_group_shift(): return lax.ppermute(x, ('lat', 'lev'), pairs)  6.37 us
    ppermute x2, starting transfers between devices, shift(): return lax.ppermute(x, axis, pairs)  6.02 us
    dot_general x1, matrix products, lowpass_rows(): lax.dot_general(spec_odd * parity_weight(1, cut), odd_table, dims, precis...  4.37 us
    dot_general x1, matrix products, lowpass_rows(): jnp.dot(first - second, odd_table, precision=mxu_precision, preferred_ele...  4.3 us
  transfers between devices with their start and end apart: 8, of which 2 were waited for; matrix products, arithmetic and copies ran while one was open for 17% of the time, Pallas kernels for 0%

profile of v8, /device:TPU:47, one launch (start us, length us, event | category | flops | bytes accessed | tf_op | source)
XLA Modules:
  0.0 122.0 jit_solution(2788017868331232857)
XLA Ops:
  0.6 1.7 %pad_maximum_fusion = f32[3,4,16,2880]{3,2,1,0:T(8,128)S(1)} fusion(f32[1,4,16,2880]{3,2,1,0:T(8,128)} %bitcast.78, f32[1,4,16,2880]{3,2,1,0:T(8,128)} %bitcast.79, f32[1,4,16,2880]{3,2,1,0:T(8,128)} %bitcast.80), kind=kLoop, calls=%fused_computation.37 | loop fusion | flops 1105920 | bytes 4423680 | tf_op jit(solution)/shard_map/stack | solution.py:101
  2.4 0.9 fusion.30
  3.3 4.1 %collective-permute-start = (f32[3,4,1,2880]{3,2,1,0:T(1,128)}, f32[3,4,1,2880]{3,2,1,0:T(1,128)}, u32[]{:S(2)}, u32[]{:S(2)}) collective-permute-start(f32[3,4,1,2880]{3,2,1,0:T(1,128)} %get-tuple-element.130), channel_id=1, source_target_pairs={{0,8},{8,16},{16,24},{24,32},{32,40},{40,48},{48,56},{56,64},{64,7... | collective-permute-start | bytes 414728 | tf_op jit(solution)/shard_map/ppermute | solution.py:25
  7.4 1.9 %collective-permute-start.1 = (f32[3,4,1,2880]{3,2,1,0:T(1,128)}, f32[3,4,1,2880]{3,2,1,0:T(1,128)}, u32[]{:S(2)}, u32[]{:S(2)}) collective-permute-start(f32[3,4,1,2880]{3,2,1,0:T(1,128)} %get-tuple-element.129), channel_id=1, source_target_pairs={{8,0},{16,8},{24,16},{32,24},{40,32},{48,40},{56,48},{64,56},{72,6... | collective-permute-start | bytes 414728 | tf_op jit(solution)/shard_map/ppermute | solution.py:25
  9.3 0.9 slice_bitcast_fusion.4
  10.3 1.0 fusion.31
  11.4 0.6 gather_fusion
  12.0 0.6 compare_reduce_fusion.1
  12.7 0.7 compare_reduce_fusion
  13.4 3.8 %multiply_add_fusion.1 = f32[30,48,720]{2,1,0:T(8,128)} fusion(f32[30,720]{1,0:T(8,128)S(1)} %copy-done.8, f32[48,720]{1,0:T(8,128)} %constant.117.clone, f32[30,720]{1,0:T(8,128)} %constant.116.clone, f32[48,720]{1,0:T(8,128)} %constant.115.clone), kind=kLoop, calls=%fused_computation.26 | loop fusion | flops 3110400 | bytes 4596480 | tf_op jit(solution)/shard_map/add | solution.py:57
  17.2 2.7 %multiply_add_fusion = f32[30,48,720]{2,1,0:T(8,128)} fusion(f32[30,720]{1,0:T(8,128)S(1)} %copy-done.6, f32[48,720]{1,0:T(8,128)S(1)} %copy-done.4, f32[30,720]{1,0:T(8,128)S(1)} %copy-done.7, f32[48,720]{1,0:T(8,128)S(1)} %copy-done.5), kind=kLoop, calls=%fused_computation.25 | loop fusion | flops 3110400 | bytes 4596480 | tf_op jit(solution)/shard_map/add | solution.py:57
  19.9 0.8 compare_reduce_fusion.4
  25.2 13.9 %conditional.2 = (f32[192,2880]{1,0:T(8,128)S(1)}) conditional(s32[]{:T(128)} %convert_element_type.20, f32[192,2880]{1,0:T(8,128)S(1)} %bitcast.55, (s32[16]{0:T(128)S(1)}, f32[192,2880]{1,0:T(8,128)S(1)}, f32[1440,720]{1,0:T(8,128)}, s32[720]{0:T(1024)S(1)}, f32[1440,720]{1,0:T(8,128)}, /*index=5*/s32[720]{0:T(1024)S(1)}) %tuple.72), branch_computations={%region_1.0_spmd, %region_2.3_spmd} | conditional | flops 4780619776 | bytes 48159480 | solution.py:89
  25.3 4.3 %convolution_multiply_fusion = f32[192,720]{1,0:T(8,128)S(1)} fusion(f32[1440,720]{1,0:T(8,128)} %get-tuple-element.80, f32[192,2880]{1,0:T(8,128)S(1)} %get-tuple-element.77, f32[720]{0:T(1024)S(1)} %get-tuple-element.111, s32[720]{0:T(1024)S(1)} %get-tuple-element.81, s32[192]{0:T(256)S(1)} %reshape.158), kind=kOutput, calls=%fused_computation.2 | convolution fusion | flops 1195084800 | bytes 7068672 | tf_op jit(solution)/shard_map/cond/branch_1_fun/dot_general | solution.py:74
  29.6 4.4 %fusion.32 = f32[192,1440]{1,0:T(8,128)S(1)} fusion(f32[192,720]{1,0:T(8,128)S(1)} %convolution_multiply_fusion, f32[1440,720]{1,0:T(8,128)} %get-tuple-element.80), kind=kOutput, calls=%fused_computation.87 | convolution fusion | flops 1194393600 | bytes 5806080 | tf_op jit(solution)/shard_map/cond/branch_1_fun/dot_general | solution.py:79
  34.0 1.9 %convolution_multiply_fusion.1 = f32[192,720]{1,0:T(8,128)S(1)} fusion(f32[1440,720]{1,0:T(8,128)S(1)} %bitcast.69, f32[192,2880]{1,0:T(8,128)S(1)} %get-tuple-element.77, f32[720]{0:T(1024)S(1)} %get-tuple-element.112, s32[720]{0:T(1024)S(1)} %get-tuple-element.79, s32[192]{0:T(256)S(1)} %reshape.158), kind=kOutput, calls=%fused_computation.3 | convolution fusion | flops 1195084800 | bytes 7345152 | tf_op jit(solution)/shard_map/cond/branch_1_fun/dot_general | solution.py:72
  36.0 2.2 %fusion.26 = (f32[192,1440]{1,0:T(8,128)S(1)}, f32[192,1440]{1,0:T(8,128)S(1)}) fusion(f32[192,1440]{1,0:T(8,128)S(1)} %fusion.32, f32[192,720]{1,0:T(8,128)S(1)} %convolution_multiply_fusion.1, f32[1440,720]{1,0:T(8,128)S(1)} %bitcast.69), kind=kOutput, calls=%fused_computation.81 | convolution fusion | flops 1194946560 | bytes 8017920 | tf_op jit(solution)/shard_map/cond/branch_1_fun/dot_general | solution.py:77
  38.2 0.7 maximum_select_fusion
  39.2 0.9 fusion.29
  40.1 0.6 slice.191
  40.8 0.3 slice.194
  41.1 0.7 copy-done.2
  41.8 1.2 pad_maximum_fusion.3
  43.0 7.0 %collective-permute-start.4 = (f32[4,16,2880]{2,1,0:T(8,128)}, f32[4,16,2880]{2,1,0:T(8,128)}, u32[]{:S(2)}, u32[]{:S(2)}) collective-permute-start(f32[4,16,2880]{2,1,0:T(8,128)} %get-tuple-element.136), channel_id=1, source_target_pairs={{0,1},{1,2},{2,3},{3,4},{4,5},{5,6},{6,7},{8,9},{9,10},{10,11},{11... | collective-permute-start | bytes 2211848 | tf_op jit(solution)/shard_map/ppermute | solution.py:35
  50.0 1.5 %collective-permute-start.5 = (f32[4,16,2880]{2,1,0:T(8,128)}, f32[4,16,2880]{2,1,0:T(8,128)}, u32[]{:S(2)}, u32[]{:S(2)}) collective-permute-start(f32[4,16,2880]{2,1,0:T(8,128)} %get-tuple-element.135), channel_id=1, source_target_pairs={{40,41},{41,42},{42,43},{43,44},{44,45},{45,46},{46,47},{48,49},{4... | collective-permute-start | bytes 2211848 | tf_op jit(solution)/shard_map/ppermute | solution.py:35
  51.6 1.2 %pad_maximum_fusion.5 = (f32[4,16,2880]{2,1,0:T(8,128)}, f32[4,16,2880]{2,1,0:T(8,128)}) fusion(f32[1,16,2880]{2,1,0:T(8,128)S(1)} %get-tuple-element.131, f32[3,16,2880]{2,1,0:T(8,128)S(1)} %get-tuple-element.125, f32[3,16,2880]{2,1,0:T(8,128)S(1)} %get-tuple-element.127), kind=kLoop, calls=%fused_computation.49 | loop fusion | flops 368640 | bytes 2764800 | tf_op jit(solution)/shard_map/concatenate | solution.py:107
  52.8 3.1 %collective-permute-start.6 = (f32[4,16,2880]{2,1,0:T(8,128)}, f32[4,16,2880]{2,1,0:T(8,128)}, u32[]{:S(2)}, u32[]{:S(2)}) collective-permute-start(f32[4,16,2880]{2,1,0:T(8,128)} %get-tuple-element.134), channel_id=1, source_target_pairs={{1,0},{2,1},{3,2},{4,3},{5,4},{6,5},{7,6},{9,8},{10,9},{11,10},{12... | collective-permute-start | bytes 2211848 | tf_op jit(solution)/shard_map/ppermute | solution.py:35
  55.9 1.6 %collective-permute-start.7 = (f32[4,16,2880]{2,1,0:T(8,128)}, f32[4,16,2880]{2,1,0:T(8,128)}, u32[]{:S(2)}, u32[]{:S(2)}) collective-permute-start(f32[4,16,2880]{2,1,0:T(8,128)} %get-tuple-element.133), channel_id=1, source_target_pairs={{41,40},{42,41},{43,42},{44,43},{45,44},{46,45},{47,46},{49,48},{5... | collective-permute-start | bytes 2211848 | tf_op jit(solution)/shard_map/ppermute | solution.py:35
  57.4 4.9 %collective-permute-start.2 = (f32[3,4,1,2880]{3,2,1,0:T(1,128)}, f32[3,4,1,2880]{3,2,1,0:T(1,128)}, u32[]{:S(2)}, u32[]{:S(2)}) collective-permute-start(f32[3,4,1,2880]{3,2,1,0:T(1,128)} %get-tuple-element.124), channel_id=1, source_target_pairs={{0,8},{1,9},{2,10},{3,11},{4,12},{5,13},{6,14},{7,15},{8,16},{9,17... | collective-permute-start | bytes 414728 | tf_op jit(solution)/shard_map/ppermute | solution.py:43
  62.4 1.6 %fusion.18 = f32[3,4,16,2880]{3,2,1,0:T(8,128)} fusion(f32[3,4,16,2880]{3,2,1,0:T(8,128)S(1)} %bitcast.61, f32[3,4,16,1]{3,2,1,0:T(8,128)S(1)} %slice.192, f32[3,4,16,2879]{3,2,1,0:T(8,128)S(1)} %slice.191, f32[4,16,2880]{2,1,0:T(8,128)S(1)} %fusion.23), kind=kLoop, calls=%fused_computation.39 | loop fusion | flops 1658880 | bytes 7372800 | tf_op jit(solution)/shard_map/mul | solution.py:150
  64.0 1.2 %pad_maximum_fusion.7 = f32[3,4,2,2880]{3,2,1,0:T(2,128)S(1)} fusion(f32[3,4,1,2880]{3,2,1,0:T(1,128)} %collective-permute-done.1, f32[3,4,1,2880]{3,2,1,0:T(1,128)} %collective-permute-done), kind=kLoop, calls=%fused_computation.66 | loop fusion | flops 69120 | bytes 552960 | tf_op jit(solution)/shard_map/concatenate | solution.py:131
  65.3 0.2 reshape.167
  65.5 1.0 slice.196
  66.5 0.4 conditional.3
  66.5 0.2 reshape.159
  66.7 0.2 fusion.25
  66.9 38.4 %collective-permute-done.2 = f32[3,4,1,2880]{3,2,1,0:T(1,128)} collective-permute-done((f32[3,4,1,2880]{3,2,1,0:T(1,128)}, f32[3,4,1,2880]{3,2,1,0:T(1,128)}, u32[]{:S(2)}, u32[]{:S(2)}) %collective-permute-start.2) | collective-permute-done | bytes 138272 | tf_op jit(solution)/shard_map/ppermute | solution.py:43
  105.3 1.5 %collective-permute-start.3 = (f32[3,4,1,2880]{3,2,1,0:T(1,128)}, f32[3,4,1,2880]{3,2,1,0:T(1,128)S(1)}, u32[]{:S(2)}, u32[]{:S(2)}) collective-permute-start(f32[3,4,1,2880]{3,2,1,0:T(1,128)} %get-tuple-element.123), channel_id=1, source_target_pairs={{8,0},{9,1},{10,2},{11,3},{12,4},{13,5},{14,6},{15,7},{16,8},{17,9... | collective-permute-start | bytes 414728 | tf_op jit(solution)/shard_map/ppermute | solution.py:43
  107.0 5.7 %collective-permute-done.3 = f32[3,4,1,2880]{3,2,1,0:T(1,128)S(1)} collective-permute-done((f32[3,4,1,2880]{3,2,1,0:T(1,128)}, f32[3,4,1,2880]{3,2,1,0:T(1,128)S(1)}, u32[]{:S(2)}, u32[]{:S(2)}) %collective-permute-start.3) | collective-permute-done | bytes 138272 | tf_op jit(solution)/shard_map/ppermute | solution.py:43
  112.8 0.2 fusion.21
  113.0 0.2 fusion.20
  113.2 0.6 fusion.12
  113.8 1.8 %broadcast_select_fusion.1 = f32[4,16,2880]{2,1,0:T(8,128)S(1)} fusion(f32[4,16,2880]{2,1,0:T(8,128)} %collective-permute-done.4, f32[4,16,2880]{2,1,0:T(8,128)} %collective-permute-done.5, pred[]{:T(512)} %get-tuple-element.102), kind=kLoop, calls=%fused_computation.65 | loop fusion | flops 184320 | bytes 2211841 | tf_op jit(solution)/shard_map/jit(_where)/select_n | solution.py:121
  115.7 1.9 %broadcast_select_fusion = f32[4,16,2880]{2,1,0:T(8,128)S(1)} fusion(f32[4,16,2880]{2,1,0:T(8,128)} %collective-permute-done.6, f32[4,16,2880]{2,1,0:T(8,128)} %collective-permute-done.7, pred[]{:T(512)} %get-tuple-element.102), kind=kLoop, calls=%fused_computation.64 | loop fusion | flops 184320 | bytes 2211841 | tf_op jit(solution)/shard_map/jit(_where)/select_n | solution.py:122
  117.8 0.3 fusion.13
  118.1 1.3 %copy-done.1 = f32[3,4,16,2880]{3,2,1,0:T(8,128)S(1)} copy-done((f32[3,4,16,2880]{3,2,1,0:T(8,128)S(1)}, f32[3,4,16,2880]{3,2,1,0:T(8,128)}, u32[]{:S(2)}) %copy-start.1) | copy-done | bytes 2211864
  119.4 1.2 fusion.14
  120.6 1.4 %slice_bitcast_fusion = (f32[4,16,2880]{2,1,0:T(8,128)}, f32[4,16,2880]{2,1,0:T(8,128)}, f32[4,16,2880]{2,1,0:T(8,128)}) fusion(f32[3,4,16,2880]{3,2,1,0:T(8,128)S(1)} %fusion.14), kind=kLoop, calls=%fused_computation.53 | loop fusion | bytes 4423680 | tf_op jit(solution)/shard_map/squeeze | solution.py:165
  (53 shorter events, 1.1 us)
Async XLA Ops:
  2.4 9.0 %copy-start = (s32[512]{0:T(512)S(1)}, s32[512]{0:T(512)}, u32[]{:S(2)}) copy-start(s32[512]{0:T(512)} %param.28) | copy-start | bytes 6148
  2.4 10.3 %copy-start.11 = (s32[10]{0:T(128)S(1)}, s32[10]{0:T(128)}, u32[]{:S(2)}) copy-start(s32[10]{0:T(128)} %constant.125.clone) | copy-start | bytes 124
  2.4 11.0 %copy-start.8 = (f32[30,720]{1,0:T(8,128)S(1)}, f32[30,720]{1,0:T(8,128)}, u32[]{:S(2)}) copy-start(f32[30,720]{1,0:T(8,128)} %constant.118.clone) | copy-start | bytes 259204
  3.3 21.9 %collective-permute-start = (f32[3,4,1,2880]{3,2,1,0:T(1,128)}, f32[3,4,1,2880]{3,2,1,0:T(1,128)}, u32[]{:S(2)}, u32[]{:S(2)}) collective-permute-start(f32[3,4,1,2880]{3,2,1,0:T(1,128)} %get-tuple-element.130), channel_id=1, source_target_pairs={{0,8},{8,16},{16,24},{24,32},{32,40},{40,48},{48,56},{56,64},{64,7... | collective-permute-start | bytes 414728 | tf_op jit(solution)/shard_map/ppermute | solution.py:25
  7.4 17.8 %collective-permute-start.1 = (f32[3,4,1,2880]{3,2,1,0:T(1,128)}, f32[3,4,1,2880]{3,2,1,0:T(1,128)}, u32[]{:S(2)}, u32[]{:S(2)}) collective-permute-start(f32[3,4,1,2880]{3,2,1,0:T(1,128)} %get-tuple-element.129), channel_id=1, source_target_pairs={{8,0},{16,8},{24,16},{32,24},{40,32},{48,40},{56,48},{64,56},{72,6... | collective-permute-start | bytes 414728 | tf_op jit(solution)/shard_map/ppermute | solution.py:25
  13.4 3.8 %copy-start.4 = (f32[48,720]{1,0:T(8,128)S(1)}, f32[48,720]{1,0:T(8,128)}, u32[]{:S(2)}) copy-start(f32[48,720]{1,0:T(8,128)} %constant.121.clone) | copy-start | bytes 414724
  13.4 3.8 %copy-start.5 = (f32[48,720]{1,0:T(8,128)S(1)}, f32[48,720]{1,0:T(8,128)}, u32[]{:S(2)}) copy-start(f32[48,720]{1,0:T(8,128)} %constant.119.clone) | copy-start | bytes 414724
  13.4 3.8 %copy-start.6 = (f32[30,720]{1,0:T(8,128)S(1)}, f32[30,720]{1,0:T(8,128)}, u32[]{:S(2)}) copy-start(f32[30,720]{1,0:T(8,128)} %constant.122.clone) | copy-start | bytes 259204
  13.4 3.8 %copy-start.7 = (f32[30,720]{1,0:T(8,128)S(1)}, f32[30,720]{1,0:T(8,128)}, u32[]{:S(2)}) copy-start(f32[30,720]{1,0:T(8,128)} %constant.120.clone) | copy-start | bytes 259204
  17.2 8.0 %copy-start.9 = (s32[720]{0:T(1024)S(1)}, s32[720]{0:T(1024)}, u32[]{:S(2)}) copy-start(s32[720]{0:T(1024)} %constant.123.clone) | copy-start | bytes 8644
  17.2 8.0 %copy-start.10 = (s32[720]{0:T(1024)S(1)}, s32[720]{0:T(1024)}, u32[]{:S(2)}) copy-start(s32[720]{0:T(1024)} %constant.124.clone) | copy-start | bytes 8644
  25.2 8.8 %slice-start = ((s8[4423680]{0:T(1024)(128)(4,1)}), s8[229376]{0:T(1024)(128)(4,1)S(1)}, s32[]{:S(2)}) async-start(s8[4423680]{0:T(1024)(128)(4,1)} %bitcast.68), calls=%async_computation | async-start | bytes 458752 | tf_op jit(solution)/shard_map/cond
  25.3 8.7 %slice-start.1 = ((s8[4423680]{0:T(1024)(128)(4,1)}), s8[4194304]{0:T(1024)(128)(4,1)S(1)}, s32[]{:S(2)}) async-start(s8[4423680]{0:T(1024)(128)(4,1)} %bitcast.68), calls=%async_computation.1 | async-start | bytes 8388608 | tf_op jit(solution)/shard_map/cond
  40.7 1.1 copy-start.2
  43.0 70.8 %collective-permute-start.4 = (f32[4,16,2880]{2,1,0:T(8,128)}, f32[4,16,2880]{2,1,0:T(8,128)}, u32[]{:S(2)}, u32[]{:S(2)}) collective-permute-start(f32[4,16,2880]{2,1,0:T(8,128)} %get-tuple-element.136), channel_id=1, source_target_pairs={{0,1},{1,2},{2,3},{3,4},{4,5},{5,6},{6,7},{8,9},{9,10},{10,11},{11... | collective-permute-start | bytes 2211848 | tf_op jit(solution)/shard_map/ppermute | solution.py:35
  50.0 63.8 %collective-permute-start.5 = (f32[4,16,2880]{2,1,0:T(8,128)}, f32[4,16,2880]{2,1,0:T(8,128)}, u32[]{:S(2)}, u32[]{:S(2)}) collective-permute-start(f32[4,16,2880]{2,1,0:T(8,128)} %get-tuple-element.135), channel_id=1, source_target_pairs={{40,41},{41,42},{42,43},{43,44},{44,45},{45,46},{46,47},{48,49},{4... | collective-permute-start | bytes 2211848 | tf_op jit(solution)/shard_map/ppermute | solution.py:35
  52.8 62.9 %collective-permute-start.6 = (f32[4,16,2880]{2,1,0:T(8,128)}, f32[4,16,2880]{2,1,0:T(8,128)}, u32[]{:S(2)}, u32[]{:S(2)}) collective-permute-start(f32[4,16,2880]{2,1,0:T(8,128)} %get-tuple-element.134), channel_id=1, source_target_pairs={{1,0},{2,1},{3,2},{4,3},{5,4},{6,5},{7,6},{9,8},{10,9},{11,10},{12... | collective-permute-start | bytes 2211848 | tf_op jit(solution)/shard_map/ppermute | solution.py:35
  55.9 59.9 %collective-permute-start.7 = (f32[4,16,2880]{2,1,0:T(8,128)}, f32[4,16,2880]{2,1,0:T(8,128)}, u32[]{:S(2)}, u32[]{:S(2)}) collective-permute-start(f32[4,16,2880]{2,1,0:T(8,128)} %get-tuple-element.133), channel_id=1, source_target_pairs={{41,40},{42,41},{43,42},{44,43},{45,44},{46,45},{47,46},{49,48},{5... | collective-permute-start | bytes 2211848 | tf_op jit(solution)/shard_map/ppermute | solution.py:35
  57.4 47.9 %collective-permute-start.2 = (f32[3,4,1,2880]{3,2,1,0:T(1,128)}, f32[3,4,1,2880]{3,2,1,0:T(1,128)}, u32[]{:S(2)}, u32[]{:S(2)}) collective-permute-start(f32[3,4,1,2880]{3,2,1,0:T(1,128)} %get-tuple-element.124), channel_id=1, source_target_pairs={{0,8},{1,9},{2,10},{3,11},{4,12},{5,13},{6,14},{7,15},{8,16},{9,17... | collective-permute-start | bytes 414728 | tf_op jit(solution)/shard_map/ppermute | solution.py:43
  105.3 7.3 %collective-permute-start.3 = (f32[3,4,1,2880]{3,2,1,0:T(1,128)}, f32[3,4,1,2880]{3,2,1,0:T(1,128)S(1)}, u32[]{:S(2)}, u32[]{:S(2)}) collective-permute-start(f32[3,4,1,2880]{3,2,1,0:T(1,128)} %get-tuple-element.123), channel_id=1, source_target_pairs={{8,0},{9,1},{10,2},{11,3},{12,4},{13,5},{14,6},{15,7},{16,8},{17,9... | collective-permute-start | bytes 414728 | tf_op jit(solution)/shard_map/ppermute | solution.py:43
  115.7 2.0 %copy-start.3 = (f32[4,16,2880]{2,1,0:T(8,128)S(1)}, f32[4,16,2880]{2,1,0:T(8,128)}, u32[]{:S(2)}) copy-start(f32[4,16,2880]{2,1,0:T(8,128)} %param.27) | copy-start | bytes 2211844
  117.8 1.6 %copy-start.1 = (f32[3,4,16,2880]{3,2,1,0:T(8,128)S(1)}, f32[3,4,16,2880]{3,2,1,0:T(8,128)}, u32[]{:S(2)}) copy-start(f32[3,4,16,2880]{3,2,1,0:T(8,128)} %fusion.18) | copy-start | bytes 6635524

commit v9 on v8

--- a/solution.py
+++ b/solution.py
@@ -43,8 +43,7 @@
     return lax.ppermute(x, ("lat", "lev"), pairs)
 
 
-def parity_table(parity):
-    low = 48
+def parity_table(parity, low=48):
     modes = np.arange(parity, KMAX, 2)
     k = np.concatenate([modes, modes])[None, :]
     is_sin = np.arange(KMAX)[None, :] >= KMAX // 2
@@ -82,11 +81,12 @@
     return jnp.where((cut < HALF)[:, None], summed, x)
 
 
-def filtered(x, cut, tables):
+def filtered(x, cut, run=None, low=48):
     shape = x.shape
     rows = x.reshape(-1, NLON)
     cuts = jnp.broadcast_to(cut, shape[:-1]).reshape(-1)
-    out = lax.cond(jnp.any(cut < HALF), lambda: lowpass_rows(rows, cuts, tables), lambda: rows)
+    run = jnp.any(cut < HALF) if run is None else run
+    out = lax.cond(run, lambda: lowpass_rows(rows, cuts, (parity_table(0, low), parity_table(1, low))), lambda: rows)
     return out.reshape(shape)
 
 
@@ -108,16 +108,20 @@
     below_plain = group_shift(top, plain_lat, True)
     above_plain = group_shift(bottom, plain_lat, False)
 
-    tables = (parity_table(0), parity_table(1))
-    south_plain = shift(stacked[:, :, lat_rows - 1 :], "lat", True)
-    north_plain = shift(stacked[:, :, :1], "lat", False)
-    stacked, south_plain, north_plain = lax.optimization_barrier((stacked, south_plain, north_plain))
-    field = filtered(stacked, own_cut, tables)
+    south_raw = shift(stacked[:, :, lat_rows - 1 :], "lat", True)
+    north_raw = shift(stacked[:, :, :1], "lat", False)
+    is_filter = jnp.any(lat_index == jnp.asarray(filter_lat, jnp.int32))
+    halo_ids = jnp.stack([row_start - 1, row_start + lat_rows])
+    halo_cut = cutoff[jnp.clip(halo_ids, 0, total_rows - 1)]
+    halo_own = filtered(jnp.concatenate([south_raw, north_raw], axis=2), halo_cut,
+                        jnp.logical_and(jnp.logical_not(is_filter), jnp.any(halo_cut < HALF)), 40)
+    stacked, below_plain, above_plain, halo_own = lax.optimization_barrier(
+        (stacked, below_plain, above_plain, halo_own))
+    field = filtered(stacked, own_cut)
     top = jnp.concatenate([field[:, levels - 1], vertical_wind[levels - 1 :]], axis=0)
     bottom = jnp.concatenate([field[:, 0], vertical_wind[:1]], axis=0)
     below_filtered = group_shift(top, filter_lat, True)
     above_filtered = group_shift(bottom, filter_lat, False)
-    is_filter = jnp.any(lat_index == jnp.asarray(filter_lat, jnp.int32))
     below_all = jnp.where(is_filter, below_filtered, below_plain)
     above_all = jnp.where(is_filter, above_filtered, above_plain)
     below, below_wind = below_all[:3, None], below_all[3:]
@@ -126,14 +130,6 @@
     north_filtered = lat_group_shift(field[:, :, :1], filter_lat, False)
     south_is_filter = jnp.any(lat_index - 1 == jnp.asarray(filter_lat, jnp.int32))
     north_is_filter = jnp.any(lat_index + 1 == jnp.asarray(filter_lat, jnp.int32))
-    halo_ids = jnp.stack([row_start - 1, row_start + lat_rows])
-    halo_cut = cutoff[jnp.clip(halo_ids, 0, total_rows - 1)]
-    halo_raw = jnp.concatenate([south_plain, north_plain], axis=2)
-    halo_rows = halo_raw.reshape(-1, NLON)
-    halo_cuts = jnp.broadcast_to(halo_cut, halo_raw.shape[:-1]).reshape(-1)
-    halo_own = lax.cond(jnp.logical_and(jnp.logical_not(is_filter), jnp.any(halo_cut < HALF)),
-                        lambda: lowpass_rows(halo_rows, halo_cuts, tables), lambda: halo_rows)
-    halo_own = halo_own.reshape(halo_raw.shape)
     south = jnp.where(jnp.logical_and(is_filter, south_is_filter), south_filtered, halo_own[:, :, :1])
     north = jnp.where(jnp.logical_and(is_filter, north_is_filter), north_filtered, halo_own[:, :, 1:])
 

time: 124 us -> 105 us (0.85)
  other arithmetic: 23.2 us -> 15 us
  local copies, waits for them, and re-layouts: 10.7 us -> 5.12 us
  matrix products: 12.8 us -> 9.99 us
  starting transfers between devices: 25.6 us -> 23.6 us
    ppermute x4, waiting for transfers between devices: 0.01 us -> 45 us  [group_shift(): return lax.ppermute(x, ('lat', 'lev'), pairs)]
    ppermute x2, waiting for transfers between devices: 44.1 us -> 0.01 us  [lat_group_shift(): return lax.ppermute(x, ('lat', 'lev'), pairs)]
    add x2, other arithmetic: 6.45 us -> 2.31 us  [parity_table(): as_f32(first)[None] * as_f32(np.cos(hi))[:, None]]
    dot_general x1, matrix products: 4.3 us -> 2.19 us  [lowpass_rows(): jnp.dot(first - second, odd_table, precision=mxu_precision, preferred_ele...]
    dot_general x1, matrix products: 4.37 us -> 2.29 us  [lowpass_rows(): lax.dot_general(spec_odd * parity_weight(1, cut), odd_table, dims, precis...]
    unnamed x24 -> x22, local copies, waits for them, and re-layouts: 2.11 us -> 0.06 us
    slice x3 -> x2, local copies, waits for them, and re-layouts: 2.16 us -> 0.22 us  [the longest x1 0.2 us: on_device(): south_raw = shift(stacked[:, :, lat_rows - 1:], 'lat', True)]
    ppermute x2, starting transfers between devices: 6.37 us -> 4.93 us  [lat_group_shift(): return lax.ppermute(x, ('lat', 'lev'), pairs)]
  transfers between devices with their start and end apart: 8 -> 8, of which waited for: 2 -> 2; matrix products, arithmetic and copies ran while one was open for 17% -> 8% of each run, Pallas kernels for 0% -> 0%
where the time goes in v9:
time: 105 us; the launch traced here: 104 us
  waiting for transfers between devices  45 us (43%)
  starting transfers between devices  23.6 us (22%)
  other arithmetic  15 us (14%)
  matrix products  9.99 us (10%)
  between operations  5.29 us (5%)
  local copies, waits for them, and re-layouts  5.12 us (5%)
    ppermute x4, waiting for transfers between devices, group_shift(): return lax.ppermute(x, ('lat', 'lev'), pairs)  45 us
    ppermute x4, starting transfers between devices, group_shift(): return lax.ppermute(x, ('lat', 'lev'), pairs)  12.5 us
    ppermute x2, starting transfers between devices, shift(): return lax.ppermute(x, axis, pairs)  6.16 us
    ppermute x2, starting transfers between devices, lat_group_shift(): return lax.ppermute(x, ('lat', 'lev'), pairs)  4.93 us
    dot_general x1, matrix products, lowpass_rows(): lax.dot_general(spec_even * parity_weight(0, cut), even_table, dims, prec...  3.34 us
    add x2, other arithmetic, parity_table(): as_f32(first)[None] * as_f32(np.cos(hi))[:, None]  2.31 us
    dot_general x1, matrix products, lowpass_rows(): lax.dot_general(spec_odd * parity_weight(1, cut), odd_table, dims, precis...  2.29 us
    dot_general x1, matrix products, lowpass_rows(): jnp.dot(first - second, odd_table, precision=mxu_precision, preferred_ele...  2.19 us
  transfers between devices with their start and end apart: 8, of which 2 were waited for; matrix products, arithmetic and copies ran while one was open for 8% of the time, Pallas kernels for 0%

profile of v9, /device:TPU:47, one launch (start us, length us, event | category | flops | bytes accessed | tf_op | source)
XLA Modules:
  0.0 104.1 jit_solution(8669905110231598934)
XLA Ops:
  0.6 1.7 %pad_maximum_fusion = f32[3,4,16,2880]{3,2,1,0:T(8,128)S(1)} fusion(f32[1,4,16,2880]{3,2,1,0:T(8,128)} %bitcast.82, f32[1,4,16,2880]{3,2,1,0:T(8,128)} %bitcast.83, f32[1,4,16,2880]{3,2,1,0:T(8,128)} %bitcast.84), kind=kLoop, calls=%fused_computation.39 | loop fusion | flops 1105920 | bytes 4423680 | tf_op jit(solution)/shard_map/stack | solution.py:101
  2.4 0.2 fusion.28
  2.6 4.2 %collective-permute-start.2 = (f32[3,4,1,2880]{3,2,1,0:T(1,128)S(1)}, f32[3,4,1,2880]{3,2,1,0:T(1,128)S(1)}, u32[]{:S(2)}, u32[]{:S(2)}) collective-permute-start(f32[3,4,1,2880]{3,2,1,0:T(1,128)S(1)} %get-tuple-element.190), channel_id=1, source_target_pairs={{0,8},{8,16},{16,24},{24,32},{32,40},{40,48},{48,56},{56,64},{64,7... | collective-permute-start | bytes 414728 | tf_op jit(solution)/shard_map/ppermute | solution.py:25
  6.8 1.9 %collective-permute-start.3 = (f32[3,4,1,2880]{3,2,1,0:T(1,128)S(1)}, f32[3,4,1,2880]{3,2,1,0:T(1,128)S(1)}, u32[]{:S(2)}, u32[]{:S(2)}) collective-permute-start(f32[3,4,1,2880]{3,2,1,0:T(1,128)S(1)} %get-tuple-element.191), channel_id=1, source_target_pairs={{8,0},{16,8},{24,16},{32,24},{40,32},{48,40},{56,48},{64,56},{72,6... | collective-permute-start | bytes 414728 | tf_op jit(solution)/shard_map/ppermute | solution.py:25
  8.9 0.9 pad_maximum_fusion.4
  9.9 1.6 %collective-permute-start = (f32[4,16,2880]{2,1,0:T(8,128)}, f32[4,16,2880]{2,1,0:T(8,128)}, u32[]{:S(2)}, u32[]{:S(2)}) collective-permute-start(f32[4,16,2880]{2,1,0:T(8,128)} %pad_maximum_fusion.4), channel_id=1, source_target_pairs={{40,41},{41,42},{42,43},{43,44},{44,45},{45,46},{46,47},{48,49},{4... | collective-permute-start | bytes 2211848 | tf_op jit(solution)/shard_map/ppermute | solution.py:35
  11.5 0.9 pad_maximum_fusion.6
  12.4 1.5 %collective-permute-start.1 = (f32[4,16,2880]{2,1,0:T(8,128)}, f32[4,16,2880]{2,1,0:T(8,128)}, u32[]{:S(2)}, u32[]{:S(2)}) collective-permute-start(f32[4,16,2880]{2,1,0:T(8,128)} %pad_maximum_fusion.6), channel_id=1, source_target_pairs={{41,40},{42,41},{43,42},{44,43},{45,44},{46,45},{47,46},{49,48},{5... | collective-permute-start | bytes 2211848 | tf_op jit(solution)/shard_map/ppermute | solution.py:35
  13.9 0.1 fusion.24
  14.0 0.6 gather_fusion
  14.7 0.6 compare_reduce_fusion.2
  15.4 0.8 compare_reduce_fusion
  16.1 0.7 compare_reduce_fusion.4
  21.1 0.3 pad_maximum_fusion.7
  21.3 0.2 reshape.182
  21.6 0.9 reshape.207
  22.5 14.6 %conditional.3 = (f32[192,2880]{1,0:T(8,128)S(1)}) conditional(s32[]{:T(128)} %convert_element_type.20, f32[192,2880]{1,0:T(8,128)S(1)} %bitcast.59, (s32[16]{0:T(128)S(1)}, f32[192,2880]{1,0:T(8,128)S(1)}, s32[720]{0:T(1024)S(1)}, s32[720]{0:T(1024)S(1)}) %tuple.145), branch_computations={%region_5.6_spmd, %region_6.7_spmd.clone.clone} | conditional | flops 4786840576 | bytes 46154776 | solution.py:89
  22.5 0.1 le.65
  22.6 1.7 %multiply_add_fusion.2 = f32[30,48,720]{2,1,0:T(8,128)S(1)} fusion(f32[30,720]{1,0:T(8,128)} %constant.131.clone.3, f32[48,720]{1,0:T(8,128)} %constant.130.clone.3, f32[30,720]{1,0:T(8,128)} %constant.129.clone.3, f32[48,720]{1,0:T(8,128)} %constant.128.clone.3), kind=kLoop, calls=%fused_computation.15 | loop fusion | flops 3110400 | bytes 4596480 | tf_op jit(solution)/shard_map/cond/branch_1_fun/add | solution.py:56
  24.3 2.2 %convolution_multiply_fusion.2 = f32[192,720]{1,0:T(8,128)S(1)} fusion(f32[1440,720]{1,0:T(8,128)S(1)} %bitcast.76, f32[192,2880]{1,0:T(8,128)S(1)} %get-tuple-element.160, f32[720]{0:T(1024)S(1)} %get-tuple-element.181, s32[720]{0:T(1024)S(1)} %get-tuple-element.162, s32[192]{0:T(256)S(1)} %le.65), kind=kOutput, calls=%fused_computation.18 | convolution fusion | flops 1195084800 | bytes 7345152 | tf_op jit(solution)/shard_map/cond/branch_1_fun/dot_general | solution.py:73
  26.5 2.3 %fusion.31 = f32[192,1440]{1,0:T(8,128)S(1)} fusion(f32[192,720]{1,0:T(8,128)S(1)} %convolution_multiply_fusion.2, f32[1440,720]{1,0:T(8,128)S(1)} %bitcast.77), kind=kOutput, calls=%fused_computation.88 | convolution fusion | flops 1194393600 | bytes 5806080 | tf_op jit(solution)/shard_map/cond/branch_1_fun/dot_general | solution.py:78
  28.9 0.6 multiply_add_fusion.3
  29.5 2.2 %convolution_multiply_fusion.3 = f32[192,720]{1,0:T(8,128)S(1)} fusion(f32[1440,720]{1,0:T(8,128)S(1)} %bitcast.72, f32[192,2880]{1,0:T(8,128)S(1)} %get-tuple-element.160, f32[720]{0:T(1024)S(1)} %get-tuple-element.182, s32[720]{0:T(1024)S(1)} %get-tuple-element.161, s32[192]{0:T(256)S(1)} %le.65), kind=kOutput, calls=%fused_computation.19 | convolution fusion | flops 1195084800 | bytes 7345152 | tf_op jit(solution)/shard_map/cond/branch_1_fun/dot_general | solution.py:71
  31.7 3.3 %fusion.26 = (f32[192,1440]{1,0:T(8,128)S(1)}, f32[192,1440]{1,0:T(8,128)}) fusion(f32[192,1440]{1,0:T(8,128)S(1)} %fusion.31, f32[192,720]{1,0:T(8,128)S(1)} %convolution_multiply_fusion.3, f32[1440,720]{1,0:T(8,128)S(1)} %bitcast.73), kind=kOutput, calls=%fused_computation.83 | convolution fusion | flops 1194946560 | bytes 8017920 | tf_op jit(solution)/shard_map/cond/branch_1_fun/dot_general | solution.py:76
  35.0 0.1 reshape.208
  35.1 2.0 %maximum_select_fusion.1 = f32[192,2880]{1,0:T(8,128)S(1)} fusion(f32[192,2880]{1,0:T(8,128)S(1)} %get-tuple-element.160, f32[192,1440]{1,0:T(8,128)} %get-tuple-element.179, f32[192,1440]{1,0:T(8,128)S(1)} %get-tuple-element.178, pred[192]{0:T(512)(128)(4,1)S(1)} %reshape.208), kind=kLoop, calls=%fused_computation.17 | loop fusion | flops 1105920 | bytes 6635712 | tf_op jit(solution)/shard_map/cond/branch_1_fun/jit(_where)/select_n | solution.py:81
  37.2 0.3 slice.180
  37.5 0.6 slice.177
  38.1 0.2 fusion.27
  38.4 0.1 fusion.23
  38.5 0.3 fusion.18
  38.8 0.1 slice.182
  38.9 3.6 %collective-permute-start.4 = (f32[3,4,1,2880]{3,2,1,0:T(1,128)S(1)}, f32[3,4,1,2880]{3,2,1,0:T(1,128)S(1)}, u32[]{:S(2)}, u32[]{:S(2)}) collective-permute-start(f32[3,4,1,2880]{3,2,1,0:T(1,128)S(1)} %get-tuple-element.187), channel_id=1, source_target_pairs={{0,8},{1,9},{2,10},{3,11},{4,12},{5,13},{6,14},{7,15},{8,16},{9,17... | collective-permute-start | bytes 414728 | tf_op jit(solution)/shard_map/ppermute | solution.py:43
  42.6 1.3 %collective-permute-start.5 = (f32[3,4,1,2880]{3,2,1,0:T(1,128)S(1)}, f32[3,4,1,2880]{3,2,1,0:T(1,128)S(1)}, u32[]{:S(2)}, u32[]{:S(2)}) collective-permute-start(f32[3,4,1,2880]{3,2,1,0:T(1,128)S(1)} %get-tuple-element.186), channel_id=1, source_target_pairs={{8,0},{9,1},{10,2},{11,3},{12,4},{13,5},{14,6},{15,7},{16,8},{17,9... | collective-permute-start | bytes 414728 | tf_op jit(solution)/shard_map/ppermute | solution.py:43
  43.9 6.9 %collective-permute-start.7 = (f32[4,16,2880]{2,1,0:T(8,128)S(1)}, f32[4,16,2880]{2,1,0:T(8,128)S(1)}, u32[]{:S(2)}, u32[]{:S(2)}) collective-permute-start(f32[4,16,2880]{2,1,0:T(8,128)S(1)} %pad_maximum_fusion.5), channel_id=1, source_target_pairs={{1,0},{2,1},{3,2},{4,3},{5,4},{6,5},{7,6},{9,8},{10,9},{11,10},{12... | collective-permute-start | bytes 2211848 | tf_op jit(solution)/shard_map/ppermute | solution.py:35
  50.9 2.5 %collective-permute-start.6 = (f32[4,16,2880]{2,1,0:T(8,128)S(1)}, f32[4,16,2880]{2,1,0:T(8,128)S(1)}, u32[]{:S(2)}, u32[]{:S(2)}) collective-permute-start(f32[4,16,2880]{2,1,0:T(8,128)S(1)} %pad_maximum_fusion.3), channel_id=1, source_target_pairs={{0,1},{1,2},{2,3},{3,4},{4,5},{5,6},{6,7},{8,9},{9,10},{10,11},{11... | collective-permute-start | bytes 2211848 | tf_op jit(solution)/shard_map/ppermute | solution.py:35
  53.5 0.3 broadcast_select_fusion.2
  53.8 0.2 fusion.21
  53.9 0.2 fusion.20
  54.1 0.6 fusion.12
  54.8 13.5 %collective-permute-done.7 = f32[4,16,2880]{2,1,0:T(8,128)S(1)} collective-permute-done((f32[4,16,2880]{2,1,0:T(8,128)S(1)}, f32[4,16,2880]{2,1,0:T(8,128)S(1)}, u32[]{:S(2)}, u32[]{:S(2)}) %collective-permute-start.7) | collective-permute-done | bytes 737312 | tf_op jit(solution)/shard_map/ppermute | solution.py:35
  68.3 0.7 broadcast_select_fusion
  69.0 31.5 %collective-permute-done.6 = f32[4,16,2880]{2,1,0:T(8,128)S(1)} collective-permute-done((f32[4,16,2880]{2,1,0:T(8,128)S(1)}, f32[4,16,2880]{2,1,0:T(8,128)S(1)}, u32[]{:S(2)}, u32[]{:S(2)}) %collective-permute-start.6) | collective-permute-done | bytes 737312 | tf_op jit(solution)/shard_map/ppermute | solution.py:35
  100.5 0.7 broadcast_select_fusion.1
  101.2 0.1 fusion.22
  101.3 0.3 fusion.13
  101.7 1.1 %fusion.14 = f32[3,4,16,2880]{3,2,1,0:T(8,128)S(1)} fusion(f32[3,5,16,2880]{3,2,1,0:T(8,128)S(1)} %fusion.13, f32[3,4,16,2880]{3,2,1,0:T(8,128)S(1)} %bitcast.69, f32[3,4,17,2880]{3,2,1,0:T(8,128)S(1)} %fusion.12, f32[3,4,16,2880]{3,2,1,0:T(8,128)S(1)} %fusion.18, f32[3,4,16,2879]{3,2,1,0:T(8,128)S(1)} %bitcast.78, f32[3,4,16,1]{3,2,1,0:T(8,128)S(1)} %slice.182, ...), kind=kLoop, calls=%fused_computation.34 | loop fusion | flops 4423680 | bytes 17694784 | tf_op jit(solution)/shard_map/sub | solution.py:160
  102.7 1.4 %slice_bitcast_fusion = (f32[4,16,2880]{2,1,0:T(8,128)}, f32[4,16,2880]{2,1,0:T(8,128)}, f32[4,16,2880]{2,1,0:T(8,128)}) fusion(f32[3,4,16,2880]{3,2,1,0:T(8,128)S(1)} %fusion.14), kind=kLoop, calls=%fused_computation.55 | loop fusion | bytes 4423680 | tf_op jit(solution)/shard_map/squeeze | solution.py:161
  (57 shorter events, 0.7 us)
Async XLA Ops:
  2.4 6.5 %copy-start.2 = (f32[4,16,2880]{2,1,0:T(8,128)S(1)}, f32[4,16,2880]{2,1,0:T(8,128)}, u32[]{:S(2)}) copy-start(f32[4,16,2880]{2,1,0:T(8,128)} %param.35) | copy-start | bytes 2211844
  2.6 18.5 %collective-permute-start.2 = (f32[3,4,1,2880]{3,2,1,0:T(1,128)S(1)}, f32[3,4,1,2880]{3,2,1,0:T(1,128)S(1)}, u32[]{:S(2)}, u32[]{:S(2)}) collective-permute-start(f32[3,4,1,2880]{3,2,1,0:T(1,128)S(1)} %get-tuple-element.190), channel_id=1, source_target_pairs={{0,8},{8,16},{16,24},{24,32},{32,40},{40,48},{48,56},{56,64},{64,7... | collective-permute-start | bytes 414728 | tf_op jit(solution)/shard_map/ppermute | solution.py:25
  6.8 14.3 %collective-permute-start.3 = (f32[3,4,1,2880]{3,2,1,0:T(1,128)S(1)}, f32[3,4,1,2880]{3,2,1,0:T(1,128)S(1)}, u32[]{:S(2)}, u32[]{:S(2)}) collective-permute-start(f32[3,4,1,2880]{3,2,1,0:T(1,128)S(1)} %get-tuple-element.191), channel_id=1, source_target_pairs={{8,0},{16,8},{24,16},{32,24},{40,32},{48,40},{56,48},{64,56},{72,6... | collective-permute-start | bytes 414728 | tf_op jit(solution)/shard_map/ppermute | solution.py:25
  8.8 5.2 %copy-start = (s32[512]{0:T(512)S(1)}, s32[512]{0:T(512)}, u32[]{:S(2)}) copy-start(s32[512]{0:T(512)} %param.36) | copy-start | bytes 6148
  8.9 6.5 %copy-start.19 = (s32[10]{0:T(128)S(1)}, s32[10]{0:T(128)}, u32[]{:S(2)}) copy-start(s32[10]{0:T(128)} %constant.113.clone) | copy-start | bytes 124
  8.9 3.5 %copy-start.4 = (f32[1,16,2880]{2,1,0:T(8,128)}, f32[1,16,2880]{2,1,0:T(8,128)S(1)}, u32[]{:S(2)}) copy-start(f32[1,16,2880]{2,1,0:T(8,128)S(1)} %get-tuple-element.195) | copy-start | bytes 552964
  8.9 5.0 %copy-start.6 = (f32[1,16,2880]{2,1,0:T(8,128)}, f32[1,16,2880]{2,1,0:T(8,128)S(1)}, u32[]{:S(2)}) copy-start(f32[1,16,2880]{2,1,0:T(8,128)S(1)} %get-tuple-element.194) | copy-start | bytes 552964
  8.9 12.6 %copy-start.17 = (s32[720]{0:T(1024)S(1)}, s32[720]{0:T(1024)}, u32[]{:S(2)}) copy-start(s32[720]{0:T(1024)} %constant.122.clone) | copy-start | bytes 8644
  8.9 12.6 %copy-start.18 = (s32[720]{0:T(1024)S(1)}, s32[720]{0:T(1024)}, u32[]{:S(2)}) copy-start(s32[720]{0:T(1024)} %constant.123.clone) | copy-start | bytes 8644
  9.9 12.6 %collective-permute-start = (f32[4,16,2880]{2,1,0:T(8,128)}, f32[4,16,2880]{2,1,0:T(8,128)}, u32[]{:S(2)}, u32[]{:S(2)}) collective-permute-start(f32[4,16,2880]{2,1,0:T(8,128)} %pad_maximum_fusion.4), channel_id=1, source_target_pairs={{40,41},{41,42},{42,43},{43,44},{44,45},{45,46},{46,47},{48,49},{4... | collective-permute-start | bytes 2211848 | tf_op jit(solution)/shard_map/ppermute | solution.py:35
  12.4 10.1 %collective-permute-start.1 = (f32[4,16,2880]{2,1,0:T(8,128)}, f32[4,16,2880]{2,1,0:T(8,128)}, u32[]{:S(2)}, u32[]{:S(2)}) collective-permute-start(f32[4,16,2880]{2,1,0:T(8,128)} %pad_maximum_fusion.6), channel_id=1, source_target_pairs={{41,40},{42,41},{43,42},{44,43},{45,44},{46,45},{47,46},{49,48},{5... | collective-permute-start | bytes 2211848 | tf_op jit(solution)/shard_map/ppermute | solution.py:35
  26.5 2.3 %copy-start.9 = (f32[48,720]{1,0:T(8,128)S(1)}, f32[48,720]{1,0:T(8,128)}, u32[]{:S(2)}) copy-start(f32[48,720]{1,0:T(8,128)} %constant.124.clone.3) | copy-start | bytes 414724 | tf_op jit(solution)/shard_map/cond
  26.5 2.3 %copy-start.10 = (f32[48,720]{1,0:T(8,128)S(1)}, f32[48,720]{1,0:T(8,128)}, u32[]{:S(2)}) copy-start(f32[48,720]{1,0:T(8,128)} %constant.126.clone.3) | copy-start | bytes 414724 | tf_op jit(solution)/shard_map/cond
  26.5 2.3 %copy-start.15 = (f32[30,720]{1,0:T(8,128)S(1)}, f32[30,720]{1,0:T(8,128)}, u32[]{:S(2)}) copy-start(f32[30,720]{1,0:T(8,128)} %constant.125.clone.3) | copy-start | bytes 259204 | tf_op jit(solution)/shard_map/cond
  26.5 2.3 %copy-start.16 = (f32[30,720]{1,0:T(8,128)S(1)}, f32[30,720]{1,0:T(8,128)}, u32[]{:S(2)}) copy-start(f32[30,720]{1,0:T(8,128)} %constant.127.clone.3) | copy-start | bytes 259204 | tf_op jit(solution)/shard_map/cond
  38.5 5.4 %copy-start.7 = (f32[1,16,2880]{2,1,0:T(8,128)S(1)}, f32[1,16,2880]{2,1,0:T(8,128)}, u32[]{:S(2)}) copy-start(f32[1,16,2880]{2,1,0:T(8,128)} %copy-done.6) | copy-start | bytes 552964
  38.5 12.3 %copy-start.5 = (f32[1,16,2880]{2,1,0:T(8,128)S(1)}, f32[1,16,2880]{2,1,0:T(8,128)}, u32[]{:S(2)}) copy-start(f32[1,16,2880]{2,1,0:T(8,128)} %copy-done.4) | copy-start | bytes 552964
  38.8 14.6 %copy-start.8 = (f32[3,4,2,2880]{3,2,1,0:T(2,128)S(1)}, f32[3,4,2,2880]{3,2,1,0:T(2,128)}, u32[]{:S(2)}) copy-start(f32[3,4,2,2880]{3,2,1,0:T(2,128)} %reshape.207) | copy-start | bytes 829444
  38.9 14.5 %collective-permute-start.4 = (f32[3,4,1,2880]{3,2,1,0:T(1,128)S(1)}, f32[3,4,1,2880]{3,2,1,0:T(1,128)S(1)}, u32[]{:S(2)}, u32[]{:S(2)}) collective-permute-start(f32[3,4,1,2880]{3,2,1,0:T(1,128)S(1)} %get-tuple-element.187), channel_id=1, source_target_pairs={{0,8},{1,9},{2,10},{3,11},{4,12},{5,13},{6,14},{7,15},{8,16},{9,17... | collective-permute-start | bytes 414728 | tf_op jit(solution)/shard_map/ppermute | solution.py:43
  42.6 10.9 %collective-permute-start.5 = (f32[3,4,1,2880]{3,2,1,0:T(1,128)S(1)}, f32[3,4,1,2880]{3,2,1,0:T(1,128)S(1)}, u32[]{:S(2)}, u32[]{:S(2)}) collective-permute-start(f32[3,4,1,2880]{3,2,1,0:T(1,128)S(1)} %get-tuple-element.186), channel_id=1, source_target_pairs={{8,0},{9,1},{10,2},{11,3},{12,4},{13,5},{14,6},{15,7},{16,8},{17,9... | collective-permute-start | bytes 414728 | tf_op jit(solution)/shard_map/ppermute | solution.py:43
  43.9 24.4 %collective-permute-start.7 = (f32[4,16,2880]{2,1,0:T(8,128)S(1)}, f32[4,16,2880]{2,1,0:T(8,128)S(1)}, u32[]{:S(2)}, u32[]{:S(2)}) collective-permute-start(f32[4,16,2880]{2,1,0:T(8,128)S(1)} %pad_maximum_fusion.5), channel_id=1, source_target_pairs={{1,0},{2,1},{3,2},{4,3},{5,4},{6,5},{7,6},{9,8},{10,9},{11,10},{12... | collective-permute-start | bytes 2211848 | tf_op jit(solution)/shard_map/ppermute | solution.py:35
  50.9 49.6 %collective-permute-start.6 = (f32[4,16,2880]{2,1,0:T(8,128)S(1)}, f32[4,16,2880]{2,1,0:T(8,128)S(1)}, u32[]{:S(2)}, u32[]{:S(2)}) collective-permute-start(f32[4,16,2880]{2,1,0:T(8,128)S(1)} %pad_maximum_fusion.3), channel_id=1, source_target_pairs={{0,1},{1,2},{2,3},{3,4},{4,5},{5,6},{6,7},{8,9},{9,10},{10,11},{11... | collective-permute-start | bytes 2211848 | tf_op jit(solution)/shard_map/ppermute | solution.py:35
  69.0 32.3 %copy-start.3 = (f32[4,16,2880]{2,1,0:T(8,128)S(1)}, f32[4,16,2880]{2,1,0:T(8,128)}, u32[]{:S(2)}) copy-start(f32[4,16,2880]{2,1,0:T(8,128)} %param.35) | copy-start | bytes 2211844

commit v10 on v7

--- a/solution.py
+++ b/solution.py
@@ -123,8 +123,10 @@
     above_all = jnp.where(is_filter, above_filtered, above_plain)
     below, below_wind = below_all[:3, None], below_all[3:]
     above, above_wind = above_all[:3, None], above_all[3:]
-    south_filtered = lat_group_shift(field[:, :, lat_rows - 1 :], filter_lat, True)
-    north_filtered = lat_group_shift(field[:, :, :1], filter_lat, False)
+    south_source, north_source, _ = lax.optimization_barrier(
+        (field[:, :, lat_rows - 1 :], field[:, :, :1], (below_filtered, above_filtered)))
+    south_filtered = lat_group_shift(south_source, filter_lat, True)
+    north_filtered = lat_group_shift(north_source, filter_lat, False)
     south_is_filter = jnp.any(lat_index - 1 == jnp.asarray(filter_lat, jnp.int32))
     north_is_filter = jnp.any(lat_index + 1 == jnp.asarray(filter_lat, jnp.int32))
     south = jnp.where(south_is_filter, south_filtered, south_plain)

time: 99.2 us -> 100 us (level)
  the two profiles are of different devices: /device:TPU:80 before, /device:TPU:47 now
where the time goes in v10:
time: 100 us; the launch traced here: 99 us
  waiting for transfers between devices  48.2 us (48%)
  starting transfers between devices  21.2 us (21%)
  other arithmetic  15.4 us (15%)
  matrix products  8.56 us (9%)
  local copies, waits for them, and re-layouts  4.04 us (4%)
  between operations  1.52 us (2%)
    ppermute x4, waiting for transfers between devices, group_shift(): return lax.ppermute(x, ('lat', 'lev'), pairs)  42.2 us
    ppermute x4, starting transfers between devices, group_shift(): return lax.ppermute(x, ('lat', 'lev'), pairs)  13 us
    ppermute x4, starting transfers between devices, lat_group_shift(): return lax.ppermute(x, ('lat', 'lev'), pairs)  8.16 us
    ppermute x4, waiting for transfers between devices, lat_group_shift(): return lax.ppermute(x, ('lat', 'lev'), pairs)  6.04 us
    add x2, other arithmetic, parity_table(): as_f32(first)[None] * as_f32(np.cos(hi))[:, None]  2.33 us
    dot_general x1, matrix products, lowpass_rows(): lax.dot_general(spec_odd * parity_weight(1, cut), odd_table, dims, precis...  2.28 us
    dot_general x1, matrix products, lowpass_rows(): jnp.dot(first - second, odd_table, precision=mxu_precision, preferred_ele...  2.19 us
    dot_general x1, matrix products, lowpass_rows(): lax.dot_general(spec_even * parity_weight(0, cut), even_table, dims, prec...  2.16 us
  transfers between devices with their start and end apart: 8, of which 5 were waited for; matrix products, arithmetic and copies ran while one was open for 7% of the time, Pallas kernels for 0%

profile of v10, /device:TPU:47, one launch (start us, length us, event | category | flops | bytes accessed | tf_op | source)
XLA Modules:
  0.0 99.0 jit_solution(5622768435410007584)
XLA Ops:
  0.6 1.8 %pad_maximum_fusion = f32[3,4,16,2880]{3,2,1,0:T(8,128)S(1)} fusion(f32[1,4,16,2880]{3,2,1,0:T(8,128)} %bitcast.64, f32[1,4,16,2880]{3,2,1,0:T(8,128)} %bitcast.65, f32[1,4,16,2880]{3,2,1,0:T(8,128)} %bitcast.66), kind=kLoop, calls=%fused_computation.22 | loop fusion | flops 1105920 | bytes 4423680 | tf_op jit(solution)/shard_map/stack | solution.py:101
  2.4 0.1 slice_bitcast_fusion.7
  2.6 0.9 pad_maximum_fusion.4
  3.5 1.6 %collective-permute-start = (f32[4,16,2880]{2,1,0:T(8,128)}, f32[4,16,2880]{2,1,0:T(8,128)}, u32[]{:S(2)}, u32[]{:S(2)}) collective-permute-start(f32[4,16,2880]{2,1,0:T(8,128)} %pad_maximum_fusion.4), channel_id=1, source_target_pairs={{40,41},{41,42},{42,43},{43,44},{44,45},{45,46},{46,47},{48,49},{4... | collective-permute-start | bytes 2211848 | tf_op jit(solution)/shard_map/ppermute | solution.py:35
  5.1 0.9 pad_maximum_fusion.6
  6.0 1.6 %collective-permute-start.1 = (f32[4,16,2880]{2,1,0:T(8,128)}, f32[4,16,2880]{2,1,0:T(8,128)}, u32[]{:S(2)}, u32[]{:S(2)}) collective-permute-start(f32[4,16,2880]{2,1,0:T(8,128)} %pad_maximum_fusion.6), channel_id=1, source_target_pairs={{41,40},{42,41},{43,42},{44,43},{45,44},{46,45},{47,46},{49,48},{5... | collective-permute-start | bytes 2211848 | tf_op jit(solution)/shard_map/ppermute | solution.py:35
  7.5 0.9 fusion.20
  8.4 1.3 %collective-permute-start.2 = (f32[3,4,1,2880]{3,2,1,0:T(1,128)}, f32[3,4,1,2880]{3,2,1,0:T(1,128)S(1)}, u32[]{:S(2)}, u32[]{:S(2)}) collective-permute-start(f32[3,4,1,2880]{3,2,1,0:T(1,128)} %get-tuple-element.146), channel_id=1, source_target_pairs={{40,48},{41,49},{42,50},{43,51},{44,52},{45,53},{46,54},{47,55},{4... | collective-permute-start | bytes 414728 | tf_op jit(solution)/shard_map/ppermute | solution.py:43
  9.7 1.3 %collective-permute-start.3 = (f32[3,4,1,2880]{3,2,1,0:T(1,128)}, f32[3,4,1,2880]{3,2,1,0:T(1,128)}, u32[]{:S(2)}, u32[]{:S(2)}) collective-permute-start(f32[3,4,1,2880]{3,2,1,0:T(1,128)} %get-tuple-element.145), channel_id=1, source_target_pairs={{40,32},{41,33},{42,34},{43,35},{44,36},{45,37},{46,38},{47,39},{4... | collective-permute-start | bytes 414728 | tf_op jit(solution)/shard_map/ppermute | solution.py:43
  11.0 0.6 sine_multiply_fusion
  11.7 1.4 %compare_reduce_fusion.3 = (pred[]{:T(512)}, s32[16]{0:T(128)S(1)}) fusion(s32[512]{0:T(512)} %param.24, s32[]{:T(128)S(6)} %select_n.52), kind=kLoop, calls=%fused_computation.56 | loop fusion | flops 31 | bytes 133 | tf_op jit(solution)/shard_map/reduce_or | solution.py:89
  13.7 0.7 compare_reduce_fusion.1
  14.4 5.2 %collective-permute-done.2 = f32[3,4,1,2880]{3,2,1,0:T(1,128)S(1)} collective-permute-done((f32[3,4,1,2880]{3,2,1,0:T(1,128)}, f32[3,4,1,2880]{3,2,1,0:T(1,128)S(1)}, u32[]{:S(2)}, u32[]{:S(2)}) %collective-permute-start.2) | collective-permute-done | bytes 138272 | tf_op jit(solution)/shard_map/ppermute | solution.py:43
  19.6 12.0 %conditional.1 = (f32[192,2880]{1,0:T(8,128)S(1)}) conditional(s32[]{:T(128)} %convert_element_type.17, f32[192,2880]{1,0:T(8,128)S(1)} %bitcast.45, (s32[16]{0:T(128)S(1)}, f32[192,2880]{1,0:T(8,128)S(1)}) %tuple.94), branch_computations={%region_1.0_spmd, %region_2.3_spmd.clone} | conditional | flops 4786836480 | bytes 46174092 | solution.py:89
  19.6 0.1 reshape.114
  19.7 1.7 %multiply_add_fusion = f32[30,48,720]{2,1,0:T(8,128)S(1)} fusion(f32[30,720]{1,0:T(8,128)} %constant.90.clone.2, f32[48,720]{1,0:T(8,128)} %constant.89.clone.2, f32[30,720]{1,0:T(8,128)} %constant.88.clone.2, f32[48,720]{1,0:T(8,128)} %constant.87.clone.2), kind=kLoop, calls=%fused_computation | loop fusion | flops 3110400 | bytes 4596480 | tf_op jit(solution)/shard_map/add | solution.py:57
  21.5 2.2 %convolution_multiply_fusion = f32[192,720]{1,0:T(8,128)S(1)} fusion(f32[1440,720]{1,0:T(8,128)S(1)} %bitcast.58, f32[192,2880]{1,0:T(8,128)S(1)} %get-tuple-element.127, s32[720]{0:T(1024)S(1)} %copy-done.7, s32[192]{0:T(256)S(1)} %reshape.114), kind=kOutput, calls=%fused_computation.3 | convolution fusion | flops 1195084800 | bytes 7341056 | tf_op jit(solution)/shard_map/cond/branch_1_fun/dot_general | solution.py:74
  23.7 2.3 %fusion.22 = f32[192,1440]{1,0:T(8,128)S(1)} fusion(f32[192,720]{1,0:T(8,128)S(1)} %convolution_multiply_fusion, f32[1440,720]{1,0:T(8,128)S(1)} %bitcast.59), kind=kOutput, calls=%fused_computation.63 | convolution fusion | flops 1194393600 | bytes 5806080 | tf_op jit(solution)/shard_map/cond/branch_1_fun/dot_general | solution.py:79
  26.1 0.6 multiply_add_fusion.1
  26.7 1.9 %convolution_multiply_fusion.1 = f32[192,720]{1,0:T(8,128)S(1)} fusion(f32[1440,720]{1,0:T(8,128)S(1)} %bitcast.56, f32[192,2880]{1,0:T(8,128)S(1)} %get-tuple-element.127, f32[720]{0:T(1024)S(1)} %copy-done.5, s32[720]{0:T(1024)S(1)} %copy-done.6, s32[192]{0:T(256)S(1)} %reshape.114), kind=kOutput, calls=%fused_computation.4 | convolution fusion | flops 1195084800 | bytes 7345152 | tf_op jit(solution)/shard_map/cond/branch_1_fun/dot_general | solution.py:72
  28.7 2.2 %fusion.18 = (f32[192,1440]{1,0:T(8,128)S(1)}, f32[192,1440]{1,0:T(8,128)S(1)}) fusion(f32[192,1440]{1,0:T(8,128)S(1)} %fusion.22, f32[192,720]{1,0:T(8,128)S(1)} %convolution_multiply_fusion.1, f32[1440,720]{1,0:T(8,128)S(1)} %bitcast.57), kind=kOutput, calls=%fused_computation.59 | convolution fusion | flops 1194946560 | bytes 8017920 | tf_op jit(solution)/shard_map/cond/branch_1_fun/dot_general | solution.py:77
  30.9 0.7 maximum_select_fusion
  31.7 0.3 slice.162
  31.9 0.6 slice.159
  32.6 0.1 slice_bitcast_fusion.5
  32.7 8.0 %collective-permute-start.5 = (f32[4,16,2880]{2,1,0:T(8,128)S(1)}, f32[4,16,2880]{2,1,0:T(8,128)S(1)}, u32[]{:S(2)}, u32[]{:S(2)}) collective-permute-start(f32[4,16,2880]{2,1,0:T(8,128)S(1)} %pad_maximum_fusion.5), channel_id=1, source_target_pairs={{1,0},{2,1},{3,2},{4,3},{5,4},{6,5},{7,6},{9,8},{10,9},{11,10},{12... | collective-permute-start | bytes 2211848 | tf_op jit(solution)/shard_map/ppermute | solution.py:35
  40.7 0.1 fusion.17
  40.8 0.4 fusion.12
  41.3 0.1 slice.164
  41.3 1.9 %collective-permute-start.4 = (f32[4,16,2880]{2,1,0:T(8,128)S(1)}, f32[4,16,2880]{2,1,0:T(8,128)S(1)}, u32[]{:S(2)}, u32[]{:S(2)}) collective-permute-start(f32[4,16,2880]{2,1,0:T(8,128)S(1)} %pad_maximum_fusion.3), channel_id=1, source_target_pairs={{0,1},{1,2},{2,3},{3,4},{4,5},{5,6},{6,7},{8,9},{9,10},{10,11},{11... | collective-permute-start | bytes 2211848 | tf_op jit(solution)/shard_map/ppermute | solution.py:35
  43.3 0.2 fusion.19
  43.5 34.9 %collective-permute-done.5 = f32[4,16,2880]{2,1,0:T(8,128)S(1)} collective-permute-done((f32[4,16,2880]{2,1,0:T(8,128)S(1)}, f32[4,16,2880]{2,1,0:T(8,128)S(1)}, u32[]{:S(2)}, u32[]{:S(2)}) %collective-permute-start.5) | collective-permute-done | bytes 737312 | tf_op jit(solution)/shard_map/ppermute | solution.py:35
  78.4 0.7 broadcast_select_fusion
  79.1 7.3 %collective-permute-done.4 = f32[4,16,2880]{2,1,0:T(8,128)S(1)} collective-permute-done((f32[4,16,2880]{2,1,0:T(8,128)S(1)}, f32[4,16,2880]{2,1,0:T(8,128)S(1)}, u32[]{:S(2)}, u32[]{:S(2)}) %collective-permute-start.4) | collective-permute-done | bytes 737312 | tf_op jit(solution)/shard_map/ppermute | solution.py:35
  86.4 0.7 broadcast_select_fusion.1
  87.1 2.6 %collective-permute-start.7 = (f32[3,4,1,2880]{3,2,1,0:T(1,128)S(1)}, f32[3,4,1,2880]{3,2,1,0:T(1,128)S(1)}, u32[]{:S(2)}, u32[]{:S(2)}) collective-permute-start(f32[3,4,1,2880]{3,2,1,0:T(1,128)S(1)} %get-tuple-element.102), channel_id=1, source_target_pairs={{8,0},{9,1},{10,2},{11,3},{12,4},{13,5},{14,6},{15,7},{16,8},{17,9... | collective-permute-start | bytes 414728 | tf_op jit(solution)/shard_map/ppermute | solution.py:43
  89.7 3.0 %collective-permute-start.6 = (f32[3,4,1,2880]{3,2,1,0:T(1,128)S(1)}, f32[3,4,1,2880]{3,2,1,0:T(1,128)S(1)}, u32[]{:S(2)}, u32[]{:S(2)}) collective-permute-start(f32[3,4,1,2880]{3,2,1,0:T(1,128)S(1)} %get-tuple-element.100), channel_id=1, source_target_pairs={{0,8},{1,9},{2,10},{3,11},{4,12},{5,13},{6,14},{7,15},{8,16},{9,17... | collective-permute-start | bytes 414728 | tf_op jit(solution)/shard_map/ppermute | solution.py:43
  92.7 0.1 fusion.16
  92.8 0.3 fusion.7
  93.1 0.4 collective-permute-done.7
  93.5 0.8 broadcast_select_fusion.2
  94.3 0.4 collective-permute-done.6
  94.7 0.8 broadcast_select_fusion.3
  95.5 0.2 fusion.15
  95.6 0.2 fusion.14
  95.8 0.6 fusion.6
  96.4 1.2 %fusion.8 = f32[3,4,16,2880]{3,2,1,0:T(8,128)S(1)} fusion(f32[3,5,16,2880]{3,2,1,0:T(8,128)S(1)} %fusion.7, f32[3,4,16,2880]{3,2,1,0:T(8,128)S(1)} %bitcast.55, f32[3,4,17,2880]{3,2,1,0:T(8,128)S(1)} %fusion.6, f32[3,4,16,2880]{3,2,1,0:T(8,128)S(1)} %fusion.12, f32[3,4,16,2879]{3,2,1,0:T(8,128)S(1)} %bitcast.60, f32[3,4,16,1]{3,2,1,0:T(8,128)S(1)} %slice.164, ...), kind=kLoop, calls=%fused_computation.17 | loop fusion | flops 4423680 | bytes 17694784 | tf_op jit(solution)/shard_map/sub | solution.py:159
  97.6 1.4 %slice_bitcast_fusion = (f32[4,16,2880]{2,1,0:T(8,128)}, f32[4,16,2880]{2,1,0:T(8,128)}, f32[4,16,2880]{2,1,0:T(8,128)}) fusion(f32[3,4,16,2880]{3,2,1,0:T(8,128)S(1)} %fusion.8), kind=kLoop, calls=%fused_computation.38 | loop fusion | bytes 4423680 | tf_op jit(solution)/shard_map/squeeze | solution.py:160
  (36 shorter events, 0.5 us)
Async XLA Ops:
  0.6 1.9 %copy-start = (f32[4,16,2880]{2,1,0:T(8,128)S(1)}, f32[4,16,2880]{2,1,0:T(8,128)}, u32[]{:S(2)}) copy-start(f32[4,16,2880]{2,1,0:T(8,128)} %param.23) | copy-start | bytes 2211844
  2.5 11.2 %copy-start.8 = (s32[10]{0:T(128)S(1)}, s32[10]{0:T(128)}, u32[]{:S(2)}) copy-start(s32[10]{0:T(128)} %constant.93.clone) | copy-start | bytes 124
  3.5 16.1 %collective-permute-start = (f32[4,16,2880]{2,1,0:T(8,128)}, f32[4,16,2880]{2,1,0:T(8,128)}, u32[]{:S(2)}, u32[]{:S(2)}) collective-permute-start(f32[4,16,2880]{2,1,0:T(8,128)} %pad_maximum_fusion.4), channel_id=1, source_target_pairs={{40,41},{41,42},{42,43},{43,44},{44,45},{45,46},{46,47},{48,49},{4... | collective-permute-start | bytes 2211848 | tf_op jit(solution)/shard_map/ppermute | solution.py:35
  6.0 13.6 %collective-permute-start.1 = (f32[4,16,2880]{2,1,0:T(8,128)}, f32[4,16,2880]{2,1,0:T(8,128)}, u32[]{:S(2)}, u32[]{:S(2)}) collective-permute-start(f32[4,16,2880]{2,1,0:T(8,128)} %pad_maximum_fusion.6), channel_id=1, source_target_pairs={{41,40},{42,41},{43,42},{44,43},{45,44},{46,45},{47,46},{49,48},{5... | collective-permute-start | bytes 2211848 | tf_op jit(solution)/shard_map/ppermute | solution.py:35
  8.4 11.2 %collective-permute-start.2 = (f32[3,4,1,2880]{3,2,1,0:T(1,128)}, f32[3,4,1,2880]{3,2,1,0:T(1,128)S(1)}, u32[]{:S(2)}, u32[]{:S(2)}) collective-permute-start(f32[3,4,1,2880]{3,2,1,0:T(1,128)} %get-tuple-element.146), channel_id=1, source_target_pairs={{40,48},{41,49},{42,50},{43,51},{44,52},{45,53},{46,54},{47,55},{4... | collective-permute-start | bytes 414728 | tf_op jit(solution)/shard_map/ppermute | solution.py:43
  9.7 9.9 %collective-permute-start.3 = (f32[3,4,1,2880]{3,2,1,0:T(1,128)}, f32[3,4,1,2880]{3,2,1,0:T(1,128)}, u32[]{:S(2)}, u32[]{:S(2)}) collective-permute-start(f32[3,4,1,2880]{3,2,1,0:T(1,128)} %get-tuple-element.145), channel_id=1, source_target_pairs={{40,32},{41,33},{42,34},{43,35},{44,36},{45,37},{46,38},{47,39},{4... | collective-permute-start | bytes 414728 | tf_op jit(solution)/shard_map/ppermute | solution.py:43
  19.7 1.7 %copy-start.7 = (s32[720]{0:T(1024)S(1)}, s32[720]{0:T(1024)}, u32[]{:S(2)}) copy-start(s32[720]{0:T(1024)} %constant.92.clone.2) | copy-start | bytes 8644 | tf_op jit(solution)/shard_map/cond
  23.6 2.3 %copy-start.1 = (f32[48,720]{1,0:T(8,128)S(1)}, f32[48,720]{1,0:T(8,128)}, u32[]{:S(2)}) copy-start(f32[48,720]{1,0:T(8,128)} %constant.83.clone.2) | copy-start | bytes 414724 | tf_op jit(solution)/shard_map/cond
  23.7 2.3 %copy-start.2 = (f32[48,720]{1,0:T(8,128)S(1)}, f32[48,720]{1,0:T(8,128)}, u32[]{:S(2)}) copy-start(f32[48,720]{1,0:T(8,128)} %constant.85.clone.2) | copy-start | bytes 414724 | tf_op jit(solution)/shard_map/cond
  23.7 2.3 %copy-start.3 = (f32[30,720]{1,0:T(8,128)S(1)}, f32[30,720]{1,0:T(8,128)}, u32[]{:S(2)}) copy-start(f32[30,720]{1,0:T(8,128)} %constant.84.clone.2) | copy-start | bytes 259204 | tf_op jit(solution)/shard_map/cond
  23.7 2.3 %copy-start.4 = (f32[30,720]{1,0:T(8,128)S(1)}, f32[30,720]{1,0:T(8,128)}, u32[]{:S(2)}) copy-start(f32[30,720]{1,0:T(8,128)} %constant.86.clone.2) | copy-start | bytes 259204 | tf_op jit(solution)/shard_map/cond
  26.0 0.7 copy-start.5
  26.0 0.7 copy-start.6
  32.7 45.6 %collective-permute-start.5 = (f32[4,16,2880]{2,1,0:T(8,128)S(1)}, f32[4,16,2880]{2,1,0:T(8,128)S(1)}, u32[]{:S(2)}, u32[]{:S(2)}) collective-permute-start(f32[4,16,2880]{2,1,0:T(8,128)S(1)} %pad_maximum_fusion.5), channel_id=1, source_target_pairs={{1,0},{2,1},{3,2},{4,3},{5,4},{6,5},{7,6},{9,8},{10,9},{11,10},{12... | collective-permute-start | bytes 2211848 | tf_op jit(solution)/shard_map/ppermute | solution.py:35
  41.3 45.0 %collective-permute-start.4 = (f32[4,16,2880]{2,1,0:T(8,128)S(1)}, f32[4,16,2880]{2,1,0:T(8,128)S(1)}, u32[]{:S(2)}, u32[]{:S(2)}) collective-permute-start(f32[4,16,2880]{2,1,0:T(8,128)S(1)} %pad_maximum_fusion.3), channel_id=1, source_target_pairs={{0,1},{1,2},{2,3},{3,4},{4,5},{5,6},{6,7},{8,9},{9,10},{10,11},{11... | collective-permute-start | bytes 2211848 | tf_op jit(solution)/shard_map/ppermute | solution.py:35
  87.1 6.4 %collective-permute-start.7 = (f32[3,4,1,2880]{3,2,1,0:T(1,128)S(1)}, f32[3,4,1,2880]{3,2,1,0:T(1,128)S(1)}, u32[]{:S(2)}, u32[]{:S(2)}) collective-permute-start(f32[3,4,1,2880]{3,2,1,0:T(1,128)S(1)} %get-tuple-element.102), channel_id=1, source_target_pairs={{8,0},{9,1},{10,2},{11,3},{12,4},{13,5},{14,6},{15,7},{16,8},{17,9... | collective-permute-start | bytes 414728 | tf_op jit(solution)/shard_map/ppermute | solution.py:43
  89.7 5.0 %collective-permute-start.6 = (f32[3,4,1,2880]{3,2,1,0:T(1,128)S(1)}, f32[3,4,1,2880]{3,2,1,0:T(1,128)S(1)}, u32[]{:S(2)}, u32[]{:S(2)}) collective-permute-start(f32[3,4,1,2880]{3,2,1,0:T(1,128)S(1)} %get-tuple-element.100), channel_id=1, source_target_pairs={{0,8},{1,9},{2,10},{3,11},{4,12},{5,13},{6,14},{7,15},{8,16},{9,17... | collective-permute-start | bytes 414728 | tf_op jit(solution)/shard_map/ppermute | solution.py:43
  93.5 2.1 %copy-start.9 = (f32[17]{0:T(128)S(1)}, f32[17]{0:T(128)}, u32[]{:S(2)}) copy-start(f32[17]{0:T(128)} %sine_multiply_fusion) | copy-start | bytes 208

commit v11 on v7

--- a/solution.py
+++ b/solution.py
@@ -105,8 +105,10 @@
     plain_lat = [i for i in range(lat_count) if i not in filter_lat]
     top = jnp.concatenate([stacked[:, levels - 1], vertical_wind[levels - 1 :]], axis=0)
     bottom = jnp.concatenate([stacked[:, 0], vertical_wind[:1]], axis=0)
-    below_plain = group_shift(top, plain_lat, True)
-    above_plain = group_shift(bottom, plain_lat, False)
+    late_lat = [i for i in range(lat_count) if i in filter_lat or i - 1 in filter_lat or i + 1 in filter_lat]
+    early_lat = [i for i in range(lat_count) if i not in late_lat]
+    below_plain = group_shift(top, early_lat, True)
+    above_plain = group_shift(bottom, early_lat, False)
 
     tables = (parity_table(0), parity_table(1))
     south_plain = lat_group_shift(stacked[:, :, lat_rows - 1 :], plain_lat, True)
@@ -116,11 +118,11 @@
     field = filtered(stacked, own_cut, tables)
     top = jnp.concatenate([field[:, levels - 1], vertical_wind[levels - 1 :]], axis=0)
     bottom = jnp.concatenate([field[:, 0], vertical_wind[:1]], axis=0)
-    below_filtered = group_shift(top, filter_lat, True)
-    above_filtered = group_shift(bottom, filter_lat, False)
-    is_filter = jnp.any(lat_index == jnp.asarray(filter_lat, jnp.int32))
-    below_all = jnp.where(is_filter, below_filtered, below_plain)
-    above_all = jnp.where(is_filter, above_filtered, above_plain)
+    below_filtered = group_shift(top, late_lat, True)
+    above_filtered = group_shift(bottom, late_lat, False)
+    is_late = jnp.any(lat_index == jnp.asarray(late_lat, jnp.int32))
+    below_all = jnp.where(is_late, below_filtered, below_plain)
+    above_all = jnp.where(is_late, above_filtered, above_plain)
     below, below_wind = below_all[:3, None], below_all[3:]
     above, above_wind = above_all[:3, None], above_all[3:]
     south_filtered = lat_group_shift(field[:, :, lat_rows - 1 :], filter_lat, True)

time: 99.2 us -> 117 us (1.18)
  waiting for transfers between devices: 37.7 us -> 53.8 us
    ppermute x4, waiting for transfers between devices: 37.7 us -> 53.8 us  [lat_group_shift(): return lax.ppermute(x, ('lat', 'lev'), pairs)]
  transfers between devices with their start and end apart: 8 -> 8, of which waited for: 2 -> 2; matrix products, arithmetic and copies ran while one was open for 9% -> 8% of each run, Pallas kernels for 0% -> 0%
where the time goes in v11:
time: 117 us
  waiting for transfers between devices  53.8 us (46%)
  starting transfers between devices  30.2 us (26%)
  other arithmetic  17.1 us (15%)
  matrix products  8.57 us (7%)
  local copies, waits for them, and re-layouts  5.05 us (4%)
  between operations  1.55 us (1%)
    ppermute x4, waiting for transfers between devices, lat_group_shift(): return lax.ppermute(x, ('lat', 'lev'), pairs)  53.8 us
    ppermute x4, starting transfers between devices, lat_group_shift(): return lax.ppermute(x, ('lat', 'lev'), pairs)  17.3 us
    ppermute x4, starting transfers between devices, group_shift(): return lax.ppermute(x, ('lat', 'lev'), pairs)  12.9 us
  transfers between devices with their start and end apart: 8, of which 2 were waited for; matrix products, arithmetic and copies ran while one was open for 8% of the time, Pallas kernels for 0%

profile of v11, /device:TPU:80, one launch (start us, length us, event | category | flops | bytes accessed | tf_op | source)
XLA Modules:
  0.0 116.5 jit_solution(1888341736822999400)
XLA Ops:
  0.6 1.7 %pad_maximum_fusion = f32[3,4,16,2880]{3,2,1,0:T(8,128)S(1)} fusion(f32[1,4,16,2880]{3,2,1,0:T(8,128)} %bitcast.64, f32[1,4,16,2880]{3,2,1,0:T(8,128)} %bitcast.65, f32[1,4,16,2880]{3,2,1,0:T(8,128)} %bitcast.66), kind=kLoop, calls=%fused_computation.22 | loop fusion | flops 1105920 | bytes 4423680 | tf_op jit(solution)/shard_map/stack | solution.py:101
  2.4 0.1 slice_bitcast_fusion.7
  2.5 1.0 copy-done
  3.5 0.9 pad_maximum_fusion.4
  4.5 1.6 %collective-permute-start = (f32[4,16,2880]{2,1,0:T(8,128)}, f32[4,16,2880]{2,1,0:T(8,128)}, u32[]{:S(2)}, u32[]{:S(2)}) collective-permute-start(f32[4,16,2880]{2,1,0:T(8,128)} %pad_maximum_fusion.4), channel_id=1, source_target_pairs={{48,49},{49,50},{50,51},{51,52},{52,53},{53,54},{54,55},{56,57},{5... | collective-permute-start | bytes 2211848 | tf_op jit(solution)/shard_map/ppermute | solution.py:35
  6.0 0.9 pad_maximum_fusion.6
  7.0 1.6 %collective-permute-start.1 = (f32[4,16,2880]{2,1,0:T(8,128)}, f32[4,16,2880]{2,1,0:T(8,128)}, u32[]{:S(2)}, u32[]{:S(2)}) collective-permute-start(f32[4,16,2880]{2,1,0:T(8,128)} %pad_maximum_fusion.6), channel_id=1, source_target_pairs={{49,48},{50,49},{51,50},{52,51},{53,52},{54,53},{55,54},{57,56},{5... | collective-permute-start | bytes 2211848 | tf_op jit(solution)/shard_map/ppermute | solution.py:35
  8.5 0.9 fusion.20
  9.4 0.7 collective-permute-start.2
  10.1 1.3 %collective-permute-start.3 = (f32[3,4,1,2880]{3,2,1,0:T(1,128)}, f32[3,4,1,2880]{3,2,1,0:T(1,128)}, u32[]{:S(2)}, u32[]{:S(2)}) collective-permute-start(f32[3,4,1,2880]{3,2,1,0:T(1,128)} %get-tuple-element.140), channel_id=1, source_target_pairs={{40,32},{41,33},{42,34},{43,35},{44,36},{45,37},{46,38},{47,39},{4... | collective-permute-start | bytes 414728 | tf_op jit(solution)/shard_map/ppermute | solution.py:43
  11.4 0.6 sine_multiply_fusion
  12.0 0.7 compare_reduce_fusion
  12.7 1.4 %compare_reduce_fusion.3 = (pred[]{:T(512)}, s32[16]{0:T(128)S(1)}) fusion(s32[512]{0:T(512)} %param.24, s32[]{:T(128)S(6)} %select_n.52), kind=kLoop, calls=%fused_computation.56 | loop fusion | flops 31 | bytes 133 | tf_op jit(solution)/shard_map/reduce_or | solution.py:89
  14.8 0.7 compare_reduce_fusion.1
  15.5 8.5 %collective-permute-done.3 = f32[3,4,1,2880]{3,2,1,0:T(1,128)} collective-permute-done((f32[3,4,1,2880]{3,2,1,0:T(1,128)}, f32[3,4,1,2880]{3,2,1,0:T(1,128)}, u32[]{:S(2)}, u32[]{:S(2)}) %collective-permute-start.3) | collective-permute-done | bytes 138272 | tf_op jit(solution)/shard_map/ppermute | solution.py:43
  24.0 12.1 %conditional.1 = (f32[192,2880]{1,0:T(8,128)S(1)}) conditional(s32[]{:T(128)} %convert_element_type.17, f32[192,2880]{1,0:T(8,128)S(1)} %bitcast.45, (s32[16]{0:T(128)S(1)}, f32[192,2880]{1,0:T(8,128)S(1)}) %tuple.91), branch_computations={%region_1.0_spmd, %region_2.3_spmd.clone} | conditional | flops 4786836480 | bytes 46174092 | solution.py:89
  24.0 0.1 reshape.114
  24.1 1.7 %multiply_add_fusion = f32[30,48,720]{2,1,0:T(8,128)S(1)} fusion(f32[30,720]{1,0:T(8,128)} %constant.92.clone.2, f32[48,720]{1,0:T(8,128)} %constant.91.clone.2, f32[30,720]{1,0:T(8,128)} %constant.90.clone.2, f32[48,720]{1,0:T(8,128)} %constant.89.clone.2), kind=kLoop, calls=%fused_computation | loop fusion | flops 3110400 | bytes 4596480 | tf_op jit(solution)/shard_map/add | solution.py:57
  25.8 2.2 %convolution_multiply_fusion = f32[192,720]{1,0:T(8,128)S(1)} fusion(f32[1440,720]{1,0:T(8,128)S(1)} %bitcast.58, f32[192,2880]{1,0:T(8,128)S(1)} %get-tuple-element.123, s32[720]{0:T(1024)S(1)} %copy-done.7, s32[192]{0:T(256)S(1)} %reshape.114), kind=kOutput, calls=%fused_computation.3 | convolution fusion | flops 1195084800 | bytes 7341056 | tf_op jit(solution)/shard_map/cond/branch_1_fun/dot_general | solution.py:74
  28.1 2.3 %fusion.22 = f32[192,1440]{1,0:T(8,128)S(1)} fusion(f32[192,720]{1,0:T(8,128)S(1)} %convolution_multiply_fusion, f32[1440,720]{1,0:T(8,128)S(1)} %bitcast.59), kind=kOutput, calls=%fused_computation.63 | convolution fusion | flops 1194393600 | bytes 5806080 | tf_op jit(solution)/shard_map/cond/branch_1_fun/dot_general | solution.py:79
  30.4 0.6 multiply_add_fusion.1
  31.1 1.9 %convolution_multiply_fusion.1 = f32[192,720]{1,0:T(8,128)S(1)} fusion(f32[1440,720]{1,0:T(8,128)S(1)} %bitcast.56, f32[192,2880]{1,0:T(8,128)S(1)} %get-tuple-element.123, f32[720]{0:T(1024)S(1)} %copy-done.5, s32[720]{0:T(1024)S(1)} %copy-done.6, s32[192]{0:T(256)S(1)} %reshape.114), kind=kOutput, calls=%fused_computation.4 | convolution fusion | flops 1195084800 | bytes 7345152 | tf_op jit(solution)/shard_map/cond/branch_1_fun/dot_general | solution.py:72
  33.0 2.2 %fusion.18 = (f32[192,1440]{1,0:T(8,128)S(1)}, f32[192,1440]{1,0:T(8,128)S(1)}) fusion(f32[192,1440]{1,0:T(8,128)S(1)} %fusion.22, f32[192,720]{1,0:T(8,128)S(1)} %convolution_multiply_fusion.1, f32[1440,720]{1,0:T(8,128)S(1)} %bitcast.57), kind=kOutput, calls=%fused_computation.59 | convolution fusion | flops 1194946560 | bytes 8017920 | tf_op jit(solution)/shard_map/cond/branch_1_fun/dot_general | solution.py:77
  35.2 0.7 maximum_select_fusion
  36.2 0.3 slice.162
  36.5 0.6 slice.159
  37.1 0.2 fusion.19
  37.3 0.1 slice_bitcast_fusion.4
  37.4 0.1 fusion.17
  37.5 0.3 fusion.12
  37.9 0.1 slice.164
  38.0 1.3 %collective-permute-start.5 = (f32[3,4,1,2880]{3,2,1,0:T(1,128)S(1)}, f32[3,4,1,2880]{3,2,1,0:T(1,128)S(1)}, u32[]{:S(2)}, u32[]{:S(2)}) collective-permute-start(f32[3,4,1,2880]{3,2,1,0:T(1,128)S(1)} %get-tuple-element.136), channel_id=1, source_target_pairs={{8,0},{9,1},{10,2},{11,3},{12,4},{13,5},{14,6},{15,7},{16,8},{17,9... | collective-permute-start | bytes 414728 | tf_op jit(solution)/shard_map/ppermute | solution.py:43
  39.3 14.1 %collective-permute-start.4 = (f32[3,4,1,2880]{3,2,1,0:T(1,128)S(1)}, f32[3,4,1,2880]{3,2,1,0:T(1,128)S(1)}, u32[]{:S(2)}, u32[]{:S(2)}) collective-permute-start(f32[3,4,1,2880]{3,2,1,0:T(1,128)S(1)} %get-tuple-element.137), channel_id=1, source_target_pairs={{0,8},{1,9},{2,10},{3,11},{4,12},{5,13},{6,14},{7,15},{8,16},{9,17... | collective-permute-start | bytes 414728 | tf_op jit(solution)/shard_map/ppermute | solution.py:43
  53.3 0.1 pad_maximum_fusion.5
  53.4 4.2 %collective-permute-start.7 = (f32[4,16,2880]{2,1,0:T(8,128)S(1)}, f32[4,16,2880]{2,1,0:T(8,128)S(1)}, u32[]{:S(2)}, u32[]{:S(2)}) collective-permute-start(f32[4,16,2880]{2,1,0:T(8,128)S(1)} %pad_maximum_fusion.5), channel_id=1, source_target_pairs={{1,0},{2,1},{3,2},{4,3},{5,4},{6,5},{7,6},{9,8},{10,9},{11,10},{12... | collective-permute-start | bytes 2211848 | tf_op jit(solution)/shard_map/ppermute | solution.py:35
  57.7 5.5 %collective-permute-start.6 = (f32[4,16,2880]{2,1,0:T(8,128)S(1)}, f32[4,16,2880]{2,1,0:T(8,128)S(1)}, u32[]{:S(2)}, u32[]{:S(2)}) collective-permute-start(f32[4,16,2880]{2,1,0:T(8,128)S(1)} %pad_maximum_fusion.3), channel_id=1, source_target_pairs={{0,1},{1,2},{2,3},{3,4},{4,5},{5,6},{6,7},{8,9},{9,10},{10,11},{11... | collective-permute-start | bytes 2211848 | tf_op jit(solution)/shard_map/ppermute | solution.py:35
  63.2 1.7 %broadcast_select_fusion.2 = f32[3,4,1,2880]{3,2,1,0:T(1,128)S(1)} fusion(f32[3,4,1,2880]{3,2,1,0:T(1,128)S(1)} %collective-permute-done.5, f32[3,4,1,2880]{3,2,1,0:T(1,128)} %collective-permute-done.3, pred[]{:T(512)} %get-tuple-element.126), kind=kLoop, calls=%fused_computation.51 | loop fusion | flops 34560 | bytes 414721 | tf_op jit(solution)/shard_map/jit(_where)/select_n | solution.py:133
  64.9 45.2 %collective-permute-done.4 = f32[3,4,1,2880]{3,2,1,0:T(1,128)S(1)} collective-permute-done((f32[3,4,1,2880]{3,2,1,0:T(1,128)S(1)}, f32[3,4,1,2880]{3,2,1,0:T(1,128)S(1)}, u32[]{:S(2)}, u32[]{:S(2)}) %collective-permute-start.4) | collective-permute-done | bytes 138272 | tf_op jit(solution)/shard_map/ppermute | solution.py:43
  110.2 0.8 broadcast_select_fusion.3
  110.9 0.2 fusion.15
  111.1 0.2 fusion.14
  111.3 0.6 fusion.6
  111.9 0.7 broadcast_select_fusion
  112.7 0.7 broadcast_select_fusion.1
  113.5 0.1 fusion.16
  113.6 0.3 fusion.7
  113.9 1.2 %fusion.8 = f32[3,4,16,2880]{3,2,1,0:T(8,128)S(1)} fusion(f32[3,5,16,2880]{3,2,1,0:T(8,128)S(1)} %fusion.7, f32[3,4,16,2880]{3,2,1,0:T(8,128)S(1)} %bitcast.55, f32[3,4,17,2880]{3,2,1,0:T(8,128)S(1)} %fusion.6, f32[3,4,16,2880]{3,2,1,0:T(8,128)S(1)} %fusion.12, f32[3,4,16,2879]{3,2,1,0:T(8,128)S(1)} %bitcast.60, f32[3,4,16,1]{3,2,1,0:T(8,128)S(1)} %slice.164, ...), kind=kLoop, calls=%fused_computation.17 | loop fusion | flops 4423680 | bytes 17694784 | tf_op jit(solution)/shard_map/sub | solution.py:159
  115.1 1.4 %slice_bitcast_fusion = (f32[4,16,2880]{2,1,0:T(8,128)}, f32[4,16,2880]{2,1,0:T(8,128)}, f32[4,16,2880]{2,1,0:T(8,128)}) fusion(f32[3,4,16,2880]{3,2,1,0:T(8,128)S(1)} %fusion.8), kind=kLoop, calls=%fused_computation.38 | loop fusion | bytes 4423680 | tf_op jit(solution)/shard_map/squeeze | solution.py:160
  (39 shorter events, 0.4 us)
Async XLA Ops:
  2.4 1.1 copy-start
  3.5 8.5 %copy-start.10 = (s32[12]{0:T(128)S(1)}, s32[12]{0:T(128)}, u32[]{:S(2)}) copy-start(s32[12]{0:T(128)} %constant.95.clone) | copy-start | bytes 148
  3.5 11.3 %copy-start.8 = (s32[10]{0:T(128)S(1)}, s32[10]{0:T(128)}, u32[]{:S(2)}) copy-start(s32[10]{0:T(128)} %constant.96.clone) | copy-start | bytes 124
  4.5 19.5 %collective-permute-start = (f32[4,16,2880]{2,1,0:T(8,128)}, f32[4,16,2880]{2,1,0:T(8,128)}, u32[]{:S(2)}, u32[]{:S(2)}) collective-permute-start(f32[4,16,2880]{2,1,0:T(8,128)} %pad_maximum_fusion.4), channel_id=1, source_target_pairs={{48,49},{49,50},{50,51},{51,52},{52,53},{53,54},{54,55},{56,57},{5... | collective-permute-start | bytes 2211848 | tf_op jit(solution)/shard_map/ppermute | solution.py:35
  7.0 17.0 %collective-permute-start.1 = (f32[4,16,2880]{2,1,0:T(8,128)}, f32[4,16,2880]{2,1,0:T(8,128)}, u32[]{:S(2)}, u32[]{:S(2)}) collective-permute-start(f32[4,16,2880]{2,1,0:T(8,128)} %pad_maximum_fusion.6), channel_id=1, source_target_pairs={{49,48},{50,49},{51,50},{52,51},{53,52},{54,53},{55,54},{57,56},{5... | collective-permute-start | bytes 2211848 | tf_op jit(solution)/shard_map/ppermute | solution.py:35
  9.4 6.0 %collective-permute-start.2 = (f32[3,4,1,2880]{3,2,1,0:T(1,128)}, f32[3,4,1,2880]{3,2,1,0:T(1,128)S(1)}, u32[]{:S(2)}, u32[]{:S(2)}) collective-permute-start(f32[3,4,1,2880]{3,2,1,0:T(1,128)} %get-tuple-element.141), channel_id=1, source_target_pairs={{40,48},{41,49},{42,50},{43,51},{44,52},{45,53},{46,54},{47,55},{4... | collective-permute-start | bytes 414728 | tf_op jit(solution)/shard_map/ppermute | solution.py:43
  10.1 13.9 %collective-permute-start.3 = (f32[3,4,1,2880]{3,2,1,0:T(1,128)}, f32[3,4,1,2880]{3,2,1,0:T(1,128)}, u32[]{:S(2)}, u32[]{:S(2)}) collective-permute-start(f32[3,4,1,2880]{3,2,1,0:T(1,128)} %get-tuple-element.140), channel_id=1, source_target_pairs={{40,32},{41,33},{42,34},{43,35},{44,36},{45,37},{46,38},{47,39},{4... | collective-permute-start | bytes 414728 | tf_op jit(solution)/shard_map/ppermute | solution.py:43
  24.1 1.7 %copy-start.7 = (s32[720]{0:T(1024)S(1)}, s32[720]{0:T(1024)}, u32[]{:S(2)}) copy-start(s32[720]{0:T(1024)} %constant.94.clone.2) | copy-start | bytes 8644 | tf_op jit(solution)/shard_map/cond
  28.0 2.3 %copy-start.1 = (f32[48,720]{1,0:T(8,128)S(1)}, f32[48,720]{1,0:T(8,128)}, u32[]{:S(2)}) copy-start(f32[48,720]{1,0:T(8,128)} %constant.85.clone.2) | copy-start | bytes 414724 | tf_op jit(solution)/shard_map/cond
  28.0 2.3 %copy-start.2 = (f32[48,720]{1,0:T(8,128)S(1)}, f32[48,720]{1,0:T(8,128)}, u32[]{:S(2)}) copy-start(f32[48,720]{1,0:T(8,128)} %constant.87.clone.2) | copy-start | bytes 414724 | tf_op jit(solution)/shard_map/cond
  28.0 2.3 %copy-start.3 = (f32[30,720]{1,0:T(8,128)S(1)}, f32[30,720]{1,0:T(8,128)}, u32[]{:S(2)}) copy-start(f32[30,720]{1,0:T(8,128)} %constant.86.clone.2) | copy-start | bytes 259204 | tf_op jit(solution)/shard_map/cond
  28.0 2.3 %copy-start.4 = (f32[30,720]{1,0:T(8,128)S(1)}, f32[30,720]{1,0:T(8,128)}, u32[]{:S(2)}) copy-start(f32[30,720]{1,0:T(8,128)} %constant.88.clone.2) | copy-start | bytes 259204 | tf_op jit(solution)/shard_map/cond
  30.4 0.7 copy-start.5
  30.4 0.7 copy-start.6
  38.0 25.3 %collective-permute-start.5 = (f32[3,4,1,2880]{3,2,1,0:T(1,128)S(1)}, f32[3,4,1,2880]{3,2,1,0:T(1,128)S(1)}, u32[]{:S(2)}, u32[]{:S(2)}) collective-permute-start(f32[3,4,1,2880]{3,2,1,0:T(1,128)S(1)} %get-tuple-element.136), channel_id=1, source_target_pairs={{8,0},{9,1},{10,2},{11,3},{12,4},{13,5},{14,6},{15,7},{16,8},{17,9... | collective-permute-start | bytes 414728 | tf_op jit(solution)/shard_map/ppermute | solution.py:43
  39.3 70.9 %collective-permute-start.4 = (f32[3,4,1,2880]{3,2,1,0:T(1,128)S(1)}, f32[3,4,1,2880]{3,2,1,0:T(1,128)S(1)}, u32[]{:S(2)}, u32[]{:S(2)}) collective-permute-start(f32[3,4,1,2880]{3,2,1,0:T(1,128)S(1)} %get-tuple-element.137), channel_id=1, source_target_pairs={{0,8},{1,9},{2,10},{3,11},{4,12},{5,13},{6,14},{7,15},{8,16},{9,17... | collective-permute-start | bytes 414728 | tf_op jit(solution)/shard_map/ppermute | solution.py:43
  53.4 58.5 %collective-permute-start.7 = (f32[4,16,2880]{2,1,0:T(8,128)S(1)}, f32[4,16,2880]{2,1,0:T(8,128)S(1)}, u32[]{:S(2)}, u32[]{:S(2)}) collective-permute-start(f32[4,16,2880]{2,1,0:T(8,128)S(1)} %pad_maximum_fusion.5), channel_id=1, source_target_pairs={{1,0},{2,1},{3,2},{4,3},{5,4},{6,5},{7,6},{9,8},{10,9},{11,10},{12... | collective-permute-start | bytes 2211848 | tf_op jit(solution)/shard_map/ppermute | solution.py:35
  57.7 55.0 %collective-permute-start.6 = (f32[4,16,2880]{2,1,0:T(8,128)S(1)}, f32[4,16,2880]{2,1,0:T(8,128)S(1)}, u32[]{:S(2)}, u32[]{:S(2)}) collective-permute-start(f32[4,16,2880]{2,1,0:T(8,128)S(1)} %pad_maximum_fusion.3), channel_id=1, source_target_pairs={{0,1},{1,2},{2,3},{3,4},{4,5},{5,6},{6,7},{8,9},{9,10},{10,11},{11... | collective-permute-start | bytes 2211848 | tf_op jit(solution)/shard_map/ppermute | solution.py:35
  63.2 47.9 %copy-start.9 = (f32[17]{0:T(128)S(1)}, f32[17]{0:T(128)}, u32[]{:S(2)}) copy-start(f32[17]{0:T(128)} %sine_multiply_fusion) | copy-start | bytes 208

commit v12 on v7

--- a/solution.py
+++ b/solution.py
@@ -111,8 +111,7 @@
     tables = (parity_table(0), parity_table(1))
     south_plain = lat_group_shift(stacked[:, :, lat_rows - 1 :], plain_lat, True)
     north_plain = lat_group_shift(stacked[:, :, :1], plain_lat, False)
-    stacked, below_plain, above_plain, south_plain, north_plain = lax.optimization_barrier(
-        (stacked, below_plain, above_plain, south_plain, north_plain))
+    stacked, south_plain, north_plain = lax.optimization_barrier((stacked, south_plain, north_plain))
     field = filtered(stacked, own_cut, tables)
     top = jnp.concatenate([field[:, levels - 1], vertical_wind[levels - 1 :]], axis=0)
     bottom = jnp.concatenate([field[:, 0], vertical_wind[:1]], axis=0)

time: 99.2 us -> 103 us (1.038)
  the two profiles are of different devices: /device:TPU:80 before, /device:TPU:175 now
where the time goes in v12:
time: 103 us
  waiting for transfers between devices  53.1 us (52%)
  starting transfers between devices  19.7 us (19%)
  other arithmetic  13.5 us (13%)
  matrix products  8.52 us (8%)
  local copies, waits for them, and re-layouts  5.99 us (6%)
  between operations  1.6 us (2%)
    ppermute x4, waiting for transfers between devices, lat_group_shift(): return lax.ppermute(x, ('lat', 'lev'), pairs)  53 us
    ppermute x4, starting transfers between devices, group_shift(): return lax.ppermute(x, ('lat', 'lev'), pairs)  11.5 us
    ppermute x4, starting transfers between devices, lat_group_shift(): return lax.ppermute(x, ('lat', 'lev'), pairs)  8.17 us
    add x2, other arithmetic, parity_table(): as_f32(first)[None] * as_f32(np.cos(hi))[:, None]  2.34 us
    dot_general x1, matrix products, lowpass_rows(): lax.dot_general(spec_even * parity_weight(0, cut), even_table, dims, prec...  2.29 us
    dot_general x1, matrix products, lowpass_rows(): jnp.dot(first + second, even_table, precision=mxu_precision, preferred_el...  2.18 us
    dot_general x1, matrix products, lowpass_rows(): lax.dot_general(spec_odd * parity_weight(1, cut), odd_table, dims, precis...  2.14 us
  transfers between devices with their start and end apart: 8, of which 1 were waited for; matrix products, arithmetic and copies ran while one was open for 8% of the time, Pallas kernels for 0%

profile of v12, /device:TPU:175, one launch (start us, length us, event | category | flops | bytes accessed | tf_op | source)
XLA Modules:
  0.0 102.7 jit_solution(5526019103591281543)
XLA Ops:
  0.6 1.7 %pad_maximum_fusion = f32[3,4,16,2880]{3,2,1,0:T(8,128)S(1)} fusion(f32[1,4,16,2880]{3,2,1,0:T(8,128)} %bitcast.64, f32[1,4,16,2880]{3,2,1,0:T(8,128)} %bitcast.65, f32[1,4,16,2880]{3,2,1,0:T(8,128)} %bitcast.66), kind=kLoop, calls=%fused_computation.22 | loop fusion | flops 1105920 | bytes 4423680 | tf_op jit(solution)/shard_map/stack | solution.py:101
  2.4 0.9 fusion.20
  3.3 1.3 %collective-permute-start = (f32[3,4,1,2880]{3,2,1,0:T(1,128)}, f32[3,4,1,2880]{3,2,1,0:T(1,128)S(1)}, u32[]{:S(2)}, u32[]{:S(2)}) collective-permute-start(f32[3,4,1,2880]{3,2,1,0:T(1,128)} %get-tuple-element.140), channel_id=1, source_target_pairs={{40,48},{41,49},{42,50},{43,51},{44,52},{45,53},{46,54},{47,55},{4... | collective-permute-start | bytes 414728 | tf_op jit(solution)/shard_map/ppermute | solution.py:43
  4.6 1.3 %collective-permute-start.1 = (f32[3,4,1,2880]{3,2,1,0:T(1,128)}, f32[3,4,1,2880]{3,2,1,0:T(1,128)}, u32[]{:S(2)}, u32[]{:S(2)}) collective-permute-start(f32[3,4,1,2880]{3,2,1,0:T(1,128)} %get-tuple-element.139), channel_id=1, source_target_pairs={{40,32},{41,33},{42,34},{43,35},{44,36},{45,37},{46,38},{47,39},{4... | collective-permute-start | bytes 414728 | tf_op jit(solution)/shard_map/ppermute | solution.py:43
  5.9 0.1 slice_bitcast_fusion.4
  6.0 0.6 sine_multiply_fusion
  6.6 1.8 %fusion.21 = (f32[1,16,2880]{2,1,0:T(8,128)}, f32[1,16,2880]{2,1,0:T(8,128)}) fusion(f32[4,16,2880]{2,1,0:T(8,128)} %param.23), kind=kLoop, calls=%fused_computation.62 | loop fusion | bytes 737280 | tf_op jit(solution)/shard_map/slice | solution.py:117
  8.4 1.4 %compare_reduce_fusion.3 = (pred[]{:T(512)}, s32[16]{0:T(128)S(1)}) fusion(s32[512]{0:T(512)} %param.24, s32[]{:T(128)S(6)} %select_n.52), kind=kLoop, calls=%fused_computation.56 | loop fusion | flops 31 | bytes 133 | tf_op jit(solution)/shard_map/reduce_or | solution.py:89
  10.4 0.7 compare_reduce_fusion.1
  11.2 12.1 %conditional.1 = (f32[192,2880]{1,0:T(8,128)S(1)}) conditional(s32[]{:T(128)} %convert_element_type.17, f32[192,2880]{1,0:T(8,128)S(1)} %bitcast.45, (s32[16]{0:T(128)S(1)}, f32[192,2880]{1,0:T(8,128)S(1)}) %tuple.94), branch_computations={%region_1.0_spmd, %region_2.3_spmd.clone} | conditional | flops 4786836480 | bytes 46174092 | solution.py:89
  11.2 0.1 reshape.114
  11.3 1.7 %multiply_add_fusion = f32[30,48,720]{2,1,0:T(8,128)S(1)} fusion(f32[30,720]{1,0:T(8,128)} %constant.90.clone.2, f32[48,720]{1,0:T(8,128)} %constant.89.clone.2, f32[30,720]{1,0:T(8,128)} %constant.88.clone.2, f32[48,720]{1,0:T(8,128)} %constant.87.clone.2), kind=kLoop, calls=%fused_computation | loop fusion | flops 3110400 | bytes 4596480 | tf_op jit(solution)/shard_map/add | solution.py:57
  13.0 1.9 %convolution_multiply_fusion = f32[192,720]{1,0:T(8,128)S(1)} fusion(f32[1440,720]{1,0:T(8,128)S(1)} %bitcast.58, f32[192,2880]{1,0:T(8,128)S(1)} %get-tuple-element.119, s32[720]{0:T(1024)S(1)} %copy-done.9, s32[192]{0:T(256)S(1)} %reshape.114), kind=kOutput, calls=%fused_computation.3 | convolution fusion | flops 1195084800 | bytes 7341056 | tf_op jit(solution)/shard_map/cond/branch_1_fun/dot_general | solution.py:74
  15.0 2.1 %fusion.22 = f32[192,1440]{1,0:T(8,128)S(1)} fusion(f32[192,720]{1,0:T(8,128)S(1)} %convolution_multiply_fusion, f32[1440,720]{1,0:T(8,128)S(1)} %bitcast.59), kind=kOutput, calls=%fused_computation.63 | convolution fusion | flops 1194393600 | bytes 5806080 | tf_op jit(solution)/shard_map/cond/branch_1_fun/dot_general | solution.py:79
  17.2 0.6 multiply_add_fusion.1
  17.8 0.0 copy-done.7
  17.9 2.2 %convolution_multiply_fusion.1 = f32[192,720]{1,0:T(8,128)S(1)} fusion(f32[1440,720]{1,0:T(8,128)S(1)} %bitcast.56, f32[192,2880]{1,0:T(8,128)S(1)} %get-tuple-element.119, f32[720]{0:T(1024)S(1)} %copy-done.7, s32[720]{0:T(1024)S(1)} %copy-done.8, s32[192]{0:T(256)S(1)} %reshape.114), kind=kOutput, calls=%fused_computation.4 | convolution fusion | flops 1195084800 | bytes 7345152 | tf_op jit(solution)/shard_map/cond/branch_1_fun/dot_general | solution.py:72
  20.1 2.3 %fusion.18 = (f32[192,1440]{1,0:T(8,128)S(1)}, f32[192,1440]{1,0:T(8,128)S(1)}) fusion(f32[192,1440]{1,0:T(8,128)S(1)} %fusion.22, f32[192,720]{1,0:T(8,128)S(1)} %convolution_multiply_fusion.1, f32[1440,720]{1,0:T(8,128)S(1)} %bitcast.57), kind=kOutput, calls=%fused_computation.59 | convolution fusion | flops 1194946560 | bytes 8017920 | tf_op jit(solution)/shard_map/cond/branch_1_fun/dot_general | solution.py:77
  22.4 0.7 maximum_select_fusion
  23.3 0.1 slice.159
  23.3 0.3 slice.160
  23.6 0.6 slice.157
  24.3 0.2 fusion.19
  24.5 0.1 slice_bitcast_fusion.5
  24.6 0.1 fusion.17
  24.7 0.4 fusion.12
  25.0 0.1 slice.162
  25.1 1.9 %collective-permute-start.3 = (f32[3,4,1,2880]{3,2,1,0:T(1,128)S(1)}, f32[3,4,1,2880]{3,2,1,0:T(1,128)S(1)}, u32[]{:S(2)}, u32[]{:S(2)}) collective-permute-start(f32[3,4,1,2880]{3,2,1,0:T(1,128)S(1)} %get-tuple-element.133), channel_id=1, source_target_pairs={{8,0},{9,1},{10,2},{11,3},{12,4},{13,5},{14,6},{15,7},{16,8},{17,9... | collective-permute-start | bytes 414728 | tf_op jit(solution)/shard_map/ppermute | solution.py:43
  27.1 3.6 %collective-permute-start.2 = (f32[3,4,1,2880]{3,2,1,0:T(1,128)S(1)}, f32[3,4,1,2880]{3,2,1,0:T(1,128)S(1)}, u32[]{:S(2)}, u32[]{:S(2)}) collective-permute-start(f32[3,4,1,2880]{3,2,1,0:T(1,128)S(1)} %get-tuple-element.134), channel_id=1, source_target_pairs={{0,8},{1,9},{2,10},{3,11},{4,12},{5,13},{6,14},{7,15},{8,16},{9,17... | collective-permute-start | bytes 414728 | tf_op jit(solution)/shard_map/ppermute | solution.py:43
  30.7 0.1 pad_maximum_fusion.5
  30.9 1.9 %collective-permute-start.6 = (f32[4,16,2880]{2,1,0:T(8,128)S(1)}, f32[4,16,2880]{2,1,0:T(8,128)S(1)}, u32[]{:S(2)}, u32[]{:S(2)}) collective-permute-start(f32[4,16,2880]{2,1,0:T(8,128)S(1)} %get-tuple-element.144), channel_id=1, source_target_pairs={{1,0},{2,1},{3,2},{4,3},{5,4},{6,5},{7,6},{9,8},{10,9},{11,10},{12... | collective-permute-start | bytes 2211848 | tf_op jit(solution)/shard_map/ppermute | solution.py:35
  32.8 0.7 collective-permute-start.7
  33.5 0.1 pad_maximum_fusion.3
  33.6 8.2 %collective-permute-start.4 = (f32[4,16,2880]{2,1,0:T(8,128)S(1)}, f32[4,16,2880]{2,1,0:T(8,128)S(1)}, u32[]{:S(2)}, u32[]{:S(2)}) collective-permute-start(f32[4,16,2880]{2,1,0:T(8,128)S(1)} %get-tuple-element.146), channel_id=1, source_target_pairs={{0,1},{1,2},{2,3},{3,4},{4,5},{5,6},{6,7},{8,9},{9,10},{10,11},{11... | collective-permute-start | bytes 2211848 | tf_op jit(solution)/shard_map/ppermute | solution.py:35
  41.8 53.0 %collective-permute-done.3 = f32[3,4,1,2880]{3,2,1,0:T(1,128)S(1)} collective-permute-done((f32[3,4,1,2880]{3,2,1,0:T(1,128)S(1)}, f32[3,4,1,2880]{3,2,1,0:T(1,128)S(1)}, u32[]{:S(2)}, u32[]{:S(2)}) %collective-permute-start.3) | collective-permute-done | bytes 138272 | tf_op jit(solution)/shard_map/ppermute | solution.py:43
  94.8 0.7 collective-permute-start.5
  95.6 0.7 broadcast_select_fusion.2
  96.3 0.8 broadcast_select_fusion.3
  97.1 0.2 fusion.15
  97.3 0.2 fusion.14
  97.5 0.6 fusion.6
  98.1 0.7 broadcast_select_fusion
  98.9 0.8 broadcast_select_fusion.1
  99.8 0.2 copy-done
  100.0 0.1 fusion.16
  100.1 0.3 fusion.7
  100.4 0.9 fusion.8
  101.3 1.4 %slice_bitcast_fusion = (f32[4,16,2880]{2,1,0:T(8,128)}, f32[4,16,2880]{2,1,0:T(8,128)}, f32[4,16,2880]{2,1,0:T(8,128)}) fusion(f32[3,4,16,2880]{3,2,1,0:T(8,128)S(1)} %fusion.8), kind=kLoop, calls=%fused_computation.38 | loop fusion | bytes 4423680 | tf_op jit(solution)/shard_map/squeeze | solution.py:157
  (38 shorter events, 0.3 us)
Async XLA Ops:
  2.4 8.1 %copy-start.10 = (s32[10]{0:T(128)S(1)}, s32[10]{0:T(128)}, u32[]{:S(2)}) copy-start(s32[10]{0:T(128)} %constant.93.clone) | copy-start | bytes 124
  3.3 7.9 %collective-permute-start = (f32[3,4,1,2880]{3,2,1,0:T(1,128)}, f32[3,4,1,2880]{3,2,1,0:T(1,128)S(1)}, u32[]{:S(2)}, u32[]{:S(2)}) collective-permute-start(f32[3,4,1,2880]{3,2,1,0:T(1,128)} %get-tuple-element.140), channel_id=1, source_target_pairs={{40,48},{41,49},{42,50},{43,51},{44,52},{45,53},{46,54},{47,55},{4... | collective-permute-start | bytes 414728 | tf_op jit(solution)/shard_map/ppermute | solution.py:43
  4.6 6.6 %collective-permute-start.1 = (f32[3,4,1,2880]{3,2,1,0:T(1,128)}, f32[3,4,1,2880]{3,2,1,0:T(1,128)}, u32[]{:S(2)}, u32[]{:S(2)}) collective-permute-start(f32[3,4,1,2880]{3,2,1,0:T(1,128)} %get-tuple-element.139), channel_id=1, source_target_pairs={{40,32},{41,33},{42,34},{43,35},{44,36},{45,37},{46,38},{47,39},{4... | collective-permute-start | bytes 414728 | tf_op jit(solution)/shard_map/ppermute | solution.py:43
  11.3 1.7 %copy-start.9 = (s32[720]{0:T(1024)S(1)}, s32[720]{0:T(1024)}, u32[]{:S(2)}) copy-start(s32[720]{0:T(1024)} %constant.92.clone.2) | copy-start | bytes 8644 | tf_op jit(solution)/shard_map/cond
  14.9 2.2 %copy-start.3 = (f32[48,720]{1,0:T(8,128)S(1)}, f32[48,720]{1,0:T(8,128)}, u32[]{:S(2)}) copy-start(f32[48,720]{1,0:T(8,128)} %constant.83.clone.2) | copy-start | bytes 414724 | tf_op jit(solution)/shard_map/cond
  14.9 2.2 %copy-start.4 = (f32[48,720]{1,0:T(8,128)S(1)}, f32[48,720]{1,0:T(8,128)}, u32[]{:S(2)}) copy-start(f32[48,720]{1,0:T(8,128)} %constant.85.clone.2) | copy-start | bytes 414724 | tf_op jit(solution)/shard_map/cond
  14.9 2.2 %copy-start.5 = (f32[30,720]{1,0:T(8,128)S(1)}, f32[30,720]{1,0:T(8,128)}, u32[]{:S(2)}) copy-start(f32[30,720]{1,0:T(8,128)} %constant.84.clone.2) | copy-start | bytes 259204 | tf_op jit(solution)/shard_map/cond
  15.0 2.2 %copy-start.6 = (f32[30,720]{1,0:T(8,128)S(1)}, f32[30,720]{1,0:T(8,128)}, u32[]{:S(2)}) copy-start(f32[30,720]{1,0:T(8,128)} %constant.86.clone.2) | copy-start | bytes 259204 | tf_op jit(solution)/shard_map/cond
  17.2 0.7 copy-start.7
  17.2 0.7 copy-start.8
  24.7 6.1 %copy-start.2 = (f32[1,16,2880]{2,1,0:T(8,128)S(1)}, f32[1,16,2880]{2,1,0:T(8,128)}, u32[]{:S(2)}) copy-start(f32[1,16,2880]{2,1,0:T(8,128)} %get-tuple-element.141) | copy-start | bytes 552964
  25.0 8.5 %copy-start.1 = (f32[1,16,2880]{2,1,0:T(8,128)S(1)}, f32[1,16,2880]{2,1,0:T(8,128)}, u32[]{:S(2)}) copy-start(f32[1,16,2880]{2,1,0:T(8,128)} %get-tuple-element.142) | copy-start | bytes 552964
  25.1 69.7 %collective-permute-start.3 = (f32[3,4,1,2880]{3,2,1,0:T(1,128)S(1)}, f32[3,4,1,2880]{3,2,1,0:T(1,128)S(1)}, u32[]{:S(2)}, u32[]{:S(2)}) collective-permute-start(f32[3,4,1,2880]{3,2,1,0:T(1,128)S(1)} %get-tuple-element.133), channel_id=1, source_target_pairs={{8,0},{9,1},{10,2},{11,3},{12,4},{13,5},{14,6},{15,7},{16,8},{17,9... | collective-permute-start | bytes 414728 | tf_op jit(solution)/shard_map/ppermute | solution.py:43
  27.1 69.2 %collective-permute-start.2 = (f32[3,4,1,2880]{3,2,1,0:T(1,128)S(1)}, f32[3,4,1,2880]{3,2,1,0:T(1,128)S(1)}, u32[]{:S(2)}, u32[]{:S(2)}) collective-permute-start(f32[3,4,1,2880]{3,2,1,0:T(1,128)S(1)} %get-tuple-element.134), channel_id=1, source_target_pairs={{0,8},{1,9},{2,10},{3,11},{4,12},{5,13},{6,14},{7,15},{8,16},{9,17... | collective-permute-start | bytes 414728 | tf_op jit(solution)/shard_map/ppermute | solution.py:43
  30.9 67.2 %collective-permute-start.6 = (f32[4,16,2880]{2,1,0:T(8,128)S(1)}, f32[4,16,2880]{2,1,0:T(8,128)S(1)}, u32[]{:S(2)}, u32[]{:S(2)}) collective-permute-start(f32[4,16,2880]{2,1,0:T(8,128)S(1)} %get-tuple-element.144), channel_id=1, source_target_pairs={{1,0},{2,1},{3,2},{4,3},{5,4},{6,5},{7,6},{9,8},{10,9},{11,10},{12... | collective-permute-start | bytes 2211848 | tf_op jit(solution)/shard_map/ppermute | solution.py:35
  32.8 65.3 %collective-permute-start.7 = (f32[4,16,2880]{2,1,0:T(8,128)S(1)}, f32[4,16,2880]{2,1,0:T(8,128)S(1)}, u32[]{:S(2)}, u32[]{:S(2)}) collective-permute-start(f32[4,16,2880]{2,1,0:T(8,128)S(1)} %get-tuple-element.143), channel_id=1, source_target_pairs={{41,40},{42,41},{43,42},{44,43},{45,44},{46,45},{47,46},{49,48},{5... | collective-permute-start | bytes 2211848 | tf_op jit(solution)/shard_map/ppermute | solution.py:35
  33.6 65.3 %collective-permute-start.4 = (f32[4,16,2880]{2,1,0:T(8,128)S(1)}, f32[4,16,2880]{2,1,0:T(8,128)S(1)}, u32[]{:S(2)}, u32[]{:S(2)}) collective-permute-start(f32[4,16,2880]{2,1,0:T(8,128)S(1)} %get-tuple-element.146), channel_id=1, source_target_pairs={{0,1},{1,2},{2,3},{3,4},{4,5},{5,6},{6,7},{8,9},{9,10},{10,11},{11... | collective-permute-start | bytes 2211848 | tf_op jit(solution)/shard_map/ppermute | solution.py:35
  94.8 4.1 %collective-permute-start.5 = (f32[4,16,2880]{2,1,0:T(8,128)S(1)}, f32[4,16,2880]{2,1,0:T(8,128)S(1)}, u32[]{:S(2)}, u32[]{:S(2)}) collective-permute-start(f32[4,16,2880]{2,1,0:T(8,128)S(1)} %get-tuple-element.145), channel_id=1, source_target_pairs={{40,41},{41,42},{42,43},{43,44},{44,45},{45,46},{46,47},{48,49},{4... | collective-permute-start | bytes 2211848 | tf_op jit(solution)/shard_map/ppermute | solution.py:35
  95.5 1.7 %copy-start.11 = (f32[17]{0:T(128)S(1)}, f32[17]{0:T(128)}, u32[]{:S(2)}) copy-start(f32[17]{0:T(128)} %sine_multiply_fusion) | copy-start | bytes 208
  98.8 1.1 %copy-start = (f32[4,16,2880]{2,1,0:T(8,128)S(1)}, f32[4,16,2880]{2,1,0:T(8,128)}, u32[]{:S(2)}) copy-start(f32[4,16,2880]{2,1,0:T(8,128)} %param.23) | copy-start | bytes 2211844

commit v13 on v12

--- a/solution.py
+++ b/solution.py
@@ -105,13 +105,21 @@
     plain_lat = [i for i in range(lat_count) if i not in filter_lat]
     top = jnp.concatenate([stacked[:, levels - 1], vertical_wind[levels - 1 :]], axis=0)
     bottom = jnp.concatenate([stacked[:, 0], vertical_wind[:1]], axis=0)
-    below_plain = group_shift(top, plain_lat, True)
-    above_plain = group_shift(bottom, plain_lat, False)
+    edge_lat = [i for i in plain_lat if i - 1 in filter_lat or i + 1 in filter_lat]
+    inner_lat = [i for i in plain_lat if i not in edge_lat]
+    below_inner = group_shift(top, inner_lat, True)
+    above_inner = group_shift(bottom, inner_lat, False)
+    below_edge = group_shift(top, edge_lat, True)
+    above_edge = group_shift(bottom, edge_lat, False)
 
     tables = (parity_table(0), parity_table(1))
     south_plain = lat_group_shift(stacked[:, :, lat_rows - 1 :], plain_lat, True)
     north_plain = lat_group_shift(stacked[:, :, :1], plain_lat, False)
-    stacked, south_plain, north_plain = lax.optimization_barrier((stacked, south_plain, north_plain))
+    stacked, below_inner, above_inner, south_plain, north_plain = lax.optimization_barrier(
+        (stacked, below_inner, above_inner, south_plain, north_plain))
+    is_edge = jnp.any(lat_index == jnp.asarray(edge_lat, jnp.int32))
+    below_plain = jnp.where(is_edge, below_edge, below_inner)
+    above_plain = jnp.where(is_edge, above_edge, above_inner)
     field = filtered(stacked, own_cut, tables)
     top = jnp.concatenate([field[:, levels - 1], vertical_wind[levels - 1 :]], axis=0)
     bottom = jnp.concatenate([field[:, 0], vertical_wind[:1]], axis=0)

time: 103 us -> 110 us (1.068)
  the two profiles are of different devices: /device:TPU:175 before, /device:TPU:47 now
where the time goes in v13:
time: 110 us
  starting transfers between devices  38.9 us (35%)
  waiting for transfers between devices  35.4 us (32%)
  other arithmetic  19.7 us (18%)
  matrix products  8.56 us (8%)
  local copies, waits for them, and re-layouts  5.04 us (5%)
  between operations  1.62 us (1%)
    ppermute x4, starting transfers between devices, lat_group_shift(): return lax.ppermute(x, ('lat', 'lev'), pairs)  22.9 us
    ppermute x4, waiting for transfers between devices, lat_group_shift(): return lax.ppermute(x, ('lat', 'lev'), pairs)  18.2 us
    ppermute x6, waiting for transfers between devices, group_shift(): return lax.ppermute(x, ('lat', 'lev'), pairs)  17.1 us
    ppermute x6, starting transfers between devices, group_shift(): return lax.ppermute(x, ('lat', 'lev'), pairs)  16 us
    select_n x1, other arithmetic, on_device(): below_all = jnp.where(is_filter, below_filtered, below_plain)  2.56 us
    select_n x1, other arithmetic, on_device(): above_all = jnp.where(is_filter, above_filtered, above_plain)  2.56 us
    add x2, other arithmetic, parity_table(): as_f32(first)[None] * as_f32(np.cos(hi))[:, None]  2.33 us
    dot_general x1, matrix products, lowpass_rows(): lax.dot_general(spec_odd * parity_weight(1, cut), odd_table, dims, precis...  2.28 us
  transfers between devices with their start and end apart: 10, of which 4 were waited for; matrix products, arithmetic and copies ran while one was open for 22% of the time, Pallas kernels for 0%

profile of v13, /device:TPU:47, one launch (start us, length us, event | category | flops | bytes accessed | tf_op | source)
XLA Modules:
  0.0 109.5 jit_solution(3361598997685225699)
XLA Ops:
  0.6 1.7 %pad_maximum_fusion = f32[3,4,16,2880]{3,2,1,0:T(8,128)S(1)} fusion(f32[1,4,16,2880]{3,2,1,0:T(8,128)} %bitcast.64, f32[1,4,16,2880]{3,2,1,0:T(8,128)} %bitcast.65, f32[1,4,16,2880]{3,2,1,0:T(8,128)} %bitcast.66), kind=kLoop, calls=%fused_computation.22 | loop fusion | flops 1105920 | bytes 4423680 | tf_op jit(solution)/shard_map/stack | solution.py:101
  2.5 1.0 copy-done
  3.5 0.9 pad_maximum_fusion.6
  4.4 1.5 %collective-permute-start.1 = (f32[4,16,2880]{2,1,0:T(8,128)}, f32[4,16,2880]{2,1,0:T(8,128)}, u32[]{:S(2)}, u32[]{:S(2)}) collective-permute-start(f32[4,16,2880]{2,1,0:T(8,128)} %pad_maximum_fusion.6), channel_id=1, source_target_pairs={{49,48},{50,49},{51,50},{52,51},{53,52},{54,53},{55,54},{57,56},{5... | collective-permute-start | bytes 2211848 | tf_op jit(solution)/shard_map/ppermute | solution.py:35
  6.0 1.6 %collective-permute-start.9 = (f32[4,16,2880]{2,1,0:T(8,128)}, f32[4,16,2880]{2,1,0:T(8,128)}, u32[]{:S(2)}, u32[]{:S(2)}) collective-permute-start(f32[4,16,2880]{2,1,0:T(8,128)} %pad_maximum_fusion.6), channel_id=1, source_target_pairs={{41,40},{42,41},{43,42},{44,43},{45,44},{46,45},{47,46},{209,208},... | collective-permute-start | bytes 2211848 | tf_op jit(solution)/shard_map/ppermute | solution.py:35
  7.5 0.9 pad_maximum_fusion.4
  8.4 1.6 %collective-permute-start = (f32[4,16,2880]{2,1,0:T(8,128)}, f32[4,16,2880]{2,1,0:T(8,128)}, u32[]{:S(2)}, u32[]{:S(2)}) collective-permute-start(f32[4,16,2880]{2,1,0:T(8,128)} %pad_maximum_fusion.4), channel_id=1, source_target_pairs={{48,49},{49,50},{50,51},{51,52},{52,53},{53,54},{54,55},{56,57},{5... | collective-permute-start | bytes 2211848 | tf_op jit(solution)/shard_map/ppermute | solution.py:35
  10.0 0.9 fusion.20
  10.9 1.3 %collective-permute-start.2 = (f32[3,4,1,2880]{3,2,1,0:T(1,128)}, f32[3,4,1,2880]{3,2,1,0:T(1,128)S(1)}, u32[]{:S(2)}, u32[]{:S(2)}) collective-permute-start(f32[3,4,1,2880]{3,2,1,0:T(1,128)} %get-tuple-element.142), channel_id=1, source_target_pairs={{40,48},{41,49},{42,50},{43,51},{44,52},{45,53},{46,54},{47,55},{4... | collective-permute-start | bytes 414728 | tf_op jit(solution)/shard_map/ppermute | solution.py:43
  12.2 1.3 %collective-permute-start.3 = (f32[3,4,1,2880]{3,2,1,0:T(1,128)}, f32[3,4,1,2880]{3,2,1,0:T(1,128)}, u32[]{:S(2)}, u32[]{:S(2)}) collective-permute-start(f32[3,4,1,2880]{3,2,1,0:T(1,128)} %get-tuple-element.141), channel_id=1, source_target_pairs={{40,32},{41,33},{42,34},{43,35},{44,36},{45,37},{46,38},{47,39},{4... | collective-permute-start | bytes 414728 | tf_op jit(solution)/shard_map/ppermute | solution.py:43
  13.5 0.6 sine_multiply_fusion
  14.1 0.7 compare_reduce_fusion
  14.8 1.5 %compare_reduce_fusion.4 = (pred[]{:T(512)}, s32[16]{0:T(128)S(1)}) fusion(s32[512]{0:T(512)} %param.25, s32[]{:T(128)S(6)} %select_n.62), kind=kLoop, calls=%fused_computation.57 | loop fusion | flops 31 | bytes 133 | tf_op jit(solution)/shard_map/reduce_or | solution.py:89
  17.0 0.7 compare_reduce_fusion.2
  17.7 3.3 %collective-permute-done.2 = f32[3,4,1,2880]{3,2,1,0:T(1,128)S(1)} collective-permute-done((f32[3,4,1,2880]{3,2,1,0:T(1,128)}, f32[3,4,1,2880]{3,2,1,0:T(1,128)S(1)}, u32[]{:S(2)}, u32[]{:S(2)}) %collective-permute-start.2) | collective-permute-done | bytes 138272 | tf_op jit(solution)/shard_map/ppermute | solution.py:43
  21.0 1.5 %collective-permute-start.7 = (f32[4,16,2880]{2,1,0:T(8,128)}, f32[4,16,2880]{2,1,0:T(8,128)}, u32[]{:S(2)}, u32[]{:S(2)}) collective-permute-start(f32[4,16,2880]{2,1,0:T(8,128)} %pad_maximum_fusion.4), channel_id=1, source_target_pairs={{40,41},{41,42},{42,43},{43,44},{44,45},{45,46},{46,47},{208,209},... | collective-permute-start | bytes 2211848 | tf_op jit(solution)/shard_map/ppermute | solution.py:35
  22.6 12.1 %conditional.1 = (f32[192,2880]{1,0:T(8,128)S(1)}) conditional(s32[]{:T(128)} %convert_element_type.17, f32[192,2880]{1,0:T(8,128)S(1)} %bitcast.45, (s32[16]{0:T(128)S(1)}, f32[192,2880]{1,0:T(8,128)S(1)}) %tuple.92), branch_computations={%region_1.2_spmd, %region_2.3_spmd.clone} | conditional | flops 4786836480 | bytes 46174092 | solution.py:89
  22.6 0.1 reshape.114
  22.7 1.7 %multiply_add_fusion = f32[30,48,720]{2,1,0:T(8,128)S(1)} fusion(f32[30,720]{1,0:T(8,128)} %constant.92.clone.2, f32[48,720]{1,0:T(8,128)} %constant.91.clone.2, f32[30,720]{1,0:T(8,128)} %constant.90.clone.2, f32[48,720]{1,0:T(8,128)} %constant.89.clone.2), kind=kLoop, calls=%fused_computation | loop fusion | flops 3110400 | bytes 4596480 | tf_op jit(solution)/shard_map/add | solution.py:57
  24.4 2.2 %convolution_multiply_fusion = f32[192,720]{1,0:T(8,128)S(1)} fusion(f32[1440,720]{1,0:T(8,128)S(1)} %bitcast.58, f32[192,2880]{1,0:T(8,128)S(1)} %get-tuple-element.123, s32[720]{0:T(1024)S(1)} %copy-done.7, s32[192]{0:T(256)S(1)} %reshape.114), kind=kOutput, calls=%fused_computation.3 | convolution fusion | flops 1195084800 | bytes 7341056 | tf_op jit(solution)/shard_map/cond/branch_1_fun/dot_general | solution.py:74
  26.6 2.3 %fusion.22 = f32[192,1440]{1,0:T(8,128)S(1)} fusion(f32[192,720]{1,0:T(8,128)S(1)} %convolution_multiply_fusion, f32[1440,720]{1,0:T(8,128)S(1)} %bitcast.59), kind=kOutput, calls=%fused_computation.64 | convolution fusion | flops 1194393600 | bytes 5806080 | tf_op jit(solution)/shard_map/cond/branch_1_fun/dot_general | solution.py:79
  29.0 0.6 multiply_add_fusion.1
  29.7 1.9 %convolution_multiply_fusion.1 = f32[192,720]{1,0:T(8,128)S(1)} fusion(f32[1440,720]{1,0:T(8,128)S(1)} %bitcast.56, f32[192,2880]{1,0:T(8,128)S(1)} %get-tuple-element.123, f32[720]{0:T(1024)S(1)} %copy-done.5, s32[720]{0:T(1024)S(1)} %copy-done.6, s32[192]{0:T(256)S(1)} %reshape.114), kind=kOutput, calls=%fused_computation.4 | convolution fusion | flops 1195084800 | bytes 7345152 | tf_op jit(solution)/shard_map/cond/branch_1_fun/dot_general | solution.py:72
  31.6 2.2 %fusion.18 = (f32[192,1440]{1,0:T(8,128)S(1)}, f32[192,1440]{1,0:T(8,128)S(1)}) fusion(f32[192,1440]{1,0:T(8,128)S(1)} %fusion.22, f32[192,720]{1,0:T(8,128)S(1)} %convolution_multiply_fusion.1, f32[1440,720]{1,0:T(8,128)S(1)} %bitcast.57), kind=kOutput, calls=%fused_computation.60 | convolution fusion | flops 1194946560 | bytes 8017920 | tf_op jit(solution)/shard_map/cond/branch_1_fun/dot_general | solution.py:77
  33.8 0.7 maximum_select_fusion
  34.8 0.3 slice.162
  35.0 0.6 slice.159
  35.7 0.2 fusion.19
  36.0 0.1 fusion.17
  36.1 0.3 fusion.12
  36.5 19.0 %collective-permute-start.5 = (f32[3,4,1,2880]{3,2,1,0:T(1,128)S(1)}, f32[3,4,1,2880]{3,2,1,0:T(1,128)S(1)}, u32[]{:S(2)}, u32[]{:S(2)}) collective-permute-start(f32[3,4,1,2880]{3,2,1,0:T(1,128)S(1)} %get-tuple-element.137), channel_id=1, source_target_pairs={{8,0},{9,1},{10,2},{11,3},{12,4},{13,5},{14,6},{15,7},{16,8},{17,9... | collective-permute-start | bytes 414728 | tf_op jit(solution)/shard_map/ppermute | solution.py:43
  55.5 1.3 %collective-permute-start.4 = (f32[3,4,1,2880]{3,2,1,0:T(1,128)S(1)}, f32[3,4,1,2880]{3,2,1,0:T(1,128)S(1)}, u32[]{:S(2)}, u32[]{:S(2)}) collective-permute-start(f32[3,4,1,2880]{3,2,1,0:T(1,128)S(1)} %get-tuple-element.138), channel_id=1, source_target_pairs={{0,8},{1,9},{2,10},{3,11},{4,12},{5,13},{6,14},{7,15},{8,16},{9,17... | collective-permute-start | bytes 414728 | tf_op jit(solution)/shard_map/ppermute | solution.py:43
  56.9 7.8 %collective-permute-start.8 = (f32[4,16,2880]{2,1,0:T(8,128)S(1)}, f32[4,16,2880]{2,1,0:T(8,128)S(1)}, u32[]{:S(2)}, u32[]{:S(2)}) collective-permute-start(f32[4,16,2880]{2,1,0:T(8,128)S(1)} %pad_maximum_fusion.5), channel_id=1, source_target_pairs={{1,0},{2,1},{3,2},{4,3},{5,4},{6,5},{7,6},{9,8},{10,9},{11,10},{12... | collective-permute-start | bytes 2211848 | tf_op jit(solution)/shard_map/ppermute | solution.py:35
  64.8 2.0 %collective-permute-start.6 = (f32[4,16,2880]{2,1,0:T(8,128)S(1)}, f32[4,16,2880]{2,1,0:T(8,128)S(1)}, u32[]{:S(2)}, u32[]{:S(2)}) collective-permute-start(f32[4,16,2880]{2,1,0:T(8,128)S(1)} %pad_maximum_fusion.3), channel_id=1, source_target_pairs={{0,1},{1,2},{2,3},{3,4},{4,5},{5,6},{6,7},{8,9},{9,10},{10,11},{11... | collective-permute-start | bytes 2211848 | tf_op jit(solution)/shard_map/ppermute | solution.py:35
  66.8 0.8 broadcast_select_fusion
  67.6 14.9 %collective-permute-done.4 = f32[3,4,1,2880]{3,2,1,0:T(1,128)S(1)} collective-permute-done((f32[3,4,1,2880]{3,2,1,0:T(1,128)S(1)}, f32[3,4,1,2880]{3,2,1,0:T(1,128)S(1)}, u32[]{:S(2)}, u32[]{:S(2)}) %collective-permute-start.4) | collective-permute-done | bytes 138272 | tf_op jit(solution)/shard_map/ppermute | solution.py:43
  82.5 0.7 broadcast_select_fusion.1
  83.2 0.2 fusion.15
  83.4 0.2 fusion.14
  83.6 0.6 fusion.6
  84.2 11.8 %collective-permute-done.8 = f32[4,16,2880]{2,1,0:T(8,128)S(1)} collective-permute-done((f32[4,16,2880]{2,1,0:T(8,128)S(1)}, f32[4,16,2880]{2,1,0:T(8,128)S(1)}, u32[]{:S(2)}, u32[]{:S(2)}) %collective-permute-start.8) | collective-permute-done | bytes 737312 | tf_op jit(solution)/shard_map/ppermute | solution.py:35
  96.0 2.6 %select_select_fusion = f32[4,16,2880]{2,1,0:T(8,128)S(1)} fusion(f32[4,16,2880]{2,1,0:T(8,128)S(1)} %collective-permute-done.8, f32[4,16,2880]{2,1,0:T(8,128)} %collective-permute-done.9, f32[4,16,2880]{2,1,0:T(8,128)} %collective-permute-done.1, pred[]{:T(512)} %compare_reduce_fusion, pred[]{:T(512)} %get-tuple-element.128), kind=kLoop, calls=%fused_computation.43 | loop fusion | flops 368640 | bytes 2949122 | tf_op jit(solution)/shard_map/jit(_where)/select_n | solution.py:130
  98.7 5.3 %collective-permute-done.6 = f32[4,16,2880]{2,1,0:T(8,128)S(1)} collective-permute-done((f32[4,16,2880]{2,1,0:T(8,128)S(1)}, f32[4,16,2880]{2,1,0:T(8,128)S(1)}, u32[]{:S(2)}, u32[]{:S(2)}) %collective-permute-start.6) | collective-permute-done | bytes 737312 | tf_op jit(solution)/shard_map/ppermute | solution.py:35
  104.0 2.6 %select_select_fusion.1 = f32[4,16,2880]{2,1,0:T(8,128)S(1)} fusion(f32[4,16,2880]{2,1,0:T(8,128)S(1)} %collective-permute-done.6, f32[4,16,2880]{2,1,0:T(8,128)} %collective-permute-done.7, f32[4,16,2880]{2,1,0:T(8,128)} %collective-permute-done, pred[]{:T(512)} %compare_reduce_fusion, pred[]{:T(512)} %get-tuple-element.128), kind=kLoop, calls=%fused_computation.44 | loop fusion | flops 368640 | bytes 2949122 | tf_op jit(solution)/shard_map/jit(_where)/select_n | solution.py:129
  106.6 0.1 fusion.16
  106.7 0.3 fusion.7
  107.1 1.1 fusion.8
  108.1 1.4 %slice_bitcast_fusion = (f32[4,16,2880]{2,1,0:T(8,128)}, f32[4,16,2880]{2,1,0:T(8,128)}, f32[4,16,2880]{2,1,0:T(8,128)}) fusion(f32[3,4,16,2880]{3,2,1,0:T(8,128)S(1)} %fusion.8), kind=kLoop, calls=%fused_computation.38 | loop fusion | bytes 4423680 | tf_op jit(solution)/shard_map/squeeze | solution.py:165
  (43 shorter events, 0.7 us)
Async XLA Ops:
  2.4 1.1 %copy-start = (f32[4,16,2880]{2,1,0:T(8,128)S(1)}, f32[4,16,2880]{2,1,0:T(8,128)}, u32[]{:S(2)}) copy-start(f32[4,16,2880]{2,1,0:T(8,128)} %param.24) | copy-start | bytes 2211844
  3.5 10.6 %copy-start.10 = (s32[2]{0:T(128)S(1)}, s32[2]{0:T(128)}, u32[]{:S(2)}) copy-start(s32[2]{0:T(128)} %constant.93.clone) | copy-start | bytes 28
  3.5 13.5 %copy-start.8 = (s32[10]{0:T(128)S(1)}, s32[10]{0:T(128)}, u32[]{:S(2)}) copy-start(s32[10]{0:T(128)} %constant.96.clone) | copy-start | bytes 124
  4.4 18.1 %collective-permute-start.1 = (f32[4,16,2880]{2,1,0:T(8,128)}, f32[4,16,2880]{2,1,0:T(8,128)}, u32[]{:S(2)}, u32[]{:S(2)}) collective-permute-start(f32[4,16,2880]{2,1,0:T(8,128)} %pad_maximum_fusion.6), channel_id=1, source_target_pairs={{49,48},{50,49},{51,50},{52,51},{53,52},{54,53},{55,54},{57,56},{5... | collective-permute-start | bytes 2211848 | tf_op jit(solution)/shard_map/ppermute | solution.py:35
  6.0 78.3 %collective-permute-start.9 = (f32[4,16,2880]{2,1,0:T(8,128)}, f32[4,16,2880]{2,1,0:T(8,128)}, u32[]{:S(2)}, u32[]{:S(2)}) collective-permute-start(f32[4,16,2880]{2,1,0:T(8,128)} %pad_maximum_fusion.6), channel_id=1, source_target_pairs={{41,40},{42,41},{43,42},{44,43},{45,44},{46,45},{47,46},{209,208},... | collective-permute-start | bytes 2211848 | tf_op jit(solution)/shard_map/ppermute | solution.py:35
  8.4 14.1 %collective-permute-start = (f32[4,16,2880]{2,1,0:T(8,128)}, f32[4,16,2880]{2,1,0:T(8,128)}, u32[]{:S(2)}, u32[]{:S(2)}) collective-permute-start(f32[4,16,2880]{2,1,0:T(8,128)} %pad_maximum_fusion.4), channel_id=1, source_target_pairs={{48,49},{49,50},{50,51},{51,52},{52,53},{53,54},{54,55},{56,57},{5... | collective-permute-start | bytes 2211848 | tf_op jit(solution)/shard_map/ppermute | solution.py:35
  10.9 10.2 %collective-permute-start.2 = (f32[3,4,1,2880]{3,2,1,0:T(1,128)}, f32[3,4,1,2880]{3,2,1,0:T(1,128)S(1)}, u32[]{:S(2)}, u32[]{:S(2)}) collective-permute-start(f32[3,4,1,2880]{3,2,1,0:T(1,128)} %get-tuple-element.142), channel_id=1, source_target_pairs={{40,48},{41,49},{42,50},{43,51},{44,52},{45,53},{46,54},{47,55},{4... | collective-permute-start | bytes 414728 | tf_op jit(solution)/shard_map/ppermute | solution.py:43
  12.2 10.4 %collective-permute-start.3 = (f32[3,4,1,2880]{3,2,1,0:T(1,128)}, f32[3,4,1,2880]{3,2,1,0:T(1,128)}, u32[]{:S(2)}, u32[]{:S(2)}) collective-permute-start(f32[3,4,1,2880]{3,2,1,0:T(1,128)} %get-tuple-element.141), channel_id=1, source_target_pairs={{40,32},{41,33},{42,34},{43,35},{44,36},{45,37},{46,38},{47,39},{4... | collective-permute-start | bytes 414728 | tf_op jit(solution)/shard_map/ppermute | solution.py:43
  21.0 77.6 %collective-permute-start.7 = (f32[4,16,2880]{2,1,0:T(8,128)}, f32[4,16,2880]{2,1,0:T(8,128)}, u32[]{:S(2)}, u32[]{:S(2)}) collective-permute-start(f32[4,16,2880]{2,1,0:T(8,128)} %pad_maximum_fusion.4), channel_id=1, source_target_pairs={{40,41},{41,42},{42,43},{43,44},{44,45},{45,46},{46,47},{208,209},... | collective-permute-start | bytes 2211848 | tf_op jit(solution)/shard_map/ppermute | solution.py:35
  22.7 1.7 %copy-start.7 = (s32[720]{0:T(1024)S(1)}, s32[720]{0:T(1024)}, u32[]{:S(2)}) copy-start(s32[720]{0:T(1024)} %constant.95.clone.2) | copy-start | bytes 8644 | tf_op jit(solution)/shard_map/cond
  26.6 2.3 %copy-start.1 = (f32[48,720]{1,0:T(8,128)S(1)}, f32[48,720]{1,0:T(8,128)}, u32[]{:S(2)}) copy-start(f32[48,720]{1,0:T(8,128)} %constant.85.clone.2) | copy-start | bytes 414724 | tf_op jit(solution)/shard_map/cond
  26.6 2.3 %copy-start.2 = (f32[48,720]{1,0:T(8,128)S(1)}, f32[48,720]{1,0:T(8,128)}, u32[]{:S(2)}) copy-start(f32[48,720]{1,0:T(8,128)} %constant.87.clone.2) | copy-start | bytes 414724 | tf_op jit(solution)/shard_map/cond
  26.6 2.3 %copy-start.3 = (f32[30,720]{1,0:T(8,128)S(1)}, f32[30,720]{1,0:T(8,128)}, u32[]{:S(2)}) copy-start(f32[30,720]{1,0:T(8,128)} %constant.86.clone.2) | copy-start | bytes 259204 | tf_op jit(solution)/shard_map/cond
  26.6 2.3 %copy-start.4 = (f32[30,720]{1,0:T(8,128)S(1)}, f32[30,720]{1,0:T(8,128)}, u32[]{:S(2)}) copy-start(f32[30,720]{1,0:T(8,128)} %constant.88.clone.2) | copy-start | bytes 259204 | tf_op jit(solution)/shard_map/cond
  29.0 0.7 copy-start.5
  29.0 0.7 copy-start.6
  36.5 28.2 %collective-permute-start.5 = (f32[3,4,1,2880]{3,2,1,0:T(1,128)S(1)}, f32[3,4,1,2880]{3,2,1,0:T(1,128)S(1)}, u32[]{:S(2)}, u32[]{:S(2)}) collective-permute-start(f32[3,4,1,2880]{3,2,1,0:T(1,128)S(1)} %get-tuple-element.137), channel_id=1, source_target_pairs={{8,0},{9,1},{10,2},{11,3},{12,4},{13,5},{14,6},{15,7},{16,8},{17,9... | collective-permute-start | bytes 414728 | tf_op jit(solution)/shard_map/ppermute | solution.py:43
  55.5 27.0 %collective-permute-start.4 = (f32[3,4,1,2880]{3,2,1,0:T(1,128)S(1)}, f32[3,4,1,2880]{3,2,1,0:T(1,128)S(1)}, u32[]{:S(2)}, u32[]{:S(2)}) collective-permute-start(f32[3,4,1,2880]{3,2,1,0:T(1,128)S(1)} %get-tuple-element.138), channel_id=1, source_target_pairs={{0,8},{1,9},{2,10},{3,11},{4,12},{5,13},{6,14},{7,15},{8,16},{9,17... | collective-permute-start | bytes 414728 | tf_op jit(solution)/shard_map/ppermute | solution.py:43
  56.9 39.1 %collective-permute-start.8 = (f32[4,16,2880]{2,1,0:T(8,128)S(1)}, f32[4,16,2880]{2,1,0:T(8,128)S(1)}, u32[]{:S(2)}, u32[]{:S(2)}) collective-permute-start(f32[4,16,2880]{2,1,0:T(8,128)S(1)} %pad_maximum_fusion.5), channel_id=1, source_target_pairs={{1,0},{2,1},{3,2},{4,3},{5,4},{6,5},{7,6},{9,8},{10,9},{11,10},{12... | collective-permute-start | bytes 2211848 | tf_op jit(solution)/shard_map/ppermute | solution.py:35
  64.8 39.2 %collective-permute-start.6 = (f32[4,16,2880]{2,1,0:T(8,128)S(1)}, f32[4,16,2880]{2,1,0:T(8,128)S(1)}, u32[]{:S(2)}, u32[]{:S(2)}) collective-permute-start(f32[4,16,2880]{2,1,0:T(8,128)S(1)} %pad_maximum_fusion.3), channel_id=1, source_target_pairs={{0,1},{1,2},{2,3},{3,4},{4,5},{5,6},{6,7},{8,9},{9,10},{10,11},{11... | collective-permute-start | bytes 2211848 | tf_op jit(solution)/shard_map/ppermute | solution.py:35
  66.8 16.6 %copy-start.9 = (f32[17]{0:T(128)S(1)}, f32[17]{0:T(128)}, u32[]{:S(2)}) copy-start(f32[17]{0:T(128)} %sine_multiply_fusion) | copy-start | bytes 208

commit v14 on v10

--- a/solution.py
+++ b/solution.py
@@ -40,6 +40,14 @@
     step = 1 if up else -1
     pairs = [(lat * lev_size + lev, (lat + step) * lev_size + lev)
              for lat in sources if 0 <= lat + step < lat_size for lev in range(lev_size)]
+    return lax.ppermute(x, ("lat", "lev"), pairs)
+
+
+def lat_pair_shift(x, sources, targets, up):
+    lev_size = lax.axis_size("lev")
+    step = 1 if up else -1
+    pairs = [(lat * lev_size + lev, (lat + step) * lev_size + lev)
+             for lat in sources if lat + step in targets for lev in range(lev_size)]
     return lax.ppermute(x, ("lat", "lev"), pairs)
 
 
@@ -123,10 +131,14 @@
     above_all = jnp.where(is_filter, above_filtered, above_plain)
     below, below_wind = below_all[:3, None], below_all[3:]
     above, above_wind = above_all[:3, None], above_all[3:]
+    south_inner = lat_pair_shift(field[:, :, lat_rows - 1 :], filter_lat, filter_lat, True)
+    north_inner = lat_pair_shift(field[:, :, :1], filter_lat, filter_lat, False)
     south_source, north_source, _ = lax.optimization_barrier(
         (field[:, :, lat_rows - 1 :], field[:, :, :1], (below_filtered, above_filtered)))
-    south_filtered = lat_group_shift(south_source, filter_lat, True)
-    north_filtered = lat_group_shift(north_source, filter_lat, False)
+    south_edge = lat_pair_shift(south_source, filter_lat, plain_lat, True)
+    north_edge = lat_pair_shift(north_source, filter_lat, plain_lat, False)
+    south_filtered = jnp.where(is_filter, south_inner, south_edge)
+    north_filtered = jnp.where(is_filter, north_inner, north_edge)
     south_is_filter = jnp.any(lat_index - 1 == jnp.asarray(filter_lat, jnp.int32))
     north_is_filter = jnp.any(lat_index + 1 == jnp.asarray(filter_lat, jnp.int32))
     south = jnp.where(south_is_filter, south_filtered, south_plain)

time: 100 us -> 101 us (1.010)
  the two profiles are of different devices: /device:TPU:47 before, /device:TPU:14 now
where the time goes in v14:
time: 101 us; the launch traced here: 100 us
  waiting for transfers between devices  54.7 us (54%)
  starting transfers between devices  23.5 us (23%)
  other arithmetic  16.8 us (17%)
  local copies, waits for them, and re-layouts  3.85 us (4%)
  between operations  1.53 us (2%)
    ppermute x2, waiting for transfers between devices, lat_group_shift(): return lax.ppermute(x, ('lat', 'lev'), pairs)  54.7 us
    ppermute x4, starting transfers between devices, group_shift(): return lax.ppermute(x, ('lat', 'lev'), pairs)  12.6 us
    ppermute x2, starting transfers between devices, lat_group_shift(): return lax.ppermute(x, ('lat', 'lev'), pairs)  8.25 us
    ppermute x4, starting transfers between devices, lat_pair_shift(): return lax.ppermute(x, ('lat', 'lev'), pairs)  2.68 us
    select_n x1, other arithmetic, on_device(): north = jnp.where(north_is_filter, north_filtered, north_plain)  2.28 us
  transfers between devices with their start and end apart: 10, of which 1 were waited for; matrix products, arithmetic and copies ran while one was open for 12% of the time, Pallas kernels for 0%

profile of v14, /device:TPU:14, one launch (start us, length us, event | category | flops | bytes accessed | tf_op | source)
XLA Modules:
  0.0 100.5 jit_solution(15412840451657153369)
XLA Ops:
  0.6 1.8 %pad_maximum_fusion = f32[3,4,16,2880]{3,2,1,0:T(8,128)S(1)} fusion(f32[1,4,16,2880]{3,2,1,0:T(8,128)} %bitcast.64, f32[1,4,16,2880]{3,2,1,0:T(8,128)} %bitcast.65, f32[1,4,16,2880]{3,2,1,0:T(8,128)} %bitcast.66), kind=kLoop, calls=%fused_computation.22 | loop fusion | flops 1105920 | bytes 4423680 | tf_op jit(solution)/shard_map/stack | solution.py:109
  2.4 0.1 slice_bitcast_fusion.7
  2.5 0.0 copy-start.8
  2.6 0.9 pad_maximum_fusion.4
  3.5 9.1 %collective-permute-start = (f32[4,16,2880]{2,1,0:T(8,128)}, f32[4,16,2880]{2,1,0:T(8,128)}, u32[]{:S(2)}, u32[]{:S(2)}) collective-permute-start(f32[4,16,2880]{2,1,0:T(8,128)} %pad_maximum_fusion.4), channel_id=1, source_target_pairs={{40,41},{41,42},{42,43},{43,44},{44,45},{45,46},{46,47},{48,49},{4... | collective-permute-start | bytes 2211848 | tf_op jit(solution)/shard_map/ppermute | solution.py:35
  12.6 0.9 pad_maximum_fusion.6
  13.6 1.9 %collective-permute-start.1 = (f32[4,16,2880]{2,1,0:T(8,128)}, f32[4,16,2880]{2,1,0:T(8,128)}, u32[]{:S(2)}, u32[]{:S(2)}) collective-permute-start(f32[4,16,2880]{2,1,0:T(8,128)} %pad_maximum_fusion.6), channel_id=1, source_target_pairs={{41,40},{42,41},{43,42},{44,43},{45,44},{46,45},{47,46},{49,48},{5... | collective-permute-start | bytes 2211848 | tf_op jit(solution)/shard_map/ppermute | solution.py:35
  15.5 0.9 fusion.20
  16.4 1.9 %collective-permute-start.2 = (f32[3,4,1,2880]{3,2,1,0:T(1,128)}, f32[3,4,1,2880]{3,2,1,0:T(1,128)S(1)}, u32[]{:S(2)}, u32[]{:S(2)}) collective-permute-start(f32[3,4,1,2880]{3,2,1,0:T(1,128)} %get-tuple-element.146), channel_id=1, source_target_pairs={{40,48},{41,49},{42,50},{43,51},{44,52},{45,53},{46,54},{47,55},{4... | collective-permute-start | bytes 414728 | tf_op jit(solution)/shard_map/ppermute | solution.py:43
  18.3 6.3 %collective-permute-start.3 = (f32[3,4,1,2880]{3,2,1,0:T(1,128)}, f32[3,4,1,2880]{3,2,1,0:T(1,128)}, u32[]{:S(2)}, u32[]{:S(2)}) collective-permute-start(f32[3,4,1,2880]{3,2,1,0:T(1,128)} %get-tuple-element.145), channel_id=1, source_target_pairs={{40,32},{41,33},{42,34},{43,35},{44,36},{45,37},{46,38},{47,39},{4... | collective-permute-start | bytes 414728 | tf_op jit(solution)/shard_map/ppermute | solution.py:43
  24.6 0.6 sine_multiply_fusion
  25.3 1.4 %compare_reduce_fusion.3 = (pred[]{:T(512)}, s32[16]{0:T(128)S(1)}) fusion(s32[512]{0:T(512)} %param.24, s32[]{:T(128)S(6)} %select_n.62), kind=kLoop, calls=%fused_computation.58 | loop fusion | flops 31 | bytes 133 | tf_op jit(solution)/shard_map/reduce_or | solution.py:97
  27.2 0.7 compare_reduce_fusion
  27.9 54.7 %collective-permute-done.2 = f32[3,4,1,2880]{3,2,1,0:T(1,128)S(1)} collective-permute-done((f32[3,4,1,2880]{3,2,1,0:T(1,128)}, f32[3,4,1,2880]{3,2,1,0:T(1,128)S(1)}, u32[]{:S(2)}, u32[]{:S(2)}) %collective-permute-start.2) | collective-permute-done | bytes 138272 | tf_op jit(solution)/shard_map/ppermute | solution.py:43
  82.6 0.0 collective-permute-done.3
  82.6 0.0 collective-permute-done
  82.6 0.0 collective-permute-done.1
  82.6 0.1 slice.163
  82.7 0.3 slice.164
  82.9 0.6 slice.161
  83.6 0.1 slice_bitcast_fusion.5
  83.7 0.1 pad_maximum_fusion.5
  83.7 0.9 collective-permute-start.6
  84.6 0.1 fusion.17
  84.7 0.4 fusion.12
  85.1 0.1 pad_maximum_fusion.3
  85.2 0.1 slice.166
  85.3 0.7 collective-permute-start.5
  86.0 0.2 fusion.19
  86.2 0.7 collective-permute-start.8
  86.9 0.7 collective-permute-start.4
  87.6 1.9 %broadcast_select_fusion = f32[4,16,2880]{2,1,0:T(8,128)S(1)} fusion(f32[4,16,2880]{2,1,0:T(8,128)S(1)} %collective-permute-done.6, f32[4,16,2880]{2,1,0:T(8,128)} %collective-permute-done.1, pred[]{:T(512)} %get-tuple-element.132), kind=kLoop, calls=%fused_computation.49 | loop fusion | flops 184320 | bytes 2211841 | tf_op jit(solution)/shard_map/jit(_where)/select_n | solution.py:131
  89.5 0.0 collective-permute-done.5
  89.5 1.9 %broadcast_select_fusion.1 = f32[4,16,2880]{2,1,0:T(8,128)S(1)} fusion(f32[4,16,2880]{2,1,0:T(8,128)S(1)} %collective-permute-done.5, f32[4,16,2880]{2,1,0:T(8,128)} %collective-permute-done, pred[]{:T(512)} %get-tuple-element.132), kind=kLoop, calls=%fused_computation.50 | loop fusion | flops 184320 | bytes 2211841 | tf_op jit(solution)/shard_map/jit(_where)/select_n | solution.py:130
  91.4 0.7 collective-permute-start.9
  92.1 0.7 collective-permute-start.7
  92.8 0.1 fusion.16
  92.9 0.3 fusion.7
  93.2 0.0 collective-permute-done.9
  93.2 2.3 %broadcast_select_fusion.2 = f32[3,4,1,2880]{3,2,1,0:T(1,128)S(1)} fusion(f32[3,4,1,2880]{3,2,1,0:T(1,128)} %collective-permute-done.3, pred[]{:T(512)} %get-tuple-element.130, f32[3,4,1,2880]{3,2,1,0:T(1,128)S(1)} %collective-permute-done.8, f32[3,4,1,2880]{3,2,1,0:T(1,128)S(1)} %collective-permute-done.9, pred[]{:T(512)} %get-tuple-element.132), kind=kLoop, calls=%fused_computation.51 | loop fusion | flops 69120 | bytes 552962 | tf_op jit(solution)/shard_map/jit(_where)/select_n | solution.py:145
  95.5 0.0 collective-permute-done.4
  95.5 0.0 collective-permute-done.7
  95.6 1.4 %broadcast_select_fusion.5 = f32[3,4,1,2880]{3,2,1,0:T(1,128)S(1)} fusion(f32[3,4,1,2880]{3,2,1,0:T(1,128)S(1)} %collective-permute-done.2, pred[]{:T(512)} %get-tuple-element.131, f32[3,4,1,2880]{3,2,1,0:T(1,128)S(1)} %collective-permute-done.4, f32[3,4,1,2880]{3,2,1,0:T(1,128)S(1)} %collective-permute-done.7, pred[]{:T(512)} %get-tuple-element.132), kind=kLoop, calls=%fused_computation.54 | loop fusion | flops 69120 | bytes 552962 | tf_op jit(solution)/shard_map/jit(_where)/select_n | solution.py:144
  97.0 0.2 fusion.15
  97.2 0.2 fusion.14
  97.4 0.6 fusion.6
  98.0 1.0 %fusion.8 = f32[3,4,16,2880]{3,2,1,0:T(8,128)S(1)} fusion(f32[3,5,16,2880]{3,2,1,0:T(8,128)S(1)} %fusion.7, f32[3,4,16,2880]{3,2,1,0:T(8,128)S(1)} %bitcast.55, f32[3,4,17,2880]{3,2,1,0:T(8,128)S(1)} %fusion.6, f32[3,4,16,2880]{3,2,1,0:T(8,128)S(1)} %fusion.12, f32[3,4,16,2879]{3,2,1,0:T(8,128)S(1)} %bitcast.60, f32[3,4,16,1]{3,2,1,0:T(8,128)S(1)} %slice.166, ...), kind=kLoop, calls=%fused_computation.17 | loop fusion | flops 4423680 | bytes 17694784 | tf_op jit(solution)/shard_map/sub | solution.py:171
  99.0 1.4 %slice_bitcast_fusion = (f32[4,16,2880]{2,1,0:T(8,128)}, f32[4,16,2880]{2,1,0:T(8,128)}, f32[4,16,2880]{2,1,0:T(8,128)}) fusion(f32[3,4,16,2880]{3,2,1,0:T(8,128)S(1)} %fusion.8), kind=kLoop, calls=%fused_computation.38 | loop fusion | bytes 4423680 | tf_op jit(solution)/shard_map/squeeze | solution.py:172
  (16 shorter events, 0.2 us)
Async XLA Ops:
  0.6 1.9 %copy-start = (f32[4,16,2880]{2,1,0:T(8,128)S(1)}, f32[4,16,2880]{2,1,0:T(8,128)}, u32[]{:S(2)}) copy-start(f32[4,16,2880]{2,1,0:T(8,128)} %param.23) | copy-start | bytes 2211844
  2.5 24.6 %copy-start.8 = (s32[10]{0:T(128)S(1)}, s32[10]{0:T(128)}, u32[]{:S(2)}) copy-start(s32[10]{0:T(128)} %constant.93.clone) | copy-start | bytes 124
  3.5 79.0 %collective-permute-start = (f32[4,16,2880]{2,1,0:T(8,128)}, f32[4,16,2880]{2,1,0:T(8,128)}, u32[]{:S(2)}, u32[]{:S(2)}) collective-permute-start(f32[4,16,2880]{2,1,0:T(8,128)} %pad_maximum_fusion.4), channel_id=1, source_target_pairs={{40,41},{41,42},{42,43},{43,44},{44,45},{45,46},{46,47},{48,49},{4... | collective-permute-start | bytes 2211848 | tf_op jit(solution)/shard_map/ppermute | solution.py:35
  13.6 69.0 %collective-permute-start.1 = (f32[4,16,2880]{2,1,0:T(8,128)}, f32[4,16,2880]{2,1,0:T(8,128)}, u32[]{:S(2)}, u32[]{:S(2)}) collective-permute-start(f32[4,16,2880]{2,1,0:T(8,128)} %pad_maximum_fusion.6), channel_id=1, source_target_pairs={{41,40},{42,41},{43,42},{44,43},{45,44},{46,45},{47,46},{49,48},{5... | collective-permute-start | bytes 2211848 | tf_op jit(solution)/shard_map/ppermute | solution.py:35
  16.4 66.2 %collective-permute-start.2 = (f32[3,4,1,2880]{3,2,1,0:T(1,128)}, f32[3,4,1,2880]{3,2,1,0:T(1,128)S(1)}, u32[]{:S(2)}, u32[]{:S(2)}) collective-permute-start(f32[3,4,1,2880]{3,2,1,0:T(1,128)} %get-tuple-element.146), channel_id=1, source_target_pairs={{40,48},{41,49},{42,50},{43,51},{44,52},{45,53},{46,54},{47,55},{4... | collective-permute-start | bytes 414728 | tf_op jit(solution)/shard_map/ppermute | solution.py:43
  18.3 64.3 %collective-permute-start.3 = (f32[3,4,1,2880]{3,2,1,0:T(1,128)}, f32[3,4,1,2880]{3,2,1,0:T(1,128)}, u32[]{:S(2)}, u32[]{:S(2)}) collective-permute-start(f32[3,4,1,2880]{3,2,1,0:T(1,128)} %get-tuple-element.145), channel_id=1, source_target_pairs={{40,32},{41,33},{42,34},{43,35},{44,36},{45,37},{46,38},{47,39},{4... | collective-permute-start | bytes 414728 | tf_op jit(solution)/shard_map/ppermute | solution.py:43
  83.7 3.8 %collective-permute-start.6 = (f32[4,16,2880]{2,1,0:T(8,128)S(1)}, f32[4,16,2880]{2,1,0:T(8,128)S(1)}, u32[]{:S(2)}, u32[]{:S(2)}) collective-permute-start(f32[4,16,2880]{2,1,0:T(8,128)S(1)} %pad_maximum_fusion.5), channel_id=1, source_target_pairs={{1,0},{2,1},{3,2},{4,3},{5,4},{6,5},{7,6},{9,8},{10,9},{11,10},{12... | collective-permute-start | bytes 2211848 | tf_op jit(solution)/shard_map/ppermute | solution.py:35
  85.3 4.2 %collective-permute-start.5 = (f32[4,16,2880]{2,1,0:T(8,128)S(1)}, f32[4,16,2880]{2,1,0:T(8,128)S(1)}, u32[]{:S(2)}, u32[]{:S(2)}) collective-permute-start(f32[4,16,2880]{2,1,0:T(8,128)S(1)} %pad_maximum_fusion.3), channel_id=1, source_target_pairs={{0,1},{1,2},{2,3},{3,4},{4,5},{5,6},{6,7},{8,9},{9,10},{10,11},{11... | collective-permute-start | bytes 2211848 | tf_op jit(solution)/shard_map/ppermute | solution.py:35
  86.2 7.0 %collective-permute-start.8 = (f32[3,4,1,2880]{3,2,1,0:T(1,128)S(1)}, f32[3,4,1,2880]{3,2,1,0:T(1,128)S(1)}, u32[]{:S(2)}, u32[]{:S(2)}) collective-permute-start(f32[3,4,1,2880]{3,2,1,0:T(1,128)S(1)} %get-tuple-element.102), channel_id=1, source_target_pairs={{8,0},{9,1},{10,2},{11,3},{12,4},{13,5},{14,6},{15,7},{16,8},{17,9... | collective-permute-start | bytes 414728 | tf_op jit(solution)/shard_map/ppermute | solution.py:51
  86.9 8.7 %collective-permute-start.4 = (f32[3,4,1,2880]{3,2,1,0:T(1,128)S(1)}, f32[3,4,1,2880]{3,2,1,0:T(1,128)S(1)}, u32[]{:S(2)}, u32[]{:S(2)}) collective-permute-start(f32[3,4,1,2880]{3,2,1,0:T(1,128)S(1)} %get-tuple-element.100), channel_id=1, source_target_pairs={{0,8},{1,9},{2,10},{3,11},{4,12},{5,13},{6,14},{7,15},{8,16},{9,17... | collective-permute-start | bytes 414728 | tf_op jit(solution)/shard_map/ppermute | solution.py:51
  91.4 1.8 %collective-permute-start.9 = (f32[3,4,1,2880]{3,2,1,0:T(1,128)S(1)}, f32[3,4,1,2880]{3,2,1,0:T(1,128)S(1)}, u32[]{:S(2)}, u32[]{:S(2)}) collective-permute-start(f32[3,4,1,2880]{3,2,1,0:T(1,128)S(1)} %get-tuple-element.102), channel_id=1, source_target_pairs={{216,208},{217,209},{218,210},{219,211},{220,212},{221,213},{222,2... | collective-permute-start | bytes 414728 | tf_op jit(solution)/shard_map/ppermute | solution.py:51
  92.1 3.4 %collective-permute-start.7 = (f32[3,4,1,2880]{3,2,1,0:T(1,128)S(1)}, f32[3,4,1,2880]{3,2,1,0:T(1,128)S(1)}, u32[]{:S(2)}, u32[]{:S(2)}) collective-permute-start(f32[3,4,1,2880]{3,2,1,0:T(1,128)S(1)} %get-tuple-element.100), channel_id=1, source_target_pairs={{32,40},{33,41},{34,42},{35,43},{36,44},{37,45},{38,46},{39,47}} | collective-permute-start | bytes 414728 | tf_op jit(solution)/shard_map/ppermute | solution.py:51
  95.5 1.6 %copy-start.9 = (f32[17]{0:T(128)S(1)}, f32[17]{0:T(128)}, u32[]{:S(2)}) copy-start(f32[17]{0:T(128)} %sine_multiply_fusion) | copy-start | bytes 208

commit v15 on v7

--- a/solution.py
+++ b/solution.py
@@ -108,21 +108,21 @@
     below_plain = group_shift(top, plain_lat, True)
     above_plain = group_shift(bottom, plain_lat, False)
 
+    below_wind_f = group_shift(vertical_wind[levels - 1 :], filter_lat, True)
+    above_wind_f = group_shift(vertical_wind[:1], filter_lat, False)
     tables = (parity_table(0), parity_table(1))
     south_plain = lat_group_shift(stacked[:, :, lat_rows - 1 :], plain_lat, True)
     north_plain = lat_group_shift(stacked[:, :, :1], plain_lat, False)
     stacked, below_plain, above_plain, south_plain, north_plain = lax.optimization_barrier(
         (stacked, below_plain, above_plain, south_plain, north_plain))
     field = filtered(stacked, own_cut, tables)
-    top = jnp.concatenate([field[:, levels - 1], vertical_wind[levels - 1 :]], axis=0)
-    bottom = jnp.concatenate([field[:, 0], vertical_wind[:1]], axis=0)
-    below_filtered = group_shift(top, filter_lat, True)
-    above_filtered = group_shift(bottom, filter_lat, False)
+    below_filtered = group_shift(field[:, levels - 1], filter_lat, True)
+    above_filtered = group_shift(field[:, 0], filter_lat, False)
     is_filter = jnp.any(lat_index == jnp.asarray(filter_lat, jnp.int32))
-    below_all = jnp.where(is_filter, below_filtered, below_plain)
-    above_all = jnp.where(is_filter, above_filtered, above_plain)
-    below, below_wind = below_all[:3, None], below_all[3:]
-    above, above_wind = above_all[:3, None], above_all[3:]
+    below = jnp.where(is_filter, below_filtered, below_plain[:3])[:, None]
+    above = jnp.where(is_filter, above_filtered, above_plain[:3])[:, None]
+    below_wind = jnp.where(is_filter, below_wind_f, below_plain[3:])
+    above_wind = jnp.where(is_filter, above_wind_f, above_plain[3:])
     south_filtered = lat_group_shift(field[:, :, lat_rows - 1 :], filter_lat, True)
     north_filtered = lat_group_shift(field[:, :, :1], filter_lat, False)
     south_is_filter = jnp.any(lat_index - 1 == jnp.asarray(filter_lat, jnp.int32))

time: 99.2 us -> 103 us (1.038)
  the two profiles are of different devices: /device:TPU:80 before, /device:TPU:14 now
where the time goes in v15:
time: 103 us; the launch traced here: 102 us
  waiting for transfers between devices  53.1 us (52%)
  starting transfers between devices  24.7 us (24%)
  other arithmetic  18.8 us (18%)
  local copies, waits for them, and re-layouts  3.76 us (4%)
  between operations  1.57 us (2%)
    ppermute x4, waiting for transfers between devices, lat_group_shift(): return lax.ppermute(x, ('lat', 'lev'), pairs)  53.1 us
    ppermute x6, starting transfers between devices, group_shift(): return lax.ppermute(x, ('lat', 'lev'), pairs)  15.1 us
    ppermute x4, starting transfers between devices, lat_group_shift(): return lax.ppermute(x, ('lat', 'lev'), pairs)  9.59 us
  transfers between devices with their start and end apart: 10, of which 1 were waited for; matrix products, arithmetic and copies ran while one was open for 15% of the time, Pallas kernels for 0%

profile of v15, /device:TPU:14, one launch (start us, length us, event | category | flops | bytes accessed | tf_op | source)
XLA Modules:
  0.0 102.1 jit_solution(4573534219285478242)
XLA Ops:
  0.6 1.8 %pad_maximum_fusion = f32[3,4,16,2880]{3,2,1,0:T(8,128)S(1)} fusion(f32[1,4,16,2880]{3,2,1,0:T(8,128)} %bitcast.64, f32[1,4,16,2880]{3,2,1,0:T(8,128)} %bitcast.65, f32[1,4,16,2880]{3,2,1,0:T(8,128)} %bitcast.66), kind=kLoop, calls=%fused_computation.22 | loop fusion | flops 1105920 | bytes 4423680 | tf_op jit(solution)/shard_map/stack | solution.py:101
  2.4 0.1 slice_bitcast_fusion.5
  2.5 0.0 copy-start.8
  2.6 0.9 pad_maximum_fusion.3
  3.5 9.1 %collective-permute-start = (f32[4,16,2880]{2,1,0:T(8,128)}, f32[4,16,2880]{2,1,0:T(8,128)}, u32[]{:S(2)}, u32[]{:S(2)}) collective-permute-start(f32[4,16,2880]{2,1,0:T(8,128)} %pad_maximum_fusion.3), channel_id=1, source_target_pairs={{40,41},{41,42},{42,43},{43,44},{44,45},{45,46},{46,47},{48,49},{4... | collective-permute-start | bytes 2211848 | tf_op jit(solution)/shard_map/ppermute | solution.py:35
  12.6 1.3 %collective-permute-start.9 = (f32[1,16,2880]{2,1,0:T(8,128)S(1)}, f32[1,16,2880]{2,1,0:T(8,128)}, u32[]{:S(2)}, u32[]{:S(2)}) collective-permute-start(f32[1,16,2880]{2,1,0:T(8,128)S(1)} %get-tuple-element.145), channel_id=1, source_target_pairs={{1,0},{2,1},{3,2},{4,3},{5,4},{6,5},{7,6},{9,8},{10,9},{11,10},{12... | collective-permute-start | bytes 552968 | tf_op jit(solution)/shard_map/ppermute | solution.py:35
  14.0 0.9 pad_maximum_fusion.4
  14.9 1.9 %collective-permute-start.1 = (f32[4,16,2880]{2,1,0:T(8,128)}, f32[4,16,2880]{2,1,0:T(8,128)}, u32[]{:S(2)}, u32[]{:S(2)}) collective-permute-start(f32[4,16,2880]{2,1,0:T(8,128)} %pad_maximum_fusion.4), channel_id=1, source_target_pairs={{41,40},{42,41},{43,42},{44,43},{45,44},{46,45},{47,46},{49,48},{5... | collective-permute-start | bytes 2211848 | tf_op jit(solution)/shard_map/ppermute | solution.py:35
  16.8 0.9 fusion.20
  17.7 1.9 %collective-permute-start.2 = (f32[3,4,1,2880]{3,2,1,0:T(1,128)}, f32[3,4,1,2880]{3,2,1,0:T(1,128)S(1)}, u32[]{:S(2)}, u32[]{:S(2)}) collective-permute-start(f32[3,4,1,2880]{3,2,1,0:T(1,128)} %get-tuple-element.142), channel_id=1, source_target_pairs={{40,48},{41,49},{42,50},{43,51},{44,52},{45,53},{46,54},{47,55},{4... | collective-permute-start | bytes 414728 | tf_op jit(solution)/shard_map/ppermute | solution.py:43
  19.6 6.3 %collective-permute-start.3 = (f32[3,4,1,2880]{3,2,1,0:T(1,128)}, f32[3,4,1,2880]{3,2,1,0:T(1,128)}, u32[]{:S(2)}, u32[]{:S(2)}) collective-permute-start(f32[3,4,1,2880]{3,2,1,0:T(1,128)} %get-tuple-element.141), channel_id=1, source_target_pairs={{40,32},{41,33},{42,34},{43,35},{44,36},{45,37},{46,38},{47,39},{4... | collective-permute-start | bytes 414728 | tf_op jit(solution)/shard_map/ppermute | solution.py:43
  26.0 0.6 sine_multiply_fusion
  26.6 1.4 %compare_reduce_fusion.3 = (pred[]{:T(512)}, s32[16]{0:T(128)S(1)}) fusion(s32[512]{0:T(512)} %param.24, s32[]{:T(128)S(6)} %select_n.64), kind=kLoop, calls=%fused_computation.54 | loop fusion | flops 31 | bytes 133 | tf_op jit(solution)/shard_map/reduce_or | solution.py:89
  28.6 0.7 compare_reduce_fusion.1
  29.4 53.1 %collective-permute-done.2 = f32[3,4,1,2880]{3,2,1,0:T(1,128)S(1)} collective-permute-done((f32[3,4,1,2880]{3,2,1,0:T(1,128)}, f32[3,4,1,2880]{3,2,1,0:T(1,128)S(1)}, u32[]{:S(2)}, u32[]{:S(2)}) %collective-permute-start.2) | collective-permute-done | bytes 138272 | tf_op jit(solution)/shard_map/ppermute | solution.py:43
  82.5 1.3 %collective-permute-start.8 = (f32[1,16,2880]{2,1,0:T(8,128)S(1)}, f32[1,16,2880]{2,1,0:T(8,128)}, u32[]{:S(2)}, u32[]{:S(2)}) collective-permute-start(f32[1,16,2880]{2,1,0:T(8,128)S(1)} %get-tuple-element.146), channel_id=1, source_target_pairs={{0,1},{1,2},{2,3},{3,4},{4,5},{5,6},{6,7},{8,9},{9,10},{10,11},{11... | collective-permute-start | bytes 552968 | tf_op jit(solution)/shard_map/ppermute | solution.py:35
  83.8 0.0 collective-permute-done.3
  83.8 0.0 collective-permute-done.1
  83.8 0.2 conditional.1
  84.0 0.1 slice.161
  84.1 0.3 slice.162
  84.3 0.6 slice.159
  85.0 0.1 slice_bitcast_fusion.3
  85.1 0.1 fusion.17
  85.2 0.3 fusion.12
  85.5 0.2 fusion.19
  85.7 0.1 slice.164
  85.8 0.7 collective-permute-start.5
  86.5 0.7 collective-permute-start.4
  87.2 0.7 collective-permute-start.7
  87.9 0.7 collective-permute-start.6
  88.6 1.6 %slice_select_fusion = f32[1,16,2880]{2,1,0:T(8,128)S(1)} fusion(f32[1,16,2880]{2,1,0:T(8,128)} %collective-permute-done.9, f32[4,16,2880]{2,1,0:T(8,128)} %collective-permute-done.1, pred[]{:T(512)} %get-tuple-element.128), kind=kLoop, calls=%fused_computation.49 | loop fusion | flops 46080 | bytes 552961 | tf_op jit(solution)/shard_map/jit(_where)/select_n | solution.py:125
  90.3 0.0 collective-permute-done.8
  90.3 1.6 %slice_select_fusion.1 = f32[1,16,2880]{2,1,0:T(8,128)S(1)} fusion(f32[1,16,2880]{2,1,0:T(8,128)} %collective-permute-done.8, f32[4,16,2880]{2,1,0:T(8,128)} %collective-permute-done, pred[]{:T(512)} %get-tuple-element.128), kind=kLoop, calls=%fused_computation.50 | loop fusion | flops 46080 | bytes 552961 | tf_op jit(solution)/shard_map/jit(_where)/select_n | solution.py:124
  91.9 0.1 fusion.16
  92.0 0.0 collective-permute-done.5
  92.0 1.6 %broadcast_select_fusion = f32[3,4,1,2880]{3,2,1,0:T(1,128)S(1)} fusion(f32[3,4,1,2880]{3,2,1,0:T(1,128)S(1)} %collective-permute-done.5, f32[3,4,1,2880]{3,2,1,0:T(1,128)} %collective-permute-done.3, pred[]{:T(512)} %get-tuple-element.126), kind=kLoop, calls=%fused_computation.47 | loop fusion | flops 34560 | bytes 414721 | tf_op jit(solution)/shard_map/jit(_where)/select_n | solution.py:131
  93.6 0.0 collective-permute-done.4
  93.7 0.8 broadcast_select_fusion.1
  94.5 0.2 fusion.15
  94.7 0.2 fusion.14
  94.9 0.6 fusion.6
  95.5 0.0 collective-permute-done.7
  95.5 1.8 %select_bitcast_fusion = f32[3,1,16,2880]{3,2,1,0:T(8,128)S(1)} fusion(f32[3,16,2880]{2,1,0:T(8,128)S(1)} %collective-permute-done.7, f32[4,16,2880]{2,1,0:T(8,128)} %collective-permute-done.1, pred[]{:T(512)} %get-tuple-element.128), kind=kLoop, calls=%fused_computation.45 | loop fusion | flops 138240 | bytes 1658881 | tf_op jit(solution)/shard_map/broadcast_in_dim | solution.py:123
  97.3 1.8 %select_bitcast_fusion.1 = f32[3,1,16,2880]{3,2,1,0:T(8,128)S(1)} fusion(f32[3,16,2880]{2,1,0:T(8,128)S(1)} %collective-permute-done.6, f32[4,16,2880]{2,1,0:T(8,128)} %collective-permute-done, pred[]{:T(512)} %get-tuple-element.128), kind=kLoop, calls=%fused_computation.46 | loop fusion | flops 138240 | bytes 1658881 | tf_op jit(solution)/shard_map/broadcast_in_dim | solution.py:122
  99.1 0.3 fusion.7
  99.4 1.2 %fusion.8 = f32[3,4,16,2880]{3,2,1,0:T(8,128)S(1)} fusion(f32[3,5,16,2880]{3,2,1,0:T(8,128)S(1)} %fusion.7, f32[3,4,16,2880]{3,2,1,0:T(8,128)S(1)} %bitcast.55, f32[3,4,17,2880]{3,2,1,0:T(8,128)S(1)} %fusion.6, f32[3,4,16,2880]{3,2,1,0:T(8,128)S(1)} %fusion.12, f32[3,4,16,2879]{3,2,1,0:T(8,128)S(1)} %bitcast.60, f32[3,4,16,1]{3,2,1,0:T(8,128)S(1)} %slice.164, ...), kind=kLoop, calls=%fused_computation.17 | loop fusion | flops 4423680 | bytes 17694784 | tf_op jit(solution)/shard_map/sub | solution.py:157
  100.6 1.4 %slice_bitcast_fusion = (f32[4,16,2880]{2,1,0:T(8,128)}, f32[4,16,2880]{2,1,0:T(8,128)}, f32[4,16,2880]{2,1,0:T(8,128)}) fusion(f32[3,4,16,2880]{3,2,1,0:T(8,128)S(1)} %fusion.8), kind=kLoop, calls=%fused_computation.34 | loop fusion | bytes 4423680 | tf_op jit(solution)/shard_map/squeeze | solution.py:158
  (12 shorter events, 0.1 us)
Async XLA Ops:
  0.6 1.9 %copy-start = (f32[4,16,2880]{2,1,0:T(8,128)S(1)}, f32[4,16,2880]{2,1,0:T(8,128)}, u32[]{:S(2)}) copy-start(f32[4,16,2880]{2,1,0:T(8,128)} %param.23) | copy-start | bytes 2211844
  2.5 26.1 %copy-start.8 = (s32[10]{0:T(128)S(1)}, s32[10]{0:T(128)}, u32[]{:S(2)}) copy-start(s32[10]{0:T(128)} %constant.93.clone) | copy-start | bytes 124
  3.5 80.3 %collective-permute-start = (f32[4,16,2880]{2,1,0:T(8,128)}, f32[4,16,2880]{2,1,0:T(8,128)}, u32[]{:S(2)}, u32[]{:S(2)}) collective-permute-start(f32[4,16,2880]{2,1,0:T(8,128)} %pad_maximum_fusion.3), channel_id=1, source_target_pairs={{40,41},{41,42},{42,43},{43,44},{44,45},{45,46},{46,47},{48,49},{4... | collective-permute-start | bytes 2211848 | tf_op jit(solution)/shard_map/ppermute | solution.py:35
  12.6 75.3 %collective-permute-start.9 = (f32[1,16,2880]{2,1,0:T(8,128)S(1)}, f32[1,16,2880]{2,1,0:T(8,128)}, u32[]{:S(2)}, u32[]{:S(2)}) collective-permute-start(f32[1,16,2880]{2,1,0:T(8,128)S(1)} %get-tuple-element.145), channel_id=1, source_target_pairs={{1,0},{2,1},{3,2},{4,3},{5,4},{6,5},{7,6},{9,8},{10,9},{11,10},{12... | collective-permute-start | bytes 552968 | tf_op jit(solution)/shard_map/ppermute | solution.py:35
  14.9 68.9 %collective-permute-start.1 = (f32[4,16,2880]{2,1,0:T(8,128)}, f32[4,16,2880]{2,1,0:T(8,128)}, u32[]{:S(2)}, u32[]{:S(2)}) collective-permute-start(f32[4,16,2880]{2,1,0:T(8,128)} %pad_maximum_fusion.4), channel_id=1, source_target_pairs={{41,40},{42,41},{43,42},{44,43},{45,44},{46,45},{47,46},{49,48},{5... | collective-permute-start | bytes 2211848 | tf_op jit(solution)/shard_map/ppermute | solution.py:35
  17.7 64.8 %collective-permute-start.2 = (f32[3,4,1,2880]{3,2,1,0:T(1,128)}, f32[3,4,1,2880]{3,2,1,0:T(1,128)S(1)}, u32[]{:S(2)}, u32[]{:S(2)}) collective-permute-start(f32[3,4,1,2880]{3,2,1,0:T(1,128)} %get-tuple-element.142), channel_id=1, source_target_pairs={{40,48},{41,49},{42,50},{43,51},{44,52},{45,53},{46,54},{47,55},{4... | collective-permute-start | bytes 414728 | tf_op jit(solution)/shard_map/ppermute | solution.py:43
  19.6 64.2 %collective-permute-start.3 = (f32[3,4,1,2880]{3,2,1,0:T(1,128)}, f32[3,4,1,2880]{3,2,1,0:T(1,128)}, u32[]{:S(2)}, u32[]{:S(2)}) collective-permute-start(f32[3,4,1,2880]{3,2,1,0:T(1,128)} %get-tuple-element.141), channel_id=1, source_target_pairs={{40,32},{41,33},{42,34},{43,35},{44,36},{45,37},{46,38},{47,39},{4... | collective-permute-start | bytes 414728 | tf_op jit(solution)/shard_map/ppermute | solution.py:43
  82.5 7.8 %collective-permute-start.8 = (f32[1,16,2880]{2,1,0:T(8,128)S(1)}, f32[1,16,2880]{2,1,0:T(8,128)}, u32[]{:S(2)}, u32[]{:S(2)}) collective-permute-start(f32[1,16,2880]{2,1,0:T(8,128)S(1)} %get-tuple-element.146), channel_id=1, source_target_pairs={{0,1},{1,2},{2,3},{3,4},{4,5},{5,6},{6,7},{8,9},{9,10},{10,11},{11... | collective-permute-start | bytes 552968 | tf_op jit(solution)/shard_map/ppermute | solution.py:35
  85.8 6.2 %collective-permute-start.5 = (f32[3,4,1,2880]{3,2,1,0:T(1,128)S(1)}, f32[3,4,1,2880]{3,2,1,0:T(1,128)S(1)}, u32[]{:S(2)}, u32[]{:S(2)}) collective-permute-start(f32[3,4,1,2880]{3,2,1,0:T(1,128)S(1)} %get-tuple-element.137), channel_id=1, source_target_pairs={{8,0},{9,1},{10,2},{11,3},{12,4},{13,5},{14,6},{15,7},{16,8},{17,9... | collective-permute-start | bytes 414728 | tf_op jit(solution)/shard_map/ppermute | solution.py:43
  86.5 7.1 %collective-permute-start.4 = (f32[3,4,1,2880]{3,2,1,0:T(1,128)S(1)}, f32[3,4,1,2880]{3,2,1,0:T(1,128)S(1)}, u32[]{:S(2)}, u32[]{:S(2)}) collective-permute-start(f32[3,4,1,2880]{3,2,1,0:T(1,128)S(1)} %get-tuple-element.138), channel_id=1, source_target_pairs={{0,8},{1,9},{2,10},{3,11},{4,12},{5,13},{6,14},{7,15},{8,16},{9,17... | collective-permute-start | bytes 414728 | tf_op jit(solution)/shard_map/ppermute | solution.py:43
  87.2 8.3 %collective-permute-start.7 = (f32[3,16,2880]{2,1,0:T(8,128)S(1)}, f32[3,16,2880]{2,1,0:T(8,128)S(1)}, u32[]{:S(2)}, u32[]{:S(2)}) collective-permute-start(f32[3,16,2880]{2,1,0:T(8,128)S(1)} %get-tuple-element.139), channel_id=1, source_target_pairs={{1,0},{2,1},{3,2},{4,3},{5,4},{6,5},{7,6},{9,8},{10,9},{11,10},{12... | collective-permute-start | bytes 1658888 | tf_op jit(solution)/shard_map/ppermute | solution.py:35
  87.9 9.4 %collective-permute-start.6 = (f32[3,16,2880]{2,1,0:T(8,128)S(1)}, f32[3,16,2880]{2,1,0:T(8,128)S(1)}, u32[]{:S(2)}, u32[]{:S(2)}) collective-permute-start(f32[3,16,2880]{2,1,0:T(8,128)S(1)} %get-tuple-element.140), channel_id=1, source_target_pairs={{0,1},{1,2},{2,3},{3,4},{4,5},{5,6},{6,7},{8,9},{9,10},{10,11},{11... | collective-permute-start | bytes 1658888 | tf_op jit(solution)/shard_map/ppermute | solution.py:35
  92.0 2.6 %copy-start.9 = (f32[17]{0:T(128)S(1)}, f32[17]{0:T(128)}, u32[]{:S(2)}) copy-start(f32[17]{0:T(128)} %sine_multiply_fusion) | copy-start | bytes 208

commit v16 on v12

--- a/solution.py
+++ b/solution.py
@@ -111,7 +111,7 @@
     tables = (parity_table(0), parity_table(1))
     south_plain = lat_group_shift(stacked[:, :, lat_rows - 1 :], plain_lat, True)
     north_plain = lat_group_shift(stacked[:, :, :1], plain_lat, False)
-    stacked, south_plain, north_plain = lax.optimization_barrier((stacked, south_plain, north_plain))
+    stacked, below_plain, above_plain = lax.optimization_barrier((stacked, below_plain, above_plain))
     field = filtered(stacked, own_cut, tables)
     top = jnp.concatenate([field[:, levels - 1], vertical_wind[levels - 1 :]], axis=0)
     bottom = jnp.concatenate([field[:, 0], vertical_wind[:1]], axis=0)

time: 103 us -> 96 us (0.932)
  the two profiles are of different devices: /device:TPU:175 before, /device:TPU:47 now
where the time goes in v16:
time: 96 us; the launch traced here: 95.1 us
  waiting for transfers between devices  41.3 us (43%)
  starting transfers between devices  23.3 us (24%)
  other arithmetic  16.1 us (17%)
  matrix products  8.51 us (9%)
  local copies, waits for them, and re-layouts  3.98 us (4%)
  between operations  1.55 us (2%)
    ppermute x4, waiting for transfers between devices, group_shift(): return lax.ppermute(x, ('lat', 'lev'), pairs)  40.9 us
    ppermute x4, starting transfers between devices, group_shift(): return lax.ppermute(x, ('lat', 'lev'), pairs)  12.9 us
    ppermute x4, starting transfers between devices, lat_group_shift(): return lax.ppermute(x, ('lat', 'lev'), pairs)  10.4 us
    add x2, other arithmetic, parity_table(): as_f32(first)[None] * as_f32(np.cos(hi))[:, None]  2.34 us
    dot_general x1, matrix products, lowpass_rows(): lax.dot_general(spec_even * parity_weight(0, cut), even_table, dims, prec...  2.28 us
    dot_general x1, matrix products, lowpass_rows(): jnp.dot(first + second, even_table, precision=mxu_precision, preferred_el...  2.18 us
    dot_general x1, matrix products, lowpass_rows(): lax.dot_general(spec_odd * parity_weight(1, cut), odd_table, dims, precis...  2.13 us
    dot_general x1, matrix products, lowpass_rows(): jnp.dot(first - second, odd_table, precision=mxu_precision, preferred_ele...  1.92 us
  transfers between devices with their start and end apart: 8, of which 3 were waited for; matrix products, arithmetic and copies ran while one was open for 23% of the time, Pallas kernels for 0%

profile of v16, /device:TPU:47, one launch (start us, length us, event | category | flops | bytes accessed | tf_op | source)
XLA Modules:
  0.0 95.1 jit_solution(1258846936582315219)
XLA Ops:
  0.6 1.8 %pad_maximum_fusion = f32[3,4,16,2880]{3,2,1,0:T(8,128)S(1)} fusion(f32[1,4,16,2880]{3,2,1,0:T(8,128)} %bitcast.64, f32[1,4,16,2880]{3,2,1,0:T(8,128)} %bitcast.65, f32[1,4,16,2880]{3,2,1,0:T(8,128)} %bitcast.66), kind=kLoop, calls=%fused_computation.22 | loop fusion | flops 1105920 | bytes 4423680 | tf_op jit(solution)/shard_map/stack | solution.py:101
  2.4 0.1 slice_bitcast_fusion.7
  2.6 0.9 pad_maximum_fusion.4
  3.5 1.6 %collective-permute-start = (f32[4,16,2880]{2,1,0:T(8,128)}, f32[4,16,2880]{2,1,0:T(8,128)}, u32[]{:S(2)}, u32[]{:S(2)}) collective-permute-start(f32[4,16,2880]{2,1,0:T(8,128)} %pad_maximum_fusion.4), channel_id=1, source_target_pairs={{40,41},{41,42},{42,43},{43,44},{44,45},{45,46},{46,47},{48,49},{4... | collective-permute-start | bytes 2211848 | tf_op jit(solution)/shard_map/ppermute | solution.py:35
  5.1 0.9 pad_maximum_fusion.6
  6.0 1.6 %collective-permute-start.1 = (f32[4,16,2880]{2,1,0:T(8,128)}, f32[4,16,2880]{2,1,0:T(8,128)}, u32[]{:S(2)}, u32[]{:S(2)}) collective-permute-start(f32[4,16,2880]{2,1,0:T(8,128)} %pad_maximum_fusion.6), channel_id=1, source_target_pairs={{41,40},{42,41},{43,42},{44,43},{45,44},{46,45},{47,46},{49,48},{5... | collective-permute-start | bytes 2211848 | tf_op jit(solution)/shard_map/ppermute | solution.py:35
  7.5 0.9 fusion.19
  8.4 1.3 %collective-permute-start.5 = (f32[3,4,1,2880]{3,2,1,0:T(1,128)}, f32[3,4,1,2880]{3,2,1,0:T(1,128)}, u32[]{:S(2)}, u32[]{:S(2)}) collective-permute-start(f32[3,4,1,2880]{3,2,1,0:T(1,128)} %get-tuple-element.133), channel_id=1, source_target_pairs={{40,32},{41,33},{42,34},{43,35},{44,36},{45,37},{46,38},{47,39},{4... | collective-permute-start | bytes 414728 | tf_op jit(solution)/shard_map/ppermute | solution.py:43
  9.7 1.3 %collective-permute-start.3 = (f32[3,4,1,2880]{3,2,1,0:T(1,128)S(1)}, f32[3,4,1,2880]{3,2,1,0:T(1,128)}, u32[]{:S(2)}, u32[]{:S(2)}) collective-permute-start(f32[3,4,1,2880]{3,2,1,0:T(1,128)S(1)} %get-tuple-element.134), channel_id=1, source_target_pairs={{40,48},{41,49},{42,50},{43,51},{44,52},{45,53},{46,54},{47,55},{4... | collective-permute-start | bytes 414728 | tf_op jit(solution)/shard_map/ppermute | solution.py:43
  11.0 1.4 %compare_reduce_fusion.3 = (pred[]{:T(512)}, s32[16]{0:T(128)S(1)}) fusion(s32[512]{0:T(512)} %param.24, s32[]{:T(128)S(6)} %select_n.52), kind=kLoop, calls=%fused_computation.56 | loop fusion | flops 31 | bytes 133 | tf_op jit(solution)/shard_map/reduce_or | solution.py:89
  13.0 0.6 sine_multiply_fusion
  13.7 0.7 compare_reduce_fusion.1
  14.4 12.1 %conditional.1 = (f32[192,2880]{1,0:T(8,128)S(1)}) conditional(s32[]{:T(128)} %convert_element_type.17, f32[192,2880]{1,0:T(8,128)S(1)} %bitcast.45, (s32[16]{0:T(128)S(1)}, f32[192,2880]{1,0:T(8,128)S(1)}) %tuple.92), branch_computations={%region_1.0_spmd, %region_2.3_spmd.clone} | conditional | flops 4786836480 | bytes 46174092 | solution.py:89
  14.4 0.1 reshape.114
  14.5 1.7 %multiply_add_fusion = f32[30,48,720]{2,1,0:T(8,128)S(1)} fusion(f32[30,720]{1,0:T(8,128)} %constant.90.clone.2, f32[48,720]{1,0:T(8,128)} %constant.89.clone.2, f32[30,720]{1,0:T(8,128)} %constant.88.clone.2, f32[48,720]{1,0:T(8,128)} %constant.87.clone.2), kind=kLoop, calls=%fused_computation | loop fusion | flops 3110400 | bytes 4596480 | tf_op jit(solution)/shard_map/add | solution.py:57
  16.2 1.9 %convolution_multiply_fusion = f32[192,720]{1,0:T(8,128)S(1)} fusion(f32[1440,720]{1,0:T(8,128)S(1)} %bitcast.58, f32[192,2880]{1,0:T(8,128)S(1)} %get-tuple-element.119, s32[720]{0:T(1024)S(1)} %copy-done.7, s32[192]{0:T(256)S(1)} %reshape.114), kind=kOutput, calls=%fused_computation.3 | convolution fusion | flops 1195084800 | bytes 7341056 | tf_op jit(solution)/shard_map/cond/branch_1_fun/dot_general | solution.py:74
  18.2 2.1 %fusion.22 = f32[192,1440]{1,0:T(8,128)S(1)} fusion(f32[192,720]{1,0:T(8,128)S(1)} %convolution_multiply_fusion, f32[1440,720]{1,0:T(8,128)S(1)} %bitcast.59), kind=kOutput, calls=%fused_computation.63 | convolution fusion | flops 1194393600 | bytes 5806080 | tf_op jit(solution)/shard_map/cond/branch_1_fun/dot_general | solution.py:79
  20.4 0.6 multiply_add_fusion.1
  21.1 2.2 %convolution_multiply_fusion.1 = f32[192,720]{1,0:T(8,128)S(1)} fusion(f32[1440,720]{1,0:T(8,128)S(1)} %bitcast.56, f32[192,2880]{1,0:T(8,128)S(1)} %get-tuple-element.119, f32[720]{0:T(1024)S(1)} %copy-done.5, s32[720]{0:T(1024)S(1)} %copy-done.6, s32[192]{0:T(256)S(1)} %reshape.114), kind=kOutput, calls=%fused_computation.4 | convolution fusion | flops 1195084800 | bytes 7345152 | tf_op jit(solution)/shard_map/cond/branch_1_fun/dot_general | solution.py:72
  23.2 2.3 %fusion.18 = (f32[192,1440]{1,0:T(8,128)S(1)}, f32[192,1440]{1,0:T(8,128)S(1)}) fusion(f32[192,1440]{1,0:T(8,128)S(1)} %fusion.22, f32[192,720]{1,0:T(8,128)S(1)} %convolution_multiply_fusion.1, f32[1440,720]{1,0:T(8,128)S(1)} %bitcast.57), kind=kOutput, calls=%fused_computation.59 | convolution fusion | flops 1194946560 | bytes 8017920 | tf_op jit(solution)/shard_map/cond/branch_1_fun/dot_general | solution.py:77
  25.5 0.7 maximum_select_fusion
  26.5 0.3 slice.160
  26.8 0.6 slice.157
  27.5 0.2 fusion.20
  27.7 0.1 slice_bitcast_fusion.4
  27.7 0.1 fusion.17
  27.9 0.4 fusion.12
  28.2 0.1 slice.162
  28.3 6.5 %collective-permute-start.4 = (f32[3,4,1,2880]{3,2,1,0:T(1,128)S(1)}, f32[3,4,1,2880]{3,2,1,0:T(1,128)S(1)}, u32[]{:S(2)}, u32[]{:S(2)}) collective-permute-start(f32[3,4,1,2880]{3,2,1,0:T(1,128)S(1)} %get-tuple-element.135), channel_id=1, source_target_pairs={{8,0},{9,1},{10,2},{11,3},{12,4},{13,5},{14,6},{15,7},{16,8},{17,9... | collective-permute-start | bytes 414728 | tf_op jit(solution)/shard_map/ppermute | solution.py:43
  34.8 1.3 %collective-permute-start.2 = (f32[3,4,1,2880]{3,2,1,0:T(1,128)S(1)}, f32[3,4,1,2880]{3,2,1,0:T(1,128)S(1)}, u32[]{:S(2)}, u32[]{:S(2)}) collective-permute-start(f32[3,4,1,2880]{3,2,1,0:T(1,128)S(1)} %get-tuple-element.136), channel_id=1, source_target_pairs={{0,8},{1,9},{2,10},{3,11},{4,12},{5,13},{6,14},{7,15},{8,16},{9,17... | collective-permute-start | bytes 414728 | tf_op jit(solution)/shard_map/ppermute | solution.py:43
  36.1 0.1 pad_maximum_fusion.5
  36.2 7.8 %collective-permute-start.7 = (f32[4,16,2880]{2,1,0:T(8,128)S(1)}, f32[4,16,2880]{2,1,0:T(8,128)S(1)}, u32[]{:S(2)}, u32[]{:S(2)}) collective-permute-start(f32[4,16,2880]{2,1,0:T(8,128)S(1)} %pad_maximum_fusion.5), channel_id=1, source_target_pairs={{1,0},{2,1},{3,2},{4,3},{5,4},{6,5},{7,6},{9,8},{10,9},{11,10},{12... | collective-permute-start | bytes 2211848 | tf_op jit(solution)/shard_map/ppermute | solution.py:35
  44.0 0.1 pad_maximum_fusion.3
  44.0 2.0 %collective-permute-start.6 = (f32[4,16,2880]{2,1,0:T(8,128)S(1)}, f32[4,16,2880]{2,1,0:T(8,128)S(1)}, u32[]{:S(2)}, u32[]{:S(2)}) collective-permute-start(f32[4,16,2880]{2,1,0:T(8,128)S(1)} %pad_maximum_fusion.3), channel_id=1, source_target_pairs={{0,1},{1,2},{2,3},{3,4},{4,5},{5,6},{6,7},{8,9},{9,10},{10,11},{11... | collective-permute-start | bytes 2211848 | tf_op jit(solution)/shard_map/ppermute | solution.py:35
  46.1 0.8 broadcast_select_fusion.2
  46.9 0.4 collective-permute-done.2
  47.3 1.6 %broadcast_select_fusion.3 = f32[3,4,1,2880]{3,2,1,0:T(1,128)S(1)} fusion(f32[3,4,1,2880]{3,2,1,0:T(1,128)S(1)} %collective-permute-done.2, f32[3,4,1,2880]{3,2,1,0:T(1,128)} %collective-permute-done.3, pred[]{:T(512)} %get-tuple-element.123), kind=kLoop, calls=%fused_computation.52 | loop fusion | flops 34560 | bytes 414721 | tf_op jit(solution)/shard_map/jit(_where)/select_n | solution.py:129
  48.9 0.2 fusion.15
  49.1 0.2 fusion.14
  49.3 0.6 fusion.6
  49.9 33.7 %collective-permute-done.7 = f32[4,16,2880]{2,1,0:T(8,128)S(1)} collective-permute-done((f32[4,16,2880]{2,1,0:T(8,128)S(1)}, f32[4,16,2880]{2,1,0:T(8,128)S(1)}, u32[]{:S(2)}, u32[]{:S(2)}) %collective-permute-start.7) | collective-permute-done | bytes 737312 | tf_op jit(solution)/shard_map/ppermute | solution.py:35
  83.6 0.7 broadcast_select_fusion
  84.4 7.2 %collective-permute-done.6 = f32[4,16,2880]{2,1,0:T(8,128)S(1)} collective-permute-done((f32[4,16,2880]{2,1,0:T(8,128)S(1)}, f32[4,16,2880]{2,1,0:T(8,128)S(1)}, u32[]{:S(2)}, u32[]{:S(2)}) %collective-permute-start.6) | collective-permute-done | bytes 737312 | tf_op jit(solution)/shard_map/ppermute | solution.py:35
  91.6 0.7 broadcast_select_fusion.1
  92.3 0.1 fusion.16
  92.4 0.4 fusion.7
  92.8 0.9 fusion.8
  93.7 1.4 %slice_bitcast_fusion = (f32[4,16,2880]{2,1,0:T(8,128)}, f32[4,16,2880]{2,1,0:T(8,128)}, f32[4,16,2880]{2,1,0:T(8,128)}) fusion(f32[3,4,16,2880]{3,2,1,0:T(8,128)S(1)} %fusion.8), kind=kLoop, calls=%fused_computation.38 | loop fusion | bytes 4423680 | tf_op jit(solution)/shard_map/squeeze | solution.py:157
  (36 shorter events, 0.4 us)
Async XLA Ops:
  0.6 1.9 %copy-start = (f32[4,16,2880]{2,1,0:T(8,128)S(1)}, f32[4,16,2880]{2,1,0:T(8,128)}, u32[]{:S(2)}) copy-start(f32[4,16,2880]{2,1,0:T(8,128)} %param.23) | copy-start | bytes 2211844
  2.5 11.1 %copy-start.8 = (s32[10]{0:T(128)S(1)}, s32[10]{0:T(128)}, u32[]{:S(2)}) copy-start(s32[10]{0:T(128)} %constant.93.clone) | copy-start | bytes 124
  3.5 10.9 %collective-permute-start = (f32[4,16,2880]{2,1,0:T(8,128)}, f32[4,16,2880]{2,1,0:T(8,128)}, u32[]{:S(2)}, u32[]{:S(2)}) collective-permute-start(f32[4,16,2880]{2,1,0:T(8,128)} %pad_maximum_fusion.4), channel_id=1, source_target_pairs={{40,41},{41,42},{42,43},{43,44},{44,45},{45,46},{46,47},{48,49},{4... | collective-permute-start | bytes 2211848 | tf_op jit(solution)/shard_map/ppermute | solution.py:35
  6.0 8.4 %collective-permute-start.1 = (f32[4,16,2880]{2,1,0:T(8,128)}, f32[4,16,2880]{2,1,0:T(8,128)}, u32[]{:S(2)}, u32[]{:S(2)}) collective-permute-start(f32[4,16,2880]{2,1,0:T(8,128)} %pad_maximum_fusion.6), channel_id=1, source_target_pairs={{41,40},{42,41},{43,42},{44,43},{45,44},{46,45},{47,46},{49,48},{5... | collective-permute-start | bytes 2211848 | tf_op jit(solution)/shard_map/ppermute | solution.py:35
  8.4 35.6 %collective-permute-start.5 = (f32[3,4,1,2880]{3,2,1,0:T(1,128)}, f32[3,4,1,2880]{3,2,1,0:T(1,128)}, u32[]{:S(2)}, u32[]{:S(2)}) collective-permute-start(f32[3,4,1,2880]{3,2,1,0:T(1,128)} %get-tuple-element.133), channel_id=1, source_target_pairs={{40,32},{41,33},{42,34},{43,35},{44,36},{45,37},{46,38},{47,39},{4... | collective-permute-start | bytes 414728 | tf_op jit(solution)/shard_map/ppermute | solution.py:43
  9.7 37.2 %collective-permute-start.3 = (f32[3,4,1,2880]{3,2,1,0:T(1,128)S(1)}, f32[3,4,1,2880]{3,2,1,0:T(1,128)}, u32[]{:S(2)}, u32[]{:S(2)}) collective-permute-start(f32[3,4,1,2880]{3,2,1,0:T(1,128)S(1)} %get-tuple-element.134), channel_id=1, source_target_pairs={{40,48},{41,49},{42,50},{43,51},{44,52},{45,53},{46,54},{47,55},{4... | collective-permute-start | bytes 414728 | tf_op jit(solution)/shard_map/ppermute | solution.py:43
  14.5 1.7 %copy-start.7 = (s32[720]{0:T(1024)S(1)}, s32[720]{0:T(1024)}, u32[]{:S(2)}) copy-start(s32[720]{0:T(1024)} %constant.92.clone.2) | copy-start | bytes 8644 | tf_op jit(solution)/shard_map/cond
  18.1 2.2 %copy-start.1 = (f32[48,720]{1,0:T(8,128)S(1)}, f32[48,720]{1,0:T(8,128)}, u32[]{:S(2)}) copy-start(f32[48,720]{1,0:T(8,128)} %constant.83.clone.2) | copy-start | bytes 414724 | tf_op jit(solution)/shard_map/cond
  18.1 2.2 %copy-start.2 = (f32[48,720]{1,0:T(8,128)S(1)}, f32[48,720]{1,0:T(8,128)}, u32[]{:S(2)}) copy-start(f32[48,720]{1,0:T(8,128)} %constant.85.clone.2) | copy-start | bytes 414724 | tf_op jit(solution)/shard_map/cond
  18.1 2.2 %copy-start.3 = (f32[30,720]{1,0:T(8,128)S(1)}, f32[30,720]{1,0:T(8,128)}, u32[]{:S(2)}) copy-start(f32[30,720]{1,0:T(8,128)} %constant.84.clone.2) | copy-start | bytes 259204 | tf_op jit(solution)/shard_map/cond
  18.2 2.2 %copy-start.4 = (f32[30,720]{1,0:T(8,128)S(1)}, f32[30,720]{1,0:T(8,128)}, u32[]{:S(2)}) copy-start(f32[30,720]{1,0:T(8,128)} %constant.86.clone.2) | copy-start | bytes 259204 | tf_op jit(solution)/shard_map/cond
  20.4 0.7 copy-start.5
  20.4 0.7 copy-start.6
  28.3 17.8 %collective-permute-start.4 = (f32[3,4,1,2880]{3,2,1,0:T(1,128)S(1)}, f32[3,4,1,2880]{3,2,1,0:T(1,128)S(1)}, u32[]{:S(2)}, u32[]{:S(2)}) collective-permute-start(f32[3,4,1,2880]{3,2,1,0:T(1,128)S(1)} %get-tuple-element.135), channel_id=1, source_target_pairs={{8,0},{9,1},{10,2},{11,3},{12,4},{13,5},{14,6},{15,7},{16,8},{17,9... | collective-permute-start | bytes 414728 | tf_op jit(solution)/shard_map/ppermute | solution.py:43
  34.8 12.5 %collective-permute-start.2 = (f32[3,4,1,2880]{3,2,1,0:T(1,128)S(1)}, f32[3,4,1,2880]{3,2,1,0:T(1,128)S(1)}, u32[]{:S(2)}, u32[]{:S(2)}) collective-permute-start(f32[3,4,1,2880]{3,2,1,0:T(1,128)S(1)} %get-tuple-element.136), channel_id=1, source_target_pairs={{0,8},{1,9},{2,10},{3,11},{4,12},{5,13},{6,14},{7,15},{8,16},{9,17... | collective-permute-start | bytes 414728 | tf_op jit(solution)/shard_map/ppermute | solution.py:43
  36.2 47.4 %collective-permute-start.7 = (f32[4,16,2880]{2,1,0:T(8,128)S(1)}, f32[4,16,2880]{2,1,0:T(8,128)S(1)}, u32[]{:S(2)}, u32[]{:S(2)}) collective-permute-start(f32[4,16,2880]{2,1,0:T(8,128)S(1)} %pad_maximum_fusion.5), channel_id=1, source_target_pairs={{1,0},{2,1},{3,2},{4,3},{5,4},{6,5},{7,6},{9,8},{10,9},{11,10},{12... | collective-permute-start | bytes 2211848 | tf_op jit(solution)/shard_map/ppermute | solution.py:35
  44.0 47.5 %collective-permute-start.6 = (f32[4,16,2880]{2,1,0:T(8,128)S(1)}, f32[4,16,2880]{2,1,0:T(8,128)S(1)}, u32[]{:S(2)}, u32[]{:S(2)}) collective-permute-start(f32[4,16,2880]{2,1,0:T(8,128)S(1)} %pad_maximum_fusion.3), channel_id=1, source_target_pairs={{0,1},{1,2},{2,3},{3,4},{4,5},{5,6},{6,7},{8,9},{9,10},{10,11},{11... | collective-permute-start | bytes 2211848 | tf_op jit(solution)/shard_map/ppermute | solution.py:35
  46.1 3.0 %copy-start.9 = (f32[17]{0:T(128)S(1)}, f32[17]{0:T(128)}, u32[]{:S(2)}) copy-start(f32[17]{0:T(128)} %sine_multiply_fusion) | copy-start | bytes 208

commit v17 on v10

--- a/solution.py
+++ b/solution.py
@@ -111,8 +111,7 @@
     tables = (parity_table(0), parity_table(1))
     south_plain = lat_group_shift(stacked[:, :, lat_rows - 1 :], plain_lat, True)
     north_plain = lat_group_shift(stacked[:, :, :1], plain_lat, False)
-    stacked, below_plain, above_plain, south_plain, north_plain = lax.optimization_barrier(
-        (stacked, below_plain, above_plain, south_plain, north_plain))
+    stacked, below_plain, above_plain = lax.optimization_barrier((stacked, below_plain, above_plain))
     field = filtered(stacked, own_cut, tables)
     top = jnp.concatenate([field[:, levels - 1], vertical_wind[levels - 1 :]], axis=0)
     bottom = jnp.concatenate([field[:, 0], vertical_wind[:1]], axis=0)

time: 100 us -> 98.6 us (0.986)
  waiting for transfers between devices: 48.2 us -> 46.5 us
    ppermute x4, waiting for transfers between devices: 6.04 us -> 0.79 us  [lat_group_shift(): return lax.ppermute(x, ('lat', 'lev'), pairs)]
    ppermute x4, waiting for transfers between devices: 42.2 us -> 45.7 us  [group_shift(): return lax.ppermute(x, ('lat', 'lev'), pairs)]
  transfers between devices with their start and end apart: 8 -> 8, of which waited for: 5 -> 4; matrix products, arithmetic and copies ran while one was open for 7% -> 21% of each run, Pallas kernels for 0% -> 0%
where the time goes in v17:
time: 98.6 us; the launch traced here: 97.6 us
  waiting for transfers between devices  46.5 us (47%)
  starting transfers between devices  21.3 us (22%)
  other arithmetic  15.5 us (16%)
  matrix products  8.51 us (9%)
  local copies, waits for them, and re-layouts  4.01 us (4%)
  between operations  1.53 us (2%)
    ppermute x4, waiting for transfers between devices, group_shift(): return lax.ppermute(x, ('lat', 'lev'), pairs)  45.7 us
    ppermute x4, starting transfers between devices, group_shift(): return lax.ppermute(x, ('lat', 'lev'), pairs)  13.2 us
    ppermute x4, starting transfers between devices, lat_group_shift(): return lax.ppermute(x, ('lat', 'lev'), pairs)  8.17 us
    add x2, other arithmetic, parity_table(): as_f32(first)[None] * as_f32(np.cos(hi))[:, None]  2.34 us
    dot_general x1, matrix products, lowpass_rows(): lax.dot_general(spec_even * parity_weight(0, cut), even_table, dims, prec...  2.28 us
    dot_general x1, matrix products, lowpass_rows(): jnp.dot(first + second, even_table, precision=mxu_precision, preferred_el...  2.18 us
    dot_general x1, matrix products, lowpass_rows(): lax.dot_general(spec_odd * parity_weight(1, cut), odd_table, dims, precis...  2.14 us
  transfers between devices with their start and end apart: 8, of which 4 were waited for; matrix products, arithmetic and copies ran while one was open for 21% of the time, Pallas kernels for 0%

profile of v17, /device:TPU:47, one launch (start us, length us, event | category | flops | bytes accessed | tf_op | source)
XLA Modules:
  0.0 97.6 jit_solution(10101751150672174125)
XLA Ops:
  0.6 1.8 %pad_maximum_fusion = f32[3,4,16,2880]{3,2,1,0:T(8,128)S(1)} fusion(f32[1,4,16,2880]{3,2,1,0:T(8,128)} %bitcast.64, f32[1,4,16,2880]{3,2,1,0:T(8,128)} %bitcast.65, f32[1,4,16,2880]{3,2,1,0:T(8,128)} %bitcast.66), kind=kLoop, calls=%fused_computation.22 | loop fusion | flops 1105920 | bytes 4423680 | tf_op jit(solution)/shard_map/stack | solution.py:101
  2.4 0.1 slice_bitcast_fusion.7
  2.6 0.9 pad_maximum_fusion.4
  3.5 1.6 %collective-permute-start = (f32[4,16,2880]{2,1,0:T(8,128)}, f32[4,16,2880]{2,1,0:T(8,128)}, u32[]{:S(2)}, u32[]{:S(2)}) collective-permute-start(f32[4,16,2880]{2,1,0:T(8,128)} %pad_maximum_fusion.4), channel_id=1, source_target_pairs={{40,41},{41,42},{42,43},{43,44},{44,45},{45,46},{46,47},{48,49},{4... | collective-permute-start | bytes 2211848 | tf_op jit(solution)/shard_map/ppermute | solution.py:35
  5.1 0.9 pad_maximum_fusion.6
  6.0 1.6 %collective-permute-start.1 = (f32[4,16,2880]{2,1,0:T(8,128)}, f32[4,16,2880]{2,1,0:T(8,128)}, u32[]{:S(2)}, u32[]{:S(2)}) collective-permute-start(f32[4,16,2880]{2,1,0:T(8,128)} %pad_maximum_fusion.6), channel_id=1, source_target_pairs={{41,40},{42,41},{43,42},{44,43},{45,44},{46,45},{47,46},{49,48},{5... | collective-permute-start | bytes 2211848 | tf_op jit(solution)/shard_map/ppermute | solution.py:35
  7.6 0.9 fusion.19
  8.5 1.3 %collective-permute-start.7 = (f32[3,4,1,2880]{3,2,1,0:T(1,128)}, f32[3,4,1,2880]{3,2,1,0:T(1,128)}, u32[]{:S(2)}, u32[]{:S(2)}) collective-permute-start(f32[3,4,1,2880]{3,2,1,0:T(1,128)} %get-tuple-element.137), channel_id=1, source_target_pairs={{40,32},{41,33},{42,34},{43,35},{44,36},{45,37},{46,38},{47,39},{4... | collective-permute-start | bytes 414728 | tf_op jit(solution)/shard_map/ppermute | solution.py:43
  9.8 1.3 %collective-permute-start.5 = (f32[3,4,1,2880]{3,2,1,0:T(1,128)}, f32[3,4,1,2880]{3,2,1,0:T(1,128)S(1)}, u32[]{:S(2)}, u32[]{:S(2)}) collective-permute-start(f32[3,4,1,2880]{3,2,1,0:T(1,128)} %get-tuple-element.138), channel_id=1, source_target_pairs={{40,48},{41,49},{42,50},{43,51},{44,52},{45,53},{46,54},{47,55},{4... | collective-permute-start | bytes 414728 | tf_op jit(solution)/shard_map/ppermute | solution.py:43
  11.1 1.4 %compare_reduce_fusion.3 = (pred[]{:T(512)}, s32[16]{0:T(128)S(1)}) fusion(s32[512]{0:T(512)} %param.24, s32[]{:T(128)S(6)} %select_n.52), kind=kLoop, calls=%fused_computation.56 | loop fusion | flops 31 | bytes 133 | tf_op jit(solution)/shard_map/reduce_or | solution.py:89
  13.1 0.6 sine_multiply_fusion
  13.7 0.7 compare_reduce_fusion.1
  14.5 11.9 %conditional.1 = (f32[192,2880]{1,0:T(8,128)S(1)}) conditional(s32[]{:T(128)} %convert_element_type.17, f32[192,2880]{1,0:T(8,128)S(1)} %bitcast.45, (s32[16]{0:T(128)S(1)}, f32[192,2880]{1,0:T(8,128)S(1)}) %tuple.94), branch_computations={%region_1.0_spmd, %region_2.3_spmd.clone} | conditional | flops 4786836480 | bytes 46174092 | solution.py:89
  14.5 0.1 reshape.114
  14.6 1.7 %multiply_add_fusion = f32[30,48,720]{2,1,0:T(8,128)S(1)} fusion(f32[30,720]{1,0:T(8,128)} %constant.90.clone.2, f32[48,720]{1,0:T(8,128)} %constant.89.clone.2, f32[30,720]{1,0:T(8,128)} %constant.88.clone.2, f32[48,720]{1,0:T(8,128)} %constant.87.clone.2), kind=kLoop, calls=%fused_computation | loop fusion | flops 3110400 | bytes 4596480 | tf_op jit(solution)/shard_map/add | solution.py:57
  16.3 1.9 %convolution_multiply_fusion = f32[192,720]{1,0:T(8,128)S(1)} fusion(f32[1440,720]{1,0:T(8,128)S(1)} %bitcast.58, f32[192,2880]{1,0:T(8,128)S(1)} %get-tuple-element.123, s32[720]{0:T(1024)S(1)} %copy-done.7, s32[192]{0:T(256)S(1)} %reshape.114), kind=kOutput, calls=%fused_computation.3 | convolution fusion | flops 1195084800 | bytes 7341056 | tf_op jit(solution)/shard_map/cond/branch_1_fun/dot_general | solution.py:74
  18.3 2.1 %fusion.22 = f32[192,1440]{1,0:T(8,128)S(1)} fusion(f32[192,720]{1,0:T(8,128)S(1)} %convolution_multiply_fusion, f32[1440,720]{1,0:T(8,128)S(1)} %bitcast.59), kind=kOutput, calls=%fused_computation.63 | convolution fusion | flops 1194393600 | bytes 5806080 | tf_op jit(solution)/shard_map/cond/branch_1_fun/dot_general | solution.py:79
  20.5 0.6 multiply_add_fusion.1
  21.2 2.2 %convolution_multiply_fusion.1 = f32[192,720]{1,0:T(8,128)S(1)} fusion(f32[1440,720]{1,0:T(8,128)S(1)} %bitcast.56, f32[192,2880]{1,0:T(8,128)S(1)} %get-tuple-element.123, f32[720]{0:T(1024)S(1)} %copy-done.5, s32[720]{0:T(1024)S(1)} %copy-done.6, s32[192]{0:T(256)S(1)} %reshape.114), kind=kOutput, calls=%fused_computation.4 | convolution fusion | flops 1195084800 | bytes 7345152 | tf_op jit(solution)/shard_map/cond/branch_1_fun/dot_general | solution.py:72
  23.3 2.3 %fusion.18 = (f32[192,1440]{1,0:T(8,128)S(1)}, f32[192,1440]{1,0:T(8,128)S(1)}) fusion(f32[192,1440]{1,0:T(8,128)S(1)} %fusion.22, f32[192,720]{1,0:T(8,128)S(1)} %convolution_multiply_fusion.1, f32[1440,720]{1,0:T(8,128)S(1)} %bitcast.57), kind=kOutput, calls=%fused_computation.59 | convolution fusion | flops 1194946560 | bytes 8017920 | tf_op jit(solution)/shard_map/cond/branch_1_fun/dot_general | solution.py:77
  25.6 0.7 maximum_select_fusion
  26.4 0.3 slice.160
  26.7 0.6 slice.157
  27.4 0.1 slice_bitcast_fusion.5
  27.4 0.1 pad_maximum_fusion.5
  27.5 7.8 %collective-permute-start.3 = (f32[4,16,2880]{2,1,0:T(8,128)S(1)}, f32[4,16,2880]{2,1,0:T(8,128)S(1)}, u32[]{:S(2)}, u32[]{:S(2)}) collective-permute-start(f32[4,16,2880]{2,1,0:T(8,128)S(1)} %pad_maximum_fusion.5), channel_id=1, source_target_pairs={{1,0},{2,1},{3,2},{4,3},{5,4},{6,5},{7,6},{9,8},{10,9},{11,10},{12... | collective-permute-start | bytes 2211848 | tf_op jit(solution)/shard_map/ppermute | solution.py:35
  35.3 0.1 fusion.17
  35.4 0.4 fusion.12
  35.9 0.1 slice.162
  36.0 2.2 %collective-permute-start.2 = (f32[4,16,2880]{2,1,0:T(8,128)S(1)}, f32[4,16,2880]{2,1,0:T(8,128)S(1)}, u32[]{:S(2)}, u32[]{:S(2)}) collective-permute-start(f32[4,16,2880]{2,1,0:T(8,128)S(1)} %pad_maximum_fusion.3), channel_id=1, source_target_pairs={{0,1},{1,2},{2,3},{3,4},{4,5},{5,6},{6,7},{8,9},{9,10},{10,11},{11... | collective-permute-start | bytes 2211848 | tf_op jit(solution)/shard_map/ppermute | solution.py:35
  38.2 0.2 fusion.20
  38.4 24.3 %collective-permute-done.3 = f32[4,16,2880]{2,1,0:T(8,128)S(1)} collective-permute-done((f32[4,16,2880]{2,1,0:T(8,128)S(1)}, f32[4,16,2880]{2,1,0:T(8,128)S(1)}, u32[]{:S(2)}, u32[]{:S(2)}) %collective-permute-start.3) | collective-permute-done | bytes 737312 | tf_op jit(solution)/shard_map/ppermute | solution.py:35
  62.7 0.8 broadcast_select_fusion
  63.6 21.4 %collective-permute-done.2 = f32[4,16,2880]{2,1,0:T(8,128)S(1)} collective-permute-done((f32[4,16,2880]{2,1,0:T(8,128)S(1)}, f32[4,16,2880]{2,1,0:T(8,128)S(1)}, u32[]{:S(2)}, u32[]{:S(2)}) %collective-permute-start.2) | collective-permute-done | bytes 737312 | tf_op jit(solution)/shard_map/ppermute | solution.py:35
  84.9 0.8 broadcast_select_fusion.1
  85.7 1.9 %collective-permute-start.6 = (f32[3,4,1,2880]{3,2,1,0:T(1,128)S(1)}, f32[3,4,1,2880]{3,2,1,0:T(1,128)S(1)}, u32[]{:S(2)}, u32[]{:S(2)}) collective-permute-start(f32[3,4,1,2880]{3,2,1,0:T(1,128)S(1)} %get-tuple-element.99), channel_id=1, source_target_pairs={{8,0},{9,1},{10,2},{11,3},{12,4},{13,5},{14,6},{15,7},{16,8},{17,9... | collective-permute-start | bytes 414728 | tf_op jit(solution)/shard_map/ppermute | solution.py:43
  87.7 3.6 %collective-permute-start.4 = (f32[3,4,1,2880]{3,2,1,0:T(1,128)S(1)}, f32[3,4,1,2880]{3,2,1,0:T(1,128)S(1)}, u32[]{:S(2)}, u32[]{:S(2)}) collective-permute-start(f32[3,4,1,2880]{3,2,1,0:T(1,128)S(1)} %get-tuple-element.98), channel_id=1, source_target_pairs={{0,8},{1,9},{2,10},{3,11},{4,12},{5,13},{6,14},{7,15},{8,16},{9,17... | collective-permute-start | bytes 414728 | tf_op jit(solution)/shard_map/ppermute | solution.py:43
  91.3 0.1 fusion.16
  91.4 0.3 fusion.7
  91.8 0.4 collective-permute-done.6
  92.1 0.8 broadcast_select_fusion.2
  92.9 0.4 collective-permute-done.4
  93.3 0.8 broadcast_select_fusion.3
  94.1 0.2 fusion.15
  94.3 0.2 fusion.14
  94.5 0.6 fusion.6
  95.1 1.0 %fusion.8 = f32[3,4,16,2880]{3,2,1,0:T(8,128)S(1)} fusion(f32[3,5,16,2880]{3,2,1,0:T(8,128)S(1)} %fusion.7, f32[3,4,16,2880]{3,2,1,0:T(8,128)S(1)} %bitcast.55, f32[3,4,17,2880]{3,2,1,0:T(8,128)S(1)} %fusion.6, f32[3,4,16,2880]{3,2,1,0:T(8,128)S(1)} %fusion.12, f32[3,4,16,2879]{3,2,1,0:T(8,128)S(1)} %bitcast.60, f32[3,4,16,1]{3,2,1,0:T(8,128)S(1)} %slice.162, ...), kind=kLoop, calls=%fused_computation.17 | loop fusion | flops 4423680 | bytes 17694784 | tf_op jit(solution)/shard_map/sub | solution.py:158
  96.1 1.4 %slice_bitcast_fusion = (f32[4,16,2880]{2,1,0:T(8,128)}, f32[4,16,2880]{2,1,0:T(8,128)}, f32[4,16,2880]{2,1,0:T(8,128)}) fusion(f32[3,4,16,2880]{3,2,1,0:T(8,128)S(1)} %fusion.8), kind=kLoop, calls=%fused_computation.38 | loop fusion | bytes 4423680 | tf_op jit(solution)/shard_map/squeeze | solution.py:159
  (36 shorter events, 0.4 us)
Async XLA Ops:
  0.6 1.9 %copy-start = (f32[4,16,2880]{2,1,0:T(8,128)S(1)}, f32[4,16,2880]{2,1,0:T(8,128)}, u32[]{:S(2)}) copy-start(f32[4,16,2880]{2,1,0:T(8,128)} %param.23) | copy-start | bytes 2211844
  2.5 11.2 %copy-start.8 = (s32[10]{0:T(128)S(1)}, s32[10]{0:T(128)}, u32[]{:S(2)}) copy-start(s32[10]{0:T(128)} %constant.93.clone) | copy-start | bytes 124
  3.5 10.9 %collective-permute-start = (f32[4,16,2880]{2,1,0:T(8,128)}, f32[4,16,2880]{2,1,0:T(8,128)}, u32[]{:S(2)}, u32[]{:S(2)}) collective-permute-start(f32[4,16,2880]{2,1,0:T(8,128)} %pad_maximum_fusion.4), channel_id=1, source_target_pairs={{40,41},{41,42},{42,43},{43,44},{44,45},{45,46},{46,47},{48,49},{4... | collective-permute-start | bytes 2211848 | tf_op jit(solution)/shard_map/ppermute | solution.py:35
  6.0 8.4 %collective-permute-start.1 = (f32[4,16,2880]{2,1,0:T(8,128)}, f32[4,16,2880]{2,1,0:T(8,128)}, u32[]{:S(2)}, u32[]{:S(2)}) collective-permute-start(f32[4,16,2880]{2,1,0:T(8,128)} %pad_maximum_fusion.6), channel_id=1, source_target_pairs={{41,40},{42,41},{43,42},{44,43},{45,44},{46,45},{47,46},{49,48},{5... | collective-permute-start | bytes 2211848 | tf_op jit(solution)/shard_map/ppermute | solution.py:35
  8.5 83.3 %collective-permute-start.7 = (f32[3,4,1,2880]{3,2,1,0:T(1,128)}, f32[3,4,1,2880]{3,2,1,0:T(1,128)}, u32[]{:S(2)}, u32[]{:S(2)}) collective-permute-start(f32[3,4,1,2880]{3,2,1,0:T(1,128)} %get-tuple-element.137), channel_id=1, source_target_pairs={{40,32},{41,33},{42,34},{43,35},{44,36},{45,37},{46,38},{47,39},{4... | collective-permute-start | bytes 414728 | tf_op jit(solution)/shard_map/ppermute | solution.py:43
  9.8 83.1 %collective-permute-start.5 = (f32[3,4,1,2880]{3,2,1,0:T(1,128)}, f32[3,4,1,2880]{3,2,1,0:T(1,128)S(1)}, u32[]{:S(2)}, u32[]{:S(2)}) collective-permute-start(f32[3,4,1,2880]{3,2,1,0:T(1,128)} %get-tuple-element.138), channel_id=1, source_target_pairs={{40,48},{41,49},{42,50},{43,51},{44,52},{45,53},{46,54},{47,55},{4... | collective-permute-start | bytes 414728 | tf_op jit(solution)/shard_map/ppermute | solution.py:43
  14.6 1.7 %copy-start.7 = (s32[720]{0:T(1024)S(1)}, s32[720]{0:T(1024)}, u32[]{:S(2)}) copy-start(s32[720]{0:T(1024)} %constant.92.clone.2) | copy-start | bytes 8644 | tf_op jit(solution)/shard_map/cond
  18.2 2.2 %copy-start.1 = (f32[48,720]{1,0:T(8,128)S(1)}, f32[48,720]{1,0:T(8,128)}, u32[]{:S(2)}) copy-start(f32[48,720]{1,0:T(8,128)} %constant.83.clone.2) | copy-start | bytes 414724 | tf_op jit(solution)/shard_map/cond
  18.2 2.2 %copy-start.2 = (f32[48,720]{1,0:T(8,128)S(1)}, f32[48,720]{1,0:T(8,128)}, u32[]{:S(2)}) copy-start(f32[48,720]{1,0:T(8,128)} %constant.85.clone.2) | copy-start | bytes 414724 | tf_op jit(solution)/shard_map/cond
  18.2 2.2 %copy-start.3 = (f32[30,720]{1,0:T(8,128)S(1)}, f32[30,720]{1,0:T(8,128)}, u32[]{:S(2)}) copy-start(f32[30,720]{1,0:T(8,128)} %constant.84.clone.2) | copy-start | bytes 259204 | tf_op jit(solution)/shard_map/cond
  18.3 2.2 %copy-start.4 = (f32[30,720]{1,0:T(8,128)S(1)}, f32[30,720]{1,0:T(8,128)}, u32[]{:S(2)}) copy-start(f32[30,720]{1,0:T(8,128)} %constant.86.clone.2) | copy-start | bytes 259204 | tf_op jit(solution)/shard_map/cond
  20.4 0.7 copy-start.5
  20.5 0.7 copy-start.6
  27.5 35.2 %collective-permute-start.3 = (f32[4,16,2880]{2,1,0:T(8,128)S(1)}, f32[4,16,2880]{2,1,0:T(8,128)S(1)}, u32[]{:S(2)}, u32[]{:S(2)}) collective-permute-start(f32[4,16,2880]{2,1,0:T(8,128)S(1)} %pad_maximum_fusion.5), channel_id=1, source_target_pairs={{1,0},{2,1},{3,2},{4,3},{5,4},{6,5},{7,6},{9,8},{10,9},{11,10},{12... | collective-permute-start | bytes 2211848 | tf_op jit(solution)/shard_map/ppermute | solution.py:35
  36.0 48.9 %collective-permute-start.2 = (f32[4,16,2880]{2,1,0:T(8,128)S(1)}, f32[4,16,2880]{2,1,0:T(8,128)S(1)}, u32[]{:S(2)}, u32[]{:S(2)}) collective-permute-start(f32[4,16,2880]{2,1,0:T(8,128)S(1)} %pad_maximum_fusion.3), channel_id=1, source_target_pairs={{0,1},{1,2},{2,3},{3,4},{4,5},{5,6},{6,7},{8,9},{9,10},{10,11},{11... | collective-permute-start | bytes 2211848 | tf_op jit(solution)/shard_map/ppermute | solution.py:35
  85.7 6.4 %collective-permute-start.6 = (f32[3,4,1,2880]{3,2,1,0:T(1,128)S(1)}, f32[3,4,1,2880]{3,2,1,0:T(1,128)S(1)}, u32[]{:S(2)}, u32[]{:S(2)}) collective-permute-start(f32[3,4,1,2880]{3,2,1,0:T(1,128)S(1)} %get-tuple-element.99), channel_id=1, source_target_pairs={{8,0},{9,1},{10,2},{11,3},{12,4},{13,5},{14,6},{15,7},{16,8},{17,9... | collective-permute-start | bytes 414728 | tf_op jit(solution)/shard_map/ppermute | solution.py:43
  87.7 5.7 %collective-permute-start.4 = (f32[3,4,1,2880]{3,2,1,0:T(1,128)S(1)}, f32[3,4,1,2880]{3,2,1,0:T(1,128)S(1)}, u32[]{:S(2)}, u32[]{:S(2)}) collective-permute-start(f32[3,4,1,2880]{3,2,1,0:T(1,128)S(1)} %get-tuple-element.98), channel_id=1, source_target_pairs={{0,8},{1,9},{2,10},{3,11},{4,12},{5,13},{6,14},{7,15},{8,16},{9,17... | collective-permute-start | bytes 414728 | tf_op jit(solution)/shard_map/ppermute | solution.py:43
  92.1 2.1 %copy-start.9 = (f32[17]{0:T(128)S(1)}, f32[17]{0:T(128)}, u32[]{:S(2)}) copy-start(f32[17]{0:T(128)} %sine_multiply_fusion) | copy-start | bytes 208
